TPU v7x, 512 devices: a whole 4x8x8 slice. The times are simulated.
512 devices in a mesh: call: 8 (over z), tm: 64 (over x, y, core).
Axes of the slice: x: 4, y: 8, z: 8, core: 2. Of those that a mesh axis runs over, the one named last changes fastest.
Arguments:
- frames: bfloat16 [8, 8192, 1024], P('call', 'tm'), may hold values from -6 to 6
- lengths: int32 [8], replicated, may hold values from 2048 to 8192, as said below
- ln_attn_gain: float32 [1024], replicated, may hold values from 0.5 to 1.5
- w_qkv: bfloat16 [1024, 3072], P('tm'), may hold values from -0.1875 to 0.1875
- w_out: bfloat16 [1024, 1024], P('tm'), may hold values from -1.5 to 1.5
- ln_conv_gain: float32 [1024], replicated, may hold values from 0.5 to 1.5
- w_pw1: bfloat16 [1024, 2048], P('tm'), may hold values from -0.1875 to 0.1875
- dw_kernel: float32 [9, 1024], replicated, may hold values from -2 to 2
- bn_gain: float32 [1024], replicated, may hold values from 0.5 to 1.5
- bn_bias: float32 [1024], replicated, may hold values from -3 to 3
Outputs:
- attended: bfloat16 [8, 8192, 1024], P('call', 'tm')
- conv_act: bfloat16 [8, 8192, 1024], P('call', 'tm')
Inputs may be any that keep to these rules, and one draw needn't show every extreme that they name: `lengths`: valid frames of each call; at least one call of the batch fills all 8192 frames.
All inputs are finite; a program needn't handle non-finite values.
Results may differ from a plain program's by a relative error of at most 0.009.
Values may be sent and summed in bfloat16 or wider, within the bound.
No kernel may reach another device: no remote copies, remote signals or barrier semaphores. Data moves between devices by JAX's collectives and lax.ppermute only.
A program may use at most 64 MiB of HBM per device.

v0:
```python
import jax
import jax.numpy as jnp
from jax import lax
from jax.sharding import PartitionSpec as P

HEAD_DIM = 64
SPAN = 128
LEFT = 1024
KERNEL = 9


def passed_along(value, axis, steps):
    count = lax.axis_size(axis)
    first, last = (max(0, -steps), min(count, count - steps))
    return lax.ppermute(value, axis, [(source, source + steps) for source in range(first, last)])


def with_halo(cells, sides, width):
    for axis, dim in sides:
        count = lax.axis_size(axis)
        ends = count - 1
        head = lax.slice_in_dim(cells, 0, width, axis=dim)
        tail = lax.slice_in_dim(cells, cells.shape[dim] - width, cells.shape[dim], axis=dim)
        cells = jnp.concatenate(
            [
                lax.ppermute(tail, axis, [(i, (i + 1) % count) for i in range(ends)]),
                cells,
                lax.ppermute(head, axis, [((i + 1) % count, i) for i in range(ends)]),
            ],
            axis=dim,
        )
    return cells


def layer_norm(values, gain_vec):
    wide = values.astype(jnp.float32)
    center = wide - jnp.mean(wide, axis=-1, keepdims=True)
    spread = jnp.mean(center * center, axis=-1, keepdims=True)
    return center * lax.rsqrt(spread + 1e-05) * gain_vec


def contract_with(left, rows_piece):
    return jnp.dot(left, rows_piece, preferred_element_type=jnp.float32)


def on_device(
    frames, lengths, ln_attn_gain, w_qkv, w_out, ln_conv_gain, w_pw1, dw_kernel, bn_gain, bn_bias
):
    stream = frames[0]
    frame_count, model_width = stream.shape
    head_count = model_width // HEAD_DIM
    length = lax.dynamic_index_in_dim(lengths, lax.axis_index("call"), 0, keepdims=False)
    first_row = lax.axis_index("tm") * frame_count
    query_pos = first_row + jnp.arange(frame_count, dtype=jnp.int32)
    frame_valid = query_pos < length
    normed = layer_norm(stream, ln_attn_gain).astype(jnp.bfloat16)
    prior_blocks = LEFT // frame_count
    packed = contract_with(normed, lax.all_gather(w_qkv, "tm", axis=0, tiled=True))
    queries = packed[:, :model_width].astype(jnp.bfloat16)
    key_value = jnp.stack(
        [
            packed[:, model_width : 2 * model_width].astype(jnp.bfloat16),
            packed[:, 2 * model_width :].astype(jnp.bfloat16),
        ]
    )
    blocks = []
    current = key_value
    for hop_index in range(prior_blocks):
        current = passed_along(current, "tm", 1)
        blocks.append(current)
    context_kv = jnp.concatenate(blocks[::-1] + [key_value], axis=1)
    key_count = context_kv.shape[1]
    key_pos = first_row - prior_blocks * frame_count + jnp.arange(key_count, dtype=jnp.int32)
    span_first = query_pos // SPAN * SPAN
    allowed = (key_pos[None, :] >= 0) & (key_pos[None, :] >= span_first[:, None] - LEFT)
    allowed = allowed & (key_pos[None, :] < span_first[:, None] + SPAN)
    allowed = allowed & ((key_pos[None, :] < length) | (key_pos[None, :] == query_pos[:, None]))
    group_size = 4
    group_count = head_count // group_size
    query_groups = queries.reshape(frame_count, group_count, group_size, HEAD_DIM).transpose(
        1, 0, 2, 3
    )
    key_groups = (
        context_kv[0].reshape(key_count, group_count, group_size, HEAD_DIM).transpose(1, 0, 2, 3)
    )
    value_groups = (
        context_kv[1].reshape(key_count, group_count, group_size, HEAD_DIM).transpose(1, 0, 2, 3)
    )
    scale_factor = 1.0 / jnp.sqrt(jnp.float32(HEAD_DIM))

    def attend_group(operands):
        query_part, key_part, value_part = operands
        scores = (
            jnp.einsum("qhd,khd->hqk", query_part, key_part, preferred_element_type=jnp.float32)
            * scale_factor
        )
        raised = jnp.where(allowed[None], jnp.exp(scores), 0.0)
        probs = (raised / jnp.sum(raised, axis=-1, keepdims=True)).astype(jnp.bfloat16)
        mixed = jnp.einsum("hqk,khd->qhd", probs, value_part, preferred_element_type=jnp.float32)
        return mixed.astype(jnp.bfloat16)

    context = lax.map(attend_group, (query_groups, key_groups, value_groups))
    context = context.transpose(1, 0, 2, 3).reshape(frame_count, model_width)
    projected = contract_with(context, lax.all_gather(w_out, "tm", axis=0, tiled=True))
    attended = jnp.where(frame_valid[:, None], stream.astype(jnp.float32) + projected, 0.0).astype(
        jnp.bfloat16
    )
    conv_in = layer_norm(attended, ln_conv_gain).astype(jnp.bfloat16)
    expanded = contract_with(conv_in, lax.all_gather(w_pw1, "tm", axis=0, tiled=True))
    gated = expanded[:, :model_width] * jax.nn.sigmoid(expanded[:, model_width:])
    gated = jnp.where(frame_valid[:, None], gated, 0.0).astype(jnp.bfloat16)
    padded = with_halo(gated, (("tm", 0),), KERNEL // 2)
    depthwise = jnp.zeros((frame_count, model_width), jnp.float32)
    for tap_index in range(KERNEL):
        depthwise = (
            depthwise
            + padded[tap_index : tap_index + frame_count].astype(jnp.float32) * dw_kernel[tap_index]
        )
    masked = jnp.where(frame_valid[:, None], depthwise, 0.0)
    first_moment, second_moment = lax.psum(
        (jnp.sum(masked, axis=0), jnp.sum(masked * depthwise, axis=0)), ("call", "tm")
    )
    count_all = jnp.sum(lengths).astype(jnp.float32)
    average = first_moment / count_all
    second = second_moment / count_all
    normal_act = (depthwise - average) * lax.rsqrt(
        second - average * average + 1e-05
    ) * bn_gain + bn_bias
    activated = normal_act * jax.nn.sigmoid(normal_act)
    conv_act = jnp.where(frame_valid[:, None], activated, 0.0).astype(jnp.bfloat16)
    return (attended[None], conv_act[None])


def solution(mesh):
    return jax.shard_map(
        on_device,
        mesh=mesh,
        in_specs=(
            P("call", "tm", None),
            P(),
            P(),
            P("tm", None),
            P("tm", None),
            P(),
            P("tm", None),
            P(),
            P(),
            P(),
        ),
        out_specs=(P("call", "tm", None), P("call", "tm", None)),
        check_vma=False,
    )
```

profile of v0, /device:TPU:6, one launch (start us, length us, event | category | flops | bytes accessed | tf_op | source)
XLA Modules:
  0.0 388.8 jit_solution(18196588201639812604)
XLA Ops:
  11.0 89.1 %all-gather.4.cloned.1.call-done = bf16[1024,3072]{1,0:T(8,128)(2,1)} async-done(((bf16[16,3072]{1,0:T(8,128)(2,1)}), bf16[1024,3072]{1,0:T(8,128)(2,1)}) %all-gather.4.cloned.1.call-update) | async-done | bytes 6291472 | tf_op jit(solution)/shard_map/all_gather | solution.py:58
  100.1 4.0 %convolution_convert_fusion = bf16[128,3072]{1,0:T(8,128)(2,1)S(1)} fusion(bf16[1024,3072]{1,0:T(8,128)(2,1)} %all-gather.4.cloned.1.call-done, bf16[1,128,1024]{2,1,0:T(8,128)(2,1)} %param.12, f32[1024]{0:T(1024)} %param.14, f32[128]{0:T(128)S(1)} %add_rsqrt_fusion.2, f32[128]{0:T(128)S(1)} %broadcast_multiply_fusion.1), kind=kOutput, calls=%fused_computation.20 | convolution fusion | flops 806354944 | bytes 7345152 | tf_op jit(solution)/shard_map/dot_general | solution.py:43
  104.2 2.1 collective-permute-start
  106.3 10.5 %collective-permute-done = bf16[2,128,1024]{2,1,0:T(8,128)(2,1)S(1)} collective-permute-done((bf16[2,128,1024]{2,1,0:T(8,128)(2,1)S(1)}, bf16[2,128,1024]{2,1,0:T(8,128)(2,1)S(1)}, u32[]{:S(2)}, u32[]{:S(2)}) %collective-permute-start) | collective-permute-done | bytes 524320 | tf_op jit(solution)/shard_map/ppermute | solution.py:15
  118.7 11.1 %collective-permute-done.1 = bf16[2,128,1024]{2,1,0:T(8,128)(2,1)S(1)} collective-permute-done((bf16[2,128,1024]{2,1,0:T(8,128)(2,1)S(1)}, bf16[2,128,1024]{2,1,0:T(8,128)(2,1)S(1)}, u32[]{:S(2)}, u32[]{:S(2)}) %collective-permute-start.1) | collective-permute-done | bytes 524320 | tf_op jit(solution)/shard_map/ppermute | solution.py:15
  131.7 10.9 %collective-permute-done.2 = bf16[2,128,1024]{2,1,0:T(8,128)(2,1)S(1)} collective-permute-done((bf16[2,128,1024]{2,1,0:T(8,128)(2,1)S(1)}, bf16[2,128,1024]{2,1,0:T(8,128)(2,1)S(1)}, u32[]{:S(2)}, u32[]{:S(2)}) %collective-permute-start.2) | collective-permute-done | bytes 524320 | tf_op jit(solution)/shard_map/ppermute | solution.py:15
  144.5 10.7 %collective-permute-done.3 = bf16[2,128,1024]{2,1,0:T(8,128)(2,1)S(1)} collective-permute-done((bf16[2,128,1024]{2,1,0:T(8,128)(2,1)S(1)}, bf16[2,128,1024]{2,1,0:T(8,128)(2,1)S(1)}, u32[]{:S(2)}, u32[]{:S(2)}) %collective-permute-start.3) | collective-permute-done | bytes 524320 | tf_op jit(solution)/shard_map/ppermute | solution.py:15
  157.1 12.4 %collective-permute-done.4 = bf16[2,128,1024]{2,1,0:T(8,128)(2,1)S(1)} collective-permute-done((bf16[2,128,1024]{2,1,0:T(8,128)(2,1)S(1)}, bf16[2,128,1024]{2,1,0:T(8,128)(2,1)S(1)}, u32[]{:S(2)}, u32[]{:S(2)}) %collective-permute-start.4) | collective-permute-done | bytes 524320 | tf_op jit(solution)/shard_map/ppermute | solution.py:15
  169.5 1.9 collective-permute-start.5
  171.5 11.6 %collective-permute-done.5 = bf16[2,128,1024]{2,1,0:T(8,128)(2,1)} collective-permute-done((bf16[2,128,1024]{2,1,0:T(8,128)(2,1)S(1)}, bf16[2,128,1024]{2,1,0:T(8,128)(2,1)}, u32[]{:S(2)}, u32[]{:S(2)}) %collective-permute-start.5) | collective-permute-done | bytes 524320 | tf_op jit(solution)/shard_map/ppermute | solution.py:15
  183.0 1.9 collective-permute-start.6
  185.6 10.3 %collective-permute-done.6 = bf16[2,128,1024]{2,1,0:T(8,128)(2,1)} collective-permute-done((bf16[2,128,1024]{2,1,0:T(8,128)(2,1)}, bf16[2,128,1024]{2,1,0:T(8,128)(2,1)}, u32[]{:S(2)}, u32[]{:S(2)}) %collective-permute-start.6) | collective-permute-done | bytes 524320 | tf_op jit(solution)/shard_map/ppermute | solution.py:15
  195.9 1.9 collective-permute-start.7
  199.4 10.0 %collective-permute-done.7 = bf16[2,128,1024]{2,1,0:T(8,128)(2,1)} collective-permute-done((bf16[2,128,1024]{2,1,0:T(8,128)(2,1)}, bf16[2,128,1024]{2,1,0:T(8,128)(2,1)}, u32[]{:S(2)}, u32[]{:S(2)}) %collective-permute-start.7) | collective-permute-done | bytes 524320 | tf_op jit(solution)/shard_map/ppermute | solution.py:15
  213.9 2.0 fusion.57
  215.9 4.4 %copy.15 = bf16[1,1152,1024]{1,2,0:T(8,128)(2,1)} copy(bf16[1,1152,1024]{2,1,0:T(8,128)(2,1)} %get-tuple-element.93) | data formatting | bytes 4718592 | tf_op jit(solution)/shard_map/slice | solution.py:87
  220.3 2.6 copy.17
  222.9 15.3 %while.11 = (s32[]{:T(128)}, bf16[4,128,4,64]{1,3,2,0:T(8,128)(2,1)S(1)}, bf16[4,1152,4,64]{1,3,2,0:T(8,128)(2,1)}, bf16[4,128,4,64]{1,3,2,0:T(8,128)(2,1)S(1)},...) while((s32[]{:T(128)}, ...), condition=%wide.region_4.5_spmd.clone, body=%wide.region_2.4_spmd.clone.sunk | while | flops 154420864 | bytes 8694133 | solution.py:102
  238.2 2.1 convert_reduce_fusion
  240.6 28.4 %all-gather.8.cloned.1.call-done = bf16[1024,2048]{1,0:T(8,128)(2,1)} async-done(((bf16[16,2048]{1,0:T(8,128)(2,1)}), bf16[1024,2048]{1,0:T(8,128)(2,1)}) %all-gather.8.cloned.1.call-update) | async-done | bytes 4194320 | tf_op jit(solution)/shard_map/all_gather | solution.py:109
  269.0 3.0 fusion.45
  272.1 2.1 collective-permute-start.8
  274.3 5.5 %collective-permute-start.9 = (bf16[4,1024]{1,0:T(4,128)(2,1)S(1)}, bf16[4,1024]{1,0:T(4,128)(2,1)S(1)}, u32[]{:S(2)}, u32[]{:S(2)}) collective-permute-start(bf16[4,1024]{1,0:T(4,128)(2,1)S(1)} %get-tuple-element.98), channel_id=1, source_target_pairs={{1,0},{2,1},{3,2},{4,3},{5,4},{6,5},{7,6},{8,7},{9,8},{10,9},{11,1... | collective-permute-start | bytes 24584 | tf_op jit(solution)/shard_map/ppermute | solution.py:28
  281.9 99.5 %all-reduce = (f32[1024]{0:T(1024)S(1)}, f32[1024]{0:T(1024)S(1)}) all-reduce(f32[1024]{0:T(1024)S(1)} %get-tuple-element.66, f32[1024]{0:T(1024)S(1)} %get-tuple-element.65), channel_id=1, replica_groups=mesh['call'=8,'tm'=64] {'call','tm'}, use_global_device_ids=true, to_apply=%region_11.12 | all-reduce | flops 2048 | bytes 16384 | tf_op jit(solution)/shard_map/psum | solution.py:120
  (76 shorter events, 36.0 us)
Async XLA Ops:
  7.2 92.9 %all-gather.4.cloned.1.call-start = ((), (), s32[]{:S(2)}) async-start(), calls=%async_computation | async-start | bytes 6389760 | tf_op jit(solution)/shard_map/all_gather | solution.py:58
  7.9 230.3 %all-gather.6.cloned.1.call-start = ((), (), s32[]{:S(2)}) async-start(), calls=%async_computation.1 | async-start | bytes 2129920 | tf_op jit(solution)/shard_map/all_gather | solution.py:104
  8.6 260.3 %all-gather.8.cloned.1.call-start = ((), (), s32[]{:S(2)}) async-start(), calls=%async_computation.2 | async-start | bytes 4259840 | tf_op jit(solution)/shard_map/all_gather | solution.py:109
  10.9 174.0 %copy-start.8 = (s32[8]{0:T(128)S(1)}, s32[8]{0:T(128)}, u32[]{:S(2)}) copy-start(s32[8]{0:T(128)} %param.13) | copy-start | bytes 100
  104.2 12.6 %collective-permute-start = (bf16[2,128,1024]{2,1,0:T(8,128)(2,1)S(1)}, bf16[2,128,1024]{2,1,0:T(8,128)(2,1)S(1)}, u32[]{:S(2)}, u32[]{:S(2)}) collective-permute-start(bf16[2,128,1024]{2,1,0:T(8,128)(2,1)S(1)} %pad_maximum_fusion), channel_id=1, source_target_pairs={{0,1},{1,2},{2,3},{3,4},{4,5},{5,6},{6,7},{7,8},{8,9},{9,10},{10,1... | collective-permute-start | bytes 1572872 | tf_op jit(solution)/shard_map/ppermute | solution.py:15
  116.8 13.0 %collective-permute-start.1 = (bf16[2,128,1024]{2,1,0:T(8,128)(2,1)S(1)}, bf16[2,128,1024]{2,1,0:T(8,128)(2,1)S(1)}, u32[]{:S(2)}, u32[]{:S(2)}) collective-permute-start(bf16[2,128,1024]{2,1,0:T(8,128)(2,1)S(1)} %collective-permute-done), channel_id=1, source_target_pairs={{0,1},{1,2},{2,3},{3,4},{4,5},{5,6},{6,7},{7,8},{8,9},{9,10},{10,1... | collective-permute-start | bytes 1572872 | tf_op jit(solution)/shard_map/ppermute | solution.py:15
  129.8 12.8 %collective-permute-start.2 = (bf16[2,128,1024]{2,1,0:T(8,128)(2,1)S(1)}, bf16[2,128,1024]{2,1,0:T(8,128)(2,1)S(1)}, u32[]{:S(2)}, u32[]{:S(2)}) collective-permute-start(bf16[2,128,1024]{2,1,0:T(8,128)(2,1)S(1)} %collective-permute-done.1), channel_id=1, source_target_pairs={{0,1},{1,2},{2,3},{3,4},{4,5},{5,6},{6,7},{7,8},{8,9},{9,10},{10,1... | collective-permute-start | bytes 1572872 | tf_op jit(solution)/shard_map/ppermute | solution.py:15
  142.6 12.6 %collective-permute-start.3 = (bf16[2,128,1024]{2,1,0:T(8,128)(2,1)S(1)}, bf16[2,128,1024]{2,1,0:T(8,128)(2,1)S(1)}, u32[]{:S(2)}, u32[]{:S(2)}) collective-permute-start(bf16[2,128,1024]{2,1,0:T(8,128)(2,1)S(1)} %collective-permute-done.2), channel_id=1, source_target_pairs={{0,1},{1,2},{2,3},{3,4},{4,5},{5,6},{6,7},{7,8},{8,9},{9,10},{10,1... | collective-permute-start | bytes 1572872 | tf_op jit(solution)/shard_map/ppermute | solution.py:15
  155.2 14.4 %collective-permute-start.4 = (bf16[2,128,1024]{2,1,0:T(8,128)(2,1)S(1)}, bf16[2,128,1024]{2,1,0:T(8,128)(2,1)S(1)}, u32[]{:S(2)}, u32[]{:S(2)}) collective-permute-start(bf16[2,128,1024]{2,1,0:T(8,128)(2,1)S(1)} %collective-permute-done.3), channel_id=1, source_target_pairs={{0,1},{1,2},{2,3},{3,4},{4,5},{5,6},{6,7},{7,8},{8,9},{9,10},{10,1... | collective-permute-start | bytes 1572872 | tf_op jit(solution)/shard_map/ppermute | solution.py:15
  169.5 29.7 %copy-start.2 = (bf16[2,128,1024]{2,1,0:T(8,128)(2,1)}, bf16[2,128,1024]{2,1,0:T(8,128)(2,1)S(1)}, u32[]{:S(2)}) copy-start(bf16[2,128,1024]{2,1,0:T(8,128)(2,1)S(1)} %collective-permute-done.4) | copy-start | bytes 1572868
  169.5 13.5 %collective-permute-start.5 = (bf16[2,128,1024]{2,1,0:T(8,128)(2,1)S(1)}, bf16[2,128,1024]{2,1,0:T(8,128)(2,1)}, u32[]{:S(2)}, u32[]{:S(2)}) collective-permute-start(bf16[2,128,1024]{2,1,0:T(8,128)(2,1)S(1)} %collective-permute-done.4), channel_id=1, source_target_pairs={{0,1},{1,2},{2,3},{3,4},{4,5},{5,6},{6,7},{7,8},{8,9},{9,10},{10,1... | collective-permute-start | bytes 1572872 | tf_op jit(solution)/shard_map/ppermute | solution.py:15
  183.0 12.9 %collective-permute-start.6 = (bf16[2,128,1024]{2,1,0:T(8,128)(2,1)}, bf16[2,128,1024]{2,1,0:T(8,128)(2,1)}, u32[]{:S(2)}, u32[]{:S(2)}) collective-permute-start(bf16[2,128,1024]{2,1,0:T(8,128)(2,1)} %collective-permute-done.5), channel_id=1, source_target_pairs={{0,1},{1,2},{2,3},{3,4},{4,5},{5,6},{6,7},{7,8},{8,9},{9,10},{10,1... | collective-permute-start | bytes 1572872 | tf_op jit(solution)/shard_map/ppermute | solution.py:15
  195.9 13.4 %collective-permute-start.7 = (bf16[2,128,1024]{2,1,0:T(8,128)(2,1)}, bf16[2,128,1024]{2,1,0:T(8,128)(2,1)}, u32[]{:S(2)}, u32[]{:S(2)}) collective-permute-start(bf16[2,128,1024]{2,1,0:T(8,128)(2,1)} %collective-permute-done.6), channel_id=1, source_target_pairs={{0,1},{1,2},{2,3},{3,4},{4,5},{5,6},{6,7},{7,8},{8,9},{9,10},{10,1... | collective-permute-start | bytes 1572872 | tf_op jit(solution)/shard_map/ppermute | solution.py:15
  215.9 7.0 %copy-start.3 = (bf16[4,128,4,64]{1,3,2,0:T(8,128)(2,1)S(1)}, bf16[4,128,4,64]{1,3,2,0:T(8,128)(2,1)}, u32[]{:S(2)}) copy-start(bf16[4,128,4,64]{1,3,2,0:T(8,128)(2,1)} %custom-call.1) | copy-start | bytes 786436
  222.9 15.3 %copy-start = (bf16[1,128,1024]{2,1,0:T(8,128)(2,1)S(1)}, bf16[1,128,1024]{2,1,0:T(8,128)(2,1)}, u32[]{:S(2)}) copy-start(bf16[1,128,1024]{2,1,0:T(8,128)(2,1)} %param.12) | copy-start | bytes 786436
  222.9 46.1 %copy-start.7 = (f32[1024]{0:T(1024)S(1)}, f32[1024]{0:T(1024)}, u32[]{:S(2)}) copy-start(f32[1024]{0:T(1024)} %param.17) | copy-start | bytes 12292
  240.3 142.0 %copy-start.1 = (bf16[128,1024]{1,0:T(8,128)(2,1)}, bf16[128,1024]{1,0:T(8,128)(2,1)S(1)}, u32[]{:S(2)}) copy-start(bf16[128,1024]{1,0:T(8,128)(2,1)S(1)} %get-tuple-element.111) | copy-start | bytes 786436
  240.3 39.5 %copy-start.4 = (f32[9,1024]{1,0:T(8,128)S(1)}, f32[9,1024]{1,0:T(8,128)}, u32[]{:S(2)}) copy-start(f32[9,1024]{1,0:T(8,128)} %param.19) | copy-start | bytes 110596
  240.4 141.0 %copy-start.5 = (f32[1024]{0:T(1024)S(1)}, f32[1024]{0:T(1024)}, u32[]{:S(2)}) copy-start(f32[1024]{0:T(1024)} %param.21) | copy-start | bytes 12292
  240.4 141.0 %copy-start.6 = (f32[1024]{0:T(1024)S(1)}, f32[1024]{0:T(1024)}, u32[]{:S(2)}) copy-start(f32[1024]{0:T(1024)} %param.20) | copy-start | bytes 12292
  272.1 9.0 %collective-permute-start.8 = (bf16[4,1024]{1,0:T(4,128)(2,1)S(1)}, bf16[4,1024]{1,0:T(4,128)(2,1)S(1)}, u32[]{:S(2)}, u32[]{:S(2)}) collective-permute-start(bf16[4,1024]{1,0:T(4,128)(2,1)S(1)} %get-tuple-element.97), channel_id=1, source_target_pairs={{0,1},{1,2},{2,3},{3,4},{4,5},{5,6},{6,7},{7,8},{8,9},{9,10},{10,1... | collective-permute-start | bytes 24584 | tf_op jit(solution)/shard_map/ppermute | solution.py:26
  274.3 6.9 %collective-permute-start.9 = (bf16[4,1024]{1,0:T(4,128)(2,1)S(1)}, bf16[4,1024]{1,0:T(4,128)(2,1)S(1)}, u32[]{:S(2)}, u32[]{:S(2)}) collective-permute-start(bf16[4,1024]{1,0:T(4,128)(2,1)S(1)} %get-tuple-element.98), channel_id=1, source_target_pairs={{1,0},{2,1},{3,2},{4,3},{5,4},{6,5},{7,6},{8,7},{9,8},{10,9},{11,1... | collective-permute-start | bytes 24584 | tf_op jit(solution)/shard_map/ppermute | solution.py:28
Sparse Core Ops, SparseCore 0:
  11.3 88.7 all-gather.3
  103.4 80.3 all-gather.5
  187.2 81.7 all-gather.7
where the time goes:
time: 392 us; the launch traced here: 389 us
  waiting for transfers between devices  206 us (53%)
  blocking collectives  99.5 us (25%)
  starting transfers between devices  23.3 us (6%)
  matrix products  23 us (6%)
  between operations  14.8 us (4%)
  local copies, waits for them, and re-layouts  14.4 us (4%)
  other arithmetic  7.46 us (2%)
    psum x1, blocking collectives, on_device(): lax.psum((jnp.sum(masked, axis=0), jnp.sum(masked * depthwise, axis=0)),...  99.5 us
    all_gather x1, waiting for transfers between devices, on_device(): lax.all_gather(w_qkv, 'tm', axis=0, tiled=True)  89.1 us
    ppermute x8, waiting for transfers between devices, passed_along(): lax.ppermute(value, axis, [(source, source + steps) for source in range(f...  87.4 us
    all_gather x1, waiting for transfers between devices, on_device(): lax.all_gather(w_pw1, 'tm', axis=0, tiled=True)  28.4 us
    ppermute x8, starting transfers between devices, passed_along(): lax.ppermute(value, axis, [(source, source + steps) for source in range(f...  15.5 us
    dot_general x3, matrix products, contract_with(): return jnp.dot(left, rows_piece, preferred_element_type=jnp.float32)  9.08 us
  transfers between devices with their start and end apart: 13, of which 10 were waited for; matrix products, arithmetic and copies ran while one was open for 10% of the time, Pallas kernels for 0%

commit v1 on v0

v1 whole, which is shorter than its diff:
```python
import jax
import jax.numpy as jnp
import numpy as np
from jax import lax
from jax.sharding import Mesh
from jax.sharding import PartitionSpec as P

HEAD_DIM = 64
SPAN = 128
LEFT = 1024
KERNEL = 9
TM = ("x", "y", "core")


def passed_along(value, axis, steps):
    count = lax.axis_size(axis)
    first, last = (max(0, -steps), min(count, count - steps))
    return lax.ppermute(value, axis, [(source, source + steps) for source in range(first, last)])


def with_halo(cells, axis, width):
    count = lax.axis_size(axis)
    ends = count - 1
    head = lax.slice_in_dim(cells, 0, width, axis=0)
    tail = lax.slice_in_dim(cells, cells.shape[0] - width, cells.shape[0], axis=0)
    return jnp.concatenate(
        [
            lax.ppermute(tail, axis, [(i, (i + 1) % count) for i in range(ends)]),
            cells,
            lax.ppermute(head, axis, [((i + 1) % count, i) for i in range(ends)]),
        ],
        axis=0,
    )


def layer_norm(values, gain_vec):
    wide = values.astype(jnp.float32)
    center = wide - jnp.mean(wide, axis=-1, keepdims=True)
    spread = jnp.mean(center * center, axis=-1, keepdims=True)
    return center * lax.rsqrt(spread + 1e-05) * gain_vec


def contract_with(left, rows_piece):
    return jnp.dot(left, rows_piece, preferred_element_type=jnp.float32)


def on_device(
    frames, lengths, ln_attn_gain, w_qkv, w_out, ln_conv_gain, w_pw1, dw_kernel, bn_gain, bn_bias
):
    stream = frames[0]
    frame_count, model_width = stream.shape
    head_count = model_width // HEAD_DIM
    length = lax.dynamic_index_in_dim(lengths, lax.axis_index("call"), 0, keepdims=False)
    first_row = lax.axis_index(TM) * frame_count
    query_pos = first_row + jnp.arange(frame_count, dtype=jnp.int32)
    frame_valid = query_pos < length
    qkv_cols = w_qkv.shape[1]
    out_cols = w_out.shape[1]
    weights = lax.all_gather(
        jnp.concatenate([w_qkv, w_out, w_pw1], axis=1), TM, axis=0, tiled=True
    )
    prior_blocks = LEFT // frame_count
    blocks = []
    current = stream
    for hop_index in range(prior_blocks):
        current = passed_along(current, TM, 1)
        blocks.append(current)
    context_frames = jnp.concatenate(blocks[::-1] + [stream], axis=0)
    key_count = context_frames.shape[0]
    normed_all = layer_norm(context_frames, ln_attn_gain).astype(jnp.bfloat16)
    normed = normed_all[key_count - frame_count :]
    queries = contract_with(normed, weights[:, :model_width]).astype(jnp.bfloat16)
    key_value = contract_with(normed_all, weights[:, model_width:qkv_cols])
    keys = key_value[:, :model_width].astype(jnp.bfloat16)
    values = key_value[:, model_width:].astype(jnp.bfloat16)
    key_pos = first_row - prior_blocks * frame_count + jnp.arange(key_count, dtype=jnp.int32)
    span_first = query_pos // SPAN * SPAN
    allowed = (key_pos[None, :] >= 0) & (key_pos[None, :] >= span_first[:, None] - LEFT)
    allowed = allowed & (key_pos[None, :] < span_first[:, None] + SPAN)
    allowed = allowed & ((key_pos[None, :] < length) | (key_pos[None, :] == query_pos[:, None]))
    group_size = 4
    group_count = head_count // group_size
    query_groups = queries.reshape(frame_count, group_count, group_size, HEAD_DIM).transpose(
        1, 0, 2, 3
    )
    key_groups = keys.reshape(key_count, group_count, group_size, HEAD_DIM).transpose(1, 0, 2, 3)
    value_groups = values.reshape(key_count, group_count, group_size, HEAD_DIM).transpose(
        1, 0, 2, 3
    )
    scale_factor = 1.0 / jnp.sqrt(jnp.float32(HEAD_DIM))

    def attend_group(operands):
        query_part, key_part, value_part = operands
        scores = (
            jnp.einsum("qhd,khd->hqk", query_part, key_part, preferred_element_type=jnp.float32)
            * scale_factor
        )
        raised = jnp.where(allowed[None], jnp.exp(scores), 0.0)
        probs = (raised / jnp.sum(raised, axis=-1, keepdims=True)).astype(jnp.bfloat16)
        mixed = jnp.einsum("hqk,khd->qhd", probs, value_part, preferred_element_type=jnp.float32)
        return mixed.astype(jnp.bfloat16)

    context = lax.map(attend_group, (query_groups, key_groups, value_groups))
    context = context.transpose(1, 0, 2, 3).reshape(frame_count, model_width)
    projected = contract_with(context, weights[:, qkv_cols : qkv_cols + out_cols])
    attended = jnp.where(frame_valid[:, None], stream.astype(jnp.float32) + projected, 0.0).astype(
        jnp.bfloat16
    )
    conv_in = layer_norm(attended, ln_conv_gain).astype(jnp.bfloat16)
    expanded = contract_with(conv_in, weights[:, qkv_cols + out_cols :])
    gated = expanded[:, :model_width] * jax.nn.sigmoid(expanded[:, model_width:])
    gated = jnp.where(frame_valid[:, None], gated, 0.0).astype(jnp.bfloat16)
    padded = with_halo(gated, TM, KERNEL // 2)
    depthwise = jnp.zeros((frame_count, model_width), jnp.float32)
    for tap_index in range(KERNEL):
        depthwise = (
            depthwise
            + padded[tap_index : tap_index + frame_count].astype(jnp.float32) * dw_kernel[tap_index]
        )
    masked = jnp.where(frame_valid[:, None], depthwise, 0.0)
    moments = (jnp.sum(masked, axis=0), jnp.sum(masked * depthwise, axis=0))
    for axis in ("core", "y", "x", "call"):
        moments = lax.psum(moments, axis)
    first_moment, second_moment = moments
    count_all = jnp.sum(lengths).astype(jnp.float32)
    average = first_moment / count_all
    second = second_moment / count_all
    normal_act = (depthwise - average) * lax.rsqrt(
        second - average * average + 1e-05
    ) * bn_gain + bn_bias
    activated = normal_act * jax.nn.sigmoid(normal_act)
    conv_act = jnp.where(frame_valid[:, None], activated, 0.0).astype(jnp.bfloat16)
    return (attended[None], conv_act[None])


def physical_mesh(mesh):
    devices = mesh.devices
    calls, tms = devices.shape
    first = devices[0]
    xs = len({d.coords[0] for d in first})
    ys = len({d.coords[1] for d in first})
    cores = tms // (xs * ys)
    grid = np.array(
        [[(d.coords[0], d.coords[1], d.core_on_chip) for d in row] for row in devices]
    )
    expect = np.stack(
        np.meshgrid(np.arange(xs), np.arange(ys), np.arange(cores), indexing="ij"), -1
    ).reshape(-1, 3)
    grid = grid - grid[:, :1]
    assert (grid == expect[None]).all()
    return Mesh(devices.reshape(calls, xs, ys, cores), ("call",) + TM)


def solution(mesh):
    mesh4 = physical_mesh(mesh)
    rows = P(TM, None)
    stream = P("call", TM, None)
    return jax.shard_map(
        on_device,
        mesh=mesh4,
        in_specs=(stream, P(), P(), rows, rows, P(), rows, P(), P(), P()),
        out_specs=(stream, stream),
        check_vma=False,
    )
```

time: 392 us -> 219 us (0.56)
  waiting for transfers between devices: 206 us -> 82.2 us
  blocking collectives: 99.5 us -> 48.6 us
  matrix products: 23 us -> 28.6 us
    all_gather x3 -> x1, waiting for transfers between devices: 118 us -> 6.57 us  [on_device(): lax.all_gather(jnp.concatenate([w_qkv, w_out, w_pw1], axis=1), TM, axis=0...]
    psum x1 -> x4, blocking collectives: 99.5 us -> 48.6 us  [on_device(): moments = lax.psum(moments, axis)]
    ppermute x8, waiting for transfers between devices: 87.4 us -> 75.6 us  [passed_along(): lax.ppermute(value, axis, [(source, source + steps) for source in range(f...]
    dot_general x3 -> x4, matrix products: 9.08 us -> 14.7 us  [contract_with(): return jnp.dot(left, rows_piece, preferred_element_type=jnp.float32)]
    unnamed x26 -> x24, local copies, waits for them, and re-layouts: 4.5 us -> 0.2 us
    slice x6 -> x4, local copies, waits for them, and re-layouts: 9.19 us -> 8.84 us  [the longest x2 6.23 us: on_device(): keys = key_value[:, :model_width].astype(jnp.bfloat16)]
  transfers between devices with their start and end apart: 13 -> 11, of which waited for: 10 -> 9; matrix products, arithmetic and copies ran while one was open for 10% -> 2% of each run, Pallas kernels for 0% -> 0%
where the time goes in v1:
time: 219 us; the launch traced here: 217 us
  waiting for transfers between devices  82.2 us (38%)
  blocking collectives  48.6 us (22%)
  matrix products  28.6 us (13%)
  starting transfers between devices  23 us (11%)
  between operations  15.1 us (7%)
  local copies, waits for them, and re-layouts  10.5 us (5%)
  other arithmetic  8.67 us (4%)
    ppermute x8, waiting for transfers between devices, passed_along(): lax.ppermute(value, axis, [(source, source + steps) for source in range(f...  75.6 us
    psum x4, blocking collectives, on_device(): moments = lax.psum(moments, axis)  48.6 us
    ppermute x8, starting transfers between devices, passed_along(): lax.ppermute(value, axis, [(source, source + steps) for source in range(f...  15.3 us
    dot_general x4, matrix products, contract_with(): return jnp.dot(left, rows_piece, preferred_element_type=jnp.float32)  14.7 us
    dot_general x4, matrix products, attend_group(): jnp.einsum('hqk,khd->qhd', probs, value_part, preferred_element_type=jnp....  7 us
    dot_general x4, matrix products, attend_group(): jnp.einsum('qhd,khd->hqk', query_part, key_part, preferred_element_type=j...  6.94 us
    all_gather x1, waiting for transfers between devices, on_device(): lax.all_gather(jnp.concatenate([w_qkv, w_out, w_pw1], axis=1), TM, axis=0...  6.57 us
    slice x2, local copies, waits for them, and re-layouts, on_device(): keys = key_value[:, :model_width].astype(jnp.bfloat16)  6.23 us
  transfers between devices with their start and end apart: 11, of which 9 were waited for; matrix products, arithmetic and copies ran while one was open for 2% of the time, Pallas kernels for 0%

profile of v1, /device:TPU:6, one launch (start us, length us, event | category | flops | bytes accessed | tf_op | source)
XLA Modules:
  0.0 216.8 jit_solution(7819560203503129350)
XLA Ops:
  8.9 1.9 collective-permute-start
  10.8 8.1 %collective-permute-done = bf16[128,1024]{1,0:T(8,128)(2,1)S(1)} collective-permute-done((bf16[128,1024]{1,0:T(8,128)(2,1)}, bf16[128,1024]{1,0:T(8,128)(2,1)S(1)}, u32[]{:S(2)}, u32[]{:S(2)}) %collective-permute-start) | collective-permute-done | bytes 262176 | tf_op jit(solution)/shard_map/ppermute | solution.py:18
  18.9 1.9 collective-permute-start.1
  20.8 7.9 %collective-permute-done.1 = bf16[128,1024]{1,0:T(8,128)(2,1)S(1)} collective-permute-done((bf16[128,1024]{1,0:T(8,128)(2,1)S(1)}, bf16[128,1024]{1,0:T(8,128)(2,1)S(1)}, u32[]{:S(2)}, u32[]{:S(2)}) %collective-permute-start.1) | collective-permute-done | bytes 262176 | tf_op jit(solution)/shard_map/ppermute | solution.py:18
  30.6 9.5 %collective-permute-done.2 = bf16[128,1024]{1,0:T(8,128)(2,1)S(1)} collective-permute-done((bf16[128,1024]{1,0:T(8,128)(2,1)S(1)}, bf16[128,1024]{1,0:T(8,128)(2,1)S(1)}, u32[]{:S(2)}, u32[]{:S(2)}) %collective-permute-start.2) | collective-permute-done | bytes 262176 | tf_op jit(solution)/shard_map/ppermute | solution.py:18
  42.1 9.7 %collective-permute-done.3 = bf16[128,1024]{1,0:T(8,128)(2,1)S(1)} collective-permute-done((bf16[128,1024]{1,0:T(8,128)(2,1)S(1)}, bf16[128,1024]{1,0:T(8,128)(2,1)S(1)}, u32[]{:S(2)}, u32[]{:S(2)}) %collective-permute-start.3) | collective-permute-done | bytes 262176 | tf_op jit(solution)/shard_map/ppermute | solution.py:18
  53.7 7.9 %collective-permute-done.4 = bf16[128,1024]{1,0:T(8,128)(2,1)S(1)} collective-permute-done((bf16[128,1024]{1,0:T(8,128)(2,1)S(1)}, bf16[128,1024]{1,0:T(8,128)(2,1)S(1)}, u32[]{:S(2)}, u32[]{:S(2)}) %collective-permute-start.4) | collective-permute-done | bytes 262176 | tf_op jit(solution)/shard_map/ppermute | solution.py:18
  63.5 7.9 %collective-permute-done.5 = bf16[128,1024]{1,0:T(8,128)(2,1)S(1)} collective-permute-done((bf16[128,1024]{1,0:T(8,128)(2,1)S(1)}, bf16[128,1024]{1,0:T(8,128)(2,1)S(1)}, u32[]{:S(2)}, u32[]{:S(2)}) %collective-permute-start.5) | collective-permute-done | bytes 262176 | tf_op jit(solution)/shard_map/ppermute | solution.py:18
  74.6 12.3 %collective-permute-done.6 = bf16[128,1024]{1,0:T(8,128)(2,1)S(1)} collective-permute-done((bf16[128,1024]{1,0:T(8,128)(2,1)S(1)}, bf16[128,1024]{1,0:T(8,128)(2,1)S(1)}, u32[]{:S(2)}, u32[]{:S(2)}) %collective-permute-start.6) | collective-permute-done | bytes 262176 | tf_op jit(solution)/shard_map/ppermute | solution.py:18
  90.0 12.4 %collective-permute-done.7 = bf16[128,1024]{1,0:T(8,128)(2,1)S(1)} collective-permute-done((bf16[128,1024]{1,0:T(8,128)(2,1)S(1)}, bf16[128,1024]{1,0:T(8,128)(2,1)S(1)}, u32[]{:S(2)}, u32[]{:S(2)}) %collective-permute-start.7) | collective-permute-done | bytes 262176 | tf_op jit(solution)/shard_map/ppermute | solution.py:18
  104.6 6.6 %all-gather.2.cloned.1.call-done = bf16[1024,6144]{1,0:T(8,128)(2,1)} async-done(((bf16[16,6144]{1,0:T(8,128)(2,1)}), bf16[1024,6144]{1,0:T(8,128)(2,1)}) %all-gather.2.cloned.1.call-update) | async-done | bytes 12582928 | tf_op jit(solution)/shard_map/all_gather | solution.py:59
  111.2 2.0 fusion.39
  113.4 7.4 %convolution_convert_fusion = bf16[1152,2048]{1,0:T(8,128)(2,1)S(1)} fusion(bf16[1152,1024]{1,0:T(8,128)(2,1)S(1)} %fusion.22, bf16[1024,6144]{1,0:T(8,128)(2,1)} %all-gather.2.cloned.1.call-done), kind=kOutput, calls=%fused_computation.20 | convolution fusion | flops 4834197504 | bytes 11272192 | tf_op jit(solution)/shard_map/dot_general | solution.py:44
  122.8 4.3 %copy.17 = bf16[1152,1024]{0,1:T(8,128)(2,1)} copy(bf16[1152,1024]{1,0:T(8,128)(2,1)} %get-tuple-element.98) | data formatting | bytes 4718592 | tf_op jit(solution)/shard_map/slice | solution.py:74
  127.1 2.6 %copy.15 = bf16[1152,1024]{0,1:T(8,128)(2,1)} copy(bf16[1152,1024]{1,0:T(8,128)(2,1)S(1)} %get-tuple-element.99) | data formatting | bytes 4718592 | tf_op jit(solution)/shard_map/slice | solution.py:75
  129.7 15.3 %while.11 = (s32[]{:T(128)}, bf16[4,128,4,64]{1,3,2,0:T(8,128)(2,1)S(1)}, bf16[4,1152,4,64]{1,3,2,0:T(8,128)(2,1)}, bf16[4,128,4,64]{1,3,2,0:T(8,128)(2,1)S(1)},...) while((s32[]{:T(128)}, ...), condition=%wide.region_4.5_spmd.clone, body=%wide.region_2.4_spmd.clone.sunk | while | flops 154420864 | bytes 8694141 | solution.py:103
  145.0 2.1 convert_reduce_fusion.1
  147.4 3.0 %fusion.23 = f32[128,2048]{1,0:T(8,128)S(1)} fusion(bf16[1024,6144]{1,0:T(8,128)(2,1)} %all-gather.2.cloned.1.call-done, bf16[128,1024]{1,0:T(8,128)(2,1)S(1)} %get-tuple-element.114, f32[1024]{0:T(1024)S(1)} %copy-done.6, f32[128]{0:T(128)S(1)} %add_rsqrt_fusion.2, f32[128]{0:T(128)S(1)} %broadcast_multiply_fusion.1), kind=kOutput, calls=%fused_computation.28 | convolution fusion | flops 537526272 | bytes 5510144 | tf_op jit(solution)/shard_map/dot_general | solution.py:44
  150.6 2.2 collective-permute-start.8
  152.8 5.5 %collective-permute-start.9 = (bf16[4,1024]{1,0:T(4,128)(2,1)S(1)}, bf16[4,1024]{1,0:T(4,128)(2,1)S(1)}, u32[]{:S(2)}, u32[]{:S(2)}) collective-permute-start(bf16[4,1024]{1,0:T(4,128)(2,1)S(1)} %get-tuple-element.101), channel_id=1, source_target_pairs={{1,0},{2,1},{3,2},{4,3},{5,4},{6,5},{7,6},{8,7},{9,8},{10,9},{11,1... | collective-permute-start | bytes 24584 | tf_op jit(solution)/shard_map/ppermute | solution.py:30
  160.4 2.5 %all-reduce.3 = (f32[1024]{0:T(1024)S(1)}, f32[1024]{0:T(1024)S(1)}) all-reduce(f32[1024]{0:T(1024)S(1)} %get-tuple-element.66, f32[1024]{0:T(1024)S(1)} %get-tuple-element.65), channel_id=1, replica_groups=mesh['call'=8,'x'=4,'y'=8,'core'=2] {'core'}, use_global_device_ids=true, to_apply=%region_14.15 | all-reduce | flops 2048 | bytes 16384 | tf_op jit(solution)/shard_map/psum | solution.py:123
  162.9 15.7 %all-reduce = (f32[1024]{0:T(1024)S(1)}, f32[1024]{0:T(1024)S(1)}) all-reduce(f32[1024]{0:T(1024)S(1)} %get-tuple-element.95, f32[1024]{0:T(1024)S(1)} %get-tuple-element.96), channel_id=1, replica_groups=mesh['call'=8,'x'=4,'y'=8,'core'=2] {'y'}, use_global_device_ids=true, to_apply=%region_15.16 | all-reduce | flops 2048 | bytes 16384 | tf_op jit(solution)/shard_map/psum | solution.py:123
  178.6 11.1 %all-reduce.2 = (f32[1024]{0:T(1024)S(1)}, f32[1024]{0:T(1024)S(1)}) all-reduce(f32[1024]{0:T(1024)S(1)} %get-tuple-element.89, f32[1024]{0:T(1024)S(1)} %get-tuple-element.90), channel_id=1, replica_groups=mesh['call'=8,'x'=4,'y'=8,'core'=2] {'x'}, use_global_device_ids=true, to_apply=%region_16.17 | all-reduce | flops 2048 | bytes 16384 | tf_op jit(solution)/shard_map/psum | solution.py:123
  189.7 19.3 %all-reduce.1 = (f32[1024]{0:T(1024)S(1)}, f32[1024]{0:T(1024)S(1)}) all-reduce(f32[1024]{0:T(1024)S(1)} %get-tuple-element.93, f32[1024]{0:T(1024)S(1)} %get-tuple-element.94), channel_id=1, replica_groups=mesh['call'=8,'x'=4,'y'=8,'core'=2] {'call'}, use_global_device_ids=true, to_apply=%region_17.18 | all-reduce | flops 2048 | bytes 16384 | tf_op jit(solution)/shard_map/psum | solution.py:123
  (72 shorter events, 37.7 us)
Async XLA Ops:
  7.2 95.4 %copy-start = (bf16[1,128,1024]{2,1,0:T(8,128)(2,1)S(1)}, bf16[1,128,1024]{2,1,0:T(8,128)(2,1)}, u32[]{:S(2)}) copy-start(bf16[1,128,1024]{2,1,0:T(8,128)(2,1)} %param.12) | copy-start | bytes 786436
  7.2 104.0 %all-gather.2.cloned.1.call-start = ((), (), s32[]{:S(2)}) async-start(), calls=%async_computation | async-start | bytes 12779520 | tf_op jit(solution)/shard_map/all_gather | solution.py:59
  8.9 10.0 %collective-permute-start = (bf16[128,1024]{1,0:T(8,128)(2,1)}, bf16[128,1024]{1,0:T(8,128)(2,1)S(1)}, u32[]{:S(2)}, u32[]{:S(2)}) collective-permute-start(bf16[128,1024]{1,0:T(8,128)(2,1)} %bitcast.59), channel_id=1, source_target_pairs={{0,1},{1,2},{2,3},{3,4},{4,5},{5,6},{6,7},{7,8},{8,9},{9,10},{10,1... | collective-permute-start | bytes 786440 | tf_op jit(solution)/shard_map/ppermute | solution.py:18
  18.9 9.8 %collective-permute-start.1 = (bf16[128,1024]{1,0:T(8,128)(2,1)S(1)}, bf16[128,1024]{1,0:T(8,128)(2,1)S(1)}, u32[]{:S(2)}, u32[]{:S(2)}) collective-permute-start(bf16[128,1024]{1,0:T(8,128)(2,1)S(1)} %collective-permute-done), channel_id=1, source_target_pairs={{0,1},{1,2},{2,3},{3,4},{4,5},{5,6},{6,7},{7,8},{8,9},{9,10},{10,1... | collective-permute-start | bytes 786440 | tf_op jit(solution)/shard_map/ppermute | solution.py:18
  28.7 11.4 %collective-permute-start.2 = (bf16[128,1024]{1,0:T(8,128)(2,1)S(1)}, bf16[128,1024]{1,0:T(8,128)(2,1)S(1)}, u32[]{:S(2)}, u32[]{:S(2)}) collective-permute-start(bf16[128,1024]{1,0:T(8,128)(2,1)S(1)} %collective-permute-done.1), channel_id=1, source_target_pairs={{0,1},{1,2},{2,3},{3,4},{4,5},{5,6},{6,7},{7,8},{8,9},{9,10},{10,1... | collective-permute-start | bytes 786440 | tf_op jit(solution)/shard_map/ppermute | solution.py:18
  40.1 11.6 %collective-permute-start.3 = (bf16[128,1024]{1,0:T(8,128)(2,1)S(1)}, bf16[128,1024]{1,0:T(8,128)(2,1)S(1)}, u32[]{:S(2)}, u32[]{:S(2)}) collective-permute-start(bf16[128,1024]{1,0:T(8,128)(2,1)S(1)} %collective-permute-done.2), channel_id=1, source_target_pairs={{0,1},{1,2},{2,3},{3,4},{4,5},{5,6},{6,7},{7,8},{8,9},{9,10},{10,1... | collective-permute-start | bytes 786440 | tf_op jit(solution)/shard_map/ppermute | solution.py:18
  51.7 9.8 %collective-permute-start.4 = (bf16[128,1024]{1,0:T(8,128)(2,1)S(1)}, bf16[128,1024]{1,0:T(8,128)(2,1)S(1)}, u32[]{:S(2)}, u32[]{:S(2)}) collective-permute-start(bf16[128,1024]{1,0:T(8,128)(2,1)S(1)} %collective-permute-done.3), channel_id=1, source_target_pairs={{0,1},{1,2},{2,3},{3,4},{4,5},{5,6},{6,7},{7,8},{8,9},{9,10},{10,1... | collective-permute-start | bytes 786440 | tf_op jit(solution)/shard_map/ppermute | solution.py:18
  61.5 9.8 %collective-permute-start.5 = (bf16[128,1024]{1,0:T(8,128)(2,1)S(1)}, bf16[128,1024]{1,0:T(8,128)(2,1)S(1)}, u32[]{:S(2)}, u32[]{:S(2)}) collective-permute-start(bf16[128,1024]{1,0:T(8,128)(2,1)S(1)} %collective-permute-done.4), channel_id=1, source_target_pairs={{0,1},{1,2},{2,3},{3,4},{4,5},{5,6},{6,7},{7,8},{8,9},{9,10},{10,1... | collective-permute-start | bytes 786440 | tf_op jit(solution)/shard_map/ppermute | solution.py:18
  71.3 15.5 %collective-permute-start.6 = (bf16[128,1024]{1,0:T(8,128)(2,1)S(1)}, bf16[128,1024]{1,0:T(8,128)(2,1)S(1)}, u32[]{:S(2)}, u32[]{:S(2)}) collective-permute-start(bf16[128,1024]{1,0:T(8,128)(2,1)S(1)} %collective-permute-done.5), channel_id=1, source_target_pairs={{0,1},{1,2},{2,3},{3,4},{4,5},{5,6},{6,7},{7,8},{8,9},{9,10},{10,1... | collective-permute-start | bytes 786440 | tf_op jit(solution)/shard_map/ppermute | solution.py:18
  86.9 15.5 %collective-permute-start.7 = (bf16[128,1024]{1,0:T(8,128)(2,1)S(1)}, bf16[128,1024]{1,0:T(8,128)(2,1)S(1)}, u32[]{:S(2)}, u32[]{:S(2)}) collective-permute-start(bf16[128,1024]{1,0:T(8,128)(2,1)S(1)} %collective-permute-done.6), channel_id=1, source_target_pairs={{0,1},{1,2},{2,3},{3,4},{4,5},{5,6},{6,7},{7,8},{8,9},{9,10},{10,1... | collective-permute-start | bytes 786440 | tf_op jit(solution)/shard_map/ppermute | solution.py:18
  102.6 1.2 copy-start.5
  144.9 2.4 %copy-start.6 = (f32[1024]{0:T(1024)S(1)}, f32[1024]{0:T(1024)}, u32[]{:S(2)}) copy-start(f32[1024]{0:T(1024)} %param.17) | copy-start | bytes 12292
  147.1 3.3 %copy-start.1 = (bf16[128,1024]{1,0:T(8,128)(2,1)}, bf16[128,1024]{1,0:T(8,128)(2,1)S(1)}, u32[]{:S(2)}) copy-start(bf16[128,1024]{1,0:T(8,128)(2,1)S(1)} %get-tuple-element.114) | copy-start | bytes 786436
  147.4 11.0 %copy-start.2 = (f32[9,1024]{1,0:T(8,128)S(1)}, f32[9,1024]{1,0:T(8,128)}, u32[]{:S(2)}) copy-start(f32[9,1024]{1,0:T(8,128)} %param.19) | copy-start | bytes 110596
  147.4 11.0 %copy-start.7 = (s32[8]{0:T(128)S(1)}, s32[8]{0:T(128)}, u32[]{:S(2)}) copy-start(s32[8]{0:T(128)} %param.13) | copy-start | bytes 100
  150.4 58.6 %copy-start.3 = (f32[1024]{0:T(1024)S(1)}, f32[1024]{0:T(1024)}, u32[]{:S(2)}) copy-start(f32[1024]{0:T(1024)} %param.21) | copy-start | bytes 12292
  150.4 58.6 %copy-start.4 = (f32[1024]{0:T(1024)S(1)}, f32[1024]{0:T(1024)}, u32[]{:S(2)}) copy-start(f32[1024]{0:T(1024)} %param.20) | copy-start | bytes 12292
  150.6 9.0 %collective-permute-start.8 = (bf16[4,1024]{1,0:T(4,128)(2,1)S(1)}, bf16[4,1024]{1,0:T(4,128)(2,1)S(1)}, u32[]{:S(2)}, u32[]{:S(2)}) collective-permute-start(bf16[4,1024]{1,0:T(4,128)(2,1)S(1)} %get-tuple-element.100), channel_id=1, source_target_pairs={{0,1},{1,2},{2,3},{3,4},{4,5},{5,6},{6,7},{7,8},{8,9},{9,10},{10,1... | collective-permute-start | bytes 24584 | tf_op jit(solution)/shard_map/ppermute | solution.py:28
  152.8 6.9 %collective-permute-start.9 = (bf16[4,1024]{1,0:T(4,128)(2,1)S(1)}, bf16[4,1024]{1,0:T(4,128)(2,1)S(1)}, u32[]{:S(2)}, u32[]{:S(2)}) collective-permute-start(bf16[4,1024]{1,0:T(4,128)(2,1)S(1)} %get-tuple-element.101), channel_id=1, source_target_pairs={{1,0},{2,1},{3,2},{4,3},{5,4},{6,5},{7,6},{8,7},{9,8},{10,9},{11,1... | collective-permute-start | bytes 24584 | tf_op jit(solution)/shard_map/ppermute | solution.py:30
Sparse Core Ops, SparseCore 0:
  11.9 99.2 all-gather.1

commit v2 on v1

--- a/solution.py
+++ b/solution.py
@@ -119,9 +119,10 @@
         )
     masked = jnp.where(frame_valid[:, None], depthwise, 0.0)
     moments = (jnp.sum(masked, axis=0), jnp.sum(masked * depthwise, axis=0))
+    moments = jnp.stack(moments)
     for axis in ("core", "y", "x", "call"):
-        moments = lax.psum(moments, axis)
-    first_moment, second_moment = moments
+        moments = jnp.sum(lax.all_gather(moments, axis), axis=0)
+    first_moment, second_moment = moments[0], moments[1]
     count_all = jnp.sum(lengths).astype(jnp.float32)
     average = first_moment / count_all
     second = second_moment / count_all

time: 219 us -> 237 us (1.082)
  blocking collectives: 48.6 us -> 66.9 us
    all_gather x0 -> x4, blocking collectives: none -> 66.9 us  [on_device(): moments = jnp.sum(lax.all_gather(moments, axis), axis=0)]
    psum x4 -> x0, blocking collectives: 48.6 us -> none  [on_device(): moments = lax.psum(moments, axis)]
where the time goes in v2:
time: 237 us; the launch traced here: 235 us
  waiting for transfers between devices  82.2 us (35%)
  blocking collectives  66.9 us (28%)
  matrix products  28.6 us (12%)
  starting transfers between devices  23 us (10%)
  between operations  15.1 us (6%)
  local copies, waits for them, and re-layouts  10.5 us (4%)
  other arithmetic  8.78 us (4%)
    ppermute x8, waiting for transfers between devices, passed_along(): lax.ppermute(value, axis, [(source, source + steps) for source in range(f...  75.6 us
    all_gather x4, blocking collectives, on_device(): moments = jnp.sum(lax.all_gather(moments, axis), axis=0)  66.9 us
    ppermute x8, starting transfers between devices, passed_along(): lax.ppermute(value, axis, [(source, source + steps) for source in range(f...  15.3 us
    dot_general x4, matrix products, contract_with(): return jnp.dot(left, rows_piece, preferred_element_type=jnp.float32)  14.6 us
    dot_general x4, matrix products, attend_group(): jnp.einsum('hqk,khd->qhd', probs, value_part, preferred_element_type=jnp....  6.99 us
    dot_general x4, matrix products, attend_group(): jnp.einsum('qhd,khd->hqk', query_part, key_part, preferred_element_type=j...  6.94 us
    all_gather x1, waiting for transfers between devices, on_device(): lax.all_gather(jnp.concatenate([w_qkv, w_out, w_pw1], axis=1), TM, axis=0...  6.58 us
    slice x2, local copies, waits for them, and re-layouts, on_device(): keys = key_value[:, :model_width].astype(jnp.bfloat16)  6.23 us
  transfers between devices with their start and end apart: 11, of which 9 were waited for; matrix products, arithmetic and copies ran while one was open for 2% of the time, Pallas kernels for 0%

profile of v2, /device:TPU:6, one launch (start us, length us, event | category | flops | bytes accessed | tf_op | source)
XLA Modules:
  0.0 235.2 jit_solution(11371041187483836492)
XLA Ops:
  8.9 1.9 collective-permute-start
  10.8 8.1 %collective-permute-done = bf16[128,1024]{1,0:T(8,128)(2,1)S(1)} collective-permute-done((bf16[128,1024]{1,0:T(8,128)(2,1)}, bf16[128,1024]{1,0:T(8,128)(2,1)S(1)}, u32[]{:S(2)}, u32[]{:S(2)}) %collective-permute-start) | collective-permute-done | bytes 262176 | tf_op jit(solution)/shard_map/ppermute | solution.py:18
  18.9 1.9 collective-permute-start.1
  20.8 7.9 %collective-permute-done.1 = bf16[128,1024]{1,0:T(8,128)(2,1)S(1)} collective-permute-done((bf16[128,1024]{1,0:T(8,128)(2,1)S(1)}, bf16[128,1024]{1,0:T(8,128)(2,1)S(1)}, u32[]{:S(2)}, u32[]{:S(2)}) %collective-permute-start.1) | collective-permute-done | bytes 262176 | tf_op jit(solution)/shard_map/ppermute | solution.py:18
  30.6 9.5 %collective-permute-done.2 = bf16[128,1024]{1,0:T(8,128)(2,1)S(1)} collective-permute-done((bf16[128,1024]{1,0:T(8,128)(2,1)S(1)}, bf16[128,1024]{1,0:T(8,128)(2,1)S(1)}, u32[]{:S(2)}, u32[]{:S(2)}) %collective-permute-start.2) | collective-permute-done | bytes 262176 | tf_op jit(solution)/shard_map/ppermute | solution.py:18
  40.1 1.9 collective-permute-start.3
  42.1 9.7 %collective-permute-done.3 = bf16[128,1024]{1,0:T(8,128)(2,1)S(1)} collective-permute-done((bf16[128,1024]{1,0:T(8,128)(2,1)S(1)}, bf16[128,1024]{1,0:T(8,128)(2,1)S(1)}, u32[]{:S(2)}, u32[]{:S(2)}) %collective-permute-start.3) | collective-permute-done | bytes 262176 | tf_op jit(solution)/shard_map/ppermute | solution.py:18
  53.7 7.9 %collective-permute-done.4 = bf16[128,1024]{1,0:T(8,128)(2,1)S(1)} collective-permute-done((bf16[128,1024]{1,0:T(8,128)(2,1)S(1)}, bf16[128,1024]{1,0:T(8,128)(2,1)S(1)}, u32[]{:S(2)}, u32[]{:S(2)}) %collective-permute-start.4) | collective-permute-done | bytes 262176 | tf_op jit(solution)/shard_map/ppermute | solution.py:18
  63.5 7.9 %collective-permute-done.5 = bf16[128,1024]{1,0:T(8,128)(2,1)S(1)} collective-permute-done((bf16[128,1024]{1,0:T(8,128)(2,1)S(1)}, bf16[128,1024]{1,0:T(8,128)(2,1)S(1)}, u32[]{:S(2)}, u32[]{:S(2)}) %collective-permute-start.5) | collective-permute-done | bytes 262176 | tf_op jit(solution)/shard_map/ppermute | solution.py:18
  74.6 12.3 %collective-permute-done.6 = bf16[128,1024]{1,0:T(8,128)(2,1)S(1)} collective-permute-done((bf16[128,1024]{1,0:T(8,128)(2,1)S(1)}, bf16[128,1024]{1,0:T(8,128)(2,1)S(1)}, u32[]{:S(2)}, u32[]{:S(2)}) %collective-permute-start.6) | collective-permute-done | bytes 262176 | tf_op jit(solution)/shard_map/ppermute | solution.py:18
  90.0 12.4 %collective-permute-done.7 = bf16[128,1024]{1,0:T(8,128)(2,1)S(1)} collective-permute-done((bf16[128,1024]{1,0:T(8,128)(2,1)S(1)}, bf16[128,1024]{1,0:T(8,128)(2,1)S(1)}, u32[]{:S(2)}, u32[]{:S(2)}) %collective-permute-start.7) | collective-permute-done | bytes 262176 | tf_op jit(solution)/shard_map/ppermute | solution.py:18
  104.6 6.6 %all-gather.10.cloned.1.call-done = bf16[1024,6144]{1,0:T(8,128)(2,1)} async-done(((bf16[16,6144]{1,0:T(8,128)(2,1)}), bf16[1024,6144]{1,0:T(8,128)(2,1)}) %all-gather.10.cloned.1.call-update) | async-done | bytes 12582928 | tf_op jit(solution)/shard_map/all_gather | solution.py:59
  111.2 2.0 fusion.39
  113.4 7.4 %convolution_convert_fusion = bf16[1152,2048]{1,0:T(8,128)(2,1)S(1)} fusion(bf16[1152,1024]{1,0:T(8,128)(2,1)S(1)} %fusion.22, bf16[1024,6144]{1,0:T(8,128)(2,1)} %all-gather.10.cloned.1.call-done), kind=kOutput, calls=%fused_computation.20 | convolution fusion | flops 4834197504 | bytes 11272192 | tf_op jit(solution)/shard_map/dot_general | solution.py:44
  122.8 4.3 %copy.20 = bf16[1152,1024]{0,1:T(8,128)(2,1)} copy(bf16[1152,1024]{1,0:T(8,128)(2,1)} %get-tuple-element.92) | data formatting | bytes 4718592 | tf_op jit(solution)/shard_map/slice | solution.py:74
  127.1 2.6 %copy.18 = bf16[1152,1024]{0,1:T(8,128)(2,1)} copy(bf16[1152,1024]{1,0:T(8,128)(2,1)S(1)} %get-tuple-element.93) | data formatting | bytes 4718592 | tf_op jit(solution)/shard_map/slice | solution.py:75
  129.7 15.3 %while.11 = (s32[]{:T(128)}, bf16[4,128,4,64]{1,3,2,0:T(8,128)(2,1)S(1)}, bf16[4,1152,4,64]{1,3,2,0:T(8,128)(2,1)}, bf16[4,128,4,64]{1,3,2,0:T(8,128)(2,1)S(1)},...) while((s32[]{:T(128)}, ...), condition=%wide.region_4.5_spmd.clone, body=%wide.region_2.4_spmd.clone.sunk | while | flops 154420864 | bytes 8694141 | solution.py:103
  144.9 2.1 convert_reduce_fusion.1
  147.4 3.0 %fusion.23 = f32[128,2048]{1,0:T(8,128)S(1)} fusion(bf16[1024,6144]{1,0:T(8,128)(2,1)} %all-gather.10.cloned.1.call-done, bf16[128,1024]{1,0:T(8,128)(2,1)S(1)} %get-tuple-element.106, f32[1024]{0:T(1024)S(1)} %copy-done.6, f32[128]{0:T(128)S(1)} %add_rsqrt_fusion.2, f32[128]{0:T(128)S(1)} %broadcast_multiply_fusion.1), kind=kOutput, calls=%fused_computation.28 | convolution fusion | flops 537526272 | bytes 5510144 | tf_op jit(solution)/shard_map/dot_general | solution.py:44
  150.6 2.2 collective-permute-start.8
  152.8 5.5 %collective-permute-start.9 = (bf16[4,1024]{1,0:T(4,128)(2,1)S(1)}, bf16[4,1024]{1,0:T(4,128)(2,1)S(1)}, u32[]{:S(2)}, u32[]{:S(2)}) collective-permute-start(bf16[4,1024]{1,0:T(4,128)(2,1)S(1)} %get-tuple-element.95), channel_id=1, source_target_pairs={{1,0},{2,1},{3,2},{4,3},{5,4},{6,5},{7,6},{8,7},{9,8},{10,9},{11,1... | collective-permute-start | bytes 24584 | tf_op jit(solution)/shard_map/ppermute | solution.py:30
  162.2 24.6 %all-gather.5 = f32[8,2,1024]{2,1,0:T(2,128)S(1)} all-gather(f32[1,2,1024]{2,1,0:T(2,128)S(1)} %bitcast.70), channel_id=3, replica_groups=mesh['call'=8,'x'=4,'y'=8,'core'=2] {'y'}, dimensions={0}, use_global_device_ids=true | all-gather | bytes 73728 | tf_op jit(solution)/shard_map/all_gather | solution.py:124
  186.8 12.5 %all-gather.6 = f32[4,2,1024]{2,1,0:T(2,128)S(1)} all-gather(f32[1,2,1024]{2,1,0:T(2,128)S(1)} %bitcast.71), channel_id=4, replica_groups=mesh['call'=8,'x'=4,'y'=8,'core'=2] {'x'}, dimensions={0}, use_global_device_ids=true | all-gather | bytes 40960 | tf_op jit(solution)/shard_map/all_gather | solution.py:124
  199.4 28.0 %all-gather.7 = f32[8,2,1024]{2,1,0:T(2,128)S(1)} all-gather(f32[1,2,1024]{2,1,0:T(2,128)S(1)} %bitcast.72), channel_id=5, replica_groups=mesh['call'=8,'x'=4,'y'=8,'core'=2] {'call'}, dimensions={0}, use_global_device_ids=true | all-gather | bytes 73728 | tf_op jit(solution)/shard_map/all_gather | solution.py:124
  (77 shorter events, 37.7 us)
Async XLA Ops:
  7.2 95.4 %copy-start = (bf16[1,128,1024]{2,1,0:T(8,128)(2,1)S(1)}, bf16[1,128,1024]{2,1,0:T(8,128)(2,1)}, u32[]{:S(2)}) copy-start(bf16[1,128,1024]{2,1,0:T(8,128)(2,1)} %param.12) | copy-start | bytes 786436
  7.2 104.0 %all-gather.10.cloned.1.call-start = ((), (), s32[]{:S(2)}) async-start(), calls=%async_computation | async-start | bytes 12779520 | tf_op jit(solution)/shard_map/all_gather | solution.py:59
  8.9 10.0 %collective-permute-start = (bf16[128,1024]{1,0:T(8,128)(2,1)}, bf16[128,1024]{1,0:T(8,128)(2,1)S(1)}, u32[]{:S(2)}, u32[]{:S(2)}) collective-permute-start(bf16[128,1024]{1,0:T(8,128)(2,1)} %bitcast.68), channel_id=1, source_target_pairs={{0,1},{1,2},{2,3},{3,4},{4,5},{5,6},{6,7},{7,8},{8,9},{9,10},{10,1... | collective-permute-start | bytes 786440 | tf_op jit(solution)/shard_map/ppermute | solution.py:18
  18.9 9.8 %collective-permute-start.1 = (bf16[128,1024]{1,0:T(8,128)(2,1)S(1)}, bf16[128,1024]{1,0:T(8,128)(2,1)S(1)}, u32[]{:S(2)}, u32[]{:S(2)}) collective-permute-start(bf16[128,1024]{1,0:T(8,128)(2,1)S(1)} %collective-permute-done), channel_id=1, source_target_pairs={{0,1},{1,2},{2,3},{3,4},{4,5},{5,6},{6,7},{7,8},{8,9},{9,10},{10,1... | collective-permute-start | bytes 786440 | tf_op jit(solution)/shard_map/ppermute | solution.py:18
  28.7 11.4 %collective-permute-start.2 = (bf16[128,1024]{1,0:T(8,128)(2,1)S(1)}, bf16[128,1024]{1,0:T(8,128)(2,1)S(1)}, u32[]{:S(2)}, u32[]{:S(2)}) collective-permute-start(bf16[128,1024]{1,0:T(8,128)(2,1)S(1)} %collective-permute-done.1), channel_id=1, source_target_pairs={{0,1},{1,2},{2,3},{3,4},{4,5},{5,6},{6,7},{7,8},{8,9},{9,10},{10,1... | collective-permute-start | bytes 786440 | tf_op jit(solution)/shard_map/ppermute | solution.py:18
  40.1 11.6 %collective-permute-start.3 = (bf16[128,1024]{1,0:T(8,128)(2,1)S(1)}, bf16[128,1024]{1,0:T(8,128)(2,1)S(1)}, u32[]{:S(2)}, u32[]{:S(2)}) collective-permute-start(bf16[128,1024]{1,0:T(8,128)(2,1)S(1)} %collective-permute-done.2), channel_id=1, source_target_pairs={{0,1},{1,2},{2,3},{3,4},{4,5},{5,6},{6,7},{7,8},{8,9},{9,10},{10,1... | collective-permute-start | bytes 786440 | tf_op jit(solution)/shard_map/ppermute | solution.py:18
  51.7 9.8 %collective-permute-start.4 = (bf16[128,1024]{1,0:T(8,128)(2,1)S(1)}, bf16[128,1024]{1,0:T(8,128)(2,1)S(1)}, u32[]{:S(2)}, u32[]{:S(2)}) collective-permute-start(bf16[128,1024]{1,0:T(8,128)(2,1)S(1)} %collective-permute-done.3), channel_id=1, source_target_pairs={{0,1},{1,2},{2,3},{3,4},{4,5},{5,6},{6,7},{7,8},{8,9},{9,10},{10,1... | collective-permute-start | bytes 786440 | tf_op jit(solution)/shard_map/ppermute | solution.py:18
  61.5 9.8 %collective-permute-start.5 = (bf16[128,1024]{1,0:T(8,128)(2,1)S(1)}, bf16[128,1024]{1,0:T(8,128)(2,1)S(1)}, u32[]{:S(2)}, u32[]{:S(2)}) collective-permute-start(bf16[128,1024]{1,0:T(8,128)(2,1)S(1)} %collective-permute-done.4), channel_id=1, source_target_pairs={{0,1},{1,2},{2,3},{3,4},{4,5},{5,6},{6,7},{7,8},{8,9},{9,10},{10,1... | collective-permute-start | bytes 786440 | tf_op jit(solution)/shard_map/ppermute | solution.py:18
  71.3 15.5 %collective-permute-start.6 = (bf16[128,1024]{1,0:T(8,128)(2,1)S(1)}, bf16[128,1024]{1,0:T(8,128)(2,1)S(1)}, u32[]{:S(2)}, u32[]{:S(2)}) collective-permute-start(bf16[128,1024]{1,0:T(8,128)(2,1)S(1)} %collective-permute-done.5), channel_id=1, source_target_pairs={{0,1},{1,2},{2,3},{3,4},{4,5},{5,6},{6,7},{7,8},{8,9},{9,10},{10,1... | collective-permute-start | bytes 786440 | tf_op jit(solution)/shard_map/ppermute | solution.py:18
  86.9 15.5 %collective-permute-start.7 = (bf16[128,1024]{1,0:T(8,128)(2,1)S(1)}, bf16[128,1024]{1,0:T(8,128)(2,1)S(1)}, u32[]{:S(2)}, u32[]{:S(2)}) collective-permute-start(bf16[128,1024]{1,0:T(8,128)(2,1)S(1)} %collective-permute-done.6), channel_id=1, source_target_pairs={{0,1},{1,2},{2,3},{3,4},{4,5},{5,6},{6,7},{7,8},{8,9},{9,10},{10,1... | collective-permute-start | bytes 786440 | tf_op jit(solution)/shard_map/ppermute | solution.py:18
  102.6 1.2 copy-start.5
  144.9 2.4 %copy-start.6 = (f32[1024]{0:T(1024)S(1)}, f32[1024]{0:T(1024)}, u32[]{:S(2)}) copy-start(f32[1024]{0:T(1024)} %param.17) | copy-start | bytes 12292
  147.1 3.3 %copy-start.1 = (bf16[128,1024]{1,0:T(8,128)(2,1)}, bf16[128,1024]{1,0:T(8,128)(2,1)S(1)}, u32[]{:S(2)}) copy-start(bf16[128,1024]{1,0:T(8,128)(2,1)S(1)} %get-tuple-element.106) | copy-start | bytes 786436
  147.4 11.0 %copy-start.2 = (f32[9,1024]{1,0:T(8,128)S(1)}, f32[9,1024]{1,0:T(8,128)}, u32[]{:S(2)}) copy-start(f32[9,1024]{1,0:T(8,128)} %param.19) | copy-start | bytes 110596
  147.4 11.0 %copy-start.7 = (s32[8]{0:T(128)S(1)}, s32[8]{0:T(128)}, u32[]{:S(2)}) copy-start(s32[8]{0:T(128)} %param.13) | copy-start | bytes 100
  150.4 77.0 %copy-start.3 = (f32[1024]{0:T(1024)S(1)}, f32[1024]{0:T(1024)}, u32[]{:S(2)}) copy-start(f32[1024]{0:T(1024)} %param.21) | copy-start | bytes 12292
  150.4 77.0 %copy-start.4 = (f32[1024]{0:T(1024)S(1)}, f32[1024]{0:T(1024)}, u32[]{:S(2)}) copy-start(f32[1024]{0:T(1024)} %param.20) | copy-start | bytes 12292
  150.6 9.0 %collective-permute-start.8 = (bf16[4,1024]{1,0:T(4,128)(2,1)S(1)}, bf16[4,1024]{1,0:T(4,128)(2,1)S(1)}, u32[]{:S(2)}, u32[]{:S(2)}) collective-permute-start(bf16[4,1024]{1,0:T(4,128)(2,1)S(1)} %get-tuple-element.94), channel_id=1, source_target_pairs={{0,1},{1,2},{2,3},{3,4},{4,5},{5,6},{6,7},{7,8},{8,9},{9,10},{10,1... | collective-permute-start | bytes 24584 | tf_op jit(solution)/shard_map/ppermute | solution.py:28
  152.8 6.9 %collective-permute-start.9 = (bf16[4,1024]{1,0:T(4,128)(2,1)S(1)}, bf16[4,1024]{1,0:T(4,128)(2,1)S(1)}, u32[]{:S(2)}, u32[]{:S(2)}) collective-permute-start(bf16[4,1024]{1,0:T(4,128)(2,1)S(1)} %get-tuple-element.95), channel_id=1, source_target_pairs={{1,0},{2,1},{3,2},{4,3},{5,4},{6,5},{7,6},{8,7},{9,8},{10,9},{11,1... | collective-permute-start | bytes 24584 | tf_op jit(solution)/shard_map/ppermute | solution.py:30
Sparse Core Ops, SparseCore 0:
  11.9 99.2 all-gather.9

commit v3 on v1

--- a/solution.py
+++ b/solution.py
@@ -56,16 +56,37 @@
     frame_valid = query_pos < length
     qkv_cols = w_qkv.shape[1]
     out_cols = w_out.shape[1]
-    weights = lax.all_gather(
-        jnp.concatenate([w_qkv, w_out, w_pw1], axis=1), TM, axis=0, tiled=True
+    core = lax.axis_index("core")
+    cores = lax.axis_size("core")
+    swap = [(0, 1), (1, 0)]
+    packed = jnp.concatenate([w_qkv, w_out, w_pw1], axis=1)
+    half = packed.shape[1] // 2
+    halves = (packed[:, :half], packed[:, half:])
+    given = lax.ppermute(jnp.where(core == 0, halves[1], halves[0]), "core", swap)
+    kept = jnp.where(core == 0, halves[0], halves[1])
+    pair = jnp.where(core == 0, jnp.stack([kept, given]), jnp.stack([given, kept]))
+    gathered = lax.all_gather(pair.reshape(-1, half), ("x", "y"), axis=0, tiled=True)
+    prior_blocks = LEFT // frame_count
+    chip_hops = prior_blocks // cores
+    blocks = [stream]
+    current = stream
+    for hop_index in range(chip_hops):
+        current = passed_along(current, ("x", "y"), 1)
+        blocks.append(current)
+    mine = jnp.stack(blocks[::-1])
+    gathered, mine = lax.optimization_barrier((gathered, mine))
+    other = lax.ppermute(gathered, "core", swap)
+    weights = jnp.where(
+        core == 0,
+        jnp.concatenate([gathered, other], axis=1),
+        jnp.concatenate([other, gathered], axis=1),
     )
-    prior_blocks = LEFT // frame_count
-    blocks = []
-    current = stream
-    for hop_index in range(prior_blocks):
-        current = passed_along(current, TM, 1)
-        blocks.append(current)
-    context_frames = jnp.concatenate(blocks[::-1] + [stream], axis=0)
+    theirs = lax.ppermute(mine, "core", swap)
+    by_chip = jnp.where(core == 0, jnp.stack([mine, theirs], 1), jnp.stack([theirs, mine], 1))
+    by_chip = by_chip.reshape(-1, model_width)
+    context_frames = lax.dynamic_slice_in_dim(
+        by_chip, core * frame_count, (prior_blocks + 1) * frame_count, 0
+    )
     key_count = context_frames.shape[0]
     normed_all = layer_norm(context_frames, ln_attn_gain).astype(jnp.bfloat16)
     normed = normed_all[key_count - frame_count :]

time: 219 us -> 248 us (1.13)
  waiting for transfers between devices: 82.2 us -> 96.2 us
  other arithmetic: 8.67 us -> 19.3 us
  local copies, waits for them, and re-layouts: 10.5 us -> 18.8 us
    all_gather x1, waiting for transfers between devices: 6.57 us -> 48 us  [on_device(): lax.all_gather(pair.reshape(-1, half), ('x', 'y'), axis=0, tiled=True)]
    ppermute x8 -> x4, waiting for transfers between devices: 75.6 us -> 39.1 us  [passed_along(): lax.ppermute(value, axis, [(source, source + steps) for source in range(f...]
    select_n x0 -> x3, other arithmetic: none -> 11.3 us  [the longest x1 10.2 us: on_device(): jnp.where(core == 0, jnp.concatenate([gathered, other], axis=1), jnp.conc...]
    ppermute x0 -> x3, waiting for transfers between devices: none -> 9.08 us  [the longest x1 7.81 us: on_device(): theirs = lax.ppermute(mine, 'core', swap)]
    ppermute x0 -> x3, starting transfers between devices: none -> 6.24 us  [the longest x1 2.41 us: on_device(): theirs = lax.ppermute(mine, 'core', swap)]
    ppermute x8 -> x4, starting transfers between devices: 15.3 us -> 9.21 us  [passed_along(): lax.ppermute(value, axis, [(source, source + steps) for source in range(f...]
    unnamed x24 -> x27, local copies, waits for them, and re-layouts: 0.2 us -> 5.7 us
  transfers between devices with their start and end apart: 11 -> 10, of which waited for: 9 -> 7; matrix products, arithmetic and copies ran while one was open for 2% -> 2% of each run, Pallas kernels for 0% -> 0%
where the time goes in v3:
time: 248 us; the launch traced here: 246 us
  waiting for transfers between devices  96.2 us (39%)
  blocking collectives  46.9 us (19%)
  matrix products  26.3 us (11%)
  starting transfers between devices  23.2 us (9%)
  other arithmetic  19.3 us (8%)
  local copies, waits for them, and re-layouts  18.8 us (8%)
  between operations  15.2 us (6%)
    all_gather x1, waiting for transfers between devices, on_device(): lax.all_gather(pair.reshape(-1, half), ('x', 'y'), axis=0, tiled=True)  48 us
    psum x4, blocking collectives, on_device(): moments = lax.psum(moments, axis)  46.9 us
    ppermute x4, waiting for transfers between devices, passed_along(): lax.ppermute(value, axis, [(source, source + steps) for source in range(f...  39.1 us
    dot_general x4, matrix products, contract_with(): return jnp.dot(left, rows_piece, preferred_element_type=jnp.float32)  12.3 us
    select_n x1, other arithmetic, on_device(): jnp.where(core == 0, jnp.concatenate([gathered, other], axis=1), jnp.conc...  10.2 us
    ppermute x4, starting transfers between devices, passed_along(): lax.ppermute(value, axis, [(source, source + steps) for source in range(f...  9.21 us
    ppermute x1, waiting for transfers between devices, on_device(): theirs = lax.ppermute(mine, 'core', swap)  7.81 us
    dot_general x4, matrix products, attend_group(): jnp.einsum('hqk,khd->qhd', probs, value_part, preferred_element_type=jnp....  7 us
  transfers between devices with their start and end apart: 10, of which 7 were waited for; matrix products, arithmetic and copies ran while one was open for 2% of the time, Pallas kernels for 0%

profile of v3, /device:TPU:6, one launch (start us, length us, event | category | flops | bytes accessed | tf_op | source)
XLA Modules:
  0.0 245.9 jit_solution(3414614098629872642)
XLA Ops:
  9.8 1.9 collective-permute-start
  13.7 3.5 %collective-permute-start.1 = (bf16[128,1024]{1,0:T(8,128)(2,1)}, bf16[128,1024]{1,0:T(8,128)(2,1)S(1)}, u32[]{:S(2)}, u32[]{:S(2)}) collective-permute-start(bf16[128,1024]{1,0:T(8,128)(2,1)} %bitcast.81), channel_id=1, source_target_pairs={{0,2},{2,4},{4,6},{6,8},{8,10},{10,12},{12,14},{14,16},{16,18},{18... | collective-permute-start | bytes 786440 | tf_op jit(solution)/shard_map/ppermute | solution.py:18
  17.2 9.1 %collective-permute-done.1 = bf16[128,1024]{1,0:T(8,128)(2,1)S(1)} collective-permute-done((bf16[128,1024]{1,0:T(8,128)(2,1)}, bf16[128,1024]{1,0:T(8,128)(2,1)S(1)}, u32[]{:S(2)}, u32[]{:S(2)}) %collective-permute-start.1) | collective-permute-done | bytes 262176 | tf_op jit(solution)/shard_map/ppermute | solution.py:18
  28.2 9.7 %collective-permute-done.2 = bf16[128,1024]{1,0:T(8,128)(2,1)S(1)} collective-permute-done((bf16[128,1024]{1,0:T(8,128)(2,1)S(1)}, bf16[128,1024]{1,0:T(8,128)(2,1)S(1)}, u32[]{:S(2)}, u32[]{:S(2)}) %collective-permute-start.2) | collective-permute-done | bytes 262176 | tf_op jit(solution)/shard_map/ppermute | solution.py:18
  39.8 11.5 %collective-permute-done.3 = bf16[128,1024]{1,0:T(8,128)(2,1)S(1)} collective-permute-done((bf16[128,1024]{1,0:T(8,128)(2,1)S(1)}, bf16[128,1024]{1,0:T(8,128)(2,1)S(1)}, u32[]{:S(2)}, u32[]{:S(2)}) %collective-permute-start.3) | collective-permute-done | bytes 262176 | tf_op jit(solution)/shard_map/ppermute | solution.py:18
  53.2 8.8 %collective-permute-done.4 = bf16[128,1024]{1,0:T(8,128)(2,1)S(1)} collective-permute-done((bf16[128,1024]{1,0:T(8,128)(2,1)S(1)}, bf16[128,1024]{1,0:T(8,128)(2,1)S(1)}, u32[]{:S(2)}, u32[]{:S(2)}) %collective-permute-start.4) | collective-permute-done | bytes 262176 | tf_op jit(solution)/shard_map/ppermute | solution.py:18
  62.2 48.0 %all-gather.2.cloned.1.call-done = bf16[1024,3072]{1,0:T(8,128)(2,1)} async-done(((bf16[32,3072]{1,0:T(8,128)(2,1)}), bf16[1024,3072]{1,0:T(8,128)(2,1)}) %all-gather.2.cloned.1.call-update) | async-done | bytes 6291472 | tf_op jit(solution)/shard_map/all_gather | solution.py:68
  112.1 2.4 collective-permute-start.5
  116.5 7.8 %collective-permute-done.5 = bf16[5,128,1024]{2,1,0:T(8,128)(2,1)S(1)} collective-permute-done((bf16[5,128,1024]{2,1,0:T(8,128)(2,1)S(1)}, bf16[5,128,1024]{2,1,0:T(8,128)(2,1)S(1)}, u32[]{:S(2)}, u32[]{:S(2)}) %collective-permute-start.5) | collective-permute-done | bytes 1310752 | tf_op jit(solution)/shard_map/ppermute | solution.py:84
  127.7 10.2 %maximum_select_fusion = bf16[1024,6144]{1,0:T(8,128)(2,1)S(1)} fusion(bf16[1024,3072]{1,0:T(8,128)(2,1)} %collective-permute-done.6, bf16[1024,3072]{1,0:T(8,128)(2,1)S(1)} %bitcast.75, pred[]{:T(512)S(6)} %eq.6), kind=kLoop, calls=%fused_computation.20 | loop fusion | flops 56623104 | bytes 25165824 | tf_op jit(solution)/shard_map/jit(_where)/select_n | solution.py:79
  138.4 4.1 %copy-done = bf16[1024,6144]{1,0:T(8,128)(2,1)} copy-done((bf16[1024,6144]{1,0:T(8,128)(2,1)}, bf16[1024,6144]{1,0:T(8,128)(2,1)S(1)}, u32[]{:S(2)}) %copy-start) | copy-done | bytes 12582936
  142.5 6.7 %convolution_convert_fusion = bf16[1152,2048]{1,0:T(8,128)(2,1)} fusion(bf16[1152,1024]{1,0:T(8,128)(2,1)S(1)} %fusion.22, bf16[1024,6144]{1,0:T(8,128)(2,1)S(1)} %maximum_select_fusion), kind=kOutput, calls=%fused_computation.21 | convolution fusion | flops 4834197504 | bytes 11272192 | tf_op jit(solution)/shard_map/dot_general | solution.py:44
  149.4 4.3 %fusion.69 = (bf16[1152,1024]{1,0:T(8,128)(2,1)S(1)}, bf16[1152,1024]{1,0:T(8,128)(2,1)}) fusion(bf16[1152,2048]{1,0:T(8,128)(2,1)} %convolution_convert_fusion), kind=kLoop, calls=%fused_computation.109 | loop fusion | bytes 9437184 | tf_op jit(solution)/shard_map/slice | solution.py:95
  153.7 4.3 %copy.16 = bf16[1152,1024]{0,1:T(8,128)(2,1)} copy(bf16[1152,1024]{1,0:T(8,128)(2,1)} %get-tuple-element.103) | data formatting | bytes 4718592 | tf_op jit(solution)/shard_map/slice | solution.py:96
  158.0 2.6 %copy.18 = bf16[1152,1024]{0,1:T(8,128)(2,1)} copy(bf16[1152,1024]{1,0:T(8,128)(2,1)S(1)} %get-tuple-element.102) | data formatting | bytes 4718592 | tf_op jit(solution)/shard_map/slice | solution.py:95
  160.5 15.3 %while.11 = (s32[]{:T(128)}, bf16[4,128,4,64]{1,3,2,0:T(8,128)(2,1)S(1)}, bf16[4,1152,4,64]{1,3,2,0:T(8,128)(2,1)}, bf16[4,128,4,64]{1,3,2,0:T(8,128)(2,1)S(1)},...) while((s32[]{:T(128)}, ...), condition=%wide.region_4.5_spmd.clone, body=%wide.region_2.4_spmd.clone.sunk | while | flops 154420864 | bytes 8694133 | solution.py:124
  175.8 2.1 convert_reduce_fusion.1
  178.3 3.0 %fusion.23 = f32[128,2048]{1,0:T(8,128)S(1)} fusion(bf16[1024,6144]{1,0:T(8,128)(2,1)} %copy-done, bf16[128,1024]{1,0:T(8,128)(2,1)S(1)} %get-tuple-element.120, f32[1024]{0:T(1024)S(1)} %copy-done.7, f32[128]{0:T(128)S(1)} %add_rsqrt_fusion.2, f32[128]{0:T(128)S(1)} %broadcast_multiply_fusion.1), kind=kOutput, calls=%fused_computation.29 | convolution fusion | flops 537526272 | bytes 5510144 | tf_op jit(solution)/shard_map/dot_general | solution.py:44
  181.5 2.0 collective-permute-start.7
  183.5 5.6 %collective-permute-start.8 = (bf16[4,1024]{1,0:T(4,128)(2,1)S(1)}, bf16[4,1024]{1,0:T(4,128)(2,1)S(1)}, u32[]{:S(2)}, u32[]{:S(2)}) collective-permute-start(bf16[4,1024]{1,0:T(4,128)(2,1)S(1)} %get-tuple-element.105), channel_id=1, source_target_pairs={{1,0},{2,1},{3,2},{4,3},{5,4},{6,5},{7,6},{8,7},{9,8},{10,9},{11,1... | collective-permute-start | bytes 24584 | tf_op jit(solution)/shard_map/ppermute | solution.py:30
  191.2 2.5 %all-reduce.3 = (f32[1024]{0:T(1024)S(1)}, f32[1024]{0:T(1024)S(1)}) all-reduce(f32[1024]{0:T(1024)S(1)} %get-tuple-element.70, f32[1024]{0:T(1024)S(1)} %get-tuple-element.69), channel_id=1, replica_groups=mesh['call'=8,'x'=4,'y'=8,'core'=2] {'core'}, use_global_device_ids=true, to_apply=%region_14.15 | all-reduce | flops 2048 | bytes 16384 | tf_op jit(solution)/shard_map/psum | solution.py:144
  193.7 14.7 %all-reduce = (f32[1024]{0:T(1024)S(1)}, f32[1024]{0:T(1024)S(1)}) all-reduce(f32[1024]{0:T(1024)S(1)} %get-tuple-element.99, f32[1024]{0:T(1024)S(1)} %get-tuple-element.100), channel_id=1, replica_groups=mesh['call'=8,'x'=4,'y'=8,'core'=2] {'y'}, use_global_device_ids=true, to_apply=%region_15.16 | all-reduce | flops 2048 | bytes 16384 | tf_op jit(solution)/shard_map/psum | solution.py:144
  208.4 11.4 %all-reduce.2 = (f32[1024]{0:T(1024)S(1)}, f32[1024]{0:T(1024)S(1)}) all-reduce(f32[1024]{0:T(1024)S(1)} %get-tuple-element.93, f32[1024]{0:T(1024)S(1)} %get-tuple-element.94), channel_id=1, replica_groups=mesh['call'=8,'x'=4,'y'=8,'core'=2] {'x'}, use_global_device_ids=true, to_apply=%region_16.17 | all-reduce | flops 2048 | bytes 16384 | tf_op jit(solution)/shard_map/psum | solution.py:144
  219.8 18.4 %all-reduce.1 = (f32[1024]{0:T(1024)S(1)}, f32[1024]{0:T(1024)S(1)}) all-reduce(f32[1024]{0:T(1024)S(1)} %get-tuple-element.97, f32[1024]{0:T(1024)S(1)} %get-tuple-element.98), channel_id=1, replica_groups=mesh['call'=8,'x'=4,'y'=8,'core'=2] {'call'}, use_global_device_ids=true, to_apply=%region_17.18 | all-reduce | flops 2048 | bytes 16384 | tf_op jit(solution)/shard_map/psum | solution.py:144
  (79 shorter events, 36.0 us)
Async XLA Ops:
  7.2 55.0 %copy-start.1 = (bf16[1,128,1024]{2,1,0:T(8,128)(2,1)S(1)}, bf16[1,128,1024]{2,1,0:T(8,128)(2,1)}, u32[]{:S(2)}) copy-start(bf16[1,128,1024]{2,1,0:T(8,128)(2,1)} %param.12) | copy-start | bytes 786436
  7.2 107.4 %copy-start.8 = (s32[8]{0:T(128)S(1)}, s32[8]{0:T(128)}, u32[]{:S(2)}) copy-start(s32[8]{0:T(128)} %param.13) | copy-start | bytes 100
  7.2 103.0 %all-gather.2.cloned.1.call-start = ((), (), s32[]{:S(2)}) async-start(), calls=%async_computation | async-start | bytes 6488064 | tf_op jit(solution)/shard_map/all_gather | solution.py:68
  9.8 3.2 %collective-permute-start = (bf16[16,3072]{1,0:T(8,128)(2,1)S(1)}, bf16[16,3072]{1,0:T(8,128)(2,1)S(1)}, u32[]{:S(2)}, u32[]{:S(2)}) collective-permute-start(bf16[16,3072]{1,0:T(8,128)(2,1)S(1)} %get-tuple-element.107), channel_id=1, source_target_pairs={{0,1},{1,0},{2,3},{3,2},{4,5},{5,4},{6,7},{7,6},{8,9},{9,8},{10,11... | collective-permute-start | bytes 294920 | tf_op jit(solution)/shard_map/ppermute | solution.py:65
  13.7 12.6 %collective-permute-start.1 = (bf16[128,1024]{1,0:T(8,128)(2,1)}, bf16[128,1024]{1,0:T(8,128)(2,1)S(1)}, u32[]{:S(2)}, u32[]{:S(2)}) collective-permute-start(bf16[128,1024]{1,0:T(8,128)(2,1)} %bitcast.81), channel_id=1, source_target_pairs={{0,2},{2,4},{4,6},{6,8},{8,10},{10,12},{12,14},{14,16},{16,18},{18... | collective-permute-start | bytes 786440 | tf_op jit(solution)/shard_map/ppermute | solution.py:18
  26.3 11.6 %collective-permute-start.2 = (bf16[128,1024]{1,0:T(8,128)(2,1)S(1)}, bf16[128,1024]{1,0:T(8,128)(2,1)S(1)}, u32[]{:S(2)}, u32[]{:S(2)}) collective-permute-start(bf16[128,1024]{1,0:T(8,128)(2,1)S(1)} %collective-permute-done.1), channel_id=1, source_target_pairs={{0,2},{2,4},{4,6},{6,8},{8,10},{10,12},{12,14},{14,16},{16,18},{18... | collective-permute-start | bytes 786440 | tf_op jit(solution)/shard_map/ppermute | solution.py:18
  37.9 13.4 %collective-permute-start.3 = (bf16[128,1024]{1,0:T(8,128)(2,1)S(1)}, bf16[128,1024]{1,0:T(8,128)(2,1)S(1)}, u32[]{:S(2)}, u32[]{:S(2)}) collective-permute-start(bf16[128,1024]{1,0:T(8,128)(2,1)S(1)} %collective-permute-done.2), channel_id=1, source_target_pairs={{0,2},{2,4},{4,6},{6,8},{8,10},{10,12},{12,14},{14,16},{16,18},{18... | collective-permute-start | bytes 786440 | tf_op jit(solution)/shard_map/ppermute | solution.py:18
  51.3 10.8 %collective-permute-start.4 = (bf16[128,1024]{1,0:T(8,128)(2,1)S(1)}, bf16[128,1024]{1,0:T(8,128)(2,1)S(1)}, u32[]{:S(2)}, u32[]{:S(2)}) collective-permute-start(bf16[128,1024]{1,0:T(8,128)(2,1)S(1)} %collective-permute-done.3), channel_id=1, source_target_pairs={{0,2},{2,4},{4,6},{6,8},{8,10},{10,12},{12,14},{14,16},{16,18},{18... | collective-permute-start | bytes 786440 | tf_op jit(solution)/shard_map/ppermute | solution.py:18
  110.2 16.8 %collective-permute-start.6 = (bf16[1024,3072]{1,0:T(8,128)(2,1)}, bf16[1024,3072]{1,0:T(8,128)(2,1)}, u32[]{:S(2)}, u32[]{:S(2)}) collective-permute-start(bf16[1024,3072]{1,0:T(8,128)(2,1)} %all-gather.2.cloned.1.call-done), channel_id=1, source_target_pairs={{0,1},{1,0},{2,3},{3,2},{4,5},{5,4},{6,7},{7,6},{8,9},{9,8},{10,11... | collective-permute-start | bytes 18874376 | tf_op jit(solution)/shard_map/ppermute | solution.py:78
  112.1 12.2 %collective-permute-start.5 = (bf16[5,128,1024]{2,1,0:T(8,128)(2,1)S(1)}, bf16[5,128,1024]{2,1,0:T(8,128)(2,1)S(1)}, u32[]{:S(2)}, u32[]{:S(2)}) collective-permute-start(bf16[5,128,1024]{2,1,0:T(8,128)(2,1)S(1)} %constant_dynamic-update-slice_fusion.2), channel_id=1, source_target_pairs={{0,1},{1,0},{2,3},{3,2},{4,5},{5,4},{6,7},{7,6},{8,9},{9,8},{10,11... | collective-permute-start | bytes 3932168 | tf_op jit(solution)/shard_map/ppermute | solution.py:84
  124.8 2.3 slice-start
  125.0 1.2 copy-start.6
  125.0 2.7 %slice-start.1 = ((s8[6291456]{0:T(1024)(128)(4,1)}), s8[2097152]{0:T(1024)(128)(4,1)S(1)}, s32[]{:S(2)}) async-start(s8[6291456]{0:T(1024)(128)(4,1)} %bitcast.74), calls=%async_computation.2 | async-start | bytes 4194304
  137.9 4.6 %copy-start = (bf16[1024,6144]{1,0:T(8,128)(2,1)}, bf16[1024,6144]{1,0:T(8,128)(2,1)S(1)}, u32[]{:S(2)}) copy-start(bf16[1024,6144]{1,0:T(8,128)(2,1)S(1)} %maximum_select_fusion) | copy-start | bytes 37748740
  175.8 2.4 copy-start.7
  178.0 3.3 %copy-start.2 = (bf16[128,1024]{1,0:T(8,128)(2,1)}, bf16[128,1024]{1,0:T(8,128)(2,1)S(1)}, u32[]{:S(2)}) copy-start(bf16[128,1024]{1,0:T(8,128)(2,1)S(1)} %get-tuple-element.120) | copy-start | bytes 786436
  178.2 10.9 %copy-start.3 = (f32[9,1024]{1,0:T(8,128)S(1)}, f32[9,1024]{1,0:T(8,128)}, u32[]{:S(2)}) copy-start(f32[9,1024]{1,0:T(8,128)} %param.19) | copy-start | bytes 110596
  178.2 59.9 %copy-start.4 = (f32[1024]{0:T(1024)S(1)}, f32[1024]{0:T(1024)}, u32[]{:S(2)}) copy-start(f32[1024]{0:T(1024)} %param.21) | copy-start | bytes 12292
  178.2 59.9 %copy-start.5 = (f32[1024]{0:T(1024)S(1)}, f32[1024]{0:T(1024)}, u32[]{:S(2)}) copy-start(f32[1024]{0:T(1024)} %param.20) | copy-start | bytes 12292
  181.5 9.0 %collective-permute-start.7 = (bf16[4,1024]{1,0:T(4,128)(2,1)S(1)}, bf16[4,1024]{1,0:T(4,128)(2,1)S(1)}, u32[]{:S(2)}, u32[]{:S(2)}) collective-permute-start(bf16[4,1024]{1,0:T(4,128)(2,1)S(1)} %get-tuple-element.104), channel_id=1, source_target_pairs={{0,1},{1,2},{2,3},{3,4},{4,5},{5,6},{6,7},{7,8},{8,9},{9,10},{10,1... | collective-permute-start | bytes 24584 | tf_op jit(solution)/shard_map/ppermute | solution.py:28
  183.5 7.0 %collective-permute-start.8 = (bf16[4,1024]{1,0:T(4,128)(2,1)S(1)}, bf16[4,1024]{1,0:T(4,128)(2,1)S(1)}, u32[]{:S(2)}, u32[]{:S(2)}) collective-permute-start(bf16[4,1024]{1,0:T(4,128)(2,1)S(1)} %get-tuple-element.105), channel_id=1, source_target_pairs={{1,0},{2,1},{3,2},{4,3},{5,4},{6,5},{7,6},{8,7},{9,8},{10,9},{11,1... | collective-permute-start | bytes 24584 | tf_op jit(solution)/shard_map/ppermute | solution.py:30
Sparse Core Ops, SparseCore 0:
  13.8 96.3 all-gather.1

commit v4 on v1

--- a/solution.py
+++ b/solution.py
@@ -78,30 +78,18 @@
     allowed = (key_pos[None, :] >= 0) & (key_pos[None, :] >= span_first[:, None] - LEFT)
     allowed = allowed & (key_pos[None, :] < span_first[:, None] + SPAN)
     allowed = allowed & ((key_pos[None, :] < length) | (key_pos[None, :] == query_pos[:, None]))
-    group_size = 4
-    group_count = head_count // group_size
-    query_groups = queries.reshape(frame_count, group_count, group_size, HEAD_DIM).transpose(
-        1, 0, 2, 3
+    query_heads = queries.reshape(frame_count, head_count, HEAD_DIM)
+    key_heads = keys.reshape(key_count, head_count, HEAD_DIM)
+    value_heads = values.reshape(key_count, head_count, HEAD_DIM)
+    scale_factor = 1.0 / jnp.sqrt(jnp.float32(HEAD_DIM))
+    scores = (
+        jnp.einsum("qhd,khd->hqk", query_heads, key_heads, preferred_element_type=jnp.float32)
+        * scale_factor
     )
-    key_groups = keys.reshape(key_count, group_count, group_size, HEAD_DIM).transpose(1, 0, 2, 3)
-    value_groups = values.reshape(key_count, group_count, group_size, HEAD_DIM).transpose(
-        1, 0, 2, 3
-    )
-    scale_factor = 1.0 / jnp.sqrt(jnp.float32(HEAD_DIM))
-
-    def attend_group(operands):
-        query_part, key_part, value_part = operands
-        scores = (
-            jnp.einsum("qhd,khd->hqk", query_part, key_part, preferred_element_type=jnp.float32)
-            * scale_factor
-        )
-        raised = jnp.where(allowed[None], jnp.exp(scores), 0.0)
-        probs = (raised / jnp.sum(raised, axis=-1, keepdims=True)).astype(jnp.bfloat16)
-        mixed = jnp.einsum("hqk,khd->qhd", probs, value_part, preferred_element_type=jnp.float32)
-        return mixed.astype(jnp.bfloat16)
-
-    context = lax.map(attend_group, (query_groups, key_groups, value_groups))
-    context = context.transpose(1, 0, 2, 3).reshape(frame_count, model_width)
+    raised = jnp.where(allowed[None], jnp.exp(scores), 0.0)
+    probs = (raised / jnp.sum(raised, axis=-1, keepdims=True)).astype(jnp.bfloat16)
+    context = jnp.einsum("hqk,khd->qhd", probs, value_heads, preferred_element_type=jnp.float32)
+    context = context.astype(jnp.bfloat16).reshape(frame_count, model_width)
     projected = contract_with(context, weights[:, qkv_cols : qkv_cols + out_cols])
     attended = jnp.where(frame_valid[:, None], stream.astype(jnp.float32) + projected, 0.0).astype(
         jnp.bfloat16

time: 219 us -> 210 us (0.959)
  matrix products: 28.6 us -> 18.2 us
  waiting for transfers between devices: 82.2 us -> 85.4 us
  blocking collectives: 48.6 us -> 45.6 us
    dot_general x8 -> x2, matrix products: 13.9 us -> 7.25 us  [the longest x1 4.47 us: on_device(): jnp.einsum('qhd,khd->hqk', query_heads, key_heads, preferred_element_type...]
    ppermute x1, waiting for transfers between devices: 0.01 us -> 3.8 us  [with_halo(): lax.ppermute(tail, axis, [(i, (i + 1) % count) for i in range(ends)])]
    dot_general x4, matrix products: 14.7 us -> 10.9 us  [contract_with(): return jnp.dot(left, rows_piece, preferred_element_type=jnp.float32)]
    psum x4, blocking collectives: 48.6 us -> 45.6 us  [on_device(): moments = lax.psum(moments, axis)]
  transfers between devices with their start and end apart: 11 -> 11, of which waited for: 9 -> 10; matrix products, arithmetic and copies ran while one was open for 2% -> 3% of each run, Pallas kernels for 0% -> 0%
where the time goes in v4:
time: 210 us; the launch traced here: 206 us
  waiting for transfers between devices  85.4 us (41%)
  blocking collectives  45.6 us (22%)
  starting transfers between devices  22.8 us (11%)
  matrix products  18.2 us (9%)
  between operations  15.2 us (7%)
  local copies, waits for them, and re-layouts  11.1 us (5%)
  other arithmetic  7.82 us (4%)
    ppermute x8, waiting for transfers between devices, passed_along(): lax.ppermute(value, axis, [(source, source + steps) for source in range(f...  75.4 us
    psum x4, blocking collectives, on_device(): moments = lax.psum(moments, axis)  45.6 us
    ppermute x8, starting transfers between devices, passed_along(): lax.ppermute(value, axis, [(source, source + steps) for source in range(f...  15.4 us
    dot_general x4, matrix products, contract_with(): return jnp.dot(left, rows_piece, preferred_element_type=jnp.float32)  10.9 us
    all_gather x1, waiting for transfers between devices, on_device(): lax.all_gather(jnp.concatenate([w_qkv, w_out, w_pw1], axis=1), TM, axis=0...  6.22 us
    ppermute x1, starting transfers between devices, with_halo(): lax.ppermute(head, axis, [((i + 1) % count, i) for i in range(ends)])  5.42 us
    dot_general x1, matrix products, on_device(): jnp.einsum('qhd,khd->hqk', query_heads, key_heads, preferred_element_type...  4.47 us
    slice x2, local copies, waits for them, and re-layouts, on_device(): keys = key_value[:, :model_width].astype(jnp.bfloat16)  4.45 us
  transfers between devices with their start and end apart: 11, of which 10 were waited for; matrix products, arithmetic and copies ran while one was open for 3% of the time, Pallas kernels for 0%

profile of v4, /device:TPU:6, one launch (start us, length us, event | category | flops | bytes accessed | tf_op | source)
XLA Modules:
  0.0 206.1 jit_solution(13870788760495434567)
XLA Ops:
  8.9 2.1 collective-permute-start
  10.9 8.1 %collective-permute-done = bf16[128,1024]{1,0:T(8,128)(2,1)S(1)} collective-permute-done((bf16[128,1024]{1,0:T(8,128)(2,1)}, bf16[128,1024]{1,0:T(8,128)(2,1)S(1)}, u32[]{:S(2)}, u32[]{:S(2)}) %collective-permute-start) | collective-permute-done | bytes 262176 | tf_op jit(solution)/shard_map/ppermute | solution.py:18
  20.9 7.9 %collective-permute-done.1 = bf16[128,1024]{1,0:T(8,128)(2,1)S(1)} collective-permute-done((bf16[128,1024]{1,0:T(8,128)(2,1)S(1)}, bf16[128,1024]{1,0:T(8,128)(2,1)S(1)}, u32[]{:S(2)}, u32[]{:S(2)}) %collective-permute-start.1) | collective-permute-done | bytes 262176 | tf_op jit(solution)/shard_map/ppermute | solution.py:18
  30.7 9.6 %collective-permute-done.2 = bf16[128,1024]{1,0:T(8,128)(2,1)S(1)} collective-permute-done((bf16[128,1024]{1,0:T(8,128)(2,1)S(1)}, bf16[128,1024]{1,0:T(8,128)(2,1)S(1)}, u32[]{:S(2)}, u32[]{:S(2)}) %collective-permute-start.2) | collective-permute-done | bytes 262176 | tf_op jit(solution)/shard_map/ppermute | solution.py:18
  42.3 9.8 %collective-permute-done.3 = bf16[128,1024]{1,0:T(8,128)(2,1)S(1)} collective-permute-done((bf16[128,1024]{1,0:T(8,128)(2,1)S(1)}, bf16[128,1024]{1,0:T(8,128)(2,1)S(1)}, u32[]{:S(2)}, u32[]{:S(2)}) %collective-permute-start.3) | collective-permute-done | bytes 262176 | tf_op jit(solution)/shard_map/ppermute | solution.py:18
  54.0 7.9 %collective-permute-done.4 = bf16[128,1024]{1,0:T(8,128)(2,1)S(1)} collective-permute-done((bf16[128,1024]{1,0:T(8,128)(2,1)S(1)}, bf16[128,1024]{1,0:T(8,128)(2,1)S(1)}, u32[]{:S(2)}, u32[]{:S(2)}) %collective-permute-start.4) | collective-permute-done | bytes 262176 | tf_op jit(solution)/shard_map/ppermute | solution.py:18
  63.8 7.8 %collective-permute-done.5 = bf16[128,1024]{1,0:T(8,128)(2,1)S(1)} collective-permute-done((bf16[128,1024]{1,0:T(8,128)(2,1)S(1)}, bf16[128,1024]{1,0:T(8,128)(2,1)S(1)}, u32[]{:S(2)}, u32[]{:S(2)}) %collective-permute-start.5) | collective-permute-done | bytes 262176 | tf_op jit(solution)/shard_map/ppermute | solution.py:18
  75.5 11.6 %collective-permute-done.6 = bf16[128,1024]{1,0:T(8,128)(2,1)S(1)} collective-permute-done((bf16[128,1024]{1,0:T(8,128)(2,1)S(1)}, bf16[128,1024]{1,0:T(8,128)(2,1)S(1)}, u32[]{:S(2)}, u32[]{:S(2)}) %collective-permute-start.6) | collective-permute-done | bytes 262176 | tf_op jit(solution)/shard_map/ppermute | solution.py:18
  90.0 12.6 %collective-permute-done.7 = bf16[128,1024]{1,0:T(8,128)(2,1)S(1)} collective-permute-done((bf16[128,1024]{1,0:T(8,128)(2,1)S(1)}, bf16[128,1024]{1,0:T(8,128)(2,1)S(1)}, u32[]{:S(2)}, u32[]{:S(2)}) %collective-permute-start.7) | collective-permute-done | bytes 262176 | tf_op jit(solution)/shard_map/ppermute | solution.py:18
  104.9 6.2 %all-gather.2.cloned.1.call-done = bf16[1024,6144]{1,0:T(8,128)(2,1)} async-done(((bf16[16,6144]{1,0:T(8,128)(2,1)}), bf16[1024,6144]{1,0:T(8,128)(2,1)}) %all-gather.2.cloned.1.call-update) | async-done | bytes 12582928 | tf_op jit(solution)/shard_map/all_gather | solution.py:59
  111.1 7.4 %convolution_convert_fusion = bf16[1152,2048]{1,0:T(8,128)(2,1)S(1)} fusion(bf16[1152,1024]{1,0:T(8,128)(2,1)S(1)} %fusion.5, bf16[1024,6144]{1,0:T(8,128)(2,1)} %all-gather.2.cloned.1.call-done), kind=kOutput, calls=%fused_computation.3 | convolution fusion | flops 4834197504 | bytes 11272192 | tf_op jit(solution)/shard_map/dot_general | solution.py:44
  118.5 1.9 fusion.56
  120.5 4.3 %copy.15 = bf16[1152,1024]{0,1:T(8,128)(2,1)} copy(bf16[1152,1024]{1,0:T(8,128)(2,1)} %get-tuple-element.14) | data formatting | bytes 4718592 | tf_op jit(solution)/shard_map/slice | solution.py:75
  124.8 2.1 %fusion.23 = bf16[128,1024]{1,0:T(8,128)(2,1)S(1)} fusion(bf16[1024,6144]{1,0:T(8,128)(2,1)} %all-gather.2.cloned.1.call-done, bf16[1152,1024]{1,0:T(8,128)(2,1)} %copy-done.1), kind=kOutput, calls=%fused_computation.22 | convolution fusion | flops 268566528 | bytes 2621440 | tf_op jit(solution)/shard_map/dot_general | solution.py:44
  127.1 2.5 %copy.17 = bf16[1152,1024]{0,1:T(8,128)(2,1)} copy(bf16[1152,1024]{1,0:T(8,128)(2,1)S(1)} %get-tuple-element.13) | data formatting | bytes 4718592 | tf_op jit(solution)/shard_map/slice | solution.py:74
  129.6 4.5 %fusion = (f32[16,128]{1,0:T(8,128)S(1)}, f32[16,128,1152]{2,1,0:T(8,128)S(1)}) fusion(pred[128,1152]{1,0:T(8,128)(4,1)S(1)} %or_and_fusion, bf16[128,16,64]{0,2,1:T(8,128)(2,1)S(1)} %bitcast.31, bf16[1152,16,64]{0,2,1:T(8,128)(2,1)} %bitcast.28), kind=kOutput, calls=%fused_computation.2 | convolution fusion | flops 309065728 | bytes 12214272 | tf_op jit(solution)/shard_map/qhd,khd->hqk/dot_general | solution.py:86
  134.1 2.8 %fusion.26 = bf16[16,64,128]{2,1,0:T(8,128)(2,1)S(1)} fusion(bf16[1152,16,64]{0,2,1:T(8,128)(2,1)S(1)} %bitcast.27, f32[16,128,1152]{2,1,0:T(8,128)S(1)} %get-tuple-element.29, f32[16,128]{1,0:T(8,128)S(1)} %get-tuple-element.28, pred[128,1152]{1,0:T(8,128)(4,1)S(1)} %or_and_fusion), kind=kOutput, calls=%fused_computation.23 | convolution fusion | flops 311558144 | bytes 12214272 | tf_op jit(solution)/shard_map/hqk,khd->qhd/dot_general | solution.py:91
  139.4 5.4 %collective-permute-start.9 = (bf16[4,1024]{1,0:T(4,128)(2,1)S(1)}, bf16[4,1024]{1,0:T(4,128)(2,1)S(1)}, u32[]{:S(2)}, u32[]{:S(2)}) collective-permute-start(bf16[4,1024]{1,0:T(4,128)(2,1)S(1)} %get-tuple-element.16), channel_id=1, source_target_pairs={{1,0},{2,1},{3,2},{4,3},{5,4},{6,5},{7,6},{8,7},{9,8},{10,9},{11,1... | collective-permute-start | bytes 24584 | tf_op jit(solution)/shard_map/ppermute | solution.py:30
  144.9 1.9 collective-permute-start.8
  148.1 3.8 %collective-permute-done.8 = bf16[4,1024]{1,0:T(4,128)(2,1)S(1)} collective-permute-done((bf16[4,1024]{1,0:T(4,128)(2,1)S(1)}, bf16[4,1024]{1,0:T(4,128)(2,1)S(1)}, u32[]{:S(2)}, u32[]{:S(2)}) %collective-permute-start.8) | collective-permute-done | bytes 8224 | tf_op jit(solution)/shard_map/ppermute | solution.py:28
  152.6 2.5 %all-reduce.3 = (f32[1024]{0:T(1024)S(1)}, f32[1024]{0:T(1024)S(1)}) all-reduce(f32[1024]{0:T(1024)S(1)} %get-tuple-element.3, f32[1024]{0:T(1024)S(1)} %get-tuple-element.2), channel_id=1, replica_groups=mesh['call'=8,'x'=4,'y'=8,'core'=2] {'core'}, use_global_device_ids=true, to_apply=%region_12.13 | all-reduce | flops 2048 | bytes 16384 | tf_op jit(solution)/shard_map/psum | solution.py:111
  155.1 14.4 %all-reduce = (f32[1024]{0:T(1024)S(1)}, f32[1024]{0:T(1024)S(1)}) all-reduce(f32[1024]{0:T(1024)S(1)} %get-tuple-element.10, f32[1024]{0:T(1024)S(1)} %get-tuple-element.11), channel_id=1, replica_groups=mesh['call'=8,'x'=4,'y'=8,'core'=2] {'y'}, use_global_device_ids=true, to_apply=%region_13.14 | all-reduce | flops 2048 | bytes 16384 | tf_op jit(solution)/shard_map/psum | solution.py:111
  169.5 8.3 %all-reduce.2 = (f32[1024]{0:T(1024)S(1)}, f32[1024]{0:T(1024)S(1)}) all-reduce(f32[1024]{0:T(1024)S(1)} %get-tuple-element.4, f32[1024]{0:T(1024)S(1)} %get-tuple-element.5), channel_id=1, replica_groups=mesh['call'=8,'x'=4,'y'=8,'core'=2] {'x'}, use_global_device_ids=true, to_apply=%region_14.15 | all-reduce | flops 2048 | bytes 16384 | tf_op jit(solution)/shard_map/psum | solution.py:111
  177.8 20.4 %all-reduce.1 = (f32[1024]{0:T(1024)S(1)}, f32[1024]{0:T(1024)S(1)}) all-reduce(f32[1024]{0:T(1024)S(1)} %get-tuple-element.8, f32[1024]{0:T(1024)S(1)} %get-tuple-element.9), channel_id=1, replica_groups=mesh['call'=8,'x'=4,'y'=8,'core'=2] {'call'}, use_global_device_ids=true, to_apply=%region_15.16 | all-reduce | flops 2048 | bytes 16384 | tf_op jit(solution)/shard_map/psum | solution.py:111
  (72 shorter events, 24.9 us)
Async XLA Ops:
  7.2 103.9 %all-gather.2.cloned.1.call-start = ((), (), s32[]{:S(2)}) async-start(), calls=%async_computation | async-start | bytes 12779520 | tf_op jit(solution)/shard_map/all_gather | solution.py:59
  8.9 94.0 %copy-start.2 = (bf16[1,128,1024]{2,1,0:T(8,128)(2,1)S(1)}, bf16[1,128,1024]{2,1,0:T(8,128)(2,1)}, u32[]{:S(2)}) copy-start(bf16[1,128,1024]{2,1,0:T(8,128)(2,1)} %param.10) | copy-start | bytes 786436
  8.9 10.1 %collective-permute-start = (bf16[128,1024]{1,0:T(8,128)(2,1)}, bf16[128,1024]{1,0:T(8,128)(2,1)S(1)}, u32[]{:S(2)}, u32[]{:S(2)}) collective-permute-start(bf16[128,1024]{1,0:T(8,128)(2,1)} %bitcast.29), channel_id=1, source_target_pairs={{0,1},{1,2},{2,3},{3,4},{4,5},{5,6},{6,7},{7,8},{8,9},{9,10},{10,1... | collective-permute-start | bytes 786440 | tf_op jit(solution)/shard_map/ppermute | solution.py:18
  19.0 9.8 %collective-permute-start.1 = (bf16[128,1024]{1,0:T(8,128)(2,1)S(1)}, bf16[128,1024]{1,0:T(8,128)(2,1)S(1)}, u32[]{:S(2)}, u32[]{:S(2)}) collective-permute-start(bf16[128,1024]{1,0:T(8,128)(2,1)S(1)} %collective-permute-done), channel_id=1, source_target_pairs={{0,1},{1,2},{2,3},{3,4},{4,5},{5,6},{6,7},{7,8},{8,9},{9,10},{10,1... | collective-permute-start | bytes 786440 | tf_op jit(solution)/shard_map/ppermute | solution.py:18
  28.8 11.5 %collective-permute-start.2 = (bf16[128,1024]{1,0:T(8,128)(2,1)S(1)}, bf16[128,1024]{1,0:T(8,128)(2,1)S(1)}, u32[]{:S(2)}, u32[]{:S(2)}) collective-permute-start(bf16[128,1024]{1,0:T(8,128)(2,1)S(1)} %collective-permute-done.1), channel_id=1, source_target_pairs={{0,1},{1,2},{2,3},{3,4},{4,5},{5,6},{6,7},{7,8},{8,9},{9,10},{10,1... | collective-permute-start | bytes 786440 | tf_op jit(solution)/shard_map/ppermute | solution.py:18
  40.3 11.8 %collective-permute-start.3 = (bf16[128,1024]{1,0:T(8,128)(2,1)S(1)}, bf16[128,1024]{1,0:T(8,128)(2,1)S(1)}, u32[]{:S(2)}, u32[]{:S(2)}) collective-permute-start(bf16[128,1024]{1,0:T(8,128)(2,1)S(1)} %collective-permute-done.2), channel_id=1, source_target_pairs={{0,1},{1,2},{2,3},{3,4},{4,5},{5,6},{6,7},{7,8},{8,9},{9,10},{10,1... | collective-permute-start | bytes 786440 | tf_op jit(solution)/shard_map/ppermute | solution.py:18
  52.1 9.8 %collective-permute-start.4 = (bf16[128,1024]{1,0:T(8,128)(2,1)S(1)}, bf16[128,1024]{1,0:T(8,128)(2,1)S(1)}, u32[]{:S(2)}, u32[]{:S(2)}) collective-permute-start(bf16[128,1024]{1,0:T(8,128)(2,1)S(1)} %collective-permute-done.3), channel_id=1, source_target_pairs={{0,1},{1,2},{2,3},{3,4},{4,5},{5,6},{6,7},{7,8},{8,9},{9,10},{10,1... | collective-permute-start | bytes 786440 | tf_op jit(solution)/shard_map/ppermute | solution.py:18
  61.9 9.8 %collective-permute-start.5 = (bf16[128,1024]{1,0:T(8,128)(2,1)S(1)}, bf16[128,1024]{1,0:T(8,128)(2,1)S(1)}, u32[]{:S(2)}, u32[]{:S(2)}) collective-permute-start(bf16[128,1024]{1,0:T(8,128)(2,1)S(1)} %collective-permute-done.4), channel_id=1, source_target_pairs={{0,1},{1,2},{2,3},{3,4},{4,5},{5,6},{6,7},{7,8},{8,9},{9,10},{10,1... | collective-permute-start | bytes 786440 | tf_op jit(solution)/shard_map/ppermute | solution.py:18
  71.7 15.5 %collective-permute-start.6 = (bf16[128,1024]{1,0:T(8,128)(2,1)S(1)}, bf16[128,1024]{1,0:T(8,128)(2,1)S(1)}, u32[]{:S(2)}, u32[]{:S(2)}) collective-permute-start(bf16[128,1024]{1,0:T(8,128)(2,1)S(1)} %collective-permute-done.5), channel_id=1, source_target_pairs={{0,1},{1,2},{2,3},{3,4},{4,5},{5,6},{6,7},{7,8},{8,9},{9,10},{10,1... | collective-permute-start | bytes 786440 | tf_op jit(solution)/shard_map/ppermute | solution.py:18
  87.2 15.5 %collective-permute-start.7 = (bf16[128,1024]{1,0:T(8,128)(2,1)S(1)}, bf16[128,1024]{1,0:T(8,128)(2,1)S(1)}, u32[]{:S(2)}, u32[]{:S(2)}) collective-permute-start(bf16[128,1024]{1,0:T(8,128)(2,1)S(1)} %collective-permute-done.6), channel_id=1, source_target_pairs={{0,1},{1,2},{2,3},{3,4},{4,5},{5,6},{6,7},{7,8},{8,9},{9,10},{10,1... | collective-permute-start | bytes 786440 | tf_op jit(solution)/shard_map/ppermute | solution.py:18
  102.9 1.2 copy-start.7
  104.9 6.2 %copy-start.1 = (bf16[1152,1024]{1,0:T(8,128)(2,1)}, bf16[1152,1024]{1,0:T(8,128)(2,1)S(1)}, u32[]{:S(2)}) copy-start(bf16[1152,1024]{1,0:T(8,128)(2,1)S(1)} %fusion.5) | copy-start | bytes 7077892
  129.6 4.5 %copy-start = (bf16[1152,1024]{0,1:T(8,128)(2,1)S(1)}, bf16[1152,1024]{0,1:T(8,128)(2,1)}, u32[]{:S(2)}) copy-start(bf16[1152,1024]{0,1:T(8,128)(2,1)} %copy.15) | copy-start | bytes 7077892
  129.6 7.3 %slice-start = ((s8[12582912]{0:T(1024)(128)(4,1)}), s8[4194304]{0:T(1024)(128)(4,1)S(1)}, s32[]{:S(2)}) async-start(s8[12582912]{0:T(1024)(128)(4,1)} %bitcast.41), calls=%async_computation.1 | async-start | bytes 8388608
  134.1 2.8 %slice-start.1 = ((s8[12582912]{0:T(1024)(128)(4,1)}), s8[4194304]{0:T(1024)(128)(4,1)S(1)}, s32[]{:S(2)}) async-start(s8[12582912]{0:T(1024)(128)(4,1)} %bitcast.41), calls=%async_computation.2 | async-start | bytes 8388608
  134.1 3.5 %slice-start.2 = ((s8[12582912]{0:T(1024)(128)(4,1)}), s8[4194304]{0:T(1024)(128)(4,1)S(1)}, s32[]{:S(2)}) async-start(s8[12582912]{0:T(1024)(128)(4,1)} %bitcast.41), calls=%async_computation.3 | async-start | bytes 8388608
  136.9 1.5 copy-start.8
  138.1 1.1 copy-start.3
  138.4 8.4 %copy-start.4 = (f32[9,1024]{1,0:T(8,128)S(1)}, f32[9,1024]{1,0:T(8,128)}, u32[]{:S(2)}) copy-start(f32[9,1024]{1,0:T(8,128)} %param.17) | copy-start | bytes 110596
  138.4 8.5 %copy-start.9 = (s32[8]{0:T(128)S(1)}, s32[8]{0:T(128)}, u32[]{:S(2)}) copy-start(s32[8]{0:T(128)} %param.11) | copy-start | bytes 100
  139.2 59.1 %copy-start.5 = (f32[1024]{0:T(1024)S(1)}, f32[1024]{0:T(1024)}, u32[]{:S(2)}) copy-start(f32[1024]{0:T(1024)} %param.19) | copy-start | bytes 12292
  139.2 59.1 %copy-start.6 = (f32[1024]{0:T(1024)S(1)}, f32[1024]{0:T(1024)}, u32[]{:S(2)}) copy-start(f32[1024]{0:T(1024)} %param.18) | copy-start | bytes 12292
  139.4 8.7 %collective-permute-start.9 = (bf16[4,1024]{1,0:T(4,128)(2,1)S(1)}, bf16[4,1024]{1,0:T(4,128)(2,1)S(1)}, u32[]{:S(2)}, u32[]{:S(2)}) collective-permute-start(bf16[4,1024]{1,0:T(4,128)(2,1)S(1)} %get-tuple-element.16), channel_id=1, source_target_pairs={{1,0},{2,1},{3,2},{4,3},{5,4},{6,5},{7,6},{8,7},{9,8},{10,9},{11,1... | collective-permute-start | bytes 24584 | tf_op jit(solution)/shard_map/ppermute | solution.py:30
  144.9 7.1 %collective-permute-start.8 = (bf16[4,1024]{1,0:T(4,128)(2,1)S(1)}, bf16[4,1024]{1,0:T(4,128)(2,1)S(1)}, u32[]{:S(2)}, u32[]{:S(2)}) collective-permute-start(bf16[4,1024]{1,0:T(4,128)(2,1)S(1)} %get-tuple-element.15), channel_id=1, source_target_pairs={{0,1},{1,2},{2,3},{3,4},{4,5},{5,6},{6,7},{7,8},{8,9},{9,10},{10,1... | collective-permute-start | bytes 24584 | tf_op jit(solution)/shard_map/ppermute | solution.py:28
Sparse Core Ops, SparseCore 0:
  11.9 99.1 all-gather.1

commit v5 on v4

--- a/solution.py
+++ b/solution.py
@@ -107,9 +107,17 @@
         )
     masked = jnp.where(frame_valid[:, None], depthwise, 0.0)
     moments = (jnp.sum(masked, axis=0), jnp.sum(masked * depthwise, axis=0))
+    moments = jnp.stack(moments)
     for axis in ("core", "y", "x", "call"):
-        moments = lax.psum(moments, axis)
-    first_moment, second_moment = moments
+        count = lax.axis_size(axis)
+        assert count & (count - 1) == 0
+        stride = 1
+        while stride < count:
+            moments = moments + lax.ppermute(
+                moments, axis, [(i, (i + stride) % count) for i in range(count)]
+            )
+            stride *= 2
+    first_moment, second_moment = moments[0], moments[1]
     count_all = jnp.sum(lengths).astype(jnp.float32)
     average = first_moment / count_all
     second = second_moment / count_all

time: 210 us -> 228 us (1.086); the launches traced: 206 us -> 227 us
  blocking collectives: 45.6 us -> 0 us
  waiting for transfers between devices: 85.4 us -> 126 us
  starting transfers between devices: 22.8 us -> 49.4 us
    psum x4 -> x0, blocking collectives: 45.6 us -> none  [on_device(): moments = lax.psum(moments, axis)]
    ppermute x0 -> x9, waiting for transfers between devices: none -> 38.9 us  [on_device(): lax.ppermute(moments, axis, [(i, (i + stride) % count) for i in range(cou...]
    ppermute x0 -> x9, starting transfers between devices: none -> 26.6 us  [on_device(): lax.ppermute(moments, axis, [(i, (i + stride) % count) for i in range(cou...]
  transfers between devices with their start and end apart: 11 -> 20, of which waited for: 10 -> 19; matrix products, arithmetic and copies ran while one was open for 3% -> 2% of each run, Pallas kernels for 0% -> 0%
where the time goes in v5:
time: 228 us; the launch traced here: 227 us
  waiting for transfers between devices  126 us (55%)
  starting transfers between devices  49.4 us (22%)
  matrix products  18.2 us (8%)
  between operations  15.2 us (7%)
  local copies, waits for them, and re-layouts  11.2 us (5%)
  other arithmetic  7.91 us (3%)
    ppermute x8, waiting for transfers between devices, passed_along(): lax.ppermute(value, axis, [(source, source + steps) for source in range(f...  75.4 us
    ppermute x9, waiting for transfers between devices, on_device(): lax.ppermute(moments, axis, [(i, (i + stride) % count) for i in range(cou...  38.9 us
    ppermute x9, starting transfers between devices, on_device(): lax.ppermute(moments, axis, [(i, (i + stride) % count) for i in range(cou...  26.6 us
    ppermute x8, starting transfers between devices, passed_along(): lax.ppermute(value, axis, [(source, source + steps) for source in range(f...  15.4 us
    dot_general x4, matrix products, contract_with(): return jnp.dot(left, rows_piece, preferred_element_type=jnp.float32)  10.9 us
    all_gather x1, waiting for transfers between devices, on_device(): lax.all_gather(jnp.concatenate([w_qkv, w_out, w_pw1], axis=1), TM, axis=0...  6.22 us
    ppermute x1, starting transfers between devices, with_halo(): lax.ppermute(head, axis, [((i + 1) % count, i) for i in range(ends)])  5.43 us
    ppermute x1, waiting for transfers between devices, with_halo(): lax.ppermute(tail, axis, [(i, (i + 1) % count) for i in range(ends)])  5.09 us
  transfers between devices with their start and end apart: 20, of which 19 were waited for; matrix products, arithmetic and copies ran while one was open for 2% of the time, Pallas kernels for 0%

profile of v5, /device:TPU:6, one launch (start us, length us, event | category | flops | bytes accessed | tf_op | source)
XLA Modules:
  0.0 227.5 jit_solution(10893473714457887278)
XLA Ops:
  10.9 8.1 %collective-permute-done = bf16[128,1024]{1,0:T(8,128)(2,1)S(1)} collective-permute-done((bf16[128,1024]{1,0:T(8,128)(2,1)}, bf16[128,1024]{1,0:T(8,128)(2,1)S(1)}, u32[]{:S(2)}, u32[]{:S(2)}) %collective-permute-start) | collective-permute-done | bytes 262176 | tf_op jit(solution)/shard_map/ppermute | solution.py:18
  20.9 7.9 %collective-permute-done.1 = bf16[128,1024]{1,0:T(8,128)(2,1)S(1)} collective-permute-done((bf16[128,1024]{1,0:T(8,128)(2,1)S(1)}, bf16[128,1024]{1,0:T(8,128)(2,1)S(1)}, u32[]{:S(2)}, u32[]{:S(2)}) %collective-permute-start.1) | collective-permute-done | bytes 262176 | tf_op jit(solution)/shard_map/ppermute | solution.py:18
  30.7 9.6 %collective-permute-done.2 = bf16[128,1024]{1,0:T(8,128)(2,1)S(1)} collective-permute-done((bf16[128,1024]{1,0:T(8,128)(2,1)S(1)}, bf16[128,1024]{1,0:T(8,128)(2,1)S(1)}, u32[]{:S(2)}, u32[]{:S(2)}) %collective-permute-start.2) | collective-permute-done | bytes 262176 | tf_op jit(solution)/shard_map/ppermute | solution.py:18
  42.3 9.8 %collective-permute-done.3 = bf16[128,1024]{1,0:T(8,128)(2,1)S(1)} collective-permute-done((bf16[128,1024]{1,0:T(8,128)(2,1)S(1)}, bf16[128,1024]{1,0:T(8,128)(2,1)S(1)}, u32[]{:S(2)}, u32[]{:S(2)}) %collective-permute-start.3) | collective-permute-done | bytes 262176 | tf_op jit(solution)/shard_map/ppermute | solution.py:18
  54.0 7.9 %collective-permute-done.4 = bf16[128,1024]{1,0:T(8,128)(2,1)S(1)} collective-permute-done((bf16[128,1024]{1,0:T(8,128)(2,1)S(1)}, bf16[128,1024]{1,0:T(8,128)(2,1)S(1)}, u32[]{:S(2)}, u32[]{:S(2)}) %collective-permute-start.4) | collective-permute-done | bytes 262176 | tf_op jit(solution)/shard_map/ppermute | solution.py:18
  63.8 7.8 %collective-permute-done.5 = bf16[128,1024]{1,0:T(8,128)(2,1)S(1)} collective-permute-done((bf16[128,1024]{1,0:T(8,128)(2,1)S(1)}, bf16[128,1024]{1,0:T(8,128)(2,1)S(1)}, u32[]{:S(2)}, u32[]{:S(2)}) %collective-permute-start.5) | collective-permute-done | bytes 262176 | tf_op jit(solution)/shard_map/ppermute | solution.py:18
  75.5 11.6 %collective-permute-done.6 = bf16[128,1024]{1,0:T(8,128)(2,1)S(1)} collective-permute-done((bf16[128,1024]{1,0:T(8,128)(2,1)S(1)}, bf16[128,1024]{1,0:T(8,128)(2,1)S(1)}, u32[]{:S(2)}, u32[]{:S(2)}) %collective-permute-start.6) | collective-permute-done | bytes 262176 | tf_op jit(solution)/shard_map/ppermute | solution.py:18
  90.0 12.6 %collective-permute-done.7 = bf16[128,1024]{1,0:T(8,128)(2,1)S(1)} collective-permute-done((bf16[128,1024]{1,0:T(8,128)(2,1)S(1)}, bf16[128,1024]{1,0:T(8,128)(2,1)S(1)}, u32[]{:S(2)}, u32[]{:S(2)}) %collective-permute-start.7) | collective-permute-done | bytes 262176 | tf_op jit(solution)/shard_map/ppermute | solution.py:18
  104.9 6.2 %all-gather.2.cloned.1.call-done = bf16[1024,6144]{1,0:T(8,128)(2,1)} async-done(((bf16[16,6144]{1,0:T(8,128)(2,1)}), bf16[1024,6144]{1,0:T(8,128)(2,1)}) %all-gather.2.cloned.1.call-update) | async-done | bytes 12582928 | tf_op jit(solution)/shard_map/all_gather | solution.py:59
  111.1 7.4 %convolution_convert_fusion = bf16[1152,2048]{1,0:T(8,128)(2,1)S(1)} fusion(bf16[1152,1024]{1,0:T(8,128)(2,1)S(1)} %fusion.5, bf16[1024,6144]{1,0:T(8,128)(2,1)} %all-gather.2.cloned.1.call-done), kind=kOutput, calls=%fused_computation.3 | convolution fusion | flops 4834197504 | bytes 11272192 | tf_op jit(solution)/shard_map/dot_general | solution.py:44
  120.4 4.3 %copy.15 = bf16[1152,1024]{0,1:T(8,128)(2,1)} copy(bf16[1152,1024]{1,0:T(8,128)(2,1)} %get-tuple-element.8) | data formatting | bytes 4718592 | tf_op jit(solution)/shard_map/slice | solution.py:75
  129.7 4.5 %fusion = (f32[16,128]{1,0:T(8,128)S(1)}, f32[16,128,1152]{2,1,0:T(8,128)S(1)}) fusion(pred[128,1152]{1,0:T(8,128)(4,1)S(1)} %or_and_fusion, bf16[128,16,64]{0,2,1:T(8,128)(2,1)S(1)} %bitcast.35, bf16[1152,16,64]{0,2,1:T(8,128)(2,1)} %bitcast.32), kind=kOutput, calls=%fused_computation.2 | convolution fusion | flops 309065728 | bytes 12214272 | tf_op jit(solution)/shard_map/qhd,khd->hqk/dot_general | solution.py:86
  139.5 5.4 %collective-permute-start.9 = (bf16[4,1024]{1,0:T(4,128)(2,1)S(1)}, bf16[4,1024]{1,0:T(4,128)(2,1)S(1)}, u32[]{:S(2)}, u32[]{:S(2)}) collective-permute-start(bf16[4,1024]{1,0:T(4,128)(2,1)S(1)} %get-tuple-element.10), channel_id=1, source_target_pairs={{1,0},{2,1},{3,2},{4,3},{5,4},{6,5},{7,6},{8,7},{9,8},{10,9},{11,1... | collective-permute-start | bytes 24584 | tf_op jit(solution)/shard_map/ppermute | solution.py:30
  146.9 5.1 %collective-permute-done.8 = bf16[4,1024]{1,0:T(4,128)(2,1)S(1)} collective-permute-done((bf16[4,1024]{1,0:T(4,128)(2,1)S(1)}, bf16[4,1024]{1,0:T(4,128)(2,1)S(1)}, u32[]{:S(2)}, u32[]{:S(2)}) %collective-permute-start.8) | collective-permute-done | bytes 8224 | tf_op jit(solution)/shard_map/ppermute | solution.py:28
  157.7 4.8 %collective-permute-done.11 = f32[2,1024]{1,0:T(2,128)S(1)} collective-permute-done((f32[2,1024]{1,0:T(2,128)S(1)}, f32[2,1024]{1,0:T(2,128)S(1)}, u32[]{:S(2)}, u32[]{:S(2)}) %collective-permute-start.11) | collective-permute-done | bytes 8224 | tf_op jit(solution)/shard_map/ppermute | solution.py:116
  164.5 5.7 %collective-permute-done.12 = f32[2,1024]{1,0:T(2,128)S(1)} collective-permute-done((f32[2,1024]{1,0:T(2,128)S(1)}, f32[2,1024]{1,0:T(2,128)S(1)}, u32[]{:S(2)}, u32[]{:S(2)}) %collective-permute-start.12) | collective-permute-done | bytes 8224 | tf_op jit(solution)/shard_map/ppermute | solution.py:116
  170.2 3.4 %collective-permute-start.13 = (f32[2,1024]{1,0:T(2,128)S(1)}, f32[2,1024]{1,0:T(2,128)S(1)}, u32[]{:S(2)}, u32[]{:S(2)}) collective-permute-start(f32[2,1024]{1,0:T(2,128)S(1)} %add.190), channel_id=1, source_target_pairs={{0,8},{2,10},{4,12},{6,14},{8,0},{10,2},{12,4},{14,6},{1,9},{3,11}... | collective-permute-start | bytes 24584 | tf_op jit(solution)/shard_map/ppermute | solution.py:116
  173.7 6.0 %collective-permute-done.13 = f32[2,1024]{1,0:T(2,128)S(1)} collective-permute-done((f32[2,1024]{1,0:T(2,128)S(1)}, f32[2,1024]{1,0:T(2,128)S(1)}, u32[]{:S(2)}, u32[]{:S(2)}) %collective-permute-start.13) | collective-permute-done | bytes 8224 | tf_op jit(solution)/shard_map/ppermute | solution.py:116
  181.6 3.6 %collective-permute-done.14 = f32[2,1024]{1,0:T(2,128)S(1)} collective-permute-done((f32[2,1024]{1,0:T(2,128)S(1)}, f32[2,1024]{1,0:T(2,128)S(1)}, u32[]{:S(2)}, u32[]{:S(2)}) %collective-permute-start.14) | collective-permute-done | bytes 8224 | tf_op jit(solution)/shard_map/ppermute | solution.py:116
  185.2 4.4 %collective-permute-start.15 = (f32[2,1024]{1,0:T(2,128)S(1)}, f32[2,1024]{1,0:T(2,128)S(1)}, u32[]{:S(2)}, u32[]{:S(2)}) collective-permute-start(f32[2,1024]{1,0:T(2,128)S(1)} %add.192), channel_id=1, source_target_pairs={{0,32},{16,48},{32,0},{48,16},{1,33},{17,49},{33,1},{49,17},{2,34}... | collective-permute-start | bytes 24584 | tf_op jit(solution)/shard_map/ppermute | solution.py:116
  192.3 3.5 %collective-permute-start.16 = (f32[2,1024]{1,0:T(2,128)S(1)}, f32[2,1024]{1,0:T(2,128)S(1)}, u32[]{:S(2)}, u32[]{:S(2)}) collective-permute-start(f32[2,1024]{1,0:T(2,128)S(1)} %add.193), channel_id=1, source_target_pairs={{0,64},{64,128},{128,192},{192,256},{256,320},{320,384},{384,448},... | collective-permute-start | bytes 24584 | tf_op jit(solution)/shard_map/ppermute | solution.py:116
  195.8 6.7 %collective-permute-done.16 = f32[2,1024]{1,0:T(2,128)S(1)} collective-permute-done((f32[2,1024]{1,0:T(2,128)S(1)}, f32[2,1024]{1,0:T(2,128)S(1)}, u32[]{:S(2)}, u32[]{:S(2)}) %collective-permute-start.16) | collective-permute-done | bytes 8224 | tf_op jit(solution)/shard_map/ppermute | solution.py:116
  204.5 5.7 %collective-permute-done.17 = f32[2,1024]{1,0:T(2,128)S(1)} collective-permute-done((f32[2,1024]{1,0:T(2,128)S(1)}, f32[2,1024]{1,0:T(2,128)S(1)}, u32[]{:S(2)}, u32[]{:S(2)}) %collective-permute-start.17) | collective-permute-done | bytes 8224 | tf_op jit(solution)/shard_map/ppermute | solution.py:116
  210.2 5.7 %collective-permute-start.18 = (f32[2,1024]{1,0:T(2,128)S(1)}, f32[2,1024]{1,0:T(2,128)S(1)}, u32[]{:S(2)}, u32[]{:S(2)}) collective-permute-start(f32[2,1024]{1,0:T(2,128)S(1)} %add.195), channel_id=1, source_target_pairs={{0,256},{64,320},{128,384},{192,448},{256,0},{320,64},{384,128},{4... | collective-permute-start | bytes 24584 | tf_op jit(solution)/shard_map/ppermute | solution.py:116
  (96 shorter events, 54.2 us)
Async XLA Ops:
  7.2 103.9 %all-gather.2.cloned.1.call-start = ((), (), s32[]{:S(2)}) async-start(), calls=%async_computation | async-start | bytes 12779520 | tf_op jit(solution)/shard_map/all_gather | solution.py:59
  8.9 94.0 %copy-start.2 = (bf16[1,128,1024]{2,1,0:T(8,128)(2,1)S(1)}, bf16[1,128,1024]{2,1,0:T(8,128)(2,1)}, u32[]{:S(2)}) copy-start(bf16[1,128,1024]{2,1,0:T(8,128)(2,1)} %param.10) | copy-start | bytes 786436
  8.9 10.1 %collective-permute-start = (bf16[128,1024]{1,0:T(8,128)(2,1)}, bf16[128,1024]{1,0:T(8,128)(2,1)S(1)}, u32[]{:S(2)}, u32[]{:S(2)}) collective-permute-start(bf16[128,1024]{1,0:T(8,128)(2,1)} %bitcast.33), channel_id=1, source_target_pairs={{0,1},{1,2},{2,3},{3,4},{4,5},{5,6},{6,7},{7,8},{8,9},{9,10},{10,1... | collective-permute-start | bytes 786440 | tf_op jit(solution)/shard_map/ppermute | solution.py:18
  19.0 9.8 %collective-permute-start.1 = (bf16[128,1024]{1,0:T(8,128)(2,1)S(1)}, bf16[128,1024]{1,0:T(8,128)(2,1)S(1)}, u32[]{:S(2)}, u32[]{:S(2)}) collective-permute-start(bf16[128,1024]{1,0:T(8,128)(2,1)S(1)} %collective-permute-done), channel_id=1, source_target_pairs={{0,1},{1,2},{2,3},{3,4},{4,5},{5,6},{6,7},{7,8},{8,9},{9,10},{10,1... | collective-permute-start | bytes 786440 | tf_op jit(solution)/shard_map/ppermute | solution.py:18
  28.8 11.5 %collective-permute-start.2 = (bf16[128,1024]{1,0:T(8,128)(2,1)S(1)}, bf16[128,1024]{1,0:T(8,128)(2,1)S(1)}, u32[]{:S(2)}, u32[]{:S(2)}) collective-permute-start(bf16[128,1024]{1,0:T(8,128)(2,1)S(1)} %collective-permute-done.1), channel_id=1, source_target_pairs={{0,1},{1,2},{2,3},{3,4},{4,5},{5,6},{6,7},{7,8},{8,9},{9,10},{10,1... | collective-permute-start | bytes 786440 | tf_op jit(solution)/shard_map/ppermute | solution.py:18
  40.3 11.8 %collective-permute-start.3 = (bf16[128,1024]{1,0:T(8,128)(2,1)S(1)}, bf16[128,1024]{1,0:T(8,128)(2,1)S(1)}, u32[]{:S(2)}, u32[]{:S(2)}) collective-permute-start(bf16[128,1024]{1,0:T(8,128)(2,1)S(1)} %collective-permute-done.2), channel_id=1, source_target_pairs={{0,1},{1,2},{2,3},{3,4},{4,5},{5,6},{6,7},{7,8},{8,9},{9,10},{10,1... | collective-permute-start | bytes 786440 | tf_op jit(solution)/shard_map/ppermute | solution.py:18
  52.1 9.8 %collective-permute-start.4 = (bf16[128,1024]{1,0:T(8,128)(2,1)S(1)}, bf16[128,1024]{1,0:T(8,128)(2,1)S(1)}, u32[]{:S(2)}, u32[]{:S(2)}) collective-permute-start(bf16[128,1024]{1,0:T(8,128)(2,1)S(1)} %collective-permute-done.3), channel_id=1, source_target_pairs={{0,1},{1,2},{2,3},{3,4},{4,5},{5,6},{6,7},{7,8},{8,9},{9,10},{10,1... | collective-permute-start | bytes 786440 | tf_op jit(solution)/shard_map/ppermute | solution.py:18
  61.9 9.8 %collective-permute-start.5 = (bf16[128,1024]{1,0:T(8,128)(2,1)S(1)}, bf16[128,1024]{1,0:T(8,128)(2,1)S(1)}, u32[]{:S(2)}, u32[]{:S(2)}) collective-permute-start(bf16[128,1024]{1,0:T(8,128)(2,1)S(1)} %collective-permute-done.4), channel_id=1, source_target_pairs={{0,1},{1,2},{2,3},{3,4},{4,5},{5,6},{6,7},{7,8},{8,9},{9,10},{10,1... | collective-permute-start | bytes 786440 | tf_op jit(solution)/shard_map/ppermute | solution.py:18
  71.7 15.5 %collective-permute-start.6 = (bf16[128,1024]{1,0:T(8,128)(2,1)S(1)}, bf16[128,1024]{1,0:T(8,128)(2,1)S(1)}, u32[]{:S(2)}, u32[]{:S(2)}) collective-permute-start(bf16[128,1024]{1,0:T(8,128)(2,1)S(1)} %collective-permute-done.5), channel_id=1, source_target_pairs={{0,1},{1,2},{2,3},{3,4},{4,5},{5,6},{6,7},{7,8},{8,9},{9,10},{10,1... | collective-permute-start | bytes 786440 | tf_op jit(solution)/shard_map/ppermute | solution.py:18
  87.2 15.5 %collective-permute-start.7 = (bf16[128,1024]{1,0:T(8,128)(2,1)S(1)}, bf16[128,1024]{1,0:T(8,128)(2,1)S(1)}, u32[]{:S(2)}, u32[]{:S(2)}) collective-permute-start(bf16[128,1024]{1,0:T(8,128)(2,1)S(1)} %collective-permute-done.6), channel_id=1, source_target_pairs={{0,1},{1,2},{2,3},{3,4},{4,5},{5,6},{6,7},{7,8},{8,9},{9,10},{10,1... | collective-permute-start | bytes 786440 | tf_op jit(solution)/shard_map/ppermute | solution.py:18
  139.3 76.6 %copy-start.9 = (s32[8]{0:T(128)S(1)}, s32[8]{0:T(128)}, u32[]{:S(2)}) copy-start(s32[8]{0:T(128)} %param.11) | copy-start | bytes 100
  139.3 80.4 %copy-start.5 = (f32[1024]{0:T(1024)S(1)}, f32[1024]{0:T(1024)}, u32[]{:S(2)}) copy-start(f32[1024]{0:T(1024)} %param.19) | copy-start | bytes 12292
  139.3 80.4 %copy-start.6 = (f32[1024]{0:T(1024)S(1)}, f32[1024]{0:T(1024)}, u32[]{:S(2)}) copy-start(f32[1024]{0:T(1024)} %param.18) | copy-start | bytes 12292
  139.5 7.4 %collective-permute-start.9 = (bf16[4,1024]{1,0:T(4,128)(2,1)S(1)}, bf16[4,1024]{1,0:T(4,128)(2,1)S(1)}, u32[]{:S(2)}, u32[]{:S(2)}) collective-permute-start(bf16[4,1024]{1,0:T(4,128)(2,1)S(1)} %get-tuple-element.10), channel_id=1, source_target_pairs={{1,0},{2,1},{3,2},{4,3},{5,4},{6,5},{7,6},{8,7},{9,8},{10,9},{11,1... | collective-permute-start | bytes 24584 | tf_op jit(solution)/shard_map/ppermute | solution.py:30
  145.0 7.1 %collective-permute-start.8 = (bf16[4,1024]{1,0:T(4,128)(2,1)S(1)}, bf16[4,1024]{1,0:T(4,128)(2,1)S(1)}, u32[]{:S(2)}, u32[]{:S(2)}) collective-permute-start(bf16[4,1024]{1,0:T(4,128)(2,1)S(1)} %get-tuple-element.9), channel_id=1, source_target_pairs={{0,1},{1,2},{2,3},{3,4},{4,5},{5,6},{6,7},{7,8},{8,9},{9,10},{10,1... | collective-permute-start | bytes 24584 | tf_op jit(solution)/shard_map/ppermute | solution.py:28
  152.7 3.1 %collective-permute-start.10 = (f32[2,1024]{1,0:T(2,128)S(1)}, f32[2,1024]{1,0:T(2,128)S(1)}, u32[]{:S(2)}, u32[]{:S(2)}) collective-permute-start(f32[2,1024]{1,0:T(2,128)S(1)} %pad_maximum_fusion.3), channel_id=1, source_target_pairs={{0,1},{1,0},{2,3},{3,2},{4,5},{5,4},{6,7},{7,6},{8,9},{9,8},{10,11... | collective-permute-start | bytes 24584 | tf_op jit(solution)/shard_map/ppermute | solution.py:116
  155.8 6.8 %collective-permute-start.11 = (f32[2,1024]{1,0:T(2,128)S(1)}, f32[2,1024]{1,0:T(2,128)S(1)}, u32[]{:S(2)}, u32[]{:S(2)}) collective-permute-start(f32[2,1024]{1,0:T(2,128)S(1)} %fusion.56), channel_id=1, source_target_pairs={{0,2},{2,4},{4,6},{6,8},{8,10},{10,12},{12,14},{14,0},{1,3},{3,5},... | collective-permute-start | bytes 24584 | tf_op jit(solution)/shard_map/ppermute | solution.py:116
  162.6 7.7 %collective-permute-start.12 = (f32[2,1024]{1,0:T(2,128)S(1)}, f32[2,1024]{1,0:T(2,128)S(1)}, u32[]{:S(2)}, u32[]{:S(2)}) collective-permute-start(f32[2,1024]{1,0:T(2,128)S(1)} %fusion.65), channel_id=1, source_target_pairs={{0,4},{2,6},{4,8},{6,10},{8,12},{10,14},{12,0},{14,2},{1,5},{3,7},... | collective-permute-start | bytes 24584 | tf_op jit(solution)/shard_map/ppermute | solution.py:116
  170.2 9.4 %collective-permute-start.13 = (f32[2,1024]{1,0:T(2,128)S(1)}, f32[2,1024]{1,0:T(2,128)S(1)}, u32[]{:S(2)}, u32[]{:S(2)}) collective-permute-start(f32[2,1024]{1,0:T(2,128)S(1)} %add.190), channel_id=1, source_target_pairs={{0,8},{2,10},{4,12},{6,14},{8,0},{10,2},{12,4},{14,6},{1,9},{3,11}... | collective-permute-start | bytes 24584 | tf_op jit(solution)/shard_map/ppermute | solution.py:116
  179.7 5.5 %collective-permute-start.14 = (f32[2,1024]{1,0:T(2,128)S(1)}, f32[2,1024]{1,0:T(2,128)S(1)}, u32[]{:S(2)}, u32[]{:S(2)}) collective-permute-start(f32[2,1024]{1,0:T(2,128)S(1)} %add.191), channel_id=1, source_target_pairs={{0,16},{16,32},{32,48},{48,0},{1,17},{17,33},{33,49},{49,1},{2,18}... | collective-permute-start | bytes 24584 | tf_op jit(solution)/shard_map/ppermute | solution.py:116
  185.2 7.0 %collective-permute-start.15 = (f32[2,1024]{1,0:T(2,128)S(1)}, f32[2,1024]{1,0:T(2,128)S(1)}, u32[]{:S(2)}, u32[]{:S(2)}) collective-permute-start(f32[2,1024]{1,0:T(2,128)S(1)} %add.192), channel_id=1, source_target_pairs={{0,32},{16,48},{32,0},{48,16},{1,33},{17,49},{33,1},{49,17},{2,34}... | collective-permute-start | bytes 24584 | tf_op jit(solution)/shard_map/ppermute | solution.py:116
  192.3 10.3 %collective-permute-start.16 = (f32[2,1024]{1,0:T(2,128)S(1)}, f32[2,1024]{1,0:T(2,128)S(1)}, u32[]{:S(2)}, u32[]{:S(2)}) collective-permute-start(f32[2,1024]{1,0:T(2,128)S(1)} %add.193), channel_id=1, source_target_pairs={{0,64},{64,128},{128,192},{192,256},{256,320},{320,384},{384,448},... | collective-permute-start | bytes 24584 | tf_op jit(solution)/shard_map/ppermute | solution.py:116
  202.6 7.6 %collective-permute-start.17 = (f32[2,1024]{1,0:T(2,128)S(1)}, f32[2,1024]{1,0:T(2,128)S(1)}, u32[]{:S(2)}, u32[]{:S(2)}) collective-permute-start(f32[2,1024]{1,0:T(2,128)S(1)} %add.194), channel_id=1, source_target_pairs={{0,128},{64,192},{128,256},{192,320},{256,384},{320,448},{384,0},{... | collective-permute-start | bytes 24584 | tf_op jit(solution)/shard_map/ppermute | solution.py:116
  210.2 9.4 %collective-permute-start.18 = (f32[2,1024]{1,0:T(2,128)S(1)}, f32[2,1024]{1,0:T(2,128)S(1)}, u32[]{:S(2)}, u32[]{:S(2)}) collective-permute-start(f32[2,1024]{1,0:T(2,128)S(1)} %add.195), channel_id=1, source_target_pairs={{0,256},{64,320},{128,384},{192,448},{256,0},{320,64},{384,128},{4... | collective-permute-start | bytes 24584 | tf_op jit(solution)/shard_map/ppermute | solution.py:116
  (9 other events, 36.5 us)
Sparse Core Ops, SparseCore 0:
  11.9 99.1 all-gather.1

commit v6 on v4

--- a/solution.py
+++ b/solution.py
@@ -69,28 +69,31 @@
     key_count = context_frames.shape[0]
     normed_all = layer_norm(context_frames, ln_attn_gain).astype(jnp.bfloat16)
     normed = normed_all[key_count - frame_count :]
-    queries = contract_with(normed, weights[:, :model_width]).astype(jnp.bfloat16)
-    key_value = contract_with(normed_all, weights[:, model_width:qkv_cols])
-    keys = key_value[:, :model_width].astype(jnp.bfloat16)
-    values = key_value[:, model_width:].astype(jnp.bfloat16)
+    def heads_of(rows, columns):
+        piece = weights[:, columns : columns + model_width].reshape(model_width, head_count, HEAD_DIM)
+        return jnp.einsum(
+            "kc,chd->hkd", rows, piece, preferred_element_type=jnp.float32
+        ).astype(jnp.bfloat16)
+
+    query_heads = heads_of(normed, 0)
+    key_heads = heads_of(normed_all, model_width)
+    value_heads = heads_of(normed_all, 2 * model_width)
     key_pos = first_row - prior_blocks * frame_count + jnp.arange(key_count, dtype=jnp.int32)
     span_first = query_pos // SPAN * SPAN
     allowed = (key_pos[None, :] >= 0) & (key_pos[None, :] >= span_first[:, None] - LEFT)
     allowed = allowed & (key_pos[None, :] < span_first[:, None] + SPAN)
     allowed = allowed & ((key_pos[None, :] < length) | (key_pos[None, :] == query_pos[:, None]))
-    query_heads = queries.reshape(frame_count, head_count, HEAD_DIM)
-    key_heads = keys.reshape(key_count, head_count, HEAD_DIM)
-    value_heads = values.reshape(key_count, head_count, HEAD_DIM)
     scale_factor = 1.0 / jnp.sqrt(jnp.float32(HEAD_DIM))
     scores = (
-        jnp.einsum("qhd,khd->hqk", query_heads, key_heads, preferred_element_type=jnp.float32)
+        jnp.einsum("hqd,hkd->hqk", query_heads, key_heads, preferred_element_type=jnp.float32)
         * scale_factor
     )
     raised = jnp.where(allowed[None], jnp.exp(scores), 0.0)
     probs = (raised / jnp.sum(raised, axis=-1, keepdims=True)).astype(jnp.bfloat16)
-    context = jnp.einsum("hqk,khd->qhd", probs, value_heads, preferred_element_type=jnp.float32)
-    context = context.astype(jnp.bfloat16).reshape(frame_count, model_width)
-    projected = contract_with(context, weights[:, qkv_cols : qkv_cols + out_cols])
+    context = jnp.einsum("hqk,hkd->hqd", probs, value_heads, preferred_element_type=jnp.float32)
+    context = context.astype(jnp.bfloat16)
+    out_piece = weights[:, qkv_cols : qkv_cols + out_cols].reshape(head_count, HEAD_DIM, out_cols)
+    projected = jnp.einsum("hqd,hdo->qo", context, out_piece, preferred_element_type=jnp.float32)
     attended = jnp.where(frame_valid[:, None], stream.astype(jnp.float32) + projected, 0.0).astype(
         jnp.bfloat16
     )

time: 210 us -> 224 us (1.067)
  local copies, waits for them, and re-layouts: 11.1 us -> 19.2 us
  matrix products: 18.2 us -> 26.1 us
  waiting for transfers between devices: 85.4 us -> 80.2 us
  blocking collectives: 45.6 us -> 48.8 us
    dot_general x2 -> x4, matrix products: 7.25 us -> 23.1 us  [the longest x1 10.4 us: on_device(): jnp.einsum('hqk,hkd->hqd', probs, value_heads, preferred_element_type=jnp...]
    unnamed x34 -> x27, local copies, waits for them, and re-layouts: 0.86 us -> 12 us
    dot_general x4 -> x1, matrix products: 10.9 us -> 3.02 us  [contract_with(): return jnp.dot(left, rows_piece, preferred_element_type=jnp.float32)]
    ppermute x1, waiting for transfers between devices: 3.8 us -> 0.01 us  [with_halo(): lax.ppermute(tail, axis, [(i, (i + 1) % count) for i in range(ends)])]
    psum x4, blocking collectives: 45.6 us -> 48.8 us  [on_device(): moments = lax.psum(moments, axis)]
    slice x3 -> x1, local copies, waits for them, and re-layouts: 8.76 us -> 5.84 us  [on_device(): weights[:, qkv_cols:qkv_cols + out_cols]]
  transfers between devices with their start and end apart: 11 -> 11, of which waited for: 10 -> 9; matrix products, arithmetic and copies ran while one was open for 3% -> 3% of each run, Pallas kernels for 0% -> 0%
where the time goes in v6:
time: 224 us; the launch traced here: 222 us
  waiting for transfers between devices  80.2 us (36%)
  blocking collectives  48.8 us (22%)
  matrix products  26.1 us (12%)
  starting transfers between devices  23.1 us (10%)
  local copies, waits for them, and re-layouts  19.2 us (9%)
  between operations  15.1 us (7%)
  other arithmetic  9.27 us (4%)
    ppermute x8, waiting for transfers between devices, passed_along(): lax.ppermute(value, axis, [(source, source + steps) for source in range(f...  75.3 us
    psum x4, blocking collectives, on_device(): moments = lax.psum(moments, axis)  48.8 us
    ppermute x8, starting transfers between devices, passed_along(): lax.ppermute(value, axis, [(source, source + steps) for source in range(f...  15.4 us
    unnamed x27, local copies, waits for them, and re-layouts  12 us
    dot_general x1, matrix products, on_device(): jnp.einsum('hqk,hkd->hqd', probs, value_heads, preferred_element_type=jnp...  10.4 us
    dot_general x1, matrix products, on_device(): jnp.einsum('hqd,hkd->hqk', query_heads, key_heads, preferred_element_type...  9.85 us
    slice x1, local copies, waits for them, and re-layouts, on_device(): weights[:, qkv_cols:qkv_cols + out_cols]  5.84 us
    ppermute x1, starting transfers between devices, with_halo(): lax.ppermute(head, axis, [((i + 1) % count, i) for i in range(ends)])  5.51 us
  transfers between devices with their start and end apart: 11, of which 9 were waited for; matrix products, arithmetic and copies ran while one was open for 3% of the time, Pallas kernels for 0%

profile of v6, /device:TPU:6, one launch (start us, length us, event | category | flops | bytes accessed | tf_op | source)
XLA Modules:
  0.0 221.8 jit_solution(6056946399253528110)
XLA Ops:
  10.9 8.1 %collective-permute-done = bf16[128,1024]{1,0:T(8,128)(2,1)S(1)} collective-permute-done((bf16[128,1024]{1,0:T(8,128)(2,1)}, bf16[128,1024]{1,0:T(8,128)(2,1)S(1)}, u32[]{:S(2)}, u32[]{:S(2)}) %collective-permute-start) | collective-permute-done | bytes 262176 | tf_op jit(solution)/shard_map/ppermute | solution.py:18
  20.9 7.9 %collective-permute-done.1 = bf16[128,1024]{1,0:T(8,128)(2,1)S(1)} collective-permute-done((bf16[128,1024]{1,0:T(8,128)(2,1)S(1)}, bf16[128,1024]{1,0:T(8,128)(2,1)S(1)}, u32[]{:S(2)}, u32[]{:S(2)}) %collective-permute-start.1) | collective-permute-done | bytes 262176 | tf_op jit(solution)/shard_map/ppermute | solution.py:18
  30.7 9.6 %collective-permute-done.2 = bf16[128,1024]{1,0:T(8,128)(2,1)S(1)} collective-permute-done((bf16[128,1024]{1,0:T(8,128)(2,1)S(1)}, bf16[128,1024]{1,0:T(8,128)(2,1)S(1)}, u32[]{:S(2)}, u32[]{:S(2)}) %collective-permute-start.2) | collective-permute-done | bytes 262176 | tf_op jit(solution)/shard_map/ppermute | solution.py:18
  42.3 9.8 %collective-permute-done.3 = bf16[128,1024]{1,0:T(8,128)(2,1)S(1)} collective-permute-done((bf16[128,1024]{1,0:T(8,128)(2,1)S(1)}, bf16[128,1024]{1,0:T(8,128)(2,1)S(1)}, u32[]{:S(2)}, u32[]{:S(2)}) %collective-permute-start.3) | collective-permute-done | bytes 262176 | tf_op jit(solution)/shard_map/ppermute | solution.py:18
  54.0 7.9 %collective-permute-done.4 = bf16[128,1024]{1,0:T(8,128)(2,1)S(1)} collective-permute-done((bf16[128,1024]{1,0:T(8,128)(2,1)S(1)}, bf16[128,1024]{1,0:T(8,128)(2,1)S(1)}, u32[]{:S(2)}, u32[]{:S(2)}) %collective-permute-start.4) | collective-permute-done | bytes 262176 | tf_op jit(solution)/shard_map/ppermute | solution.py:18
  63.8 7.8 %collective-permute-done.5 = bf16[128,1024]{1,0:T(8,128)(2,1)S(1)} collective-permute-done((bf16[128,1024]{1,0:T(8,128)(2,1)S(1)}, bf16[128,1024]{1,0:T(8,128)(2,1)S(1)}, u32[]{:S(2)}, u32[]{:S(2)}) %collective-permute-start.5) | collective-permute-done | bytes 262176 | tf_op jit(solution)/shard_map/ppermute | solution.py:18
  75.5 11.6 %collective-permute-done.6 = bf16[128,1024]{1,0:T(8,128)(2,1)S(1)} collective-permute-done((bf16[128,1024]{1,0:T(8,128)(2,1)S(1)}, bf16[128,1024]{1,0:T(8,128)(2,1)S(1)}, u32[]{:S(2)}, u32[]{:S(2)}) %collective-permute-start.6) | collective-permute-done | bytes 262176 | tf_op jit(solution)/shard_map/ppermute | solution.py:18
  90.0 12.6 %collective-permute-done.7 = bf16[128,1024]{1,0:T(8,128)(2,1)S(1)} collective-permute-done((bf16[128,1024]{1,0:T(8,128)(2,1)S(1)}, bf16[128,1024]{1,0:T(8,128)(2,1)S(1)}, u32[]{:S(2)}, u32[]{:S(2)}) %collective-permute-start.7) | collective-permute-done | bytes 262176 | tf_op jit(solution)/shard_map/ppermute | solution.py:18
  104.0 2.2 fusion.5
  106.2 4.9 %all-gather.2.cloned.1.call-done = bf16[1024,6144]{1,0:T(8,128)(2,1)} async-done(((bf16[16,6144]{1,0:T(8,128)(2,1)}), bf16[1024,6144]{1,0:T(8,128)(2,1)}) %all-gather.2.cloned.1.call-update) | async-done | bytes 12582928 | tf_op jit(solution)/shard_map/all_gather | solution.py:59
  111.1 5.8 %fusion.49 = (bf16[1024,1024]{1,0:T(8,128)(2,1)S(1)}, bf16[1024,1024]{1,0:T(8,128)(2,1)}, bf16[1024,1024]{1,0:T(8,128)(2,1)}, bf16[1024,1024]{1,0:T(8,128)(2,1)}) fusion(bf16[1024,6144]{1,0:T(8,128)(2,1)} %all-gather.2.cloned.1.call-done), kind=kLoop, calls=%fused_computation.95 | loop fusion | bytes 16777216 | tf_op jit(solution)/shard_map/slice | solution.py:95
  116.9 3.9 %copy.19 = bf16[1024,1024]{0,1:T(8,128)(2,1)} copy(bf16[1024,1024]{1,0:T(8,128)(2,1)} %get-tuple-element.15) | data formatting | bytes 4194304
  120.9 3.9 %copy.20 = bf16[1024,1024]{0,1:T(8,128)(2,1)} copy(bf16[1024,1024]{1,0:T(8,128)(2,1)} %get-tuple-element.14) | data formatting | bytes 4194304
  124.8 4.0 %copy.21 = bf16[1024,1024]{0,1:T(8,128)(2,1)} copy(bf16[1024,1024]{1,0:T(8,128)(2,1)} %get-tuple-element.16) | data formatting | bytes 4194304
  128.8 2.3 %convolution_convert_fusion.2 = bf16[16,64,128]{2,1,0:T(8,128)(2,1)S(1)} fusion(bf16[1024,16,64]{0,2,1:T(8,128)(2,1)} %bitcast.52, bf16[1152,1024]{1,0:T(8,128)(2,1)} %fusion.5), kind=kOutput, calls=%fused_computation.22 | convolution fusion | flops 268566528 | bytes 2621440 | tf_op jit(solution)/shard_map/kc,chd->hkd/dot_general | solution.py:74
  131.1 9.9 %fusion = (f32[16,128]{1,0:T(8,128)S(1)}, f32[16,128,1152]{2,1,0:T(8,128)}) fusion(pred[128,1152]{1,0:T(8,128)(4,1)S(1)} %or_and_fusion, bf16[16,64,128]{2,1,0:T(8,128)(2,1)S(1)} %convolution_convert_fusion.2, bf16[1024,16,64]{0,2,1:T(8,128)(2,1)} %bitcast.51, bf16[1152,1024]{1,0:T(8,128)(2,1)} %fusion.5), kind=kOutput, calls=%fused_computation.2 | convolution fusion | flops 2726164480 | bytes 14311424 | tf_op jit(solution)/shard_map/hqd,hkd->hqk/dot_general | solution.py:88
  140.9 10.4 %fusion.18 = bf16[16,128,64]{1,2,0:T(8,128)(2,1)S(1)} fusion(bf16[1024,16,64]{0,2,1:T(8,128)(2,1)} %bitcast.50, bf16[1152,1024]{1,0:T(8,128)(2,1)} %fusion.5, f32[16,128,1152]{2,1,0:T(8,128)} %get-tuple-element.31, f32[16,128]{1,0:T(8,128)S(1)} %get-tuple-element.30, pred[128,1152]{1,0:T(8,128)(4,1)S(1)} %or_and_fusion), kind=kOutput, calls=%fused_computation.23 | convolution fusion | flops 2728656896 | bytes 14311424 | tf_op jit(solution)/shard_map/hqk,hkd->hqd/dot_general | solution.py:93
  152.2 3.0 %fusion.7 = f32[128,2048]{1,0:T(8,128)S(1)} fusion(bf16[1024,6144]{1,0:T(8,128)(2,1)} %all-gather.2.cloned.1.call-done, bf16[128,1024]{1,0:T(8,128)(2,1)S(1)} %get-tuple-element.33, f32[1024]{0:T(1024)S(1)} %copy-done.6, f32[128]{0:T(128)S(1)} %add_rsqrt_fusion.2, f32[128]{0:T(128)S(1)} %broadcast_multiply_fusion.1), kind=kOutput, calls=%fused_computation.11 | convolution fusion | flops 537526272 | bytes 5510144 | tf_op jit(solution)/shard_map/dot_general | solution.py:44
  155.4 2.2 collective-permute-start.8
  157.6 5.5 %collective-permute-start.9 = (bf16[4,1024]{1,0:T(4,128)(2,1)S(1)}, bf16[4,1024]{1,0:T(4,128)(2,1)S(1)}, u32[]{:S(2)}, u32[]{:S(2)}) collective-permute-start(bf16[4,1024]{1,0:T(4,128)(2,1)S(1)} %get-tuple-element.18), channel_id=1, source_target_pairs={{1,0},{2,1},{3,2},{4,3},{5,4},{6,5},{7,6},{8,7},{9,8},{10,9},{11,1... | collective-permute-start | bytes 24584 | tf_op jit(solution)/shard_map/ppermute | solution.py:30
  165.2 2.5 %all-reduce.3 = (f32[1024]{0:T(1024)S(1)}, f32[1024]{0:T(1024)S(1)}) all-reduce(f32[1024]{0:T(1024)S(1)} %get-tuple-element.3, f32[1024]{0:T(1024)S(1)} %get-tuple-element.2), channel_id=1, replica_groups=mesh['call'=8,'x'=4,'y'=8,'core'=2] {'core'}, use_global_device_ids=true, to_apply=%region_12.13 | all-reduce | flops 2048 | bytes 16384 | tf_op jit(solution)/shard_map/psum | solution.py:114
  167.7 15.8 %all-reduce = (f32[1024]{0:T(1024)S(1)}, f32[1024]{0:T(1024)S(1)}) all-reduce(f32[1024]{0:T(1024)S(1)} %get-tuple-element.10, f32[1024]{0:T(1024)S(1)} %get-tuple-element.11), channel_id=1, replica_groups=mesh['call'=8,'x'=4,'y'=8,'core'=2] {'y'}, use_global_device_ids=true, to_apply=%region_13.14 | all-reduce | flops 2048 | bytes 16384 | tf_op jit(solution)/shard_map/psum | solution.py:114
  183.4 11.1 %all-reduce.2 = (f32[1024]{0:T(1024)S(1)}, f32[1024]{0:T(1024)S(1)}) all-reduce(f32[1024]{0:T(1024)S(1)} %get-tuple-element.4, f32[1024]{0:T(1024)S(1)} %get-tuple-element.5), channel_id=1, replica_groups=mesh['call'=8,'x'=4,'y'=8,'core'=2] {'x'}, use_global_device_ids=true, to_apply=%region_14.15 | all-reduce | flops 2048 | bytes 16384 | tf_op jit(solution)/shard_map/psum | solution.py:114
  194.6 19.4 %all-reduce.1 = (f32[1024]{0:T(1024)S(1)}, f32[1024]{0:T(1024)S(1)}) all-reduce(f32[1024]{0:T(1024)S(1)} %get-tuple-element.8, f32[1024]{0:T(1024)S(1)} %get-tuple-element.9), channel_id=1, replica_groups=mesh['call'=8,'x'=4,'y'=8,'core'=2] {'call'}, use_global_device_ids=true, to_apply=%region_15.16 | all-reduce | flops 2048 | bytes 16384 | tf_op jit(solution)/shard_map/psum | solution.py:114
  (60 shorter events, 24.6 us)
Async XLA Ops:
  7.2 103.9 %all-gather.2.cloned.1.call-start = ((), (), s32[]{:S(2)}) async-start(), calls=%async_computation | async-start | bytes 12779520 | tf_op jit(solution)/shard_map/all_gather | solution.py:59
  8.9 94.0 %copy-start = (bf16[1,128,1024]{2,1,0:T(8,128)(2,1)S(1)}, bf16[1,128,1024]{2,1,0:T(8,128)(2,1)}, u32[]{:S(2)}) copy-start(bf16[1,128,1024]{2,1,0:T(8,128)(2,1)} %param.10) | copy-start | bytes 786436
  8.9 10.1 %collective-permute-start = (bf16[128,1024]{1,0:T(8,128)(2,1)}, bf16[128,1024]{1,0:T(8,128)(2,1)S(1)}, u32[]{:S(2)}, u32[]{:S(2)}) collective-permute-start(bf16[128,1024]{1,0:T(8,128)(2,1)} %bitcast.53), channel_id=1, source_target_pairs={{0,1},{1,2},{2,3},{3,4},{4,5},{5,6},{6,7},{7,8},{8,9},{9,10},{10,1... | collective-permute-start | bytes 786440 | tf_op jit(solution)/shard_map/ppermute | solution.py:18
  19.0 9.8 %collective-permute-start.1 = (bf16[128,1024]{1,0:T(8,128)(2,1)S(1)}, bf16[128,1024]{1,0:T(8,128)(2,1)S(1)}, u32[]{:S(2)}, u32[]{:S(2)}) collective-permute-start(bf16[128,1024]{1,0:T(8,128)(2,1)S(1)} %collective-permute-done), channel_id=1, source_target_pairs={{0,1},{1,2},{2,3},{3,4},{4,5},{5,6},{6,7},{7,8},{8,9},{9,10},{10,1... | collective-permute-start | bytes 786440 | tf_op jit(solution)/shard_map/ppermute | solution.py:18
  28.8 11.5 %collective-permute-start.2 = (bf16[128,1024]{1,0:T(8,128)(2,1)S(1)}, bf16[128,1024]{1,0:T(8,128)(2,1)S(1)}, u32[]{:S(2)}, u32[]{:S(2)}) collective-permute-start(bf16[128,1024]{1,0:T(8,128)(2,1)S(1)} %collective-permute-done.1), channel_id=1, source_target_pairs={{0,1},{1,2},{2,3},{3,4},{4,5},{5,6},{6,7},{7,8},{8,9},{9,10},{10,1... | collective-permute-start | bytes 786440 | tf_op jit(solution)/shard_map/ppermute | solution.py:18
  40.3 11.7 %collective-permute-start.3 = (bf16[128,1024]{1,0:T(8,128)(2,1)S(1)}, bf16[128,1024]{1,0:T(8,128)(2,1)S(1)}, u32[]{:S(2)}, u32[]{:S(2)}) collective-permute-start(bf16[128,1024]{1,0:T(8,128)(2,1)S(1)} %collective-permute-done.2), channel_id=1, source_target_pairs={{0,1},{1,2},{2,3},{3,4},{4,5},{5,6},{6,7},{7,8},{8,9},{9,10},{10,1... | collective-permute-start | bytes 786440 | tf_op jit(solution)/shard_map/ppermute | solution.py:18
  52.1 9.8 %collective-permute-start.4 = (bf16[128,1024]{1,0:T(8,128)(2,1)S(1)}, bf16[128,1024]{1,0:T(8,128)(2,1)S(1)}, u32[]{:S(2)}, u32[]{:S(2)}) collective-permute-start(bf16[128,1024]{1,0:T(8,128)(2,1)S(1)} %collective-permute-done.3), channel_id=1, source_target_pairs={{0,1},{1,2},{2,3},{3,4},{4,5},{5,6},{6,7},{7,8},{8,9},{9,10},{10,1... | collective-permute-start | bytes 786440 | tf_op jit(solution)/shard_map/ppermute | solution.py:18
  61.9 9.8 %collective-permute-start.5 = (bf16[128,1024]{1,0:T(8,128)(2,1)S(1)}, bf16[128,1024]{1,0:T(8,128)(2,1)S(1)}, u32[]{:S(2)}, u32[]{:S(2)}) collective-permute-start(bf16[128,1024]{1,0:T(8,128)(2,1)S(1)} %collective-permute-done.4), channel_id=1, source_target_pairs={{0,1},{1,2},{2,3},{3,4},{4,5},{5,6},{6,7},{7,8},{8,9},{9,10},{10,1... | collective-permute-start | bytes 786440 | tf_op jit(solution)/shard_map/ppermute | solution.py:18
  71.7 15.4 %collective-permute-start.6 = (bf16[128,1024]{1,0:T(8,128)(2,1)S(1)}, bf16[128,1024]{1,0:T(8,128)(2,1)S(1)}, u32[]{:S(2)}, u32[]{:S(2)}) collective-permute-start(bf16[128,1024]{1,0:T(8,128)(2,1)S(1)} %collective-permute-done.5), channel_id=1, source_target_pairs={{0,1},{1,2},{2,3},{3,4},{4,5},{5,6},{6,7},{7,8},{8,9},{9,10},{10,1... | collective-permute-start | bytes 786440 | tf_op jit(solution)/shard_map/ppermute | solution.py:18
  87.1 15.5 %collective-permute-start.7 = (bf16[128,1024]{1,0:T(8,128)(2,1)S(1)}, bf16[128,1024]{1,0:T(8,128)(2,1)S(1)}, u32[]{:S(2)}, u32[]{:S(2)}) collective-permute-start(bf16[128,1024]{1,0:T(8,128)(2,1)S(1)} %collective-permute-done.6), channel_id=1, source_target_pairs={{0,1},{1,2},{2,3},{3,4},{4,5},{5,6},{6,7},{7,8},{8,9},{9,10},{10,1... | collective-permute-start | bytes 786440 | tf_op jit(solution)/shard_map/ppermute | solution.py:18
  102.8 1.2 copy-start.5
  151.3 0.8 copy-start.6
  151.9 3.3 %copy-start.1 = (bf16[128,1024]{1,0:T(8,128)(2,1)}, bf16[128,1024]{1,0:T(8,128)(2,1)S(1)}, u32[]{:S(2)}) copy-start(bf16[128,1024]{1,0:T(8,128)(2,1)S(1)} %get-tuple-element.33) | copy-start | bytes 786436
  152.2 11.0 %copy-start.2 = (f32[9,1024]{1,0:T(8,128)S(1)}, f32[9,1024]{1,0:T(8,128)}, u32[]{:S(2)}) copy-start(f32[9,1024]{1,0:T(8,128)} %param.17) | copy-start | bytes 110596
  152.2 11.0 %copy-start.7 = (s32[8]{0:T(128)S(1)}, s32[8]{0:T(128)}, u32[]{:S(2)}) copy-start(s32[8]{0:T(128)} %param.11) | copy-start | bytes 100
  155.2 58.8 %copy-start.3 = (f32[1024]{0:T(1024)S(1)}, f32[1024]{0:T(1024)}, u32[]{:S(2)}) copy-start(f32[1024]{0:T(1024)} %param.19) | copy-start | bytes 12292
  155.2 58.8 %copy-start.4 = (f32[1024]{0:T(1024)S(1)}, f32[1024]{0:T(1024)}, u32[]{:S(2)}) copy-start(f32[1024]{0:T(1024)} %param.18) | copy-start | bytes 12292
  155.4 9.0 %collective-permute-start.8 = (bf16[4,1024]{1,0:T(4,128)(2,1)S(1)}, bf16[4,1024]{1,0:T(4,128)(2,1)S(1)}, u32[]{:S(2)}, u32[]{:S(2)}) collective-permute-start(bf16[4,1024]{1,0:T(4,128)(2,1)S(1)} %get-tuple-element.17), channel_id=1, source_target_pairs={{0,1},{1,2},{2,3},{3,4},{4,5},{5,6},{6,7},{7,8},{8,9},{9,10},{10,1... | collective-permute-start | bytes 24584 | tf_op jit(solution)/shard_map/ppermute | solution.py:28
  157.6 6.9 %collective-permute-start.9 = (bf16[4,1024]{1,0:T(4,128)(2,1)S(1)}, bf16[4,1024]{1,0:T(4,128)(2,1)S(1)}, u32[]{:S(2)}, u32[]{:S(2)}) collective-permute-start(bf16[4,1024]{1,0:T(4,128)(2,1)S(1)} %get-tuple-element.18), channel_id=1, source_target_pairs={{1,0},{2,1},{3,2},{4,3},{5,4},{6,5},{7,6},{8,7},{9,8},{10,9},{11,1... | collective-permute-start | bytes 24584 | tf_op jit(solution)/shard_map/ppermute | solution.py:30
Sparse Core Ops, SparseCore 0:
  11.9 99.1 all-gather.1

commit v7 on v4

--- a/solution.py
+++ b/solution.py
@@ -2,6 +2,7 @@
 import jax.numpy as jnp
 import numpy as np
 from jax import lax
+from jax.experimental import pallas as pl
 from jax.sharding import Mesh
 from jax.sharding import PartitionSpec as P
 
@@ -44,6 +45,48 @@
     return jnp.dot(left, rows_piece, preferred_element_type=jnp.float32)
 
 
+def attend_kernel(q_ref, k_ref, v_ref, m_ref, o_ref):
+    width = q_ref.shape[1]
+    heads = width // HEAD_DIM
+    allowed = m_ref[...] > 0.5
+    lane = lax.broadcasted_iota(jnp.int32, (1, width), 1)
+    result = jnp.zeros(o_ref.shape, jnp.float32)
+    for head in range(heads):
+        inside = (lane >= head * HEAD_DIM) & (lane < (head + 1) * HEAD_DIM)
+        query = jnp.where(inside, q_ref[...], jnp.zeros_like(q_ref[...]))
+        scores = lax.dot_general(
+            query, k_ref[...], (((1,), (1,)), ((), ())), preferred_element_type=jnp.float32
+        ) * (1.0 / jnp.sqrt(jnp.float32(HEAD_DIM)))
+        raised = jnp.where(allowed, jnp.exp(scores), 0.0)
+        probs = (raised / jnp.sum(raised, axis=-1, keepdims=True)).astype(jnp.bfloat16)
+        mixed = jnp.dot(probs, v_ref[...], preferred_element_type=jnp.float32)
+        result = jnp.where(inside, mixed, result)
+    o_ref[...] = result.astype(o_ref.dtype)
+
+def attend(queries, key_value, allowed):
+    rows, width = queries.shape
+    keys = key_value.shape[0]
+    tile = 128
+    steps = width // tile
+    return pl.pallas_call(
+        attend_kernel,
+        out_shape=jax.ShapeDtypeStruct((rows, width), jnp.bfloat16),
+        grid=(steps,),
+        in_specs=[
+            pl.BlockSpec((rows, tile), lambda i: (0, i)),
+            pl.BlockSpec((keys, tile), lambda i: (0, i)),
+            pl.BlockSpec((keys, tile), lambda i: (0, i + steps)),
+            pl.BlockSpec((rows, keys), lambda i: (0, 0)),
+        ],
+        out_specs=pl.BlockSpec((rows, tile), lambda i: (0, i)),
+        cost_estimate=pl.CostEstimate(
+            flops=4 * rows * keys * width * tile // HEAD_DIM,
+            transcendentals=rows * keys * width // HEAD_DIM,
+            bytes_accessed=2 * (2 * rows * width + 2 * keys * width) + 4 * rows * keys,
+        ),
+    )(queries, key_value, key_value, allowed.astype(jnp.float32))
+
+
 def on_device(
     frames, lengths, ln_attn_gain, w_qkv, w_out, ln_conv_gain, w_pw1, dw_kernel, bn_gain, bn_bias
 ):
@@ -70,26 +113,13 @@
     normed_all = layer_norm(context_frames, ln_attn_gain).astype(jnp.bfloat16)
     normed = normed_all[key_count - frame_count :]
     queries = contract_with(normed, weights[:, :model_width]).astype(jnp.bfloat16)
-    key_value = contract_with(normed_all, weights[:, model_width:qkv_cols])
-    keys = key_value[:, :model_width].astype(jnp.bfloat16)
-    values = key_value[:, model_width:].astype(jnp.bfloat16)
+    key_value = contract_with(normed_all, weights[:, model_width:qkv_cols]).astype(jnp.bfloat16)
     key_pos = first_row - prior_blocks * frame_count + jnp.arange(key_count, dtype=jnp.int32)
     span_first = query_pos // SPAN * SPAN
     allowed = (key_pos[None, :] >= 0) & (key_pos[None, :] >= span_first[:, None] - LEFT)
     allowed = allowed & (key_pos[None, :] < span_first[:, None] + SPAN)
     allowed = allowed & ((key_pos[None, :] < length) | (key_pos[None, :] == query_pos[:, None]))
-    query_heads = queries.reshape(frame_count, head_count, HEAD_DIM)
-    key_heads = keys.reshape(key_count, head_count, HEAD_DIM)
-    value_heads = values.reshape(key_count, head_count, HEAD_DIM)
-    scale_factor = 1.0 / jnp.sqrt(jnp.float32(HEAD_DIM))
-    scores = (
-        jnp.einsum("qhd,khd->hqk", query_heads, key_heads, preferred_element_type=jnp.float32)
-        * scale_factor
-    )
-    raised = jnp.where(allowed[None], jnp.exp(scores), 0.0)
-    probs = (raised / jnp.sum(raised, axis=-1, keepdims=True)).astype(jnp.bfloat16)
-    context = jnp.einsum("hqk,khd->qhd", probs, value_heads, preferred_element_type=jnp.float32)
-    context = context.astype(jnp.bfloat16).reshape(frame_count, model_width)
+    context = attend(queries, key_value, allowed)
     projected = contract_with(context, weights[:, qkv_cols : qkv_cols + out_cols])
     attended = jnp.where(frame_valid[:, None], stream.astype(jnp.float32) + projected, 0.0).astype(
         jnp.bfloat16

time: 210 us -> 207 us (0.986)
  Pallas kernels: 0 us -> 10.1 us
  local copies, waits for them, and re-layouts: 11.1 us -> 1.5 us
  waiting for transfers between devices: 85.4 us -> 81 us
  blocking collectives: 45.6 us -> 48.5 us
    pallas_call x0 -> x1, Pallas kernels: none -> 10.1 us  [attend(): pl.pallas_call(attend_kernel, out_shape=jax.ShapeDtypeStruct((rows, width...]
    slice x3 -> x0, local copies, waits for them, and re-layouts: 8.76 us -> none  [the longest x2 4.45 us: on_device(): keys = key_value[:, :model_width].astype(jnp.bfloat16)]
    dot_general x2 -> x0, matrix products: 7.25 us -> none  [the longest x1 4.47 us: on_device(): jnp.einsum('qhd,khd->hqk', query_heads, key_heads, preferred_element_type...]
    dot_general x4, matrix products: 10.9 us -> 16.8 us  [contract_with(): return jnp.dot(left, rows_piece, preferred_element_type=jnp.float32)]
    ppermute x1, waiting for transfers between devices: 3.8 us -> 0.01 us  [with_halo(): lax.ppermute(tail, axis, [(i, (i + 1) % count) for i in range(ends)])]
    psum x4, blocking collectives: 45.6 us -> 48.5 us  [on_device(): moments = lax.psum(moments, axis)]
  transfers between devices with their start and end apart: 11 -> 11, of which waited for: 10 -> 9; matrix products, arithmetic and copies ran while one was open for 3% -> 3% of each run, Pallas kernels for 0% -> 0%
where the time goes in v7:
time: 207 us; the launch traced here: 205 us
  waiting for transfers between devices  81 us (39%)
  blocking collectives  48.5 us (23%)
  starting transfers between devices  23 us (11%)
  matrix products  16.8 us (8%)
  between operations  15.1 us (7%)
  Pallas kernels  10.1 us (5%)
  other arithmetic  8.61 us (4%)
    ppermute x8, waiting for transfers between devices, passed_along(): lax.ppermute(value, axis, [(source, source + steps) for source in range(f...  74.4 us
    psum x4, blocking collectives, on_device(): moments = lax.psum(moments, axis)  48.5 us
    dot_general x4, matrix products, contract_with(): return jnp.dot(left, rows_piece, preferred_element_type=jnp.float32)  16.8 us
    ppermute x8, starting transfers between devices, passed_along(): lax.ppermute(value, axis, [(source, source + steps) for source in range(f...  15.3 us
    pallas_call x1, Pallas kernels, attend(): pl.pallas_call(attend_kernel, out_shape=jax.ShapeDtypeStruct((rows, width...  10.1 us
    all_gather x1, waiting for transfers between devices, on_device(): lax.all_gather(jnp.concatenate([w_qkv, w_out, w_pw1], axis=1), TM, axis=0...  6.57 us
    ppermute x1, starting transfers between devices, with_halo(): lax.ppermute(head, axis, [((i + 1) % count, i) for i in range(ends)])  5.52 us
  transfers between devices with their start and end apart: 11, of which 9 were waited for; matrix products, arithmetic and copies ran while one was open for 3% of the time, Pallas kernels for 0%

profile of v7, /device:TPU:6, one launch (start us, length us, event | category | flops | bytes accessed | tf_op | source)
XLA Modules:
  0.0 204.6 jit_solution(2304783067521088327)
XLA Ops:
  8.9 1.9 collective-permute-start
  10.8 8.1 %collective-permute-done = bf16[128,1024]{1,0:T(8,128)(2,1)S(1)} collective-permute-done((bf16[128,1024]{1,0:T(8,128)(2,1)}, bf16[128,1024]{1,0:T(8,128)(2,1)S(1)}, u32[]{:S(2)}, u32[]{:S(2)}) %collective-permute-start) | collective-permute-done | bytes 262176 | tf_op jit(solution)/shard_map/ppermute | solution.py:19
  18.9 1.9 collective-permute-start.1
  20.8 7.9 %collective-permute-done.1 = bf16[128,1024]{1,0:T(8,128)(2,1)S(1)} collective-permute-done((bf16[128,1024]{1,0:T(8,128)(2,1)S(1)}, bf16[128,1024]{1,0:T(8,128)(2,1)S(1)}, u32[]{:S(2)}, u32[]{:S(2)}) %collective-permute-start.1) | collective-permute-done | bytes 262176 | tf_op jit(solution)/shard_map/ppermute | solution.py:19
  30.6 9.5 %collective-permute-done.2 = bf16[128,1024]{1,0:T(8,128)(2,1)S(1)} collective-permute-done((bf16[128,1024]{1,0:T(8,128)(2,1)S(1)}, bf16[128,1024]{1,0:T(8,128)(2,1)S(1)}, u32[]{:S(2)}, u32[]{:S(2)}) %collective-permute-start.2) | collective-permute-done | bytes 262176 | tf_op jit(solution)/shard_map/ppermute | solution.py:19
  40.1 1.9 collective-permute-start.3
  42.0 9.7 %collective-permute-done.3 = bf16[128,1024]{1,0:T(8,128)(2,1)S(1)} collective-permute-done((bf16[128,1024]{1,0:T(8,128)(2,1)S(1)}, bf16[128,1024]{1,0:T(8,128)(2,1)S(1)}, u32[]{:S(2)}, u32[]{:S(2)}) %collective-permute-start.3) | collective-permute-done | bytes 262176 | tf_op jit(solution)/shard_map/ppermute | solution.py:19
  53.6 7.9 %collective-permute-done.4 = bf16[128,1024]{1,0:T(8,128)(2,1)S(1)} collective-permute-done((bf16[128,1024]{1,0:T(8,128)(2,1)S(1)}, bf16[128,1024]{1,0:T(8,128)(2,1)S(1)}, u32[]{:S(2)}, u32[]{:S(2)}) %collective-permute-start.4) | collective-permute-done | bytes 262176 | tf_op jit(solution)/shard_map/ppermute | solution.py:19
  61.5 1.9 collective-permute-start.5
  63.5 7.8 %collective-permute-done.5 = bf16[128,1024]{1,0:T(8,128)(2,1)S(1)} collective-permute-done((bf16[128,1024]{1,0:T(8,128)(2,1)S(1)}, bf16[128,1024]{1,0:T(8,128)(2,1)S(1)}, u32[]{:S(2)}, u32[]{:S(2)}) %collective-permute-start.5) | collective-permute-done | bytes 262176 | tf_op jit(solution)/shard_map/ppermute | solution.py:19
  75.2 11.7 %collective-permute-done.6 = bf16[128,1024]{1,0:T(8,128)(2,1)S(1)} collective-permute-done((bf16[128,1024]{1,0:T(8,128)(2,1)S(1)}, bf16[128,1024]{1,0:T(8,128)(2,1)S(1)}, u32[]{:S(2)}, u32[]{:S(2)}) %collective-permute-start.6) | collective-permute-done | bytes 262176 | tf_op jit(solution)/shard_map/ppermute | solution.py:19
  90.5 11.9 %collective-permute-done.7 = bf16[128,1024]{1,0:T(8,128)(2,1)S(1)} collective-permute-done((bf16[128,1024]{1,0:T(8,128)(2,1)S(1)}, bf16[128,1024]{1,0:T(8,128)(2,1)S(1)}, u32[]{:S(2)}, u32[]{:S(2)}) %collective-permute-start.7) | collective-permute-done | bytes 262176 | tf_op jit(solution)/shard_map/ppermute | solution.py:19
  104.6 6.6 %all-gather.2.cloned.1.call-done = bf16[1024,6144]{1,0:T(8,128)(2,1)} async-done(((bf16[16,6144]{1,0:T(8,128)(2,1)}), bf16[1024,6144]{1,0:T(8,128)(2,1)}) %all-gather.2.cloned.1.call-update) | async-done | bytes 12582928 | tf_op jit(solution)/shard_map/all_gather | solution.py:102
  111.2 8.8 %convolution_convert_fusion.k_ref.v_ref = bf16[1152,2048]{1,0:T(8,128)(2,1)} fusion(bf16[1152,1024]{1,0:T(8,128)(2,1)S(1)} %fusion.4, bf16[1024,6144]{1,0:T(8,128)(2,1)} %all-gather.2.cloned.1.call-done), kind=kOutput, calls=%fused_computation | convolution fusion | flops 4834197504 | bytes 11272192 | tf_op jit(solution)/shard_map/dot_general | solution.py:45
  120.0 2.7 %fusion.21.q_ref = bf16[128,1024]{1,0:T(8,128)(2,1)} fusion(bf16[1024,6144]{1,0:T(8,128)(2,1)} %all-gather.2.cloned.1.call-done, bf16[1152,1024]{1,0:T(8,128)(2,1)S(1)} %fusion.4), kind=kOutput, calls=%fused_computation.18 | convolution fusion | flops 268566528 | bytes 2621440 | tf_op jit(solution)/shard_map/dot_general | solution.py:45
  122.7 10.1 %shard_map.113 = bf16[128,1024]{1,0:T(8,128)(2,1)} custom-call(bf16[128,1024]{1,0:T(8,128)(2,1)} %fusion.21.q_ref, bf16[1152,2048]{1,0:T(8,128)(2,1)} %convolution_convert_fusion.k_ref.v_ref, bf16[1152,2048]{1,0:T(8,128)(2,1)} %convolution_convert_fusion.k_ref.v_ref, f32[128,1152]{1,0:T(8,128)} %and_convert_fusion.m_ref), custom_call_target="tpu_custom_call" | custom-call | flops 1207959552 | bytes 5832704 | tf_op jit(solution)/shard_map/pallas_call | solution.py:71
  132.8 2.2 %convert_reduce_fusion.1 = (f32[128]{0:T(128)S(1)}, bf16[128,1024]{1,0:T(8,128)(2,1)S(1)}) fusion(bf16[128,1024]{1,0:T(8,128)(2,1)} %shard_map.113, bf16[1024,6144]{1,0:T(8,128)(2,1)} %all-gather.2.cloned.1.call-done, bf16[1,128,1024]{2,1,0:T(8,128)(2,1)S(1)} %copy-done, pred[128]{0:T(512)(128)(4,1)S(1)} %broadcast_compare_fusion), kind=kOutput, calls=%fused_computation.22 | convolution fusion | flops 269221760 | bytes 2884224 | tf_op jit(solution)/shard_map/dot_general | solution.py:45
  135.3 3.0 %fusion.5 = f32[128,2048]{1,0:T(8,128)S(1)} fusion(bf16[1024,6144]{1,0:T(8,128)(2,1)} %all-gather.2.cloned.1.call-done, bf16[128,1024]{1,0:T(8,128)(2,1)S(1)} %get-tuple-element.27, f32[1024]{0:T(1024)S(1)} %copy-done.6, f32[128]{0:T(128)S(1)} %add_rsqrt_fusion.2, f32[128]{0:T(128)S(1)} %broadcast_multiply_fusion.1), kind=kOutput, calls=%fused_computation.8 | convolution fusion | flops 537526272 | bytes 5510144 | tf_op jit(solution)/shard_map/dot_general | solution.py:45
  138.6 2.2 %collective-permute-start.8 = (bf16[4,1024]{1,0:T(4,128)(2,1)S(1)}, bf16[4,1024]{1,0:T(4,128)(2,1)S(1)}, u32[]{:S(2)}, u32[]{:S(2)}) collective-permute-start(bf16[4,1024]{1,0:T(4,128)(2,1)S(1)} %get-tuple-element.13), channel_id=1, source_target_pairs={{0,1},{1,2},{2,3},{3,4},{4,5},{5,6},{6,7},{7,8},{8,9},{9,10},{10,1... | collective-permute-start | bytes 24584 | tf_op jit(solution)/shard_map/ppermute | solution.py:29
  140.8 5.5 %collective-permute-start.9 = (bf16[4,1024]{1,0:T(4,128)(2,1)S(1)}, bf16[4,1024]{1,0:T(4,128)(2,1)S(1)}, u32[]{:S(2)}, u32[]{:S(2)}) collective-permute-start(bf16[4,1024]{1,0:T(4,128)(2,1)S(1)} %get-tuple-element.14), channel_id=1, source_target_pairs={{1,0},{2,1},{3,2},{4,3},{5,4},{6,5},{7,6},{8,7},{9,8},{10,9},{11,1... | collective-permute-start | bytes 24584 | tf_op jit(solution)/shard_map/ppermute | solution.py:31
  148.3 2.5 %all-reduce.3 = (f32[1024]{0:T(1024)S(1)}, f32[1024]{0:T(1024)S(1)}) all-reduce(f32[1024]{0:T(1024)S(1)} %get-tuple-element.3, f32[1024]{0:T(1024)S(1)} %get-tuple-element.2), channel_id=1, replica_groups=mesh['call'=8,'x'=4,'y'=8,'core'=2] {'core'}, use_global_device_ids=true, to_apply=%region_11.12 | all-reduce | flops 2048 | bytes 16384 | tf_op jit(solution)/shard_map/psum | solution.py:141
  150.8 15.7 %all-reduce = (f32[1024]{0:T(1024)S(1)}, f32[1024]{0:T(1024)S(1)}) all-reduce(f32[1024]{0:T(1024)S(1)} %get-tuple-element.10, f32[1024]{0:T(1024)S(1)} %get-tuple-element.11), channel_id=1, replica_groups=mesh['call'=8,'x'=4,'y'=8,'core'=2] {'y'}, use_global_device_ids=true, to_apply=%region_12.13 | all-reduce | flops 2048 | bytes 16384 | tf_op jit(solution)/shard_map/psum | solution.py:141
  166.5 11.1 %all-reduce.2 = (f32[1024]{0:T(1024)S(1)}, f32[1024]{0:T(1024)S(1)}) all-reduce(f32[1024]{0:T(1024)S(1)} %get-tuple-element.4, f32[1024]{0:T(1024)S(1)} %get-tuple-element.5), channel_id=1, replica_groups=mesh['call'=8,'x'=4,'y'=8,'core'=2] {'x'}, use_global_device_ids=true, to_apply=%region_13.14 | all-reduce | flops 2048 | bytes 16384 | tf_op jit(solution)/shard_map/psum | solution.py:141
  177.6 19.2 %all-reduce.1 = (f32[1024]{0:T(1024)S(1)}, f32[1024]{0:T(1024)S(1)}) all-reduce(f32[1024]{0:T(1024)S(1)} %get-tuple-element.8, f32[1024]{0:T(1024)S(1)} %get-tuple-element.9), channel_id=1, replica_groups=mesh['call'=8,'x'=4,'y'=8,'core'=2] {'call'}, use_global_device_ids=true, to_apply=%region_14.15 | all-reduce | flops 2048 | bytes 16384 | tf_op jit(solution)/shard_map/psum | solution.py:141
  (56 shorter events, 17.8 us)
Async XLA Ops:
  7.2 104.0 %all-gather.2.cloned.1.call-start = ((), (), s32[]{:S(2)}) async-start(), calls=%async_computation | async-start | bytes 12779520 | tf_op jit(solution)/shard_map/all_gather | solution.py:102
  8.9 10.0 %collective-permute-start = (bf16[128,1024]{1,0:T(8,128)(2,1)}, bf16[128,1024]{1,0:T(8,128)(2,1)S(1)}, u32[]{:S(2)}, u32[]{:S(2)}) collective-permute-start(bf16[128,1024]{1,0:T(8,128)(2,1)} %bitcast.18), channel_id=1, source_target_pairs={{0,1},{1,2},{2,3},{3,4},{4,5},{5,6},{6,7},{7,8},{8,9},{9,10},{10,1... | collective-permute-start | bytes 786440 | tf_op jit(solution)/shard_map/ppermute | solution.py:19
  18.9 9.8 %collective-permute-start.1 = (bf16[128,1024]{1,0:T(8,128)(2,1)S(1)}, bf16[128,1024]{1,0:T(8,128)(2,1)S(1)}, u32[]{:S(2)}, u32[]{:S(2)}) collective-permute-start(bf16[128,1024]{1,0:T(8,128)(2,1)S(1)} %collective-permute-done), channel_id=1, source_target_pairs={{0,1},{1,2},{2,3},{3,4},{4,5},{5,6},{6,7},{7,8},{8,9},{9,10},{10,1... | collective-permute-start | bytes 786440 | tf_op jit(solution)/shard_map/ppermute | solution.py:19
  28.7 11.4 %collective-permute-start.2 = (bf16[128,1024]{1,0:T(8,128)(2,1)S(1)}, bf16[128,1024]{1,0:T(8,128)(2,1)S(1)}, u32[]{:S(2)}, u32[]{:S(2)}) collective-permute-start(bf16[128,1024]{1,0:T(8,128)(2,1)S(1)} %collective-permute-done.1), channel_id=1, source_target_pairs={{0,1},{1,2},{2,3},{3,4},{4,5},{5,6},{6,7},{7,8},{8,9},{9,10},{10,1... | collective-permute-start | bytes 786440 | tf_op jit(solution)/shard_map/ppermute | solution.py:19
  40.1 11.6 %collective-permute-start.3 = (bf16[128,1024]{1,0:T(8,128)(2,1)S(1)}, bf16[128,1024]{1,0:T(8,128)(2,1)S(1)}, u32[]{:S(2)}, u32[]{:S(2)}) collective-permute-start(bf16[128,1024]{1,0:T(8,128)(2,1)S(1)} %collective-permute-done.2), channel_id=1, source_target_pairs={{0,1},{1,2},{2,3},{3,4},{4,5},{5,6},{6,7},{7,8},{8,9},{9,10},{10,1... | collective-permute-start | bytes 786440 | tf_op jit(solution)/shard_map/ppermute | solution.py:19
  51.7 9.8 %collective-permute-start.4 = (bf16[128,1024]{1,0:T(8,128)(2,1)S(1)}, bf16[128,1024]{1,0:T(8,128)(2,1)S(1)}, u32[]{:S(2)}, u32[]{:S(2)}) collective-permute-start(bf16[128,1024]{1,0:T(8,128)(2,1)S(1)} %collective-permute-done.3), channel_id=1, source_target_pairs={{0,1},{1,2},{2,3},{3,4},{4,5},{5,6},{6,7},{7,8},{8,9},{9,10},{10,1... | collective-permute-start | bytes 786440 | tf_op jit(solution)/shard_map/ppermute | solution.py:19
  61.5 9.8 %collective-permute-start.5 = (bf16[128,1024]{1,0:T(8,128)(2,1)S(1)}, bf16[128,1024]{1,0:T(8,128)(2,1)S(1)}, u32[]{:S(2)}, u32[]{:S(2)}) collective-permute-start(bf16[128,1024]{1,0:T(8,128)(2,1)S(1)} %collective-permute-done.4), channel_id=1, source_target_pairs={{0,1},{1,2},{2,3},{3,4},{4,5},{5,6},{6,7},{7,8},{8,9},{9,10},{10,1... | collective-permute-start | bytes 786440 | tf_op jit(solution)/shard_map/ppermute | solution.py:19
  71.3 15.5 %collective-permute-start.6 = (bf16[128,1024]{1,0:T(8,128)(2,1)S(1)}, bf16[128,1024]{1,0:T(8,128)(2,1)S(1)}, u32[]{:S(2)}, u32[]{:S(2)}) collective-permute-start(bf16[128,1024]{1,0:T(8,128)(2,1)S(1)} %collective-permute-done.5), channel_id=1, source_target_pairs={{0,1},{1,2},{2,3},{3,4},{4,5},{5,6},{6,7},{7,8},{8,9},{9,10},{10,1... | collective-permute-start | bytes 786440 | tf_op jit(solution)/shard_map/ppermute | solution.py:19
  86.9 15.5 %collective-permute-start.7 = (bf16[128,1024]{1,0:T(8,128)(2,1)S(1)}, bf16[128,1024]{1,0:T(8,128)(2,1)S(1)}, u32[]{:S(2)}, u32[]{:S(2)}) collective-permute-start(bf16[128,1024]{1,0:T(8,128)(2,1)S(1)} %collective-permute-done.6), channel_id=1, source_target_pairs={{0,1},{1,2},{2,3},{3,4},{4,5},{5,6},{6,7},{7,8},{8,9},{9,10},{10,1... | collective-permute-start | bytes 786440 | tf_op jit(solution)/shard_map/ppermute | solution.py:19
  88.8 13.8 %copy-start = (bf16[1,128,1024]{2,1,0:T(8,128)(2,1)S(1)}, bf16[1,128,1024]{2,1,0:T(8,128)(2,1)}, u32[]{:S(2)}) copy-start(bf16[1,128,1024]{2,1,0:T(8,128)(2,1)} %param.10) | copy-start | bytes 786436
  102.6 1.2 copy-start.5
  132.8 2.5 %copy-start.6 = (f32[1024]{0:T(1024)S(1)}, f32[1024]{0:T(1024)}, u32[]{:S(2)}) copy-start(f32[1024]{0:T(1024)} %param.15) | copy-start | bytes 12292
  135.1 3.3 %copy-start.1 = (bf16[128,1024]{1,0:T(8,128)(2,1)}, bf16[128,1024]{1,0:T(8,128)(2,1)S(1)}, u32[]{:S(2)}) copy-start(bf16[128,1024]{1,0:T(8,128)(2,1)S(1)} %get-tuple-element.27) | copy-start | bytes 786436
  135.3 11.0 %copy-start.2 = (f32[9,1024]{1,0:T(8,128)S(1)}, f32[9,1024]{1,0:T(8,128)}, u32[]{:S(2)}) copy-start(f32[9,1024]{1,0:T(8,128)} %param.17) | copy-start | bytes 110596
  135.3 11.0 %copy-start.7 = (s32[8]{0:T(128)S(1)}, s32[8]{0:T(128)}, u32[]{:S(2)}) copy-start(s32[8]{0:T(128)} %param.11) | copy-start | bytes 100
  138.4 58.5 %copy-start.3 = (f32[1024]{0:T(1024)S(1)}, f32[1024]{0:T(1024)}, u32[]{:S(2)}) copy-start(f32[1024]{0:T(1024)} %param.19) | copy-start | bytes 12292
  138.4 58.5 %copy-start.4 = (f32[1024]{0:T(1024)S(1)}, f32[1024]{0:T(1024)}, u32[]{:S(2)}) copy-start(f32[1024]{0:T(1024)} %param.18) | copy-start | bytes 12292
  138.6 9.0 %collective-permute-start.8 = (bf16[4,1024]{1,0:T(4,128)(2,1)S(1)}, bf16[4,1024]{1,0:T(4,128)(2,1)S(1)}, u32[]{:S(2)}, u32[]{:S(2)}) collective-permute-start(bf16[4,1024]{1,0:T(4,128)(2,1)S(1)} %get-tuple-element.13), channel_id=1, source_target_pairs={{0,1},{1,2},{2,3},{3,4},{4,5},{5,6},{6,7},{7,8},{8,9},{9,10},{10,1... | collective-permute-start | bytes 24584 | tf_op jit(solution)/shard_map/ppermute | solution.py:29
  140.8 6.9 %collective-permute-start.9 = (bf16[4,1024]{1,0:T(4,128)(2,1)S(1)}, bf16[4,1024]{1,0:T(4,128)(2,1)S(1)}, u32[]{:S(2)}, u32[]{:S(2)}) collective-permute-start(bf16[4,1024]{1,0:T(4,128)(2,1)S(1)} %get-tuple-element.14), channel_id=1, source_target_pairs={{1,0},{2,1},{3,2},{4,3},{5,4},{6,5},{7,6},{8,7},{9,8},{10,9},{11,1... | collective-permute-start | bytes 24584 | tf_op jit(solution)/shard_map/ppermute | solution.py:31
Sparse Core Ops, SparseCore 0:
  11.9 99.2 all-gather.1

commit v8 on v7

--- a/solution.py
+++ b/solution.py
@@ -58,9 +58,9 @@
             query, k_ref[...], (((1,), (1,)), ((), ())), preferred_element_type=jnp.float32
         ) * (1.0 / jnp.sqrt(jnp.float32(HEAD_DIM)))
         raised = jnp.where(allowed, jnp.exp(scores), 0.0)
-        probs = (raised / jnp.sum(raised, axis=-1, keepdims=True)).astype(jnp.bfloat16)
-        mixed = jnp.dot(probs, v_ref[...], preferred_element_type=jnp.float32)
-        result = jnp.where(inside, mixed, result)
+        total = jnp.sum(raised, axis=-1, keepdims=True)
+        mixed = jnp.dot(raised.astype(jnp.bfloat16), v_ref[...], preferred_element_type=jnp.float32)
+        result = jnp.where(inside, mixed / total, result)
     o_ref[...] = result.astype(o_ref.dtype)
 
 def attend(queries, key_value, allowed):

time: 207 us -> 206 us (level)
  no operation moved by 1% of the time
where the time goes in v8:
time: 206 us; the launch traced here: 203 us
  waiting for transfers between devices  81 us (39%)
  blocking collectives  48.5 us (24%)
  starting transfers between devices  23 us (11%)
  matrix products  16.8 us (8%)
  between operations  15.1 us (7%)
  Pallas kernels  8.9 us (4%)
  other arithmetic  8.61 us (4%)
    ppermute x8, waiting for transfers between devices, passed_along(): lax.ppermute(value, axis, [(source, source + steps) for source in range(f...  74.4 us
    psum x4, blocking collectives, on_device(): moments = lax.psum(moments, axis)  48.5 us
    dot_general x4, matrix products, contract_with(): return jnp.dot(left, rows_piece, preferred_element_type=jnp.float32)  16.8 us
    ppermute x8, starting transfers between devices, passed_along(): lax.ppermute(value, axis, [(source, source + steps) for source in range(f...  15.3 us
    pallas_call x1, Pallas kernels, attend(): pl.pallas_call(attend_kernel, out_shape=jax.ShapeDtypeStruct((rows, width...  8.9 us
    all_gather x1, waiting for transfers between devices, on_device(): lax.all_gather(jnp.concatenate([w_qkv, w_out, w_pw1], axis=1), TM, axis=0...  6.57 us
    ppermute x1, starting transfers between devices, with_halo(): lax.ppermute(head, axis, [((i + 1) % count, i) for i in range(ends)])  5.51 us
  transfers between devices with their start and end apart: 11, of which 9 were waited for; matrix products, arithmetic and copies ran while one was open for 3% of the time, Pallas kernels for 0%

profile of v8, /device:TPU:6, one launch (start us, length us, event | category | flops | bytes accessed | tf_op | source)
XLA Modules:
  0.0 203.4 jit_solution(433745640580700521)
XLA Ops:
  8.9 1.9 collective-permute-start
  10.8 8.1 %collective-permute-done = bf16[128,1024]{1,0:T(8,128)(2,1)S(1)} collective-permute-done((bf16[128,1024]{1,0:T(8,128)(2,1)}, bf16[128,1024]{1,0:T(8,128)(2,1)S(1)}, u32[]{:S(2)}, u32[]{:S(2)}) %collective-permute-start) | collective-permute-done | bytes 262176 | tf_op jit(solution)/shard_map/ppermute | solution.py:19
  18.9 1.9 collective-permute-start.1
  20.8 7.9 %collective-permute-done.1 = bf16[128,1024]{1,0:T(8,128)(2,1)S(1)} collective-permute-done((bf16[128,1024]{1,0:T(8,128)(2,1)S(1)}, bf16[128,1024]{1,0:T(8,128)(2,1)S(1)}, u32[]{:S(2)}, u32[]{:S(2)}) %collective-permute-start.1) | collective-permute-done | bytes 262176 | tf_op jit(solution)/shard_map/ppermute | solution.py:19
  30.6 9.5 %collective-permute-done.2 = bf16[128,1024]{1,0:T(8,128)(2,1)S(1)} collective-permute-done((bf16[128,1024]{1,0:T(8,128)(2,1)S(1)}, bf16[128,1024]{1,0:T(8,128)(2,1)S(1)}, u32[]{:S(2)}, u32[]{:S(2)}) %collective-permute-start.2) | collective-permute-done | bytes 262176 | tf_op jit(solution)/shard_map/ppermute | solution.py:19
  40.1 1.9 collective-permute-start.3
  42.0 9.7 %collective-permute-done.3 = bf16[128,1024]{1,0:T(8,128)(2,1)S(1)} collective-permute-done((bf16[128,1024]{1,0:T(8,128)(2,1)S(1)}, bf16[128,1024]{1,0:T(8,128)(2,1)S(1)}, u32[]{:S(2)}, u32[]{:S(2)}) %collective-permute-start.3) | collective-permute-done | bytes 262176 | tf_op jit(solution)/shard_map/ppermute | solution.py:19
  53.6 7.9 %collective-permute-done.4 = bf16[128,1024]{1,0:T(8,128)(2,1)S(1)} collective-permute-done((bf16[128,1024]{1,0:T(8,128)(2,1)S(1)}, bf16[128,1024]{1,0:T(8,128)(2,1)S(1)}, u32[]{:S(2)}, u32[]{:S(2)}) %collective-permute-start.4) | collective-permute-done | bytes 262176 | tf_op jit(solution)/shard_map/ppermute | solution.py:19
  61.5 1.9 collective-permute-start.5
  63.5 7.8 %collective-permute-done.5 = bf16[128,1024]{1,0:T(8,128)(2,1)S(1)} collective-permute-done((bf16[128,1024]{1,0:T(8,128)(2,1)S(1)}, bf16[128,1024]{1,0:T(8,128)(2,1)S(1)}, u32[]{:S(2)}, u32[]{:S(2)}) %collective-permute-start.5) | collective-permute-done | bytes 262176 | tf_op jit(solution)/shard_map/ppermute | solution.py:19
  75.2 11.7 %collective-permute-done.6 = bf16[128,1024]{1,0:T(8,128)(2,1)S(1)} collective-permute-done((bf16[128,1024]{1,0:T(8,128)(2,1)S(1)}, bf16[128,1024]{1,0:T(8,128)(2,1)S(1)}, u32[]{:S(2)}, u32[]{:S(2)}) %collective-permute-start.6) | collective-permute-done | bytes 262176 | tf_op jit(solution)/shard_map/ppermute | solution.py:19
  90.5 11.9 %collective-permute-done.7 = bf16[128,1024]{1,0:T(8,128)(2,1)S(1)} collective-permute-done((bf16[128,1024]{1,0:T(8,128)(2,1)S(1)}, bf16[128,1024]{1,0:T(8,128)(2,1)S(1)}, u32[]{:S(2)}, u32[]{:S(2)}) %collective-permute-start.7) | collective-permute-done | bytes 262176 | tf_op jit(solution)/shard_map/ppermute | solution.py:19
  104.6 6.6 %all-gather.2.cloned.1.call-done = bf16[1024,6144]{1,0:T(8,128)(2,1)} async-done(((bf16[16,6144]{1,0:T(8,128)(2,1)}), bf16[1024,6144]{1,0:T(8,128)(2,1)}) %all-gather.2.cloned.1.call-update) | async-done | bytes 12582928 | tf_op jit(solution)/shard_map/all_gather | solution.py:102
  111.2 8.8 %convolution_convert_fusion.k_ref.v_ref = bf16[1152,2048]{1,0:T(8,128)(2,1)} fusion(bf16[1152,1024]{1,0:T(8,128)(2,1)S(1)} %fusion.4, bf16[1024,6144]{1,0:T(8,128)(2,1)} %all-gather.2.cloned.1.call-done), kind=kOutput, calls=%fused_computation | convolution fusion | flops 4834197504 | bytes 11272192 | tf_op jit(solution)/shard_map/dot_general | solution.py:45
  120.0 2.7 %fusion.21.q_ref = bf16[128,1024]{1,0:T(8,128)(2,1)} fusion(bf16[1024,6144]{1,0:T(8,128)(2,1)} %all-gather.2.cloned.1.call-done, bf16[1152,1024]{1,0:T(8,128)(2,1)S(1)} %fusion.4), kind=kOutput, calls=%fused_computation.18 | convolution fusion | flops 268566528 | bytes 2621440 | tf_op jit(solution)/shard_map/dot_general | solution.py:45
  122.7 8.9 %shard_map.113 = bf16[128,1024]{1,0:T(8,128)(2,1)} custom-call(bf16[128,1024]{1,0:T(8,128)(2,1)} %fusion.21.q_ref, bf16[1152,2048]{1,0:T(8,128)(2,1)} %convolution_convert_fusion.k_ref.v_ref, bf16[1152,2048]{1,0:T(8,128)(2,1)} %convolution_convert_fusion.k_ref.v_ref, f32[128,1152]{1,0:T(8,128)} %and_convert_fusion.m_ref), custom_call_target="tpu_custom_call" | custom-call | flops 1207959552 | bytes 5832704 | tf_op jit(solution)/shard_map/pallas_call | solution.py:71
  131.6 2.2 %convert_reduce_fusion.1 = (f32[128]{0:T(128)S(1)}, bf16[128,1024]{1,0:T(8,128)(2,1)S(1)}) fusion(bf16[128,1024]{1,0:T(8,128)(2,1)} %shard_map.113, bf16[1024,6144]{1,0:T(8,128)(2,1)} %all-gather.2.cloned.1.call-done, bf16[1,128,1024]{2,1,0:T(8,128)(2,1)S(1)} %copy-done, pred[128]{0:T(512)(128)(4,1)S(1)} %broadcast_compare_fusion), kind=kOutput, calls=%fused_computation.22 | convolution fusion | flops 269221760 | bytes 2884224 | tf_op jit(solution)/shard_map/dot_general | solution.py:45
  134.1 3.0 %fusion.5 = f32[128,2048]{1,0:T(8,128)S(1)} fusion(bf16[1024,6144]{1,0:T(8,128)(2,1)} %all-gather.2.cloned.1.call-done, bf16[128,1024]{1,0:T(8,128)(2,1)S(1)} %get-tuple-element.27, f32[1024]{0:T(1024)S(1)} %copy-done.6, f32[128]{0:T(128)S(1)} %add_rsqrt_fusion.2, f32[128]{0:T(128)S(1)} %broadcast_multiply_fusion.1), kind=kOutput, calls=%fused_computation.8 | convolution fusion | flops 537526272 | bytes 5510144 | tf_op jit(solution)/shard_map/dot_general | solution.py:45
  137.4 2.2 %collective-permute-start.8 = (bf16[4,1024]{1,0:T(4,128)(2,1)S(1)}, bf16[4,1024]{1,0:T(4,128)(2,1)S(1)}, u32[]{:S(2)}, u32[]{:S(2)}) collective-permute-start(bf16[4,1024]{1,0:T(4,128)(2,1)S(1)} %get-tuple-element.13), channel_id=1, source_target_pairs={{0,1},{1,2},{2,3},{3,4},{4,5},{5,6},{6,7},{7,8},{8,9},{9,10},{10,1... | collective-permute-start | bytes 24584 | tf_op jit(solution)/shard_map/ppermute | solution.py:29
  139.6 5.5 %collective-permute-start.9 = (bf16[4,1024]{1,0:T(4,128)(2,1)S(1)}, bf16[4,1024]{1,0:T(4,128)(2,1)S(1)}, u32[]{:S(2)}, u32[]{:S(2)}) collective-permute-start(bf16[4,1024]{1,0:T(4,128)(2,1)S(1)} %get-tuple-element.14), channel_id=1, source_target_pairs={{1,0},{2,1},{3,2},{4,3},{5,4},{6,5},{7,6},{8,7},{9,8},{10,9},{11,1... | collective-permute-start | bytes 24584 | tf_op jit(solution)/shard_map/ppermute | solution.py:31
  147.1 2.5 %all-reduce.3 = (f32[1024]{0:T(1024)S(1)}, f32[1024]{0:T(1024)S(1)}) all-reduce(f32[1024]{0:T(1024)S(1)} %get-tuple-element.3, f32[1024]{0:T(1024)S(1)} %get-tuple-element.2), channel_id=1, replica_groups=mesh['call'=8,'x'=4,'y'=8,'core'=2] {'core'}, use_global_device_ids=true, to_apply=%region_11.12 | all-reduce | flops 2048 | bytes 16384 | tf_op jit(solution)/shard_map/psum | solution.py:141
  149.6 15.7 %all-reduce = (f32[1024]{0:T(1024)S(1)}, f32[1024]{0:T(1024)S(1)}) all-reduce(f32[1024]{0:T(1024)S(1)} %get-tuple-element.10, f32[1024]{0:T(1024)S(1)} %get-tuple-element.11), channel_id=1, replica_groups=mesh['call'=8,'x'=4,'y'=8,'core'=2] {'y'}, use_global_device_ids=true, to_apply=%region_12.13 | all-reduce | flops 2048 | bytes 16384 | tf_op jit(solution)/shard_map/psum | solution.py:141
  165.3 11.1 %all-reduce.2 = (f32[1024]{0:T(1024)S(1)}, f32[1024]{0:T(1024)S(1)}) all-reduce(f32[1024]{0:T(1024)S(1)} %get-tuple-element.4, f32[1024]{0:T(1024)S(1)} %get-tuple-element.5), channel_id=1, replica_groups=mesh['call'=8,'x'=4,'y'=8,'core'=2] {'x'}, use_global_device_ids=true, to_apply=%region_13.14 | all-reduce | flops 2048 | bytes 16384 | tf_op jit(solution)/shard_map/psum | solution.py:141
  176.4 19.2 %all-reduce.1 = (f32[1024]{0:T(1024)S(1)}, f32[1024]{0:T(1024)S(1)}) all-reduce(f32[1024]{0:T(1024)S(1)} %get-tuple-element.8, f32[1024]{0:T(1024)S(1)} %get-tuple-element.9), channel_id=1, replica_groups=mesh['call'=8,'x'=4,'y'=8,'core'=2] {'call'}, use_global_device_ids=true, to_apply=%region_14.15 | all-reduce | flops 2048 | bytes 16384 | tf_op jit(solution)/shard_map/psum | solution.py:141
  (56 shorter events, 17.8 us)
Async XLA Ops:
  7.2 104.0 %all-gather.2.cloned.1.call-start = ((), (), s32[]{:S(2)}) async-start(), calls=%async_computation | async-start | bytes 12779520 | tf_op jit(solution)/shard_map/all_gather | solution.py:102
  8.9 10.0 %collective-permute-start = (bf16[128,1024]{1,0:T(8,128)(2,1)}, bf16[128,1024]{1,0:T(8,128)(2,1)S(1)}, u32[]{:S(2)}, u32[]{:S(2)}) collective-permute-start(bf16[128,1024]{1,0:T(8,128)(2,1)} %bitcast.18), channel_id=1, source_target_pairs={{0,1},{1,2},{2,3},{3,4},{4,5},{5,6},{6,7},{7,8},{8,9},{9,10},{10,1... | collective-permute-start | bytes 786440 | tf_op jit(solution)/shard_map/ppermute | solution.py:19
  18.9 9.8 %collective-permute-start.1 = (bf16[128,1024]{1,0:T(8,128)(2,1)S(1)}, bf16[128,1024]{1,0:T(8,128)(2,1)S(1)}, u32[]{:S(2)}, u32[]{:S(2)}) collective-permute-start(bf16[128,1024]{1,0:T(8,128)(2,1)S(1)} %collective-permute-done), channel_id=1, source_target_pairs={{0,1},{1,2},{2,3},{3,4},{4,5},{5,6},{6,7},{7,8},{8,9},{9,10},{10,1... | collective-permute-start | bytes 786440 | tf_op jit(solution)/shard_map/ppermute | solution.py:19
  28.7 11.4 %collective-permute-start.2 = (bf16[128,1024]{1,0:T(8,128)(2,1)S(1)}, bf16[128,1024]{1,0:T(8,128)(2,1)S(1)}, u32[]{:S(2)}, u32[]{:S(2)}) collective-permute-start(bf16[128,1024]{1,0:T(8,128)(2,1)S(1)} %collective-permute-done.1), channel_id=1, source_target_pairs={{0,1},{1,2},{2,3},{3,4},{4,5},{5,6},{6,7},{7,8},{8,9},{9,10},{10,1... | collective-permute-start | bytes 786440 | tf_op jit(solution)/shard_map/ppermute | solution.py:19
  40.1 11.6 %collective-permute-start.3 = (bf16[128,1024]{1,0:T(8,128)(2,1)S(1)}, bf16[128,1024]{1,0:T(8,128)(2,1)S(1)}, u32[]{:S(2)}, u32[]{:S(2)}) collective-permute-start(bf16[128,1024]{1,0:T(8,128)(2,1)S(1)} %collective-permute-done.2), channel_id=1, source_target_pairs={{0,1},{1,2},{2,3},{3,4},{4,5},{5,6},{6,7},{7,8},{8,9},{9,10},{10,1... | collective-permute-start | bytes 786440 | tf_op jit(solution)/shard_map/ppermute | solution.py:19
  51.7 9.8 %collective-permute-start.4 = (bf16[128,1024]{1,0:T(8,128)(2,1)S(1)}, bf16[128,1024]{1,0:T(8,128)(2,1)S(1)}, u32[]{:S(2)}, u32[]{:S(2)}) collective-permute-start(bf16[128,1024]{1,0:T(8,128)(2,1)S(1)} %collective-permute-done.3), channel_id=1, source_target_pairs={{0,1},{1,2},{2,3},{3,4},{4,5},{5,6},{6,7},{7,8},{8,9},{9,10},{10,1... | collective-permute-start | bytes 786440 | tf_op jit(solution)/shard_map/ppermute | solution.py:19
  61.5 9.8 %collective-permute-start.5 = (bf16[128,1024]{1,0:T(8,128)(2,1)S(1)}, bf16[128,1024]{1,0:T(8,128)(2,1)S(1)}, u32[]{:S(2)}, u32[]{:S(2)}) collective-permute-start(bf16[128,1024]{1,0:T(8,128)(2,1)S(1)} %collective-permute-done.4), channel_id=1, source_target_pairs={{0,1},{1,2},{2,3},{3,4},{4,5},{5,6},{6,7},{7,8},{8,9},{9,10},{10,1... | collective-permute-start | bytes 786440 | tf_op jit(solution)/shard_map/ppermute | solution.py:19
  71.3 15.5 %collective-permute-start.6 = (bf16[128,1024]{1,0:T(8,128)(2,1)S(1)}, bf16[128,1024]{1,0:T(8,128)(2,1)S(1)}, u32[]{:S(2)}, u32[]{:S(2)}) collective-permute-start(bf16[128,1024]{1,0:T(8,128)(2,1)S(1)} %collective-permute-done.5), channel_id=1, source_target_pairs={{0,1},{1,2},{2,3},{3,4},{4,5},{5,6},{6,7},{7,8},{8,9},{9,10},{10,1... | collective-permute-start | bytes 786440 | tf_op jit(solution)/shard_map/ppermute | solution.py:19
  86.9 15.5 %collective-permute-start.7 = (bf16[128,1024]{1,0:T(8,128)(2,1)S(1)}, bf16[128,1024]{1,0:T(8,128)(2,1)S(1)}, u32[]{:S(2)}, u32[]{:S(2)}) collective-permute-start(bf16[128,1024]{1,0:T(8,128)(2,1)S(1)} %collective-permute-done.6), channel_id=1, source_target_pairs={{0,1},{1,2},{2,3},{3,4},{4,5},{5,6},{6,7},{7,8},{8,9},{9,10},{10,1... | collective-permute-start | bytes 786440 | tf_op jit(solution)/shard_map/ppermute | solution.py:19
  88.8 13.8 %copy-start = (bf16[1,128,1024]{2,1,0:T(8,128)(2,1)S(1)}, bf16[1,128,1024]{2,1,0:T(8,128)(2,1)}, u32[]{:S(2)}) copy-start(bf16[1,128,1024]{2,1,0:T(8,128)(2,1)} %param.10) | copy-start | bytes 786436
  102.6 1.2 copy-start.5
  131.6 2.5 %copy-start.6 = (f32[1024]{0:T(1024)S(1)}, f32[1024]{0:T(1024)}, u32[]{:S(2)}) copy-start(f32[1024]{0:T(1024)} %param.15) | copy-start | bytes 12292
  133.9 3.3 %copy-start.1 = (bf16[128,1024]{1,0:T(8,128)(2,1)}, bf16[128,1024]{1,0:T(8,128)(2,1)S(1)}, u32[]{:S(2)}) copy-start(bf16[128,1024]{1,0:T(8,128)(2,1)S(1)} %get-tuple-element.27) | copy-start | bytes 786436
  134.1 11.0 %copy-start.2 = (f32[9,1024]{1,0:T(8,128)S(1)}, f32[9,1024]{1,0:T(8,128)}, u32[]{:S(2)}) copy-start(f32[9,1024]{1,0:T(8,128)} %param.17) | copy-start | bytes 110596
  134.1 11.0 %copy-start.7 = (s32[8]{0:T(128)S(1)}, s32[8]{0:T(128)}, u32[]{:S(2)}) copy-start(s32[8]{0:T(128)} %param.11) | copy-start | bytes 100
  137.2 58.5 %copy-start.3 = (f32[1024]{0:T(1024)S(1)}, f32[1024]{0:T(1024)}, u32[]{:S(2)}) copy-start(f32[1024]{0:T(1024)} %param.19) | copy-start | bytes 12292
  137.2 58.5 %copy-start.4 = (f32[1024]{0:T(1024)S(1)}, f32[1024]{0:T(1024)}, u32[]{:S(2)}) copy-start(f32[1024]{0:T(1024)} %param.18) | copy-start | bytes 12292
  137.4 9.0 %collective-permute-start.8 = (bf16[4,1024]{1,0:T(4,128)(2,1)S(1)}, bf16[4,1024]{1,0:T(4,128)(2,1)S(1)}, u32[]{:S(2)}, u32[]{:S(2)}) collective-permute-start(bf16[4,1024]{1,0:T(4,128)(2,1)S(1)} %get-tuple-element.13), channel_id=1, source_target_pairs={{0,1},{1,2},{2,3},{3,4},{4,5},{5,6},{6,7},{7,8},{8,9},{9,10},{10,1... | collective-permute-start | bytes 24584 | tf_op jit(solution)/shard_map/ppermute | solution.py:29
  139.6 6.9 %collective-permute-start.9 = (bf16[4,1024]{1,0:T(4,128)(2,1)S(1)}, bf16[4,1024]{1,0:T(4,128)(2,1)S(1)}, u32[]{:S(2)}, u32[]{:S(2)}) collective-permute-start(bf16[4,1024]{1,0:T(4,128)(2,1)S(1)} %get-tuple-element.14), channel_id=1, source_target_pairs={{1,0},{2,1},{3,2},{4,3},{5,4},{6,5},{7,6},{8,7},{9,8},{10,9},{11,1... | collective-permute-start | bytes 24584 | tf_op jit(solution)/shard_map/ppermute | solution.py:31
Sparse Core Ops, SparseCore 0:
  11.9 99.2 all-gather.1

commit v9 on v7

--- a/solution.py
+++ b/solution.py
@@ -66,7 +66,7 @@
 def attend(queries, key_value, allowed):
     rows, width = queries.shape
     keys = key_value.shape[0]
-    tile = 128
+    tile = 4 * HEAD_DIM
     steps = width // tile
     return pl.pallas_call(
         attend_kernel,

time: 207 us -> 207 us (level)
  no operation moved by 1% of the time
where the time goes in v9:
time: 207 us; the launch traced here: 205 us
  waiting for transfers between devices  81 us (39%)
  blocking collectives  48.5 us (23%)
  starting transfers between devices  23 us (11%)
  matrix products  16.8 us (8%)
  between operations  15.1 us (7%)
  Pallas kernels  10.9 us (5%)
  other arithmetic  8.61 us (4%)
    ppermute x8, waiting for transfers between devices, passed_along(): lax.ppermute(value, axis, [(source, source + steps) for source in range(f...  74.4 us
    psum x4, blocking collectives, on_device(): moments = lax.psum(moments, axis)  48.5 us
    dot_general x4, matrix products, contract_with(): return jnp.dot(left, rows_piece, preferred_element_type=jnp.float32)  16.8 us
    ppermute x8, starting transfers between devices, passed_along(): lax.ppermute(value, axis, [(source, source + steps) for source in range(f...  15.3 us
    pallas_call x1, Pallas kernels, attend(): pl.pallas_call(attend_kernel, out_shape=jax.ShapeDtypeStruct((rows, width...  10.9 us
    all_gather x1, waiting for transfers between devices, on_device(): lax.all_gather(jnp.concatenate([w_qkv, w_out, w_pw1], axis=1), TM, axis=0...  6.57 us
    ppermute x1, starting transfers between devices, with_halo(): lax.ppermute(head, axis, [((i + 1) % count, i) for i in range(ends)])  5.51 us
  transfers between devices with their start and end apart: 11, of which 9 were waited for; matrix products, arithmetic and copies ran while one was open for 3% of the time, Pallas kernels for 0%

profile of v9, /device:TPU:6, one launch (start us, length us, event | category | flops | bytes accessed | tf_op | source)
XLA Modules:
  0.0 205.4 jit_solution(8187955980284245797)
XLA Ops:
  8.9 1.9 collective-permute-start
  10.8 8.1 %collective-permute-done = bf16[128,1024]{1,0:T(8,128)(2,1)S(1)} collective-permute-done((bf16[128,1024]{1,0:T(8,128)(2,1)}, bf16[128,1024]{1,0:T(8,128)(2,1)S(1)}, u32[]{:S(2)}, u32[]{:S(2)}) %collective-permute-start) | collective-permute-done | bytes 262176 | tf_op jit(solution)/shard_map/ppermute | solution.py:19
  18.9 1.9 collective-permute-start.1
  20.8 7.9 %collective-permute-done.1 = bf16[128,1024]{1,0:T(8,128)(2,1)S(1)} collective-permute-done((bf16[128,1024]{1,0:T(8,128)(2,1)S(1)}, bf16[128,1024]{1,0:T(8,128)(2,1)S(1)}, u32[]{:S(2)}, u32[]{:S(2)}) %collective-permute-start.1) | collective-permute-done | bytes 262176 | tf_op jit(solution)/shard_map/ppermute | solution.py:19
  30.6 9.5 %collective-permute-done.2 = bf16[128,1024]{1,0:T(8,128)(2,1)S(1)} collective-permute-done((bf16[128,1024]{1,0:T(8,128)(2,1)S(1)}, bf16[128,1024]{1,0:T(8,128)(2,1)S(1)}, u32[]{:S(2)}, u32[]{:S(2)}) %collective-permute-start.2) | collective-permute-done | bytes 262176 | tf_op jit(solution)/shard_map/ppermute | solution.py:19
  40.1 1.9 collective-permute-start.3
  42.0 9.7 %collective-permute-done.3 = bf16[128,1024]{1,0:T(8,128)(2,1)S(1)} collective-permute-done((bf16[128,1024]{1,0:T(8,128)(2,1)S(1)}, bf16[128,1024]{1,0:T(8,128)(2,1)S(1)}, u32[]{:S(2)}, u32[]{:S(2)}) %collective-permute-start.3) | collective-permute-done | bytes 262176 | tf_op jit(solution)/shard_map/ppermute | solution.py:19
  53.6 7.9 %collective-permute-done.4 = bf16[128,1024]{1,0:T(8,128)(2,1)S(1)} collective-permute-done((bf16[128,1024]{1,0:T(8,128)(2,1)S(1)}, bf16[128,1024]{1,0:T(8,128)(2,1)S(1)}, u32[]{:S(2)}, u32[]{:S(2)}) %collective-permute-start.4) | collective-permute-done | bytes 262176 | tf_op jit(solution)/shard_map/ppermute | solution.py:19
  61.5 1.9 collective-permute-start.5
  63.5 7.8 %collective-permute-done.5 = bf16[128,1024]{1,0:T(8,128)(2,1)S(1)} collective-permute-done((bf16[128,1024]{1,0:T(8,128)(2,1)S(1)}, bf16[128,1024]{1,0:T(8,128)(2,1)S(1)}, u32[]{:S(2)}, u32[]{:S(2)}) %collective-permute-start.5) | collective-permute-done | bytes 262176 | tf_op jit(solution)/shard_map/ppermute | solution.py:19
  75.2 11.7 %collective-permute-done.6 = bf16[128,1024]{1,0:T(8,128)(2,1)S(1)} collective-permute-done((bf16[128,1024]{1,0:T(8,128)(2,1)S(1)}, bf16[128,1024]{1,0:T(8,128)(2,1)S(1)}, u32[]{:S(2)}, u32[]{:S(2)}) %collective-permute-start.6) | collective-permute-done | bytes 262176 | tf_op jit(solution)/shard_map/ppermute | solution.py:19
  90.5 11.9 %collective-permute-done.7 = bf16[128,1024]{1,0:T(8,128)(2,1)S(1)} collective-permute-done((bf16[128,1024]{1,0:T(8,128)(2,1)S(1)}, bf16[128,1024]{1,0:T(8,128)(2,1)S(1)}, u32[]{:S(2)}, u32[]{:S(2)}) %collective-permute-start.7) | collective-permute-done | bytes 262176 | tf_op jit(solution)/shard_map/ppermute | solution.py:19
  104.6 6.6 %all-gather.2.cloned.1.call-done = bf16[1024,6144]{1,0:T(8,128)(2,1)} async-done(((bf16[16,6144]{1,0:T(8,128)(2,1)}), bf16[1024,6144]{1,0:T(8,128)(2,1)}) %all-gather.2.cloned.1.call-update) | async-done | bytes 12582928 | tf_op jit(solution)/shard_map/all_gather | solution.py:102
  111.2 8.8 %convolution_convert_fusion.k_ref.v_ref = bf16[1152,2048]{1,0:T(8,128)(2,1)} fusion(bf16[1152,1024]{1,0:T(8,128)(2,1)S(1)} %fusion.4, bf16[1024,6144]{1,0:T(8,128)(2,1)} %all-gather.2.cloned.1.call-done), kind=kOutput, calls=%fused_computation | convolution fusion | flops 4834197504 | bytes 11272192 | tf_op jit(solution)/shard_map/dot_general | solution.py:45
  120.0 2.7 %fusion.21.q_ref = bf16[128,1024]{1,0:T(8,128)(2,1)} fusion(bf16[1024,6144]{1,0:T(8,128)(2,1)} %all-gather.2.cloned.1.call-done, bf16[1152,1024]{1,0:T(8,128)(2,1)S(1)} %fusion.4), kind=kOutput, calls=%fused_computation.18 | convolution fusion | flops 268566528 | bytes 2621440 | tf_op jit(solution)/shard_map/dot_general | solution.py:45
  122.7 10.9 %shard_map.113 = bf16[128,1024]{1,0:T(8,128)(2,1)} custom-call(bf16[128,1024]{1,0:T(8,128)(2,1)} %fusion.21.q_ref, bf16[1152,2048]{1,0:T(8,128)(2,1)} %convolution_convert_fusion.k_ref.v_ref, bf16[1152,2048]{1,0:T(8,128)(2,1)} %convolution_convert_fusion.k_ref.v_ref, f32[128,1152]{1,0:T(8,128)} %and_convert_fusion.m_ref), custom_call_target="tpu_custom_call" | custom-call | flops 2415919104 | bytes 5832704 | tf_op jit(solution)/shard_map/pallas_call | solution.py:71
  133.6 2.2 %convert_reduce_fusion.1 = (f32[128]{0:T(128)S(1)}, bf16[128,1024]{1,0:T(8,128)(2,1)S(1)}) fusion(bf16[128,1024]{1,0:T(8,128)(2,1)} %shard_map.113, bf16[1024,6144]{1,0:T(8,128)(2,1)} %all-gather.2.cloned.1.call-done, bf16[1,128,1024]{2,1,0:T(8,128)(2,1)S(1)} %copy-done, pred[128]{0:T(512)(128)(4,1)S(1)} %broadcast_compare_fusion), kind=kOutput, calls=%fused_computation.22 | convolution fusion | flops 269221760 | bytes 2884224 | tf_op jit(solution)/shard_map/dot_general | solution.py:45
  136.1 3.0 %fusion.5 = f32[128,2048]{1,0:T(8,128)S(1)} fusion(bf16[1024,6144]{1,0:T(8,128)(2,1)} %all-gather.2.cloned.1.call-done, bf16[128,1024]{1,0:T(8,128)(2,1)S(1)} %get-tuple-element.27, f32[1024]{0:T(1024)S(1)} %copy-done.6, f32[128]{0:T(128)S(1)} %add_rsqrt_fusion.2, f32[128]{0:T(128)S(1)} %broadcast_multiply_fusion.1), kind=kOutput, calls=%fused_computation.8 | convolution fusion | flops 537526272 | bytes 5510144 | tf_op jit(solution)/shard_map/dot_general | solution.py:45
  139.4 2.2 %collective-permute-start.8 = (bf16[4,1024]{1,0:T(4,128)(2,1)S(1)}, bf16[4,1024]{1,0:T(4,128)(2,1)S(1)}, u32[]{:S(2)}, u32[]{:S(2)}) collective-permute-start(bf16[4,1024]{1,0:T(4,128)(2,1)S(1)} %get-tuple-element.13), channel_id=1, source_target_pairs={{0,1},{1,2},{2,3},{3,4},{4,5},{5,6},{6,7},{7,8},{8,9},{9,10},{10,1... | collective-permute-start | bytes 24584 | tf_op jit(solution)/shard_map/ppermute | solution.py:29
  141.6 5.5 %collective-permute-start.9 = (bf16[4,1024]{1,0:T(4,128)(2,1)S(1)}, bf16[4,1024]{1,0:T(4,128)(2,1)S(1)}, u32[]{:S(2)}, u32[]{:S(2)}) collective-permute-start(bf16[4,1024]{1,0:T(4,128)(2,1)S(1)} %get-tuple-element.14), channel_id=1, source_target_pairs={{1,0},{2,1},{3,2},{4,3},{5,4},{6,5},{7,6},{8,7},{9,8},{10,9},{11,1... | collective-permute-start | bytes 24584 | tf_op jit(solution)/shard_map/ppermute | solution.py:31
  149.1 2.5 %all-reduce.3 = (f32[1024]{0:T(1024)S(1)}, f32[1024]{0:T(1024)S(1)}) all-reduce(f32[1024]{0:T(1024)S(1)} %get-tuple-element.3, f32[1024]{0:T(1024)S(1)} %get-tuple-element.2), channel_id=1, replica_groups=mesh['call'=8,'x'=4,'y'=8,'core'=2] {'core'}, use_global_device_ids=true, to_apply=%region_11.12 | all-reduce | flops 2048 | bytes 16384 | tf_op jit(solution)/shard_map/psum | solution.py:141
  151.6 15.7 %all-reduce = (f32[1024]{0:T(1024)S(1)}, f32[1024]{0:T(1024)S(1)}) all-reduce(f32[1024]{0:T(1024)S(1)} %get-tuple-element.10, f32[1024]{0:T(1024)S(1)} %get-tuple-element.11), channel_id=1, replica_groups=mesh['call'=8,'x'=4,'y'=8,'core'=2] {'y'}, use_global_device_ids=true, to_apply=%region_12.13 | all-reduce | flops 2048 | bytes 16384 | tf_op jit(solution)/shard_map/psum | solution.py:141
  167.3 11.1 %all-reduce.2 = (f32[1024]{0:T(1024)S(1)}, f32[1024]{0:T(1024)S(1)}) all-reduce(f32[1024]{0:T(1024)S(1)} %get-tuple-element.4, f32[1024]{0:T(1024)S(1)} %get-tuple-element.5), channel_id=1, replica_groups=mesh['call'=8,'x'=4,'y'=8,'core'=2] {'x'}, use_global_device_ids=true, to_apply=%region_13.14 | all-reduce | flops 2048 | bytes 16384 | tf_op jit(solution)/shard_map/psum | solution.py:141
  178.4 19.2 %all-reduce.1 = (f32[1024]{0:T(1024)S(1)}, f32[1024]{0:T(1024)S(1)}) all-reduce(f32[1024]{0:T(1024)S(1)} %get-tuple-element.8, f32[1024]{0:T(1024)S(1)} %get-tuple-element.9), channel_id=1, replica_groups=mesh['call'=8,'x'=4,'y'=8,'core'=2] {'call'}, use_global_device_ids=true, to_apply=%region_14.15 | all-reduce | flops 2048 | bytes 16384 | tf_op jit(solution)/shard_map/psum | solution.py:141
  (56 shorter events, 17.8 us)
Async XLA Ops:
  7.2 104.0 %all-gather.2.cloned.1.call-start = ((), (), s32[]{:S(2)}) async-start(), calls=%async_computation | async-start | bytes 12779520 | tf_op jit(solution)/shard_map/all_gather | solution.py:102
  8.9 10.0 %collective-permute-start = (bf16[128,1024]{1,0:T(8,128)(2,1)}, bf16[128,1024]{1,0:T(8,128)(2,1)S(1)}, u32[]{:S(2)}, u32[]{:S(2)}) collective-permute-start(bf16[128,1024]{1,0:T(8,128)(2,1)} %bitcast.18), channel_id=1, source_target_pairs={{0,1},{1,2},{2,3},{3,4},{4,5},{5,6},{6,7},{7,8},{8,9},{9,10},{10,1... | collective-permute-start | bytes 786440 | tf_op jit(solution)/shard_map/ppermute | solution.py:19
  18.9 9.8 %collective-permute-start.1 = (bf16[128,1024]{1,0:T(8,128)(2,1)S(1)}, bf16[128,1024]{1,0:T(8,128)(2,1)S(1)}, u32[]{:S(2)}, u32[]{:S(2)}) collective-permute-start(bf16[128,1024]{1,0:T(8,128)(2,1)S(1)} %collective-permute-done), channel_id=1, source_target_pairs={{0,1},{1,2},{2,3},{3,4},{4,5},{5,6},{6,7},{7,8},{8,9},{9,10},{10,1... | collective-permute-start | bytes 786440 | tf_op jit(solution)/shard_map/ppermute | solution.py:19
  28.7 11.4 %collective-permute-start.2 = (bf16[128,1024]{1,0:T(8,128)(2,1)S(1)}, bf16[128,1024]{1,0:T(8,128)(2,1)S(1)}, u32[]{:S(2)}, u32[]{:S(2)}) collective-permute-start(bf16[128,1024]{1,0:T(8,128)(2,1)S(1)} %collective-permute-done.1), channel_id=1, source_target_pairs={{0,1},{1,2},{2,3},{3,4},{4,5},{5,6},{6,7},{7,8},{8,9},{9,10},{10,1... | collective-permute-start | bytes 786440 | tf_op jit(solution)/shard_map/ppermute | solution.py:19
  40.1 11.6 %collective-permute-start.3 = (bf16[128,1024]{1,0:T(8,128)(2,1)S(1)}, bf16[128,1024]{1,0:T(8,128)(2,1)S(1)}, u32[]{:S(2)}, u32[]{:S(2)}) collective-permute-start(bf16[128,1024]{1,0:T(8,128)(2,1)S(1)} %collective-permute-done.2), channel_id=1, source_target_pairs={{0,1},{1,2},{2,3},{3,4},{4,5},{5,6},{6,7},{7,8},{8,9},{9,10},{10,1... | collective-permute-start | bytes 786440 | tf_op jit(solution)/shard_map/ppermute | solution.py:19
  51.7 9.8 %collective-permute-start.4 = (bf16[128,1024]{1,0:T(8,128)(2,1)S(1)}, bf16[128,1024]{1,0:T(8,128)(2,1)S(1)}, u32[]{:S(2)}, u32[]{:S(2)}) collective-permute-start(bf16[128,1024]{1,0:T(8,128)(2,1)S(1)} %collective-permute-done.3), channel_id=1, source_target_pairs={{0,1},{1,2},{2,3},{3,4},{4,5},{5,6},{6,7},{7,8},{8,9},{9,10},{10,1... | collective-permute-start | bytes 786440 | tf_op jit(solution)/shard_map/ppermute | solution.py:19
  61.5 9.8 %collective-permute-start.5 = (bf16[128,1024]{1,0:T(8,128)(2,1)S(1)}, bf16[128,1024]{1,0:T(8,128)(2,1)S(1)}, u32[]{:S(2)}, u32[]{:S(2)}) collective-permute-start(bf16[128,1024]{1,0:T(8,128)(2,1)S(1)} %collective-permute-done.4), channel_id=1, source_target_pairs={{0,1},{1,2},{2,3},{3,4},{4,5},{5,6},{6,7},{7,8},{8,9},{9,10},{10,1... | collective-permute-start | bytes 786440 | tf_op jit(solution)/shard_map/ppermute | solution.py:19
  71.3 15.5 %collective-permute-start.6 = (bf16[128,1024]{1,0:T(8,128)(2,1)S(1)}, bf16[128,1024]{1,0:T(8,128)(2,1)S(1)}, u32[]{:S(2)}, u32[]{:S(2)}) collective-permute-start(bf16[128,1024]{1,0:T(8,128)(2,1)S(1)} %collective-permute-done.5), channel_id=1, source_target_pairs={{0,1},{1,2},{2,3},{3,4},{4,5},{5,6},{6,7},{7,8},{8,9},{9,10},{10,1... | collective-permute-start | bytes 786440 | tf_op jit(solution)/shard_map/ppermute | solution.py:19
  86.9 15.5 %collective-permute-start.7 = (bf16[128,1024]{1,0:T(8,128)(2,1)S(1)}, bf16[128,1024]{1,0:T(8,128)(2,1)S(1)}, u32[]{:S(2)}, u32[]{:S(2)}) collective-permute-start(bf16[128,1024]{1,0:T(8,128)(2,1)S(1)} %collective-permute-done.6), channel_id=1, source_target_pairs={{0,1},{1,2},{2,3},{3,4},{4,5},{5,6},{6,7},{7,8},{8,9},{9,10},{10,1... | collective-permute-start | bytes 786440 | tf_op jit(solution)/shard_map/ppermute | solution.py:19
  88.8 13.8 %copy-start = (bf16[1,128,1024]{2,1,0:T(8,128)(2,1)S(1)}, bf16[1,128,1024]{2,1,0:T(8,128)(2,1)}, u32[]{:S(2)}) copy-start(bf16[1,128,1024]{2,1,0:T(8,128)(2,1)} %param.10) | copy-start | bytes 786436
  102.6 1.2 copy-start.5
  133.6 2.5 %copy-start.6 = (f32[1024]{0:T(1024)S(1)}, f32[1024]{0:T(1024)}, u32[]{:S(2)}) copy-start(f32[1024]{0:T(1024)} %param.15) | copy-start | bytes 12292
  135.9 3.3 %copy-start.1 = (bf16[128,1024]{1,0:T(8,128)(2,1)}, bf16[128,1024]{1,0:T(8,128)(2,1)S(1)}, u32[]{:S(2)}) copy-start(bf16[128,1024]{1,0:T(8,128)(2,1)S(1)} %get-tuple-element.27) | copy-start | bytes 786436
  136.1 11.0 %copy-start.2 = (f32[9,1024]{1,0:T(8,128)S(1)}, f32[9,1024]{1,0:T(8,128)}, u32[]{:S(2)}) copy-start(f32[9,1024]{1,0:T(8,128)} %param.17) | copy-start | bytes 110596
  136.1 11.0 %copy-start.7 = (s32[8]{0:T(128)S(1)}, s32[8]{0:T(128)}, u32[]{:S(2)}) copy-start(s32[8]{0:T(128)} %param.11) | copy-start | bytes 100
  139.2 58.5 %copy-start.3 = (f32[1024]{0:T(1024)S(1)}, f32[1024]{0:T(1024)}, u32[]{:S(2)}) copy-start(f32[1024]{0:T(1024)} %param.19) | copy-start | bytes 12292
  139.2 58.5 %copy-start.4 = (f32[1024]{0:T(1024)S(1)}, f32[1024]{0:T(1024)}, u32[]{:S(2)}) copy-start(f32[1024]{0:T(1024)} %param.18) | copy-start | bytes 12292
  139.4 9.0 %collective-permute-start.8 = (bf16[4,1024]{1,0:T(4,128)(2,1)S(1)}, bf16[4,1024]{1,0:T(4,128)(2,1)S(1)}, u32[]{:S(2)}, u32[]{:S(2)}) collective-permute-start(bf16[4,1024]{1,0:T(4,128)(2,1)S(1)} %get-tuple-element.13), channel_id=1, source_target_pairs={{0,1},{1,2},{2,3},{3,4},{4,5},{5,6},{6,7},{7,8},{8,9},{9,10},{10,1... | collective-permute-start | bytes 24584 | tf_op jit(solution)/shard_map/ppermute | solution.py:29
  141.6 6.9 %collective-permute-start.9 = (bf16[4,1024]{1,0:T(4,128)(2,1)S(1)}, bf16[4,1024]{1,0:T(4,128)(2,1)S(1)}, u32[]{:S(2)}, u32[]{:S(2)}) collective-permute-start(bf16[4,1024]{1,0:T(4,128)(2,1)S(1)} %get-tuple-element.14), channel_id=1, source_target_pairs={{1,0},{2,1},{3,2},{4,3},{5,4},{6,5},{7,6},{8,7},{9,8},{10,9},{11,1... | collective-permute-start | bytes 24584 | tf_op jit(solution)/shard_map/ppermute | solution.py:31
Sparse Core Ops, SparseCore 0:
  11.9 99.2 all-gather.1

commit v10 on v7

--- a/solution.py
+++ b/solution.py
@@ -45,12 +45,13 @@
     return jnp.dot(left, rows_piece, preferred_element_type=jnp.float32)
 
 
-def attend_kernel(q_ref, k_ref, v_ref, m_ref, o_ref):
+def attend_kernel(q_ref, k_ref, v_ref, m_ref, w_ref, o_ref):
+    step = pl.program_id(0)
     width = q_ref.shape[1]
     heads = width // HEAD_DIM
     allowed = m_ref[...] > 0.5
     lane = lax.broadcasted_iota(jnp.int32, (1, width), 1)
-    result = jnp.zeros(o_ref.shape, jnp.float32)
+    result = jnp.zeros(q_ref.shape, jnp.float32)
     for head in range(heads):
         inside = (lane >= head * HEAD_DIM) & (lane < (head + 1) * HEAD_DIM)
         query = jnp.where(inside, q_ref[...], jnp.zeros_like(q_ref[...]))
@@ -61,30 +62,42 @@
         probs = (raised / jnp.sum(raised, axis=-1, keepdims=True)).astype(jnp.bfloat16)
         mixed = jnp.dot(probs, v_ref[...], preferred_element_type=jnp.float32)
         result = jnp.where(inside, mixed, result)
-    o_ref[...] = result.astype(o_ref.dtype)
+    part = jnp.dot(result.astype(jnp.bfloat16), w_ref[...], preferred_element_type=jnp.float32)
 
-def attend(queries, key_value, allowed):
+    @pl.when(step == 0)
+    def _():
+        o_ref[...] = part
+
+    @pl.when(step > 0)
+    def _():
+        o_ref[...] += part
+
+
+def attend(queries, key_value, allowed, weights, out_first):
     rows, width = queries.shape
     keys = key_value.shape[0]
     tile = 128
     steps = width // tile
+    out_block = out_first // width
     return pl.pallas_call(
         attend_kernel,
-        out_shape=jax.ShapeDtypeStruct((rows, width), jnp.bfloat16),
+        out_shape=jax.ShapeDtypeStruct((rows, width), jnp.float32),
         grid=(steps,),
         in_specs=[
             pl.BlockSpec((rows, tile), lambda i: (0, i)),
             pl.BlockSpec((keys, tile), lambda i: (0, i)),
             pl.BlockSpec((keys, tile), lambda i: (0, i + steps)),
             pl.BlockSpec((rows, keys), lambda i: (0, 0)),
+            pl.BlockSpec((tile, width), lambda i: (i, out_block)),
         ],
-        out_specs=pl.BlockSpec((rows, tile), lambda i: (0, i)),
+        out_specs=pl.BlockSpec((rows, width), lambda i: (0, 0)),
         cost_estimate=pl.CostEstimate(
-            flops=4 * rows * keys * width * tile // HEAD_DIM,
+            flops=4 * rows * keys * width * tile // HEAD_DIM + 2 * rows * width * width,
             transcendentals=rows * keys * width // HEAD_DIM,
-            bytes_accessed=2 * (2 * rows * width + 2 * keys * width) + 4 * rows * keys,
+            bytes_accessed=2 * (2 * rows * width + 2 * keys * width + width * width)
+            + 4 * rows * keys,
         ),
-    )(queries, key_value, key_value, allowed.astype(jnp.float32))
+    )(queries, key_value, key_value, allowed.astype(jnp.float32), weights)
 
 
 def on_device(
@@ -119,8 +132,7 @@
     allowed = (key_pos[None, :] >= 0) & (key_pos[None, :] >= span_first[:, None] - LEFT)
     allowed = allowed & (key_pos[None, :] < span_first[:, None] + SPAN)
     allowed = allowed & ((key_pos[None, :] < length) | (key_pos[None, :] == query_pos[:, None]))
-    context = attend(queries, key_value, allowed)
-    projected = contract_with(context, weights[:, qkv_cols : qkv_cols + out_cols])
+    projected = attend(queries, key_value, allowed, weights, qkv_cols)
     attended = jnp.where(frame_valid[:, None], stream.astype(jnp.float32) + projected, 0.0).astype(
         jnp.bfloat16
     )

time: 207 us -> 208 us (level)
  matrix products: 16.8 us -> 14.6 us
    dot_general x4 -> x3, matrix products: 16.8 us -> 14.6 us  [contract_with(): return jnp.dot(left, rows_piece, preferred_element_type=jnp.float32)]
where the time goes in v10:
time: 208 us; the launch traced here: 206 us
  waiting for transfers between devices  81 us (39%)
  blocking collectives  48.5 us (23%)
  starting transfers between devices  23 us (11%)
  between operations  15.1 us (7%)
  matrix products  14.6 us (7%)
  Pallas kernels  12.1 us (6%)
  other arithmetic  9.84 us (5%)
    ppermute x8, waiting for transfers between devices, passed_along(): lax.ppermute(value, axis, [(source, source + steps) for source in range(f...  74.4 us
    psum x4, blocking collectives, on_device(): moments = lax.psum(moments, axis)  48.5 us
    ppermute x8, starting transfers between devices, passed_along(): lax.ppermute(value, axis, [(source, source + steps) for source in range(f...  15.3 us
    dot_general x3, matrix products, contract_with(): return jnp.dot(left, rows_piece, preferred_element_type=jnp.float32)  14.6 us
    pallas_call x1, Pallas kernels, attend(): pl.pallas_call(attend_kernel, out_shape=jax.ShapeDtypeStruct((rows, width...  12.1 us
    all_gather x1, waiting for transfers between devices, on_device(): lax.all_gather(jnp.concatenate([w_qkv, w_out, w_pw1], axis=1), TM, axis=0...  6.57 us
    ppermute x1, starting transfers between devices, with_halo(): lax.ppermute(head, axis, [((i + 1) % count, i) for i in range(ends)])  5.51 us
  transfers between devices with their start and end apart: 11, of which 9 were waited for; matrix products, arithmetic and copies ran while one was open for 3% of the time, Pallas kernels for 0%

profile of v10, /device:TPU:6, one launch (start us, length us, event | category | flops | bytes accessed | tf_op | source)
XLA Modules:
  0.0 205.7 jit_solution(12568581231514438118)
XLA Ops:
  8.9 1.9 collective-permute-start
  10.8 8.1 %collective-permute-done = bf16[128,1024]{1,0:T(8,128)(2,1)S(1)} collective-permute-done((bf16[128,1024]{1,0:T(8,128)(2,1)}, bf16[128,1024]{1,0:T(8,128)(2,1)S(1)}, u32[]{:S(2)}, u32[]{:S(2)}) %collective-permute-start) | collective-permute-done | bytes 262176 | tf_op jit(solution)/shard_map/ppermute | solution.py:19
  18.9 1.9 collective-permute-start.1
  20.8 7.9 %collective-permute-done.1 = bf16[128,1024]{1,0:T(8,128)(2,1)S(1)} collective-permute-done((bf16[128,1024]{1,0:T(8,128)(2,1)S(1)}, bf16[128,1024]{1,0:T(8,128)(2,1)S(1)}, u32[]{:S(2)}, u32[]{:S(2)}) %collective-permute-start.1) | collective-permute-done | bytes 262176 | tf_op jit(solution)/shard_map/ppermute | solution.py:19
  28.7 1.9 collective-permute-start.2
  30.6 9.5 %collective-permute-done.2 = bf16[128,1024]{1,0:T(8,128)(2,1)S(1)} collective-permute-done((bf16[128,1024]{1,0:T(8,128)(2,1)S(1)}, bf16[128,1024]{1,0:T(8,128)(2,1)S(1)}, u32[]{:S(2)}, u32[]{:S(2)}) %collective-permute-start.2) | collective-permute-done | bytes 262176 | tf_op jit(solution)/shard_map/ppermute | solution.py:19
  40.1 1.9 collective-permute-start.3
  42.0 9.7 %collective-permute-done.3 = bf16[128,1024]{1,0:T(8,128)(2,1)S(1)} collective-permute-done((bf16[128,1024]{1,0:T(8,128)(2,1)S(1)}, bf16[128,1024]{1,0:T(8,128)(2,1)S(1)}, u32[]{:S(2)}, u32[]{:S(2)}) %collective-permute-start.3) | collective-permute-done | bytes 262176 | tf_op jit(solution)/shard_map/ppermute | solution.py:19
  53.6 7.9 %collective-permute-done.4 = bf16[128,1024]{1,0:T(8,128)(2,1)S(1)} collective-permute-done((bf16[128,1024]{1,0:T(8,128)(2,1)S(1)}, bf16[128,1024]{1,0:T(8,128)(2,1)S(1)}, u32[]{:S(2)}, u32[]{:S(2)}) %collective-permute-start.4) | collective-permute-done | bytes 262176 | tf_op jit(solution)/shard_map/ppermute | solution.py:19
  61.5 1.9 collective-permute-start.5
  63.5 7.8 %collective-permute-done.5 = bf16[128,1024]{1,0:T(8,128)(2,1)S(1)} collective-permute-done((bf16[128,1024]{1,0:T(8,128)(2,1)S(1)}, bf16[128,1024]{1,0:T(8,128)(2,1)S(1)}, u32[]{:S(2)}, u32[]{:S(2)}) %collective-permute-start.5) | collective-permute-done | bytes 262176 | tf_op jit(solution)/shard_map/ppermute | solution.py:19
  75.2 11.7 %collective-permute-done.6 = bf16[128,1024]{1,0:T(8,128)(2,1)S(1)} collective-permute-done((bf16[128,1024]{1,0:T(8,128)(2,1)S(1)}, bf16[128,1024]{1,0:T(8,128)(2,1)S(1)}, u32[]{:S(2)}, u32[]{:S(2)}) %collective-permute-start.6) | collective-permute-done | bytes 262176 | tf_op jit(solution)/shard_map/ppermute | solution.py:19
  90.5 11.9 %collective-permute-done.7 = bf16[128,1024]{1,0:T(8,128)(2,1)S(1)} collective-permute-done((bf16[128,1024]{1,0:T(8,128)(2,1)S(1)}, bf16[128,1024]{1,0:T(8,128)(2,1)S(1)}, u32[]{:S(2)}, u32[]{:S(2)}) %collective-permute-start.7) | collective-permute-done | bytes 262176 | tf_op jit(solution)/shard_map/ppermute | solution.py:19
  104.6 6.6 %all-gather.2.cloned.1.call-done.w_ref = bf16[1024,6144]{1,0:T(8,128)(2,1)} async-done(((bf16[16,6144]{1,0:T(8,128)(2,1)}), bf16[1024,6144]{1,0:T(8,128)(2,1)}) %all-gather.2.cloned.1.call-update) | async-done | bytes 12582928 | tf_op jit(solution)/shard_map/all_gather | solution.py:115
  111.2 8.8 %convolution_convert_fusion.k_ref.v_ref = bf16[1152,2048]{1,0:T(8,128)(2,1)} fusion(bf16[1152,1024]{1,0:T(8,128)(2,1)S(1)} %fusion.4, bf16[1024,6144]{1,0:T(8,128)(2,1)} %all-gather.2.cloned.1.call-done.w_ref), kind=kOutput, calls=%fused_computation | convolution fusion | flops 4834197504 | bytes 11272192 | tf_op jit(solution)/shard_map/dot_general | solution.py:45
  120.0 2.7 %fusion.10.q_ref = bf16[128,1024]{1,0:T(8,128)(2,1)} fusion(bf16[1024,6144]{1,0:T(8,128)(2,1)} %all-gather.2.cloned.1.call-done.w_ref, bf16[1152,1024]{1,0:T(8,128)(2,1)S(1)} %fusion.4), kind=kOutput, calls=%fused_computation.13 | convolution fusion | flops 268566528 | bytes 2621440 | tf_op jit(solution)/shard_map/dot_general | solution.py:45
  122.7 12.1 %shard_map.113 = f32[128,1024]{1,0:T(8,128)} custom-call(bf16[128,1024]{1,0:T(8,128)(2,1)} %fusion.10.q_ref, bf16[1152,2048]{1,0:T(8,128)(2,1)} %convolution_convert_fusion.k_ref.v_ref, bf16[1152,2048]{1,0:T(8,128)(2,1)} %convolution_convert_fusion.k_ref.v_ref, f32[128,1152]{1,0:T(8,128)} %and_convert_fusion.m_ref, ...), custom_call_target="tpu_custom_call" | custom-call | flops 1476395008 | bytes 7929856 | tf_op jit(solution)/shard_map/pallas_call | solution.py:82
  136.4 3.0 %fusion.5 = f32[128,2048]{1,0:T(8,128)S(1)} fusion(bf16[1024,6144]{1,0:T(8,128)(2,1)} %all-gather.2.cloned.1.call-done.w_ref, bf16[128,1024]{1,0:T(8,128)(2,1)S(1)} %get-tuple-element.14, f32[1024]{0:T(1024)S(1)} %copy-done.6, f32[128]{0:T(128)S(1)} %add_rsqrt_fusion.2, f32[128]{0:T(128)S(1)} %broadcast_multiply_fusion.1), kind=kOutput, calls=%fused_computation.8 | convolution fusion | flops 537526272 | bytes 5510144 | tf_op jit(solution)/shard_map/dot_general | solution.py:45
  139.6 2.2 %collective-permute-start.8 = (bf16[4,1024]{1,0:T(4,128)(2,1)S(1)}, bf16[4,1024]{1,0:T(4,128)(2,1)S(1)}, u32[]{:S(2)}, u32[]{:S(2)}) collective-permute-start(bf16[4,1024]{1,0:T(4,128)(2,1)S(1)} %get-tuple-element.15), channel_id=1, source_target_pairs={{0,1},{1,2},{2,3},{3,4},{4,5},{5,6},{6,7},{7,8},{8,9},{9,10},{10,1... | collective-permute-start | bytes 24584 | tf_op jit(solution)/shard_map/ppermute | solution.py:29
  141.8 5.5 %collective-permute-start.9 = (bf16[4,1024]{1,0:T(4,128)(2,1)S(1)}, bf16[4,1024]{1,0:T(4,128)(2,1)S(1)}, u32[]{:S(2)}, u32[]{:S(2)}) collective-permute-start(bf16[4,1024]{1,0:T(4,128)(2,1)S(1)} %get-tuple-element.16), channel_id=1, source_target_pairs={{1,0},{2,1},{3,2},{4,3},{5,4},{6,5},{7,6},{8,7},{9,8},{10,9},{11,1... | collective-permute-start | bytes 24584 | tf_op jit(solution)/shard_map/ppermute | solution.py:31
  149.3 2.5 %all-reduce.3 = (f32[1024]{0:T(1024)S(1)}, f32[1024]{0:T(1024)S(1)}) all-reduce(f32[1024]{0:T(1024)S(1)} %get-tuple-element.3, f32[1024]{0:T(1024)S(1)} %get-tuple-element.2), channel_id=1, replica_groups=mesh['call'=8,'x'=4,'y'=8,'core'=2] {'core'}, use_global_device_ids=true, to_apply=%region_11.12 | all-reduce | flops 2048 | bytes 16384 | tf_op jit(solution)/shard_map/psum | solution.py:153
  151.8 15.7 %all-reduce = (f32[1024]{0:T(1024)S(1)}, f32[1024]{0:T(1024)S(1)}) all-reduce(f32[1024]{0:T(1024)S(1)} %get-tuple-element.10, f32[1024]{0:T(1024)S(1)} %get-tuple-element.11), channel_id=1, replica_groups=mesh['call'=8,'x'=4,'y'=8,'core'=2] {'y'}, use_global_device_ids=true, to_apply=%region_12.13 | all-reduce | flops 2048 | bytes 16384 | tf_op jit(solution)/shard_map/psum | solution.py:153
  167.5 11.1 %all-reduce.2 = (f32[1024]{0:T(1024)S(1)}, f32[1024]{0:T(1024)S(1)}) all-reduce(f32[1024]{0:T(1024)S(1)} %get-tuple-element.4, f32[1024]{0:T(1024)S(1)} %get-tuple-element.5), channel_id=1, replica_groups=mesh['call'=8,'x'=4,'y'=8,'core'=2] {'x'}, use_global_device_ids=true, to_apply=%region_13.14 | all-reduce | flops 2048 | bytes 16384 | tf_op jit(solution)/shard_map/psum | solution.py:153
  178.6 19.2 %all-reduce.1 = (f32[1024]{0:T(1024)S(1)}, f32[1024]{0:T(1024)S(1)}) all-reduce(f32[1024]{0:T(1024)S(1)} %get-tuple-element.8, f32[1024]{0:T(1024)S(1)} %get-tuple-element.9), channel_id=1, replica_groups=mesh['call'=8,'x'=4,'y'=8,'core'=2] {'call'}, use_global_device_ids=true, to_apply=%region_14.15 | all-reduce | flops 2048 | bytes 16384 | tf_op jit(solution)/shard_map/psum | solution.py:153
  (56 shorter events, 17.1 us)
Async XLA Ops:
  7.2 104.0 %all-gather.2.cloned.1.call-start = ((), (), s32[]{:S(2)}) async-start(), calls=%async_computation | async-start | bytes 12779520 | tf_op jit(solution)/shard_map/all_gather | solution.py:115
  8.9 10.0 %collective-permute-start = (bf16[128,1024]{1,0:T(8,128)(2,1)}, bf16[128,1024]{1,0:T(8,128)(2,1)S(1)}, u32[]{:S(2)}, u32[]{:S(2)}) collective-permute-start(bf16[128,1024]{1,0:T(8,128)(2,1)} %bitcast.18), channel_id=1, source_target_pairs={{0,1},{1,2},{2,3},{3,4},{4,5},{5,6},{6,7},{7,8},{8,9},{9,10},{10,1... | collective-permute-start | bytes 786440 | tf_op jit(solution)/shard_map/ppermute | solution.py:19
  18.9 9.8 %collective-permute-start.1 = (bf16[128,1024]{1,0:T(8,128)(2,1)S(1)}, bf16[128,1024]{1,0:T(8,128)(2,1)S(1)}, u32[]{:S(2)}, u32[]{:S(2)}) collective-permute-start(bf16[128,1024]{1,0:T(8,128)(2,1)S(1)} %collective-permute-done), channel_id=1, source_target_pairs={{0,1},{1,2},{2,3},{3,4},{4,5},{5,6},{6,7},{7,8},{8,9},{9,10},{10,1... | collective-permute-start | bytes 786440 | tf_op jit(solution)/shard_map/ppermute | solution.py:19
  28.7 11.4 %collective-permute-start.2 = (bf16[128,1024]{1,0:T(8,128)(2,1)S(1)}, bf16[128,1024]{1,0:T(8,128)(2,1)S(1)}, u32[]{:S(2)}, u32[]{:S(2)}) collective-permute-start(bf16[128,1024]{1,0:T(8,128)(2,1)S(1)} %collective-permute-done.1), channel_id=1, source_target_pairs={{0,1},{1,2},{2,3},{3,4},{4,5},{5,6},{6,7},{7,8},{8,9},{9,10},{10,1... | collective-permute-start | bytes 786440 | tf_op jit(solution)/shard_map/ppermute | solution.py:19
  40.1 11.6 %collective-permute-start.3 = (bf16[128,1024]{1,0:T(8,128)(2,1)S(1)}, bf16[128,1024]{1,0:T(8,128)(2,1)S(1)}, u32[]{:S(2)}, u32[]{:S(2)}) collective-permute-start(bf16[128,1024]{1,0:T(8,128)(2,1)S(1)} %collective-permute-done.2), channel_id=1, source_target_pairs={{0,1},{1,2},{2,3},{3,4},{4,5},{5,6},{6,7},{7,8},{8,9},{9,10},{10,1... | collective-permute-start | bytes 786440 | tf_op jit(solution)/shard_map/ppermute | solution.py:19
  51.7 9.8 %collective-permute-start.4 = (bf16[128,1024]{1,0:T(8,128)(2,1)S(1)}, bf16[128,1024]{1,0:T(8,128)(2,1)S(1)}, u32[]{:S(2)}, u32[]{:S(2)}) collective-permute-start(bf16[128,1024]{1,0:T(8,128)(2,1)S(1)} %collective-permute-done.3), channel_id=1, source_target_pairs={{0,1},{1,2},{2,3},{3,4},{4,5},{5,6},{6,7},{7,8},{8,9},{9,10},{10,1... | collective-permute-start | bytes 786440 | tf_op jit(solution)/shard_map/ppermute | solution.py:19
  61.5 9.8 %collective-permute-start.5 = (bf16[128,1024]{1,0:T(8,128)(2,1)S(1)}, bf16[128,1024]{1,0:T(8,128)(2,1)S(1)}, u32[]{:S(2)}, u32[]{:S(2)}) collective-permute-start(bf16[128,1024]{1,0:T(8,128)(2,1)S(1)} %collective-permute-done.4), channel_id=1, source_target_pairs={{0,1},{1,2},{2,3},{3,4},{4,5},{5,6},{6,7},{7,8},{8,9},{9,10},{10,1... | collective-permute-start | bytes 786440 | tf_op jit(solution)/shard_map/ppermute | solution.py:19
  71.3 15.5 %collective-permute-start.6 = (bf16[128,1024]{1,0:T(8,128)(2,1)S(1)}, bf16[128,1024]{1,0:T(8,128)(2,1)S(1)}, u32[]{:S(2)}, u32[]{:S(2)}) collective-permute-start(bf16[128,1024]{1,0:T(8,128)(2,1)S(1)} %collective-permute-done.5), channel_id=1, source_target_pairs={{0,1},{1,2},{2,3},{3,4},{4,5},{5,6},{6,7},{7,8},{8,9},{9,10},{10,1... | collective-permute-start | bytes 786440 | tf_op jit(solution)/shard_map/ppermute | solution.py:19
  86.9 15.5 %collective-permute-start.7 = (bf16[128,1024]{1,0:T(8,128)(2,1)S(1)}, bf16[128,1024]{1,0:T(8,128)(2,1)S(1)}, u32[]{:S(2)}, u32[]{:S(2)}) collective-permute-start(bf16[128,1024]{1,0:T(8,128)(2,1)S(1)} %collective-permute-done.6), channel_id=1, source_target_pairs={{0,1},{1,2},{2,3},{3,4},{4,5},{5,6},{6,7},{7,8},{8,9},{9,10},{10,1... | collective-permute-start | bytes 786440 | tf_op jit(solution)/shard_map/ppermute | solution.py:19
  88.8 13.8 %copy-start = (bf16[1,128,1024]{2,1,0:T(8,128)(2,1)S(1)}, bf16[1,128,1024]{2,1,0:T(8,128)(2,1)}, u32[]{:S(2)}) copy-start(bf16[1,128,1024]{2,1,0:T(8,128)(2,1)} %param.10) | copy-start | bytes 786436
  102.6 1.2 copy-start.5
  122.7 13.6 %copy-start.6 = (f32[1024]{0:T(1024)S(1)}, f32[1024]{0:T(1024)}, u32[]{:S(2)}) copy-start(f32[1024]{0:T(1024)} %param.15) | copy-start | bytes 12292
  136.1 3.3 %copy-start.1 = (bf16[128,1024]{1,0:T(8,128)(2,1)}, bf16[128,1024]{1,0:T(8,128)(2,1)S(1)}, u32[]{:S(2)}) copy-start(bf16[128,1024]{1,0:T(8,128)(2,1)S(1)} %get-tuple-element.14) | copy-start | bytes 786436
  136.3 11.0 %copy-start.2 = (f32[9,1024]{1,0:T(8,128)S(1)}, f32[9,1024]{1,0:T(8,128)}, u32[]{:S(2)}) copy-start(f32[9,1024]{1,0:T(8,128)} %param.17) | copy-start | bytes 110596
  136.3 11.0 %copy-start.7 = (s32[8]{0:T(128)S(1)}, s32[8]{0:T(128)}, u32[]{:S(2)}) copy-start(s32[8]{0:T(128)} %param.11) | copy-start | bytes 100
  139.4 58.5 %copy-start.3 = (f32[1024]{0:T(1024)S(1)}, f32[1024]{0:T(1024)}, u32[]{:S(2)}) copy-start(f32[1024]{0:T(1024)} %param.19) | copy-start | bytes 12292
  139.4 58.5 %copy-start.4 = (f32[1024]{0:T(1024)S(1)}, f32[1024]{0:T(1024)}, u32[]{:S(2)}) copy-start(f32[1024]{0:T(1024)} %param.18) | copy-start | bytes 12292
  139.6 9.0 %collective-permute-start.8 = (bf16[4,1024]{1,0:T(4,128)(2,1)S(1)}, bf16[4,1024]{1,0:T(4,128)(2,1)S(1)}, u32[]{:S(2)}, u32[]{:S(2)}) collective-permute-start(bf16[4,1024]{1,0:T(4,128)(2,1)S(1)} %get-tuple-element.15), channel_id=1, source_target_pairs={{0,1},{1,2},{2,3},{3,4},{4,5},{5,6},{6,7},{7,8},{8,9},{9,10},{10,1... | collective-permute-start | bytes 24584 | tf_op jit(solution)/shard_map/ppermute | solution.py:29
  141.8 6.9 %collective-permute-start.9 = (bf16[4,1024]{1,0:T(4,128)(2,1)S(1)}, bf16[4,1024]{1,0:T(4,128)(2,1)S(1)}, u32[]{:S(2)}, u32[]{:S(2)}) collective-permute-start(bf16[4,1024]{1,0:T(4,128)(2,1)S(1)} %get-tuple-element.16), channel_id=1, source_target_pairs={{1,0},{2,1},{3,2},{4,3},{5,4},{6,5},{7,6},{8,7},{9,8},{10,9},{11,1... | collective-permute-start | bytes 24584 | tf_op jit(solution)/shard_map/ppermute | solution.py:31
Sparse Core Ops, SparseCore 0:
  11.9 99.2 all-gather.1

commit v11 on v7

--- a/solution.py
+++ b/solution.py
@@ -136,10 +136,10 @@
             + padded[tap_index : tap_index + frame_count].astype(jnp.float32) * dw_kernel[tap_index]
         )
     masked = jnp.where(frame_valid[:, None], depthwise, 0.0)
-    moments = (jnp.sum(masked, axis=0), jnp.sum(masked * depthwise, axis=0))
+    moments = jnp.concatenate([jnp.sum(masked, axis=0), jnp.sum(masked * depthwise, axis=0)])
     for axis in ("core", "y", "x", "call"):
         moments = lax.psum(moments, axis)
-    first_moment, second_moment = moments
+    first_moment, second_moment = moments[:model_width], moments[model_width:]
     count_all = jnp.sum(lengths).astype(jnp.float32)
     average = first_moment / count_all
     second = second_moment / count_all

time: 207 us -> 207 us (level)
  no operation moved by 1% of the time
where the time goes in v11:
time: 207 us; the launch traced here: 205 us
  waiting for transfers between devices  81 us (39%)
  blocking collectives  48.5 us (23%)
  starting transfers between devices  23 us (11%)
  matrix products  16.8 us (8%)
  between operations  15.1 us (7%)
  Pallas kernels  10.1 us (5%)
  other arithmetic  8.61 us (4%)
    ppermute x8, waiting for transfers between devices, passed_along(): lax.ppermute(value, axis, [(source, source + steps) for source in range(f...  74.4 us
    psum x4, blocking collectives, on_device(): moments = lax.psum(moments, axis)  48.5 us
    dot_general x4, matrix products, contract_with(): return jnp.dot(left, rows_piece, preferred_element_type=jnp.float32)  16.8 us
    ppermute x8, starting transfers between devices, passed_along(): lax.ppermute(value, axis, [(source, source + steps) for source in range(f...  15.3 us
    pallas_call x1, Pallas kernels, attend(): pl.pallas_call(attend_kernel, out_shape=jax.ShapeDtypeStruct((rows, width...  10.1 us
    all_gather x1, waiting for transfers between devices, on_device(): lax.all_gather(jnp.concatenate([w_qkv, w_out, w_pw1], axis=1), TM, axis=0...  6.57 us
    ppermute x1, starting transfers between devices, with_halo(): lax.ppermute(head, axis, [((i + 1) % count, i) for i in range(ends)])  5.52 us
  transfers between devices with their start and end apart: 11, of which 9 were waited for; matrix products, arithmetic and copies ran while one was open for 3% of the time, Pallas kernels for 0%

profile of v11, /device:TPU:6, one launch (start us, length us, event | category | flops | bytes accessed | tf_op | source)
XLA Modules:
  0.0 204.6 jit_solution(17073100486533598971)
XLA Ops:
  8.9 1.9 collective-permute-start
  10.8 8.1 %collective-permute-done = bf16[128,1024]{1,0:T(8,128)(2,1)S(1)} collective-permute-done((bf16[128,1024]{1,0:T(8,128)(2,1)}, bf16[128,1024]{1,0:T(8,128)(2,1)S(1)}, u32[]{:S(2)}, u32[]{:S(2)}) %collective-permute-start) | collective-permute-done | bytes 262176 | tf_op jit(solution)/shard_map/ppermute | solution.py:19
  18.9 1.9 collective-permute-start.1
  20.8 7.9 %collective-permute-done.1 = bf16[128,1024]{1,0:T(8,128)(2,1)S(1)} collective-permute-done((bf16[128,1024]{1,0:T(8,128)(2,1)S(1)}, bf16[128,1024]{1,0:T(8,128)(2,1)S(1)}, u32[]{:S(2)}, u32[]{:S(2)}) %collective-permute-start.1) | collective-permute-done | bytes 262176 | tf_op jit(solution)/shard_map/ppermute | solution.py:19
  30.6 9.5 %collective-permute-done.2 = bf16[128,1024]{1,0:T(8,128)(2,1)S(1)} collective-permute-done((bf16[128,1024]{1,0:T(8,128)(2,1)S(1)}, bf16[128,1024]{1,0:T(8,128)(2,1)S(1)}, u32[]{:S(2)}, u32[]{:S(2)}) %collective-permute-start.2) | collective-permute-done | bytes 262176 | tf_op jit(solution)/shard_map/ppermute | solution.py:19
  40.1 1.9 collective-permute-start.3
  42.0 9.7 %collective-permute-done.3 = bf16[128,1024]{1,0:T(8,128)(2,1)S(1)} collective-permute-done((bf16[128,1024]{1,0:T(8,128)(2,1)S(1)}, bf16[128,1024]{1,0:T(8,128)(2,1)S(1)}, u32[]{:S(2)}, u32[]{:S(2)}) %collective-permute-start.3) | collective-permute-done | bytes 262176 | tf_op jit(solution)/shard_map/ppermute | solution.py:19
  53.6 7.9 %collective-permute-done.4 = bf16[128,1024]{1,0:T(8,128)(2,1)S(1)} collective-permute-done((bf16[128,1024]{1,0:T(8,128)(2,1)S(1)}, bf16[128,1024]{1,0:T(8,128)(2,1)S(1)}, u32[]{:S(2)}, u32[]{:S(2)}) %collective-permute-start.4) | collective-permute-done | bytes 262176 | tf_op jit(solution)/shard_map/ppermute | solution.py:19
  61.5 1.9 collective-permute-start.5
  63.5 7.8 %collective-permute-done.5 = bf16[128,1024]{1,0:T(8,128)(2,1)S(1)} collective-permute-done((bf16[128,1024]{1,0:T(8,128)(2,1)S(1)}, bf16[128,1024]{1,0:T(8,128)(2,1)S(1)}, u32[]{:S(2)}, u32[]{:S(2)}) %collective-permute-start.5) | collective-permute-done | bytes 262176 | tf_op jit(solution)/shard_map/ppermute | solution.py:19
  75.2 11.7 %collective-permute-done.6 = bf16[128,1024]{1,0:T(8,128)(2,1)S(1)} collective-permute-done((bf16[128,1024]{1,0:T(8,128)(2,1)S(1)}, bf16[128,1024]{1,0:T(8,128)(2,1)S(1)}, u32[]{:S(2)}, u32[]{:S(2)}) %collective-permute-start.6) | collective-permute-done | bytes 262176 | tf_op jit(solution)/shard_map/ppermute | solution.py:19
  90.5 11.9 %collective-permute-done.7 = bf16[128,1024]{1,0:T(8,128)(2,1)S(1)} collective-permute-done((bf16[128,1024]{1,0:T(8,128)(2,1)S(1)}, bf16[128,1024]{1,0:T(8,128)(2,1)S(1)}, u32[]{:S(2)}, u32[]{:S(2)}) %collective-permute-start.7) | collective-permute-done | bytes 262176 | tf_op jit(solution)/shard_map/ppermute | solution.py:19
  104.6 6.6 %all-gather.2.cloned.1.call-done = bf16[1024,6144]{1,0:T(8,128)(2,1)} async-done(((bf16[16,6144]{1,0:T(8,128)(2,1)}), bf16[1024,6144]{1,0:T(8,128)(2,1)}) %all-gather.2.cloned.1.call-update) | async-done | bytes 12582928 | tf_op jit(solution)/shard_map/all_gather | solution.py:102
  111.2 8.8 %convolution_convert_fusion.k_ref.v_ref = bf16[1152,2048]{1,0:T(8,128)(2,1)} fusion(bf16[1152,1024]{1,0:T(8,128)(2,1)S(1)} %fusion.4, bf16[1024,6144]{1,0:T(8,128)(2,1)} %all-gather.2.cloned.1.call-done), kind=kOutput, calls=%fused_computation | convolution fusion | flops 4834197504 | bytes 11272192 | tf_op jit(solution)/shard_map/dot_general | solution.py:45
  120.0 2.7 %fusion.21.q_ref = bf16[128,1024]{1,0:T(8,128)(2,1)} fusion(bf16[1024,6144]{1,0:T(8,128)(2,1)} %all-gather.2.cloned.1.call-done, bf16[1152,1024]{1,0:T(8,128)(2,1)S(1)} %fusion.4), kind=kOutput, calls=%fused_computation.18 | convolution fusion | flops 268566528 | bytes 2621440 | tf_op jit(solution)/shard_map/dot_general | solution.py:45
  122.7 10.1 %shard_map.113 = bf16[128,1024]{1,0:T(8,128)(2,1)} custom-call(bf16[128,1024]{1,0:T(8,128)(2,1)} %fusion.21.q_ref, bf16[1152,2048]{1,0:T(8,128)(2,1)} %convolution_convert_fusion.k_ref.v_ref, bf16[1152,2048]{1,0:T(8,128)(2,1)} %convolution_convert_fusion.k_ref.v_ref, f32[128,1152]{1,0:T(8,128)} %and_convert_fusion.m_ref), custom_call_target="tpu_custom_call" | custom-call | flops 1207959552 | bytes 5832704 | tf_op jit(solution)/shard_map/pallas_call | solution.py:71
  132.8 2.2 %convert_reduce_fusion.1 = (f32[128]{0:T(128)S(1)}, bf16[128,1024]{1,0:T(8,128)(2,1)S(1)}) fusion(bf16[128,1024]{1,0:T(8,128)(2,1)} %shard_map.113, bf16[1024,6144]{1,0:T(8,128)(2,1)} %all-gather.2.cloned.1.call-done, bf16[1,128,1024]{2,1,0:T(8,128)(2,1)S(1)} %copy-done, pred[128]{0:T(512)(128)(4,1)S(1)} %broadcast_compare_fusion), kind=kOutput, calls=%fused_computation.22 | convolution fusion | flops 269221760 | bytes 2884224 | tf_op jit(solution)/shard_map/dot_general | solution.py:45
  135.3 3.0 %fusion.5 = f32[128,2048]{1,0:T(8,128)S(1)} fusion(bf16[1024,6144]{1,0:T(8,128)(2,1)} %all-gather.2.cloned.1.call-done, bf16[128,1024]{1,0:T(8,128)(2,1)S(1)} %get-tuple-element.19, f32[1024]{0:T(1024)S(1)} %copy-done.6, f32[128]{0:T(128)S(1)} %add_rsqrt_fusion.1, f32[128]{0:T(128)S(1)} %broadcast_multiply_fusion.1), kind=kOutput, calls=%fused_computation.8 | convolution fusion | flops 537526272 | bytes 5510144 | tf_op jit(solution)/shard_map/dot_general | solution.py:45
  138.6 2.2 %collective-permute-start.8 = (bf16[4,1024]{1,0:T(4,128)(2,1)S(1)}, bf16[4,1024]{1,0:T(4,128)(2,1)S(1)}, u32[]{:S(2)}, u32[]{:S(2)}) collective-permute-start(bf16[4,1024]{1,0:T(4,128)(2,1)S(1)} %get-tuple-element.5), channel_id=1, source_target_pairs={{0,1},{1,2},{2,3},{3,4},{4,5},{5,6},{6,7},{7,8},{8,9},{9,10},{10,1... | collective-permute-start | bytes 24584 | tf_op jit(solution)/shard_map/ppermute | solution.py:29
  140.8 5.5 %collective-permute-start.9 = (bf16[4,1024]{1,0:T(4,128)(2,1)S(1)}, bf16[4,1024]{1,0:T(4,128)(2,1)S(1)}, u32[]{:S(2)}, u32[]{:S(2)}) collective-permute-start(bf16[4,1024]{1,0:T(4,128)(2,1)S(1)} %get-tuple-element.6), channel_id=1, source_target_pairs={{1,0},{2,1},{3,2},{4,3},{5,4},{6,5},{7,6},{8,7},{9,8},{10,9},{11,1... | collective-permute-start | bytes 24584 | tf_op jit(solution)/shard_map/ppermute | solution.py:31
  148.3 2.5 %psum.28 = f32[2048]{0:T(1024)S(1)} all-reduce(f32[2048]{0:T(1024)S(1)} %pad_maximum_fusion.3), channel_id=1, replica_groups=mesh['call'=8,'x'=4,'y'=8,'core'=2] {'core'}, use_global_device_ids=true, to_apply=%region_6.7 | all-reduce | flops 2048 | bytes 16384 | tf_op jit(solution)/shard_map/psum | solution.py:141
  150.8 15.7 %psum.29 = f32[2048]{0:T(1024)S(1)} all-reduce(f32[2048]{0:T(1024)S(1)} %psum.28), channel_id=1, replica_groups=mesh['call'=8,'x'=4,'y'=8,'core'=2] {'y'}, use_global_device_ids=true, to_apply=%region_7.8 | all-reduce | flops 2048 | bytes 16384 | tf_op jit(solution)/shard_map/psum | solution.py:141
  166.5 11.1 %psum.30 = f32[2048]{0:T(1024)S(1)} all-reduce(f32[2048]{0:T(1024)S(1)} %psum.29), channel_id=1, replica_groups=mesh['call'=8,'x'=4,'y'=8,'core'=2] {'x'}, use_global_device_ids=true, to_apply=%region_8.9 | all-reduce | flops 2048 | bytes 16384 | tf_op jit(solution)/shard_map/psum | solution.py:141
  177.6 19.2 %psum.31 = f32[2048]{0:T(1024)S(1)} all-reduce(f32[2048]{0:T(1024)S(1)} %psum.30), channel_id=1, replica_groups=mesh['call'=8,'x'=4,'y'=8,'core'=2] {'call'}, use_global_device_ids=true, to_apply=%region_9.10 | all-reduce | flops 2048 | bytes 16384 | tf_op jit(solution)/shard_map/psum | solution.py:141
  (57 shorter events, 17.8 us)
Async XLA Ops:
  7.2 104.0 %all-gather.2.cloned.1.call-start = ((), (), s32[]{:S(2)}) async-start(), calls=%async_computation | async-start | bytes 12779520 | tf_op jit(solution)/shard_map/all_gather | solution.py:102
  8.9 10.0 %collective-permute-start = (bf16[128,1024]{1,0:T(8,128)(2,1)}, bf16[128,1024]{1,0:T(8,128)(2,1)S(1)}, u32[]{:S(2)}, u32[]{:S(2)}) collective-permute-start(bf16[128,1024]{1,0:T(8,128)(2,1)} %bitcast.18), channel_id=1, source_target_pairs={{0,1},{1,2},{2,3},{3,4},{4,5},{5,6},{6,7},{7,8},{8,9},{9,10},{10,1... | collective-permute-start | bytes 786440 | tf_op jit(solution)/shard_map/ppermute | solution.py:19
  18.9 9.8 %collective-permute-start.1 = (bf16[128,1024]{1,0:T(8,128)(2,1)S(1)}, bf16[128,1024]{1,0:T(8,128)(2,1)S(1)}, u32[]{:S(2)}, u32[]{:S(2)}) collective-permute-start(bf16[128,1024]{1,0:T(8,128)(2,1)S(1)} %collective-permute-done), channel_id=1, source_target_pairs={{0,1},{1,2},{2,3},{3,4},{4,5},{5,6},{6,7},{7,8},{8,9},{9,10},{10,1... | collective-permute-start | bytes 786440 | tf_op jit(solution)/shard_map/ppermute | solution.py:19
  28.7 11.4 %collective-permute-start.2 = (bf16[128,1024]{1,0:T(8,128)(2,1)S(1)}, bf16[128,1024]{1,0:T(8,128)(2,1)S(1)}, u32[]{:S(2)}, u32[]{:S(2)}) collective-permute-start(bf16[128,1024]{1,0:T(8,128)(2,1)S(1)} %collective-permute-done.1), channel_id=1, source_target_pairs={{0,1},{1,2},{2,3},{3,4},{4,5},{5,6},{6,7},{7,8},{8,9},{9,10},{10,1... | collective-permute-start | bytes 786440 | tf_op jit(solution)/shard_map/ppermute | solution.py:19
  40.1 11.6 %collective-permute-start.3 = (bf16[128,1024]{1,0:T(8,128)(2,1)S(1)}, bf16[128,1024]{1,0:T(8,128)(2,1)S(1)}, u32[]{:S(2)}, u32[]{:S(2)}) collective-permute-start(bf16[128,1024]{1,0:T(8,128)(2,1)S(1)} %collective-permute-done.2), channel_id=1, source_target_pairs={{0,1},{1,2},{2,3},{3,4},{4,5},{5,6},{6,7},{7,8},{8,9},{9,10},{10,1... | collective-permute-start | bytes 786440 | tf_op jit(solution)/shard_map/ppermute | solution.py:19
  51.7 9.8 %collective-permute-start.4 = (bf16[128,1024]{1,0:T(8,128)(2,1)S(1)}, bf16[128,1024]{1,0:T(8,128)(2,1)S(1)}, u32[]{:S(2)}, u32[]{:S(2)}) collective-permute-start(bf16[128,1024]{1,0:T(8,128)(2,1)S(1)} %collective-permute-done.3), channel_id=1, source_target_pairs={{0,1},{1,2},{2,3},{3,4},{4,5},{5,6},{6,7},{7,8},{8,9},{9,10},{10,1... | collective-permute-start | bytes 786440 | tf_op jit(solution)/shard_map/ppermute | solution.py:19
  61.5 9.8 %collective-permute-start.5 = (bf16[128,1024]{1,0:T(8,128)(2,1)S(1)}, bf16[128,1024]{1,0:T(8,128)(2,1)S(1)}, u32[]{:S(2)}, u32[]{:S(2)}) collective-permute-start(bf16[128,1024]{1,0:T(8,128)(2,1)S(1)} %collective-permute-done.4), channel_id=1, source_target_pairs={{0,1},{1,2},{2,3},{3,4},{4,5},{5,6},{6,7},{7,8},{8,9},{9,10},{10,1... | collective-permute-start | bytes 786440 | tf_op jit(solution)/shard_map/ppermute | solution.py:19
  71.3 15.5 %collective-permute-start.6 = (bf16[128,1024]{1,0:T(8,128)(2,1)S(1)}, bf16[128,1024]{1,0:T(8,128)(2,1)S(1)}, u32[]{:S(2)}, u32[]{:S(2)}) collective-permute-start(bf16[128,1024]{1,0:T(8,128)(2,1)S(1)} %collective-permute-done.5), channel_id=1, source_target_pairs={{0,1},{1,2},{2,3},{3,4},{4,5},{5,6},{6,7},{7,8},{8,9},{9,10},{10,1... | collective-permute-start | bytes 786440 | tf_op jit(solution)/shard_map/ppermute | solution.py:19
  86.9 15.5 %collective-permute-start.7 = (bf16[128,1024]{1,0:T(8,128)(2,1)S(1)}, bf16[128,1024]{1,0:T(8,128)(2,1)S(1)}, u32[]{:S(2)}, u32[]{:S(2)}) collective-permute-start(bf16[128,1024]{1,0:T(8,128)(2,1)S(1)} %collective-permute-done.6), channel_id=1, source_target_pairs={{0,1},{1,2},{2,3},{3,4},{4,5},{5,6},{6,7},{7,8},{8,9},{9,10},{10,1... | collective-permute-start | bytes 786440 | tf_op jit(solution)/shard_map/ppermute | solution.py:19
  88.8 13.8 %copy-start = (bf16[1,128,1024]{2,1,0:T(8,128)(2,1)S(1)}, bf16[1,128,1024]{2,1,0:T(8,128)(2,1)}, u32[]{:S(2)}) copy-start(bf16[1,128,1024]{2,1,0:T(8,128)(2,1)} %param.10) | copy-start | bytes 786436
  102.6 1.2 copy-start.5
  132.8 2.5 %copy-start.6 = (f32[1024]{0:T(1024)S(1)}, f32[1024]{0:T(1024)}, u32[]{:S(2)}) copy-start(f32[1024]{0:T(1024)} %param.15) | copy-start | bytes 12292
  135.1 3.3 %copy-start.1 = (bf16[128,1024]{1,0:T(8,128)(2,1)}, bf16[128,1024]{1,0:T(8,128)(2,1)S(1)}, u32[]{:S(2)}) copy-start(bf16[128,1024]{1,0:T(8,128)(2,1)S(1)} %get-tuple-element.19) | copy-start | bytes 786436
  135.3 11.0 %copy-start.2 = (f32[9,1024]{1,0:T(8,128)S(1)}, f32[9,1024]{1,0:T(8,128)}, u32[]{:S(2)}) copy-start(f32[9,1024]{1,0:T(8,128)} %param.17) | copy-start | bytes 110596
  135.3 11.0 %copy-start.7 = (s32[8]{0:T(128)S(1)}, s32[8]{0:T(128)}, u32[]{:S(2)}) copy-start(s32[8]{0:T(128)} %param.11) | copy-start | bytes 100
  138.4 58.5 %copy-start.3 = (f32[1024]{0:T(1024)S(1)}, f32[1024]{0:T(1024)}, u32[]{:S(2)}) copy-start(f32[1024]{0:T(1024)} %param.19) | copy-start | bytes 12292
  138.4 58.5 %copy-start.4 = (f32[1024]{0:T(1024)S(1)}, f32[1024]{0:T(1024)}, u32[]{:S(2)}) copy-start(f32[1024]{0:T(1024)} %param.18) | copy-start | bytes 12292
  138.6 9.0 %collective-permute-start.8 = (bf16[4,1024]{1,0:T(4,128)(2,1)S(1)}, bf16[4,1024]{1,0:T(4,128)(2,1)S(1)}, u32[]{:S(2)}, u32[]{:S(2)}) collective-permute-start(bf16[4,1024]{1,0:T(4,128)(2,1)S(1)} %get-tuple-element.5), channel_id=1, source_target_pairs={{0,1},{1,2},{2,3},{3,4},{4,5},{5,6},{6,7},{7,8},{8,9},{9,10},{10,1... | collective-permute-start | bytes 24584 | tf_op jit(solution)/shard_map/ppermute | solution.py:29
  140.8 6.9 %collective-permute-start.9 = (bf16[4,1024]{1,0:T(4,128)(2,1)S(1)}, bf16[4,1024]{1,0:T(4,128)(2,1)S(1)}, u32[]{:S(2)}, u32[]{:S(2)}) collective-permute-start(bf16[4,1024]{1,0:T(4,128)(2,1)S(1)} %get-tuple-element.6), channel_id=1, source_target_pairs={{1,0},{2,1},{3,2},{4,3},{5,4},{6,5},{7,6},{8,7},{9,8},{10,9},{11,1... | collective-permute-start | bytes 24584 | tf_op jit(solution)/shard_map/ppermute | solution.py:31
Sparse Core Ops, SparseCore 0:
  11.9 99.2 all-gather.1

commit v12 on v11

--- a/solution.py
+++ b/solution.py
@@ -99,9 +99,11 @@
     frame_valid = query_pos < length
     qkv_cols = w_qkv.shape[1]
     out_cols = w_out.shape[1]
-    weights = lax.all_gather(
-        jnp.concatenate([w_qkv, w_out, w_pw1], axis=1), TM, axis=0, tiled=True
-    )
+    packed = jnp.zeros((w_qkv.shape[0], qkv_cols + out_cols + w_pw1.shape[1]), w_qkv.dtype)
+    packed = lax.dynamic_update_slice(packed, w_qkv, (0, 0))
+    packed = lax.dynamic_update_slice(packed, w_out, (0, qkv_cols))
+    packed = lax.dynamic_update_slice(packed, w_pw1, (0, qkv_cols + out_cols))
+    weights = lax.all_gather(packed, TM, axis=0, tiled=True)
     prior_blocks = LEFT // frame_count
     blocks = []
     current = stream

time: 207 us -> 208 us (level)
  local copies, waits for them, and re-layouts: 1.5 us -> 4.69 us
    dynamic_update_slice x0 -> x3, local copies, waits for them, and re-layouts: none -> 2.52 us  [the longest x1 0.91 us: on_device(): packed = lax.dynamic_update_slice(packed, w_qkv, (0, 0))]
where the time goes in v12:
time: 208 us; the launch traced here: 206 us
  waiting for transfers between devices  79.4 us (38%)
  blocking collectives  49.9 us (24%)
  starting transfers between devices  23 us (11%)
  matrix products  16.8 us (8%)
  between operations  15.1 us (7%)
  Pallas kernels  10.1 us (5%)
  other arithmetic  6.97 us (3%)
  local copies, waits for them, and re-layouts  4.69 us (2%)
    ppermute x8, waiting for transfers between devices, passed_along(): lax.ppermute(value, axis, [(source, source + steps) for source in range(f...  73.2 us
    psum x4, blocking collectives, on_device(): moments = lax.psum(moments, axis)  49.9 us
    dot_general x4, matrix products, contract_with(): return jnp.dot(left, rows_piece, preferred_element_type=jnp.float32)  16.8 us
    ppermute x8, starting transfers between devices, passed_along(): lax.ppermute(value, axis, [(source, source + steps) for source in range(f...  15.3 us
    pallas_call x1, Pallas kernels, attend(): pl.pallas_call(attend_kernel, out_shape=jax.ShapeDtypeStruct((rows, width...  10.1 us
    all_gather x1, waiting for transfers between devices, on_device(): weights = lax.all_gather(packed, TM, axis=0, tiled=True)  6.18 us
    ppermute x1, starting transfers between devices, with_halo(): lax.ppermute(head, axis, [((i + 1) % count, i) for i in range(ends)])  5.52 us
  transfers between devices with their start and end apart: 11, of which 9 were waited for; matrix products, arithmetic and copies ran while one was open for 3% of the time, Pallas kernels for 0%

profile of v12, /device:TPU:6, one launch (start us, length us, event | category | flops | bytes accessed | tf_op | source)
XLA Modules:
  0.0 206.0 jit_solution(5733412344983502078)
XLA Ops:
  10.4 1.9 collective-permute-start
  12.4 8.1 %collective-permute-done = bf16[128,1024]{1,0:T(8,128)(2,1)S(1)} collective-permute-done((bf16[128,1024]{1,0:T(8,128)(2,1)}, bf16[128,1024]{1,0:T(8,128)(2,1)S(1)}, u32[]{:S(2)}, u32[]{:S(2)}) %collective-permute-start) | collective-permute-done | bytes 262176 | tf_op jit(solution)/shard_map/ppermute | solution.py:19
  20.4 1.9 collective-permute-start.1
  22.4 7.9 %collective-permute-done.1 = bf16[128,1024]{1,0:T(8,128)(2,1)S(1)} collective-permute-done((bf16[128,1024]{1,0:T(8,128)(2,1)S(1)}, bf16[128,1024]{1,0:T(8,128)(2,1)S(1)}, u32[]{:S(2)}, u32[]{:S(2)}) %collective-permute-start.1) | collective-permute-done | bytes 262176 | tf_op jit(solution)/shard_map/ppermute | solution.py:19
  32.1 8.9 %collective-permute-done.2 = bf16[128,1024]{1,0:T(8,128)(2,1)S(1)} collective-permute-done((bf16[128,1024]{1,0:T(8,128)(2,1)S(1)}, bf16[128,1024]{1,0:T(8,128)(2,1)S(1)}, u32[]{:S(2)}, u32[]{:S(2)}) %collective-permute-start.2) | collective-permute-done | bytes 262176 | tf_op jit(solution)/shard_map/ppermute | solution.py:19
  41.1 1.9 collective-permute-start.3
  43.0 9.2 %collective-permute-done.3 = bf16[128,1024]{1,0:T(8,128)(2,1)S(1)} collective-permute-done((bf16[128,1024]{1,0:T(8,128)(2,1)S(1)}, bf16[128,1024]{1,0:T(8,128)(2,1)S(1)}, u32[]{:S(2)}, u32[]{:S(2)}) %collective-permute-start.3) | collective-permute-done | bytes 262176 | tf_op jit(solution)/shard_map/ppermute | solution.py:19
  54.1 7.9 %collective-permute-done.4 = bf16[128,1024]{1,0:T(8,128)(2,1)S(1)} collective-permute-done((bf16[128,1024]{1,0:T(8,128)(2,1)S(1)}, bf16[128,1024]{1,0:T(8,128)(2,1)S(1)}, u32[]{:S(2)}, u32[]{:S(2)}) %collective-permute-start.4) | collective-permute-done | bytes 262176 | tf_op jit(solution)/shard_map/ppermute | solution.py:19
  63.9 7.8 %collective-permute-done.5 = bf16[128,1024]{1,0:T(8,128)(2,1)S(1)} collective-permute-done((bf16[128,1024]{1,0:T(8,128)(2,1)S(1)}, bf16[128,1024]{1,0:T(8,128)(2,1)S(1)}, u32[]{:S(2)}, u32[]{:S(2)}) %collective-permute-start.5) | collective-permute-done | bytes 262176 | tf_op jit(solution)/shard_map/ppermute | solution.py:19
  71.8 1.9 collective-permute-start.6
  75.6 11.6 %collective-permute-done.6 = bf16[128,1024]{1,0:T(8,128)(2,1)S(1)} collective-permute-done((bf16[128,1024]{1,0:T(8,128)(2,1)S(1)}, bf16[128,1024]{1,0:T(8,128)(2,1)S(1)}, u32[]{:S(2)}, u32[]{:S(2)}) %collective-permute-start.6) | collective-permute-done | bytes 262176 | tf_op jit(solution)/shard_map/ppermute | solution.py:19
  90.9 11.8 %collective-permute-done.7 = bf16[128,1024]{1,0:T(8,128)(2,1)S(1)} collective-permute-done((bf16[128,1024]{1,0:T(8,128)(2,1)S(1)}, bf16[128,1024]{1,0:T(8,128)(2,1)S(1)}, u32[]{:S(2)}, u32[]{:S(2)}) %collective-permute-start.7) | collective-permute-done | bytes 262176 | tf_op jit(solution)/shard_map/ppermute | solution.py:19
  105.0 6.2 %all-gather.2.cloned.1.call-done = bf16[1024,6144]{1,0:T(8,128)(2,1)} async-done(((bf16[16,6144]{1,0:T(8,128)(2,1)}), bf16[1024,6144]{1,0:T(8,128)(2,1)}) %all-gather.2.cloned.1.call-update) | async-done | bytes 12582928 | tf_op jit(solution)/shard_map/all_gather | solution.py:106
  111.1 8.8 %convolution_convert_fusion.k_ref.v_ref = bf16[1152,2048]{1,0:T(8,128)(2,1)} fusion(bf16[1152,1024]{1,0:T(8,128)(2,1)S(1)} %fusion.4, bf16[1024,6144]{1,0:T(8,128)(2,1)} %all-gather.2.cloned.1.call-done), kind=kOutput, calls=%fused_computation | convolution fusion | flops 4834197504 | bytes 11272192 | tf_op jit(solution)/shard_map/dot_general | solution.py:45
  119.9 2.7 %fusion.21.q_ref = bf16[128,1024]{1,0:T(8,128)(2,1)} fusion(bf16[1024,6144]{1,0:T(8,128)(2,1)} %all-gather.2.cloned.1.call-done, bf16[1152,1024]{1,0:T(8,128)(2,1)S(1)} %fusion.4), kind=kOutput, calls=%fused_computation.18 | convolution fusion | flops 268566528 | bytes 2621440 | tf_op jit(solution)/shard_map/dot_general | solution.py:45
  122.7 10.1 %shard_map.113 = bf16[128,1024]{1,0:T(8,128)(2,1)} custom-call(bf16[128,1024]{1,0:T(8,128)(2,1)} %fusion.21.q_ref, bf16[1152,2048]{1,0:T(8,128)(2,1)} %convolution_convert_fusion.k_ref.v_ref, bf16[1152,2048]{1,0:T(8,128)(2,1)} %convolution_convert_fusion.k_ref.v_ref, f32[128,1152]{1,0:T(8,128)} %and_convert_fusion.m_ref), custom_call_target="tpu_custom_call" | custom-call | flops 1207959552 | bytes 5832704 | tf_op jit(solution)/shard_map/pallas_call | solution.py:71
  132.8 2.2 %convert_reduce_fusion.1 = (f32[128]{0:T(128)S(1)}, bf16[128,1024]{1,0:T(8,128)(2,1)S(1)}) fusion(bf16[128,1024]{1,0:T(8,128)(2,1)} %shard_map.113, bf16[1024,6144]{1,0:T(8,128)(2,1)} %all-gather.2.cloned.1.call-done, bf16[1,128,1024]{2,1,0:T(8,128)(2,1)S(1)} %copy-done.1, pred[128]{0:T(512)(128)(4,1)S(1)} %broadcast_compare_fusion), kind=kOutput, calls=%fused_computation.22 | convolution fusion | flops 269221760 | bytes 2884224 | tf_op jit(solution)/shard_map/dot_general | solution.py:45
  135.3 3.0 %fusion.5 = f32[128,2048]{1,0:T(8,128)S(1)} fusion(bf16[1024,6144]{1,0:T(8,128)(2,1)} %all-gather.2.cloned.1.call-done, bf16[128,1024]{1,0:T(8,128)(2,1)S(1)} %get-tuple-element.19, f32[1024]{0:T(1024)S(1)} %copy-done.7, f32[128]{0:T(128)S(1)} %add_rsqrt_fusion.1, f32[128]{0:T(128)S(1)} %broadcast_multiply_fusion.1), kind=kOutput, calls=%fused_computation.8 | convolution fusion | flops 537526272 | bytes 5510144 | tf_op jit(solution)/shard_map/dot_general | solution.py:45
  138.6 2.2 %collective-permute-start.8 = (bf16[4,1024]{1,0:T(4,128)(2,1)S(1)}, bf16[4,1024]{1,0:T(4,128)(2,1)S(1)}, u32[]{:S(2)}, u32[]{:S(2)}) collective-permute-start(bf16[4,1024]{1,0:T(4,128)(2,1)S(1)} %get-tuple-element.5), channel_id=1, source_target_pairs={{0,1},{1,2},{2,3},{3,4},{4,5},{5,6},{6,7},{7,8},{8,9},{9,10},{10,1... | collective-permute-start | bytes 24584 | tf_op jit(solution)/shard_map/ppermute | solution.py:29
  140.7 5.5 %collective-permute-start.9 = (bf16[4,1024]{1,0:T(4,128)(2,1)S(1)}, bf16[4,1024]{1,0:T(4,128)(2,1)S(1)}, u32[]{:S(2)}, u32[]{:S(2)}) collective-permute-start(bf16[4,1024]{1,0:T(4,128)(2,1)S(1)} %get-tuple-element.6), channel_id=1, source_target_pairs={{1,0},{2,1},{3,2},{4,3},{5,4},{6,5},{7,6},{8,7},{9,8},{10,9},{11,1... | collective-permute-start | bytes 24584 | tf_op jit(solution)/shard_map/ppermute | solution.py:31
  148.3 2.5 %psum.28 = f32[2048]{0:T(1024)S(1)} all-reduce(f32[2048]{0:T(1024)S(1)} %pad_maximum_fusion.2), channel_id=1, replica_groups=mesh['call'=8,'x'=4,'y'=8,'core'=2] {'core'}, use_global_device_ids=true, to_apply=%region_6.7 | all-reduce | flops 2048 | bytes 16384 | tf_op jit(solution)/shard_map/psum | solution.py:143
  150.8 15.8 %psum.29 = f32[2048]{0:T(1024)S(1)} all-reduce(f32[2048]{0:T(1024)S(1)} %psum.28), channel_id=1, replica_groups=mesh['call'=8,'x'=4,'y'=8,'core'=2] {'y'}, use_global_device_ids=true, to_apply=%region_7.8 | all-reduce | flops 2048 | bytes 16384 | tf_op jit(solution)/shard_map/psum | solution.py:143
  166.7 11.1 %psum.30 = f32[2048]{0:T(1024)S(1)} all-reduce(f32[2048]{0:T(1024)S(1)} %psum.29), channel_id=1, replica_groups=mesh['call'=8,'x'=4,'y'=8,'core'=2] {'x'}, use_global_device_ids=true, to_apply=%region_8.9 | all-reduce | flops 2048 | bytes 16384 | tf_op jit(solution)/shard_map/psum | solution.py:143
  177.7 20.5 %psum.31 = f32[2048]{0:T(1024)S(1)} all-reduce(f32[2048]{0:T(1024)S(1)} %psum.30), channel_id=1, replica_groups=mesh['call'=8,'x'=4,'y'=8,'core'=2] {'call'}, use_global_device_ids=true, to_apply=%region_9.10 | all-reduce | flops 2048 | bytes 16384 | tf_op jit(solution)/shard_map/psum | solution.py:143
  (61 shorter events, 19.4 us)
Async XLA Ops:
  7.2 104.0 %all-gather.2.cloned.1.call-start = ((), (), s32[]{:S(2)}) async-start(), calls=%async_computation | async-start | bytes 12779520 | tf_op jit(solution)/shard_map/all_gather | solution.py:106
  9.7 0.7 copy-start
  10.4 10.0 %collective-permute-start = (bf16[128,1024]{1,0:T(8,128)(2,1)}, bf16[128,1024]{1,0:T(8,128)(2,1)S(1)}, u32[]{:S(2)}, u32[]{:S(2)}) collective-permute-start(bf16[128,1024]{1,0:T(8,128)(2,1)} %bitcast.18), channel_id=1, source_target_pairs={{0,1},{1,2},{2,3},{3,4},{4,5},{5,6},{6,7},{7,8},{8,9},{9,10},{10,1... | collective-permute-start | bytes 786440 | tf_op jit(solution)/shard_map/ppermute | solution.py:19
  20.4 9.8 %collective-permute-start.1 = (bf16[128,1024]{1,0:T(8,128)(2,1)S(1)}, bf16[128,1024]{1,0:T(8,128)(2,1)S(1)}, u32[]{:S(2)}, u32[]{:S(2)}) collective-permute-start(bf16[128,1024]{1,0:T(8,128)(2,1)S(1)} %collective-permute-done), channel_id=1, source_target_pairs={{0,1},{1,2},{2,3},{3,4},{4,5},{5,6},{6,7},{7,8},{8,9},{9,10},{10,1... | collective-permute-start | bytes 786440 | tf_op jit(solution)/shard_map/ppermute | solution.py:19
  30.2 10.8 %collective-permute-start.2 = (bf16[128,1024]{1,0:T(8,128)(2,1)S(1)}, bf16[128,1024]{1,0:T(8,128)(2,1)S(1)}, u32[]{:S(2)}, u32[]{:S(2)}) collective-permute-start(bf16[128,1024]{1,0:T(8,128)(2,1)S(1)} %collective-permute-done.1), channel_id=1, source_target_pairs={{0,1},{1,2},{2,3},{3,4},{4,5},{5,6},{6,7},{7,8},{8,9},{9,10},{10,1... | collective-permute-start | bytes 786440 | tf_op jit(solution)/shard_map/ppermute | solution.py:19
  41.1 11.1 %collective-permute-start.3 = (bf16[128,1024]{1,0:T(8,128)(2,1)S(1)}, bf16[128,1024]{1,0:T(8,128)(2,1)S(1)}, u32[]{:S(2)}, u32[]{:S(2)}) collective-permute-start(bf16[128,1024]{1,0:T(8,128)(2,1)S(1)} %collective-permute-done.2), channel_id=1, source_target_pairs={{0,1},{1,2},{2,3},{3,4},{4,5},{5,6},{6,7},{7,8},{8,9},{9,10},{10,1... | collective-permute-start | bytes 786440 | tf_op jit(solution)/shard_map/ppermute | solution.py:19
  52.2 9.8 %collective-permute-start.4 = (bf16[128,1024]{1,0:T(8,128)(2,1)S(1)}, bf16[128,1024]{1,0:T(8,128)(2,1)S(1)}, u32[]{:S(2)}, u32[]{:S(2)}) collective-permute-start(bf16[128,1024]{1,0:T(8,128)(2,1)S(1)} %collective-permute-done.3), channel_id=1, source_target_pairs={{0,1},{1,2},{2,3},{3,4},{4,5},{5,6},{6,7},{7,8},{8,9},{9,10},{10,1... | collective-permute-start | bytes 786440 | tf_op jit(solution)/shard_map/ppermute | solution.py:19
  62.0 9.8 %collective-permute-start.5 = (bf16[128,1024]{1,0:T(8,128)(2,1)S(1)}, bf16[128,1024]{1,0:T(8,128)(2,1)S(1)}, u32[]{:S(2)}, u32[]{:S(2)}) collective-permute-start(bf16[128,1024]{1,0:T(8,128)(2,1)S(1)} %collective-permute-done.4), channel_id=1, source_target_pairs={{0,1},{1,2},{2,3},{3,4},{4,5},{5,6},{6,7},{7,8},{8,9},{9,10},{10,1... | collective-permute-start | bytes 786440 | tf_op jit(solution)/shard_map/ppermute | solution.py:19
  71.8 15.5 %collective-permute-start.6 = (bf16[128,1024]{1,0:T(8,128)(2,1)S(1)}, bf16[128,1024]{1,0:T(8,128)(2,1)S(1)}, u32[]{:S(2)}, u32[]{:S(2)}) collective-permute-start(bf16[128,1024]{1,0:T(8,128)(2,1)S(1)} %collective-permute-done.5), channel_id=1, source_target_pairs={{0,1},{1,2},{2,3},{3,4},{4,5},{5,6},{6,7},{7,8},{8,9},{9,10},{10,1... | collective-permute-start | bytes 786440 | tf_op jit(solution)/shard_map/ppermute | solution.py:19
  87.2 15.5 %collective-permute-start.7 = (bf16[128,1024]{1,0:T(8,128)(2,1)S(1)}, bf16[128,1024]{1,0:T(8,128)(2,1)S(1)}, u32[]{:S(2)}, u32[]{:S(2)}) collective-permute-start(bf16[128,1024]{1,0:T(8,128)(2,1)S(1)} %collective-permute-done.6), channel_id=1, source_target_pairs={{0,1},{1,2},{2,3},{3,4},{4,5},{5,6},{6,7},{7,8},{8,9},{9,10},{10,1... | collective-permute-start | bytes 786440 | tf_op jit(solution)/shard_map/ppermute | solution.py:19
  89.2 13.8 %copy-start.1 = (bf16[1,128,1024]{2,1,0:T(8,128)(2,1)S(1)}, bf16[1,128,1024]{2,1,0:T(8,128)(2,1)}, u32[]{:S(2)}) copy-start(bf16[1,128,1024]{2,1,0:T(8,128)(2,1)} %param.10) | copy-start | bytes 786436
  103.0 1.2 copy-start.6
  132.8 2.5 %copy-start.7 = (f32[1024]{0:T(1024)S(1)}, f32[1024]{0:T(1024)}, u32[]{:S(2)}) copy-start(f32[1024]{0:T(1024)} %param.15) | copy-start | bytes 12292
  135.0 3.3 %copy-start.2 = (bf16[128,1024]{1,0:T(8,128)(2,1)}, bf16[128,1024]{1,0:T(8,128)(2,1)S(1)}, u32[]{:S(2)}) copy-start(bf16[128,1024]{1,0:T(8,128)(2,1)S(1)} %get-tuple-element.19) | copy-start | bytes 786436
  135.3 11.0 %copy-start.3 = (f32[9,1024]{1,0:T(8,128)S(1)}, f32[9,1024]{1,0:T(8,128)}, u32[]{:S(2)}) copy-start(f32[9,1024]{1,0:T(8,128)} %param.17) | copy-start | bytes 110596
  135.3 11.0 %copy-start.8 = (s32[8]{0:T(128)S(1)}, s32[8]{0:T(128)}, u32[]{:S(2)}) copy-start(s32[8]{0:T(128)} %param.11) | copy-start | bytes 100
  138.3 59.9 %copy-start.4 = (f32[1024]{0:T(1024)S(1)}, f32[1024]{0:T(1024)}, u32[]{:S(2)}) copy-start(f32[1024]{0:T(1024)} %param.19) | copy-start | bytes 12292
  138.4 59.9 %copy-start.5 = (f32[1024]{0:T(1024)S(1)}, f32[1024]{0:T(1024)}, u32[]{:S(2)}) copy-start(f32[1024]{0:T(1024)} %param.18) | copy-start | bytes 12292
  138.6 9.0 %collective-permute-start.8 = (bf16[4,1024]{1,0:T(4,128)(2,1)S(1)}, bf16[4,1024]{1,0:T(4,128)(2,1)S(1)}, u32[]{:S(2)}, u32[]{:S(2)}) collective-permute-start(bf16[4,1024]{1,0:T(4,128)(2,1)S(1)} %get-tuple-element.5), channel_id=1, source_target_pairs={{0,1},{1,2},{2,3},{3,4},{4,5},{5,6},{6,7},{7,8},{8,9},{9,10},{10,1... | collective-permute-start | bytes 24584 | tf_op jit(solution)/shard_map/ppermute | solution.py:29
  140.7 6.9 %collective-permute-start.9 = (bf16[4,1024]{1,0:T(4,128)(2,1)S(1)}, bf16[4,1024]{1,0:T(4,128)(2,1)S(1)}, u32[]{:S(2)}, u32[]{:S(2)}) collective-permute-start(bf16[4,1024]{1,0:T(4,128)(2,1)S(1)} %get-tuple-element.6), channel_id=1, source_target_pairs={{1,0},{2,1},{3,2},{4,3},{5,4},{6,5},{7,6},{8,7},{9,8},{10,9},{11,1... | collective-permute-start | bytes 24584 | tf_op jit(solution)/shard_map/ppermute | solution.py:31
Sparse Core Ops, SparseCore 0:
  11.9 99.2 all-gather.1

commit v13 on v7

--- a/solution.py
+++ b/solution.py
@@ -45,15 +45,17 @@
     return jnp.dot(left, rows_piece, preferred_element_type=jnp.float32)
 
 
-def attend_kernel(q_ref, k_ref, v_ref, m_ref, o_ref):
-    width = q_ref.shape[1]
+def attend_kernel(x_ref, wq_ref, k_ref, v_ref, m_ref, o_ref):
+    width = o_ref.shape[1]
     heads = width // HEAD_DIM
     allowed = m_ref[...] > 0.5
     lane = lax.broadcasted_iota(jnp.int32, (1, width), 1)
+    queries = jnp.dot(x_ref[...], wq_ref[...], preferred_element_type=jnp.float32)
+    queries = queries.astype(jnp.bfloat16)
     result = jnp.zeros(o_ref.shape, jnp.float32)
     for head in range(heads):
         inside = (lane >= head * HEAD_DIM) & (lane < (head + 1) * HEAD_DIM)
-        query = jnp.where(inside, q_ref[...], jnp.zeros_like(q_ref[...]))
+        query = jnp.where(inside, queries, jnp.zeros_like(queries))
         scores = lax.dot_general(
             query, k_ref[...], (((1,), (1,)), ((), ())), preferred_element_type=jnp.float32
         ) * (1.0 / jnp.sqrt(jnp.float32(HEAD_DIM)))
@@ -63,8 +65,9 @@
         result = jnp.where(inside, mixed, result)
     o_ref[...] = result.astype(o_ref.dtype)
 
-def attend(queries, key_value, allowed):
-    rows, width = queries.shape
+
+def attend(normed, weights, key_value, allowed):
+    rows, width = normed.shape
     keys = key_value.shape[0]
     tile = 128
     steps = width // tile
@@ -73,18 +76,20 @@
         out_shape=jax.ShapeDtypeStruct((rows, width), jnp.bfloat16),
         grid=(steps,),
         in_specs=[
-            pl.BlockSpec((rows, tile), lambda i: (0, i)),
+            pl.BlockSpec((rows, width), lambda i: (0, 0)),
+            pl.BlockSpec((width, tile), lambda i: (0, i)),
             pl.BlockSpec((keys, tile), lambda i: (0, i)),
             pl.BlockSpec((keys, tile), lambda i: (0, i + steps)),
             pl.BlockSpec((rows, keys), lambda i: (0, 0)),
         ],
         out_specs=pl.BlockSpec((rows, tile), lambda i: (0, i)),
         cost_estimate=pl.CostEstimate(
-            flops=4 * rows * keys * width * tile // HEAD_DIM,
+            flops=4 * rows * keys * width * tile // HEAD_DIM + 2 * rows * width * width,
             transcendentals=rows * keys * width // HEAD_DIM,
-            bytes_accessed=2 * (2 * rows * width + 2 * keys * width) + 4 * rows * keys,
+            bytes_accessed=2 * (2 * rows * width + 2 * keys * width + width * width)
+            + 4 * rows * keys,
         ),
-    )(queries, key_value, key_value, allowed.astype(jnp.float32))
+    )(normed, weights, key_value, key_value, allowed.astype(jnp.float32))
 
 
 def on_device(
@@ -112,14 +117,13 @@
     key_count = context_frames.shape[0]
     normed_all = layer_norm(context_frames, ln_attn_gain).astype(jnp.bfloat16)
     normed = normed_all[key_count - frame_count :]
-    queries = contract_with(normed, weights[:, :model_width]).astype(jnp.bfloat16)
     key_value = contract_with(normed_all, weights[:, model_width:qkv_cols]).astype(jnp.bfloat16)
     key_pos = first_row - prior_blocks * frame_count + jnp.arange(key_count, dtype=jnp.int32)
     span_first = query_pos // SPAN * SPAN
     allowed = (key_pos[None, :] >= 0) & (key_pos[None, :] >= span_first[:, None] - LEFT)
     allowed = allowed & (key_pos[None, :] < span_first[:, None] + SPAN)
     allowed = allowed & ((key_pos[None, :] < length) | (key_pos[None, :] == query_pos[:, None]))
-    context = attend(queries, key_value, allowed)
+    context = attend(normed, weights, key_value, allowed)
     projected = contract_with(context, weights[:, qkv_cols : qkv_cols + out_cols])
     attended = jnp.where(frame_valid[:, None], stream.astype(jnp.float32) + projected, 0.0).astype(
         jnp.bfloat16

time: 207 us -> 205 us (level)
  matrix products: 16.8 us -> 14.1 us
    dot_general x4 -> x3, matrix products: 16.8 us -> 14.1 us  [contract_with(): return jnp.dot(left, rows_piece, preferred_element_type=jnp.float32)]
  transfers between devices with their start and end apart: 11 -> 11, of which waited for: 9 -> 9; matrix products, arithmetic and copies ran while one was open for 3% -> 4% of each run, Pallas kernels for 0% -> 0%
where the time goes in v13:
time: 205 us; the launch traced here: 203 us
  waiting for transfers between devices  80.3 us (39%)
  blocking collectives  48.5 us (24%)
  starting transfers between devices  23 us (11%)
  between operations  15.1 us (7%)
  matrix products  14.1 us (7%)
  Pallas kernels  11.4 us (6%)
  other arithmetic  8.61 us (4%)
  local copies, waits for them, and re-layouts  2.22 us (1%)
    ppermute x8, waiting for transfers between devices, passed_along(): lax.ppermute(value, axis, [(source, source + steps) for source in range(f...  74.4 us
    psum x4, blocking collectives, on_device(): moments = lax.psum(moments, axis)  48.5 us
    ppermute x8, starting transfers between devices, passed_along(): lax.ppermute(value, axis, [(source, source + steps) for source in range(f...  15.3 us
    dot_general x3, matrix products, contract_with(): return jnp.dot(left, rows_piece, preferred_element_type=jnp.float32)  14.1 us
    pallas_call x1, Pallas kernels, attend(): pl.pallas_call(attend_kernel, out_shape=jax.ShapeDtypeStruct((rows, width...  11.4 us
    all_gather x1, waiting for transfers between devices, on_device(): lax.all_gather(jnp.concatenate([w_qkv, w_out, w_pw1], axis=1), TM, axis=0...  5.85 us
    ppermute x1, starting transfers between devices, with_halo(): lax.ppermute(head, axis, [((i + 1) % count, i) for i in range(ends)])  5.51 us
  transfers between devices with their start and end apart: 11, of which 9 were waited for; matrix products, arithmetic and copies ran while one was open for 4% of the time, Pallas kernels for 0%

profile of v13, /device:TPU:6, one launch (start us, length us, event | category | flops | bytes accessed | tf_op | source)
XLA Modules:
  0.0 203.2 jit_solution(1833477859269592727)
XLA Ops:
  8.9 1.9 collective-permute-start
  10.8 8.1 %collective-permute-done = bf16[128,1024]{1,0:T(8,128)(2,1)S(1)} collective-permute-done((bf16[128,1024]{1,0:T(8,128)(2,1)}, bf16[128,1024]{1,0:T(8,128)(2,1)S(1)}, u32[]{:S(2)}, u32[]{:S(2)}) %collective-permute-start) | collective-permute-done | bytes 262176 | tf_op jit(solution)/shard_map/ppermute | solution.py:19
  18.9 1.9 collective-permute-start.1
  20.8 7.9 %collective-permute-done.1 = bf16[128,1024]{1,0:T(8,128)(2,1)S(1)} collective-permute-done((bf16[128,1024]{1,0:T(8,128)(2,1)S(1)}, bf16[128,1024]{1,0:T(8,128)(2,1)S(1)}, u32[]{:S(2)}, u32[]{:S(2)}) %collective-permute-start.1) | collective-permute-done | bytes 262176 | tf_op jit(solution)/shard_map/ppermute | solution.py:19
  28.7 1.9 collective-permute-start.2
  30.6 9.5 %collective-permute-done.2 = bf16[128,1024]{1,0:T(8,128)(2,1)S(1)} collective-permute-done((bf16[128,1024]{1,0:T(8,128)(2,1)S(1)}, bf16[128,1024]{1,0:T(8,128)(2,1)S(1)}, u32[]{:S(2)}, u32[]{:S(2)}) %collective-permute-start.2) | collective-permute-done | bytes 262176 | tf_op jit(solution)/shard_map/ppermute | solution.py:19
  40.1 1.9 collective-permute-start.3
  42.0 9.7 %collective-permute-done.3 = bf16[128,1024]{1,0:T(8,128)(2,1)S(1)} collective-permute-done((bf16[128,1024]{1,0:T(8,128)(2,1)S(1)}, bf16[128,1024]{1,0:T(8,128)(2,1)S(1)}, u32[]{:S(2)}, u32[]{:S(2)}) %collective-permute-start.3) | collective-permute-done | bytes 262176 | tf_op jit(solution)/shard_map/ppermute | solution.py:19
  53.6 7.9 %collective-permute-done.4 = bf16[128,1024]{1,0:T(8,128)(2,1)S(1)} collective-permute-done((bf16[128,1024]{1,0:T(8,128)(2,1)S(1)}, bf16[128,1024]{1,0:T(8,128)(2,1)S(1)}, u32[]{:S(2)}, u32[]{:S(2)}) %collective-permute-start.4) | collective-permute-done | bytes 262176 | tf_op jit(solution)/shard_map/ppermute | solution.py:19
  63.5 7.8 %collective-permute-done.5 = bf16[128,1024]{1,0:T(8,128)(2,1)S(1)} collective-permute-done((bf16[128,1024]{1,0:T(8,128)(2,1)S(1)}, bf16[128,1024]{1,0:T(8,128)(2,1)S(1)}, u32[]{:S(2)}, u32[]{:S(2)}) %collective-permute-start.5) | collective-permute-done | bytes 262176 | tf_op jit(solution)/shard_map/ppermute | solution.py:19
  75.2 11.7 %collective-permute-done.6 = bf16[128,1024]{1,0:T(8,128)(2,1)S(1)} collective-permute-done((bf16[128,1024]{1,0:T(8,128)(2,1)S(1)}, bf16[128,1024]{1,0:T(8,128)(2,1)S(1)}, u32[]{:S(2)}, u32[]{:S(2)}) %collective-permute-start.6) | collective-permute-done | bytes 262176 | tf_op jit(solution)/shard_map/ppermute | solution.py:19
  86.9 1.9 collective-permute-start.7
  90.5 11.9 %collective-permute-done.7 = bf16[128,1024]{1,0:T(8,128)(2,1)S(1)} collective-permute-done((bf16[128,1024]{1,0:T(8,128)(2,1)S(1)}, bf16[128,1024]{1,0:T(8,128)(2,1)S(1)}, u32[]{:S(2)}, u32[]{:S(2)}) %collective-permute-start.7) | collective-permute-done | bytes 262176 | tf_op jit(solution)/shard_map/ppermute | solution.py:19
  105.3 5.8 %all-gather.2.cloned.1.call-done.wq_ref = bf16[1024,6144]{1,0:T(8,128)(2,1)} async-done(((bf16[16,6144]{1,0:T(8,128)(2,1)}), bf16[1024,6144]{1,0:T(8,128)(2,1)}) %all-gather.2.cloned.1.call-update) | async-done | bytes 12582928 | tf_op jit(solution)/shard_map/all_gather | solution.py:107
  111.2 8.8 %convolution_convert_fusion.k_ref.v_ref = bf16[1152,2048]{1,0:T(8,128)(2,1)} fusion(bf16[1152,1024]{1,0:T(8,128)(2,1)S(1)} %fusion.4, bf16[1024,6144]{1,0:T(8,128)(2,1)} %all-gather.2.cloned.1.call-done.wq_ref), kind=kOutput, calls=%fused_computation | convolution fusion | flops 4834197504 | bytes 11272192 | tf_op jit(solution)/shard_map/dot_general | solution.py:45
  120.0 11.4 %shard_map.113 = bf16[128,1024]{1,0:T(8,128)(2,1)} custom-call(bf16[128,1024]{1,0:T(8,128)(2,1)} %slice.108.x_ref, bf16[1024,6144]{1,0:T(8,128)(2,1)} %all-gather.2.cloned.1.call-done.wq_ref, bf16[1152,2048]{1,0:T(8,128)(2,1)} %convolution_convert_fusion.k_ref.v_ref, bf16[1152,2048]{1,0:T(8,128)(2,1)} %convolution_convert_fusion.k_ref.v_ref, ...), custom_call_target="tpu_custom_call" | custom-call | flops 1476395008 | bytes 7929856 | tf_op jit(solution)/shard_map/pallas_call | solution.py:74
  131.4 2.2 %convert_reduce_fusion.1 = (f32[128]{0:T(128)S(1)}, bf16[128,1024]{1,0:T(8,128)(2,1)S(1)}) fusion(bf16[128,1024]{1,0:T(8,128)(2,1)} %shard_map.113, bf16[1024,6144]{1,0:T(8,128)(2,1)} %all-gather.2.cloned.1.call-done.wq_ref, bf16[1,128,1024]{2,1,0:T(8,128)(2,1)S(1)} %copy-done, pred[128]{0:T(512)(128)(4,1)S(1)} %broadcast_compare_fusion), kind=kOutput, calls=%fused_computation.19 | convolution fusion | flops 269221760 | bytes 2884224 | tf_op jit(solution)/shard_map/dot_general | solution.py:45
  133.9 3.0 %fusion.5 = f32[128,2048]{1,0:T(8,128)S(1)} fusion(bf16[1024,6144]{1,0:T(8,128)(2,1)} %all-gather.2.cloned.1.call-done.wq_ref, bf16[128,1024]{1,0:T(8,128)(2,1)S(1)} %get-tuple-element.27, f32[1024]{0:T(1024)S(1)} %copy-done.6, f32[128]{0:T(128)S(1)} %add_rsqrt_fusion.2, f32[128]{0:T(128)S(1)} %broadcast_multiply_fusion.1), kind=kOutput, calls=%fused_computation.8 | convolution fusion | flops 537526272 | bytes 5510144 | tf_op jit(solution)/shard_map/dot_general | solution.py:45
  137.1 2.2 %collective-permute-start.8 = (bf16[4,1024]{1,0:T(4,128)(2,1)S(1)}, bf16[4,1024]{1,0:T(4,128)(2,1)S(1)}, u32[]{:S(2)}, u32[]{:S(2)}) collective-permute-start(bf16[4,1024]{1,0:T(4,128)(2,1)S(1)} %get-tuple-element.13), channel_id=1, source_target_pairs={{0,1},{1,2},{2,3},{3,4},{4,5},{5,6},{6,7},{7,8},{8,9},{9,10},{10,1... | collective-permute-start | bytes 24584 | tf_op jit(solution)/shard_map/ppermute | solution.py:29
  139.3 5.5 %collective-permute-start.9 = (bf16[4,1024]{1,0:T(4,128)(2,1)S(1)}, bf16[4,1024]{1,0:T(4,128)(2,1)S(1)}, u32[]{:S(2)}, u32[]{:S(2)}) collective-permute-start(bf16[4,1024]{1,0:T(4,128)(2,1)S(1)} %get-tuple-element.14), channel_id=1, source_target_pairs={{1,0},{2,1},{3,2},{4,3},{5,4},{6,5},{7,6},{8,7},{9,8},{10,9},{11,1... | collective-permute-start | bytes 24584 | tf_op jit(solution)/shard_map/ppermute | solution.py:31
  146.9 2.5 %all-reduce.3 = (f32[1024]{0:T(1024)S(1)}, f32[1024]{0:T(1024)S(1)}) all-reduce(f32[1024]{0:T(1024)S(1)} %get-tuple-element.3, f32[1024]{0:T(1024)S(1)} %get-tuple-element.2), channel_id=1, replica_groups=mesh['call'=8,'x'=4,'y'=8,'core'=2] {'core'}, use_global_device_ids=true, to_apply=%region_11.12 | all-reduce | flops 2048 | bytes 16384 | tf_op jit(solution)/shard_map/psum | solution.py:145
  149.4 15.7 %all-reduce = (f32[1024]{0:T(1024)S(1)}, f32[1024]{0:T(1024)S(1)}) all-reduce(f32[1024]{0:T(1024)S(1)} %get-tuple-element.10, f32[1024]{0:T(1024)S(1)} %get-tuple-element.11), channel_id=1, replica_groups=mesh['call'=8,'x'=4,'y'=8,'core'=2] {'y'}, use_global_device_ids=true, to_apply=%region_12.13 | all-reduce | flops 2048 | bytes 16384 | tf_op jit(solution)/shard_map/psum | solution.py:145
  165.1 11.1 %all-reduce.2 = (f32[1024]{0:T(1024)S(1)}, f32[1024]{0:T(1024)S(1)}) all-reduce(f32[1024]{0:T(1024)S(1)} %get-tuple-element.4, f32[1024]{0:T(1024)S(1)} %get-tuple-element.5), channel_id=1, replica_groups=mesh['call'=8,'x'=4,'y'=8,'core'=2] {'x'}, use_global_device_ids=true, to_apply=%region_13.14 | all-reduce | flops 2048 | bytes 16384 | tf_op jit(solution)/shard_map/psum | solution.py:145
  176.2 19.2 %all-reduce.1 = (f32[1024]{0:T(1024)S(1)}, f32[1024]{0:T(1024)S(1)}) all-reduce(f32[1024]{0:T(1024)S(1)} %get-tuple-element.8, f32[1024]{0:T(1024)S(1)} %get-tuple-element.9), channel_id=1, replica_groups=mesh['call'=8,'x'=4,'y'=8,'core'=2] {'call'}, use_global_device_ids=true, to_apply=%region_14.15 | all-reduce | flops 2048 | bytes 16384 | tf_op jit(solution)/shard_map/psum | solution.py:145
  (56 shorter events, 16.6 us)
Async XLA Ops:
  7.2 104.0 %all-gather.2.cloned.1.call-start = ((), (), s32[]{:S(2)}) async-start(), calls=%async_computation | async-start | bytes 12779520 | tf_op jit(solution)/shard_map/all_gather | solution.py:107
  8.9 10.0 %collective-permute-start = (bf16[128,1024]{1,0:T(8,128)(2,1)}, bf16[128,1024]{1,0:T(8,128)(2,1)S(1)}, u32[]{:S(2)}, u32[]{:S(2)}) collective-permute-start(bf16[128,1024]{1,0:T(8,128)(2,1)} %bitcast.18), channel_id=1, source_target_pairs={{0,1},{1,2},{2,3},{3,4},{4,5},{5,6},{6,7},{7,8},{8,9},{9,10},{10,1... | collective-permute-start | bytes 786440 | tf_op jit(solution)/shard_map/ppermute | solution.py:19
  18.9 9.8 %collective-permute-start.1 = (bf16[128,1024]{1,0:T(8,128)(2,1)S(1)}, bf16[128,1024]{1,0:T(8,128)(2,1)S(1)}, u32[]{:S(2)}, u32[]{:S(2)}) collective-permute-start(bf16[128,1024]{1,0:T(8,128)(2,1)S(1)} %collective-permute-done), channel_id=1, source_target_pairs={{0,1},{1,2},{2,3},{3,4},{4,5},{5,6},{6,7},{7,8},{8,9},{9,10},{10,1... | collective-permute-start | bytes 786440 | tf_op jit(solution)/shard_map/ppermute | solution.py:19
  28.7 11.4 %collective-permute-start.2 = (bf16[128,1024]{1,0:T(8,128)(2,1)S(1)}, bf16[128,1024]{1,0:T(8,128)(2,1)S(1)}, u32[]{:S(2)}, u32[]{:S(2)}) collective-permute-start(bf16[128,1024]{1,0:T(8,128)(2,1)S(1)} %collective-permute-done.1), channel_id=1, source_target_pairs={{0,1},{1,2},{2,3},{3,4},{4,5},{5,6},{6,7},{7,8},{8,9},{9,10},{10,1... | collective-permute-start | bytes 786440 | tf_op jit(solution)/shard_map/ppermute | solution.py:19
  40.1 11.6 %collective-permute-start.3 = (bf16[128,1024]{1,0:T(8,128)(2,1)S(1)}, bf16[128,1024]{1,0:T(8,128)(2,1)S(1)}, u32[]{:S(2)}, u32[]{:S(2)}) collective-permute-start(bf16[128,1024]{1,0:T(8,128)(2,1)S(1)} %collective-permute-done.2), channel_id=1, source_target_pairs={{0,1},{1,2},{2,3},{3,4},{4,5},{5,6},{6,7},{7,8},{8,9},{9,10},{10,1... | collective-permute-start | bytes 786440 | tf_op jit(solution)/shard_map/ppermute | solution.py:19
  51.7 9.8 %collective-permute-start.4 = (bf16[128,1024]{1,0:T(8,128)(2,1)S(1)}, bf16[128,1024]{1,0:T(8,128)(2,1)S(1)}, u32[]{:S(2)}, u32[]{:S(2)}) collective-permute-start(bf16[128,1024]{1,0:T(8,128)(2,1)S(1)} %collective-permute-done.3), channel_id=1, source_target_pairs={{0,1},{1,2},{2,3},{3,4},{4,5},{5,6},{6,7},{7,8},{8,9},{9,10},{10,1... | collective-permute-start | bytes 786440 | tf_op jit(solution)/shard_map/ppermute | solution.py:19
  61.5 9.8 %collective-permute-start.5 = (bf16[128,1024]{1,0:T(8,128)(2,1)S(1)}, bf16[128,1024]{1,0:T(8,128)(2,1)S(1)}, u32[]{:S(2)}, u32[]{:S(2)}) collective-permute-start(bf16[128,1024]{1,0:T(8,128)(2,1)S(1)} %collective-permute-done.4), channel_id=1, source_target_pairs={{0,1},{1,2},{2,3},{3,4},{4,5},{5,6},{6,7},{7,8},{8,9},{9,10},{10,1... | collective-permute-start | bytes 786440 | tf_op jit(solution)/shard_map/ppermute | solution.py:19
  71.3 15.5 %collective-permute-start.6 = (bf16[128,1024]{1,0:T(8,128)(2,1)S(1)}, bf16[128,1024]{1,0:T(8,128)(2,1)S(1)}, u32[]{:S(2)}, u32[]{:S(2)}) collective-permute-start(bf16[128,1024]{1,0:T(8,128)(2,1)S(1)} %collective-permute-done.5), channel_id=1, source_target_pairs={{0,1},{1,2},{2,3},{3,4},{4,5},{5,6},{6,7},{7,8},{8,9},{9,10},{10,1... | collective-permute-start | bytes 786440 | tf_op jit(solution)/shard_map/ppermute | solution.py:19
  86.9 15.5 %collective-permute-start.7 = (bf16[128,1024]{1,0:T(8,128)(2,1)S(1)}, bf16[128,1024]{1,0:T(8,128)(2,1)S(1)}, u32[]{:S(2)}, u32[]{:S(2)}) collective-permute-start(bf16[128,1024]{1,0:T(8,128)(2,1)S(1)} %collective-permute-done.6), channel_id=1, source_target_pairs={{0,1},{1,2},{2,3},{3,4},{4,5},{5,6},{6,7},{7,8},{8,9},{9,10},{10,1... | collective-permute-start | bytes 786440 | tf_op jit(solution)/shard_map/ppermute | solution.py:19
  88.8 13.8 %copy-start = (bf16[1,128,1024]{2,1,0:T(8,128)(2,1)S(1)}, bf16[1,128,1024]{2,1,0:T(8,128)(2,1)}, u32[]{:S(2)}) copy-start(bf16[1,128,1024]{2,1,0:T(8,128)(2,1)} %param.10) | copy-start | bytes 786436
  102.6 1.2 copy-start.5
  131.4 2.5 %copy-start.6 = (f32[1024]{0:T(1024)S(1)}, f32[1024]{0:T(1024)}, u32[]{:S(2)}) copy-start(f32[1024]{0:T(1024)} %param.15) | copy-start | bytes 12292
  133.6 3.3 %copy-start.1 = (bf16[128,1024]{1,0:T(8,128)(2,1)}, bf16[128,1024]{1,0:T(8,128)(2,1)S(1)}, u32[]{:S(2)}) copy-start(bf16[128,1024]{1,0:T(8,128)(2,1)S(1)} %get-tuple-element.27) | copy-start | bytes 786436
  133.9 11.0 %copy-start.2 = (f32[9,1024]{1,0:T(8,128)S(1)}, f32[9,1024]{1,0:T(8,128)}, u32[]{:S(2)}) copy-start(f32[9,1024]{1,0:T(8,128)} %param.17) | copy-start | bytes 110596
  133.9 11.0 %copy-start.7 = (s32[8]{0:T(128)S(1)}, s32[8]{0:T(128)}, u32[]{:S(2)}) copy-start(s32[8]{0:T(128)} %param.11) | copy-start | bytes 100
  136.9 58.5 %copy-start.3 = (f32[1024]{0:T(1024)S(1)}, f32[1024]{0:T(1024)}, u32[]{:S(2)}) copy-start(f32[1024]{0:T(1024)} %param.19) | copy-start | bytes 12292
  136.9 58.5 %copy-start.4 = (f32[1024]{0:T(1024)S(1)}, f32[1024]{0:T(1024)}, u32[]{:S(2)}) copy-start(f32[1024]{0:T(1024)} %param.18) | copy-start | bytes 12292
  137.1 9.0 %collective-permute-start.8 = (bf16[4,1024]{1,0:T(4,128)(2,1)S(1)}, bf16[4,1024]{1,0:T(4,128)(2,1)S(1)}, u32[]{:S(2)}, u32[]{:S(2)}) collective-permute-start(bf16[4,1024]{1,0:T(4,128)(2,1)S(1)} %get-tuple-element.13), channel_id=1, source_target_pairs={{0,1},{1,2},{2,3},{3,4},{4,5},{5,6},{6,7},{7,8},{8,9},{9,10},{10,1... | collective-permute-start | bytes 24584 | tf_op jit(solution)/shard_map/ppermute | solution.py:29
  139.3 6.9 %collective-permute-start.9 = (bf16[4,1024]{1,0:T(4,128)(2,1)S(1)}, bf16[4,1024]{1,0:T(4,128)(2,1)S(1)}, u32[]{:S(2)}, u32[]{:S(2)}) collective-permute-start(bf16[4,1024]{1,0:T(4,128)(2,1)S(1)} %get-tuple-element.14), channel_id=1, source_target_pairs={{1,0},{2,1},{3,2},{4,3},{5,4},{6,5},{7,6},{8,7},{9,8},{10,9},{11,1... | collective-permute-start | bytes 24584 | tf_op jit(solution)/shard_map/ppermute | solution.py:31
Sparse Core Ops, SparseCore 0:
  11.9 99.2 all-gather.1

commit v14 on v13

--- a/solution.py
+++ b/solution.py
@@ -45,30 +45,33 @@
     return jnp.dot(left, rows_piece, preferred_element_type=jnp.float32)
 
 
-def attend_kernel(x_ref, wq_ref, k_ref, v_ref, m_ref, o_ref):
-    width = o_ref.shape[1]
+def attend_kernel(x_ref, wq_ref, wk_ref, wv_ref, m_ref, o_ref):
+    rows, width = o_ref.shape
     heads = width // HEAD_DIM
     allowed = m_ref[...] > 0.5
     lane = lax.broadcasted_iota(jnp.int32, (1, width), 1)
-    queries = jnp.dot(x_ref[...], wq_ref[...], preferred_element_type=jnp.float32)
-    queries = queries.astype(jnp.bfloat16)
+    frames = x_ref[...]
+    own = frames[frames.shape[0] - rows :]
+    queries = jnp.dot(own, wq_ref[...], preferred_element_type=jnp.float32).astype(jnp.bfloat16)
+    keys = jnp.dot(frames, wk_ref[...], preferred_element_type=jnp.float32).astype(jnp.bfloat16)
+    values = jnp.dot(frames, wv_ref[...], preferred_element_type=jnp.float32).astype(jnp.bfloat16)
     result = jnp.zeros(o_ref.shape, jnp.float32)
     for head in range(heads):
         inside = (lane >= head * HEAD_DIM) & (lane < (head + 1) * HEAD_DIM)
         query = jnp.where(inside, queries, jnp.zeros_like(queries))
         scores = lax.dot_general(
-            query, k_ref[...], (((1,), (1,)), ((), ())), preferred_element_type=jnp.float32
+            query, keys, (((1,), (1,)), ((), ())), preferred_element_type=jnp.float32
         ) * (1.0 / jnp.sqrt(jnp.float32(HEAD_DIM)))
         raised = jnp.where(allowed, jnp.exp(scores), 0.0)
         probs = (raised / jnp.sum(raised, axis=-1, keepdims=True)).astype(jnp.bfloat16)
-        mixed = jnp.dot(probs, v_ref[...], preferred_element_type=jnp.float32)
+        mixed = jnp.dot(probs, values, preferred_element_type=jnp.float32)
         result = jnp.where(inside, mixed, result)
     o_ref[...] = result.astype(o_ref.dtype)
 
 
-def attend(normed, weights, key_value, allowed):
-    rows, width = normed.shape
-    keys = key_value.shape[0]
+def attend(normed_all, weights, allowed):
+    rows, keys = allowed.shape
+    width = normed_all.shape[1]
     tile = 128
     steps = width // tile
     return pl.pallas_call(
@@ -76,20 +79,20 @@
         out_shape=jax.ShapeDtypeStruct((rows, width), jnp.bfloat16),
         grid=(steps,),
         in_specs=[
-            pl.BlockSpec((rows, width), lambda i: (0, 0)),
+            pl.BlockSpec((keys, width), lambda i: (0, 0)),
             pl.BlockSpec((width, tile), lambda i: (0, i)),
-            pl.BlockSpec((keys, tile), lambda i: (0, i)),
-            pl.BlockSpec((keys, tile), lambda i: (0, i + steps)),
+            pl.BlockSpec((width, tile), lambda i: (0, i + steps)),
+            pl.BlockSpec((width, tile), lambda i: (0, i + 2 * steps)),
             pl.BlockSpec((rows, keys), lambda i: (0, 0)),
         ],
         out_specs=pl.BlockSpec((rows, tile), lambda i: (0, i)),
         cost_estimate=pl.CostEstimate(
-            flops=4 * rows * keys * width * tile // HEAD_DIM + 2 * rows * width * width,
+            flops=4 * rows * keys * width * tile // HEAD_DIM
+            + 2 * (rows + 2 * keys) * width * width,
             transcendentals=rows * keys * width // HEAD_DIM,
-            bytes_accessed=2 * (2 * rows * width + 2 * keys * width + width * width)
-            + 4 * rows * keys,
+            bytes_accessed=2 * (keys * width + 3 * width * width + rows * width) + 4 * rows * keys,
         ),
-    )(normed, weights, key_value, key_value, allowed.astype(jnp.float32))
+    )(normed_all, weights, weights, weights, allowed.astype(jnp.float32))
 
 
 def on_device(
@@ -117,13 +120,12 @@
     key_count = context_frames.shape[0]
     normed_all = layer_norm(context_frames, ln_attn_gain).astype(jnp.bfloat16)
     normed = normed_all[key_count - frame_count :]
-    key_value = contract_with(normed_all, weights[:, model_width:qkv_cols]).astype(jnp.bfloat16)
     key_pos = first_row - prior_blocks * frame_count + jnp.arange(key_count, dtype=jnp.int32)
     span_first = query_pos // SPAN * SPAN
     allowed = (key_pos[None, :] >= 0) & (key_pos[None, :] >= span_first[:, None] - LEFT)
     allowed = allowed & (key_pos[None, :] < span_first[:, None] + SPAN)
     allowed = allowed & ((key_pos[None, :] < length) | (key_pos[None, :] == query_pos[:, None]))
-    context = attend(normed, weights, key_value, allowed)
+    context = attend(normed_all, weights, allowed)
     projected = contract_with(context, weights[:, qkv_cols : qkv_cols + out_cols])
     attended = jnp.where(frame_valid[:, None], stream.astype(jnp.float32) + projected, 0.0).astype(
         jnp.bfloat16

time: 205 us -> 206 us (level)
  Pallas kernels: 11.4 us -> 21.4 us
  matrix products: 14.1 us -> 5.26 us
    pallas_call x1, Pallas kernels: 11.4 us -> 21.4 us  [attend(): pl.pallas_call(attend_kernel, out_shape=jax.ShapeDtypeStruct((rows, width...]
    dot_general x3 -> x2, matrix products: 14.1 us -> 5.26 us  [contract_with(): return jnp.dot(left, rows_piece, preferred_element_type=jnp.float32)]
where the time goes in v14:
time: 206 us; the launch traced here: 204 us
  waiting for transfers between devices  79.6 us (39%)
  blocking collectives  48.4 us (23%)
  starting transfers between devices  23 us (11%)
  Pallas kernels  21.4 us (10%)
  between operations  15.1 us (7%)
  other arithmetic  10 us (5%)
  matrix products  5.26 us (3%)
    ppermute x8, waiting for transfers between devices, passed_along(): lax.ppermute(value, axis, [(source, source + steps) for source in range(f...  74.4 us
    psum x4, blocking collectives, on_device(): moments = lax.psum(moments, axis)  48.4 us
    pallas_call x1, Pallas kernels, attend(): pl.pallas_call(attend_kernel, out_shape=jax.ShapeDtypeStruct((rows, width...  21.4 us
    ppermute x8, starting transfers between devices, passed_along(): lax.ppermute(value, axis, [(source, source + steps) for source in range(f...  15.3 us
    ppermute x1, starting transfers between devices, with_halo(): lax.ppermute(head, axis, [((i + 1) % count, i) for i in range(ends)])  5.51 us
    dot_general x2, matrix products, contract_with(): return jnp.dot(left, rows_piece, preferred_element_type=jnp.float32)  5.26 us
    all_gather x1, waiting for transfers between devices, on_device(): lax.all_gather(jnp.concatenate([w_qkv, w_out, w_pw1], axis=1), TM, axis=0...  5.14 us
  transfers between devices with their start and end apart: 11, of which 9 were waited for; matrix products, arithmetic and copies ran while one was open for 4% of the time, Pallas kernels for 0%

profile of v14, /device:TPU:6, one launch (start us, length us, event | category | flops | bytes accessed | tf_op | source)
XLA Modules:
  0.0 204.3 jit_solution(15211383949033272291)
XLA Ops:
  8.9 1.9 collective-permute-start
  10.8 8.1 %collective-permute-done = bf16[128,1024]{1,0:T(8,128)(2,1)S(1)} collective-permute-done((bf16[128,1024]{1,0:T(8,128)(2,1)}, bf16[128,1024]{1,0:T(8,128)(2,1)S(1)}, u32[]{:S(2)}, u32[]{:S(2)}) %collective-permute-start) | collective-permute-done | bytes 262176 | tf_op jit(solution)/shard_map/ppermute | solution.py:19
  18.9 1.9 collective-permute-start.1
  20.8 7.9 %collective-permute-done.1 = bf16[128,1024]{1,0:T(8,128)(2,1)S(1)} collective-permute-done((bf16[128,1024]{1,0:T(8,128)(2,1)S(1)}, bf16[128,1024]{1,0:T(8,128)(2,1)S(1)}, u32[]{:S(2)}, u32[]{:S(2)}) %collective-permute-start.1) | collective-permute-done | bytes 262176 | tf_op jit(solution)/shard_map/ppermute | solution.py:19
  28.7 1.9 collective-permute-start.2
  30.6 9.5 %collective-permute-done.2 = bf16[128,1024]{1,0:T(8,128)(2,1)S(1)} collective-permute-done((bf16[128,1024]{1,0:T(8,128)(2,1)S(1)}, bf16[128,1024]{1,0:T(8,128)(2,1)S(1)}, u32[]{:S(2)}, u32[]{:S(2)}) %collective-permute-start.2) | collective-permute-done | bytes 262176 | tf_op jit(solution)/shard_map/ppermute | solution.py:19
  40.1 1.9 collective-permute-start.3
  42.0 9.7 %collective-permute-done.3 = bf16[128,1024]{1,0:T(8,128)(2,1)S(1)} collective-permute-done((bf16[128,1024]{1,0:T(8,128)(2,1)S(1)}, bf16[128,1024]{1,0:T(8,128)(2,1)S(1)}, u32[]{:S(2)}, u32[]{:S(2)}) %collective-permute-start.3) | collective-permute-done | bytes 262176 | tf_op jit(solution)/shard_map/ppermute | solution.py:19
  53.6 7.9 %collective-permute-done.4 = bf16[128,1024]{1,0:T(8,128)(2,1)S(1)} collective-permute-done((bf16[128,1024]{1,0:T(8,128)(2,1)S(1)}, bf16[128,1024]{1,0:T(8,128)(2,1)S(1)}, u32[]{:S(2)}, u32[]{:S(2)}) %collective-permute-start.4) | collective-permute-done | bytes 262176 | tf_op jit(solution)/shard_map/ppermute | solution.py:19
  61.5 1.9 collective-permute-start.5
  63.5 7.8 %collective-permute-done.5 = bf16[128,1024]{1,0:T(8,128)(2,1)S(1)} collective-permute-done((bf16[128,1024]{1,0:T(8,128)(2,1)S(1)}, bf16[128,1024]{1,0:T(8,128)(2,1)S(1)}, u32[]{:S(2)}, u32[]{:S(2)}) %collective-permute-start.5) | collective-permute-done | bytes 262176 | tf_op jit(solution)/shard_map/ppermute | solution.py:19
  75.2 11.7 %collective-permute-done.6 = bf16[128,1024]{1,0:T(8,128)(2,1)S(1)} collective-permute-done((bf16[128,1024]{1,0:T(8,128)(2,1)S(1)}, bf16[128,1024]{1,0:T(8,128)(2,1)S(1)}, u32[]{:S(2)}, u32[]{:S(2)}) %collective-permute-start.6) | collective-permute-done | bytes 262176 | tf_op jit(solution)/shard_map/ppermute | solution.py:19
  90.5 11.9 %collective-permute-done.7 = bf16[128,1024]{1,0:T(8,128)(2,1)S(1)} collective-permute-done((bf16[128,1024]{1,0:T(8,128)(2,1)S(1)}, bf16[128,1024]{1,0:T(8,128)(2,1)S(1)}, u32[]{:S(2)}, u32[]{:S(2)}) %collective-permute-start.7) | collective-permute-done | bytes 262176 | tf_op jit(solution)/shard_map/ppermute | solution.py:19
  103.8 2.2 %fusion.4.x_ref = bf16[1152,1024]{1,0:T(8,128)(2,1)} fusion(bf16[1152,1024]{1,0:T(8,128)(2,1)S(1)} %constant_dynamic-update-slice_fusion, f32[1024]{0:T(1024)S(1)} %copy-done.5, f32[1152]{0:T(1024)S(1)} %add_rsqrt_fusion, f32[1152]{0:T(1024)S(1)} %broadcast_multiply_fusion), kind=kLoop, calls=%fused_computation.6 | loop fusion | flops 5898240 | bytes 4731904 | tf_op jit(solution)/shard_map/convert_element_type | solution.py:121
  106.0 5.1 %all-gather.2.cloned.1.call-done.wq_ref.wk_ref.wv_ref = bf16[1024,6144]{1,0:T(8,128)(2,1)} async-done(((bf16[16,6144]{1,0:T(8,128)(2,1)}), bf16[1024,6144]{1,0:T(8,128)(2,1)}) %all-gather.2.cloned.1.call-update) | async-done | bytes 12582928 | tf_op jit(solution)/shard_map/all_gather | solution.py:110
  111.2 21.4 %shard_map.113 = bf16[128,1024]{1,0:T(8,128)(2,1)} custom-call(bf16[1152,1024]{1,0:T(8,128)(2,1)} %fusion.4.x_ref, bf16[1024,6144]{1,0:T(8,128)(2,1)} %all-gather.2.cloned.1.call-done.wq_ref.wk_ref.wv_ref, bf16[1024,6144]{1,0:T(8,128)(2,1)} %all-gather.2.cloned.1.call-done.wq_ref.wk_ref.wv_ref, ...), custom_call_target="tpu_custom_call" | custom-call | flops 6308233216 | bytes 9502720 | tf_op jit(solution)/shard_map/pallas_call | solution.py:77
  132.5 2.2 %convert_reduce_fusion.1 = (f32[128]{0:T(128)S(1)}, bf16[128,1024]{1,0:T(8,128)(2,1)S(1)}) fusion(bf16[128,1024]{1,0:T(8,128)(2,1)} %shard_map.113, bf16[1024,6144]{1,0:T(8,128)(2,1)} %all-gather.2.cloned.1.call-done.wq_ref.wk_ref.wv_ref, bf16[1,128,1024]{2,1,0:T(8,128)(2,1)S(1)} %copy-done, pred[128]{0:T(512)(128)(4,1)S(1)} %broadcast_compare_fusion), kind=kOutput, calls=%fused_computation.17 | convolution fusion | flops 269221760 | bytes 2884224 | tf_op jit(solution)/shard_map/dot_general | solution.py:45
  135.1 3.0 %fusion.5 = f32[128,2048]{1,0:T(8,128)S(1)} fusion(bf16[1024,6144]{1,0:T(8,128)(2,1)} %all-gather.2.cloned.1.call-done.wq_ref.wk_ref.wv_ref, bf16[128,1024]{1,0:T(8,128)(2,1)S(1)} %get-tuple-element.27, f32[1024]{0:T(1024)S(1)} %copy-done.6, f32[128]{0:T(128)S(1)} %add_rsqrt_fusion.2, f32[128]{0:T(128)S(1)} %broadcast_multiply_fusion.1), kind=kOutput, calls=%fused_computation.7 | convolution fusion | flops 537526272 | bytes 5510144 | tf_op jit(solution)/shard_map/dot_general | solution.py:45
  138.3 2.2 %collective-permute-start.8 = (bf16[4,1024]{1,0:T(4,128)(2,1)S(1)}, bf16[4,1024]{1,0:T(4,128)(2,1)S(1)}, u32[]{:S(2)}, u32[]{:S(2)}) collective-permute-start(bf16[4,1024]{1,0:T(4,128)(2,1)S(1)} %get-tuple-element.13), channel_id=1, source_target_pairs={{0,1},{1,2},{2,3},{3,4},{4,5},{5,6},{6,7},{7,8},{8,9},{9,10},{10,1... | collective-permute-start | bytes 24584 | tf_op jit(solution)/shard_map/ppermute | solution.py:29
  140.5 5.5 %collective-permute-start.9 = (bf16[4,1024]{1,0:T(4,128)(2,1)S(1)}, bf16[4,1024]{1,0:T(4,128)(2,1)S(1)}, u32[]{:S(2)}, u32[]{:S(2)}) collective-permute-start(bf16[4,1024]{1,0:T(4,128)(2,1)S(1)} %get-tuple-element.14), channel_id=1, source_target_pairs={{1,0},{2,1},{3,2},{4,3},{5,4},{6,5},{7,6},{8,7},{9,8},{10,9},{11,1... | collective-permute-start | bytes 24584 | tf_op jit(solution)/shard_map/ppermute | solution.py:31
  148.0 2.5 %all-reduce.3 = (f32[1024]{0:T(1024)S(1)}, f32[1024]{0:T(1024)S(1)}) all-reduce(f32[1024]{0:T(1024)S(1)} %get-tuple-element.3, f32[1024]{0:T(1024)S(1)} %get-tuple-element.2), channel_id=1, replica_groups=mesh['call'=8,'x'=4,'y'=8,'core'=2] {'core'}, use_global_device_ids=true, to_apply=%region_11.12 | all-reduce | flops 2048 | bytes 16384 | tf_op jit(solution)/shard_map/psum | solution.py:147
  150.5 15.7 %all-reduce = (f32[1024]{0:T(1024)S(1)}, f32[1024]{0:T(1024)S(1)}) all-reduce(f32[1024]{0:T(1024)S(1)} %get-tuple-element.10, f32[1024]{0:T(1024)S(1)} %get-tuple-element.11), channel_id=1, replica_groups=mesh['call'=8,'x'=4,'y'=8,'core'=2] {'y'}, use_global_device_ids=true, to_apply=%region_12.13 | all-reduce | flops 2048 | bytes 16384 | tf_op jit(solution)/shard_map/psum | solution.py:147
  166.2 11.1 %all-reduce.2 = (f32[1024]{0:T(1024)S(1)}, f32[1024]{0:T(1024)S(1)}) all-reduce(f32[1024]{0:T(1024)S(1)} %get-tuple-element.4, f32[1024]{0:T(1024)S(1)} %get-tuple-element.5), channel_id=1, replica_groups=mesh['call'=8,'x'=4,'y'=8,'core'=2] {'x'}, use_global_device_ids=true, to_apply=%region_13.14 | all-reduce | flops 2048 | bytes 16384 | tf_op jit(solution)/shard_map/psum | solution.py:147
  177.3 19.1 %all-reduce.1 = (f32[1024]{0:T(1024)S(1)}, f32[1024]{0:T(1024)S(1)}) all-reduce(f32[1024]{0:T(1024)S(1)} %get-tuple-element.8, f32[1024]{0:T(1024)S(1)} %get-tuple-element.9), channel_id=1, replica_groups=mesh['call'=8,'x'=4,'y'=8,'core'=2] {'call'}, use_global_device_ids=true, to_apply=%region_14.15 | all-reduce | flops 2048 | bytes 16384 | tf_op jit(solution)/shard_map/psum | solution.py:147
  (54 shorter events, 15.1 us)
Async XLA Ops:
  7.2 104.0 %all-gather.2.cloned.1.call-start = ((), (), s32[]{:S(2)}) async-start(), calls=%async_computation | async-start | bytes 12779520 | tf_op jit(solution)/shard_map/all_gather | solution.py:110
  8.9 10.0 %collective-permute-start = (bf16[128,1024]{1,0:T(8,128)(2,1)}, bf16[128,1024]{1,0:T(8,128)(2,1)S(1)}, u32[]{:S(2)}, u32[]{:S(2)}) collective-permute-start(bf16[128,1024]{1,0:T(8,128)(2,1)} %bitcast.17), channel_id=1, source_target_pairs={{0,1},{1,2},{2,3},{3,4},{4,5},{5,6},{6,7},{7,8},{8,9},{9,10},{10,1... | collective-permute-start | bytes 786440 | tf_op jit(solution)/shard_map/ppermute | solution.py:19
  18.9 9.8 %collective-permute-start.1 = (bf16[128,1024]{1,0:T(8,128)(2,1)S(1)}, bf16[128,1024]{1,0:T(8,128)(2,1)S(1)}, u32[]{:S(2)}, u32[]{:S(2)}) collective-permute-start(bf16[128,1024]{1,0:T(8,128)(2,1)S(1)} %collective-permute-done), channel_id=1, source_target_pairs={{0,1},{1,2},{2,3},{3,4},{4,5},{5,6},{6,7},{7,8},{8,9},{9,10},{10,1... | collective-permute-start | bytes 786440 | tf_op jit(solution)/shard_map/ppermute | solution.py:19
  28.7 11.4 %collective-permute-start.2 = (bf16[128,1024]{1,0:T(8,128)(2,1)S(1)}, bf16[128,1024]{1,0:T(8,128)(2,1)S(1)}, u32[]{:S(2)}, u32[]{:S(2)}) collective-permute-start(bf16[128,1024]{1,0:T(8,128)(2,1)S(1)} %collective-permute-done.1), channel_id=1, source_target_pairs={{0,1},{1,2},{2,3},{3,4},{4,5},{5,6},{6,7},{7,8},{8,9},{9,10},{10,1... | collective-permute-start | bytes 786440 | tf_op jit(solution)/shard_map/ppermute | solution.py:19
  40.1 11.6 %collective-permute-start.3 = (bf16[128,1024]{1,0:T(8,128)(2,1)S(1)}, bf16[128,1024]{1,0:T(8,128)(2,1)S(1)}, u32[]{:S(2)}, u32[]{:S(2)}) collective-permute-start(bf16[128,1024]{1,0:T(8,128)(2,1)S(1)} %collective-permute-done.2), channel_id=1, source_target_pairs={{0,1},{1,2},{2,3},{3,4},{4,5},{5,6},{6,7},{7,8},{8,9},{9,10},{10,1... | collective-permute-start | bytes 786440 | tf_op jit(solution)/shard_map/ppermute | solution.py:19
  51.7 9.8 %collective-permute-start.4 = (bf16[128,1024]{1,0:T(8,128)(2,1)S(1)}, bf16[128,1024]{1,0:T(8,128)(2,1)S(1)}, u32[]{:S(2)}, u32[]{:S(2)}) collective-permute-start(bf16[128,1024]{1,0:T(8,128)(2,1)S(1)} %collective-permute-done.3), channel_id=1, source_target_pairs={{0,1},{1,2},{2,3},{3,4},{4,5},{5,6},{6,7},{7,8},{8,9},{9,10},{10,1... | collective-permute-start | bytes 786440 | tf_op jit(solution)/shard_map/ppermute | solution.py:19
  61.5 9.8 %collective-permute-start.5 = (bf16[128,1024]{1,0:T(8,128)(2,1)S(1)}, bf16[128,1024]{1,0:T(8,128)(2,1)S(1)}, u32[]{:S(2)}, u32[]{:S(2)}) collective-permute-start(bf16[128,1024]{1,0:T(8,128)(2,1)S(1)} %collective-permute-done.4), channel_id=1, source_target_pairs={{0,1},{1,2},{2,3},{3,4},{4,5},{5,6},{6,7},{7,8},{8,9},{9,10},{10,1... | collective-permute-start | bytes 786440 | tf_op jit(solution)/shard_map/ppermute | solution.py:19
  71.3 15.5 %collective-permute-start.6 = (bf16[128,1024]{1,0:T(8,128)(2,1)S(1)}, bf16[128,1024]{1,0:T(8,128)(2,1)S(1)}, u32[]{:S(2)}, u32[]{:S(2)}) collective-permute-start(bf16[128,1024]{1,0:T(8,128)(2,1)S(1)} %collective-permute-done.5), channel_id=1, source_target_pairs={{0,1},{1,2},{2,3},{3,4},{4,5},{5,6},{6,7},{7,8},{8,9},{9,10},{10,1... | collective-permute-start | bytes 786440 | tf_op jit(solution)/shard_map/ppermute | solution.py:19
  86.9 15.5 %collective-permute-start.7 = (bf16[128,1024]{1,0:T(8,128)(2,1)S(1)}, bf16[128,1024]{1,0:T(8,128)(2,1)S(1)}, u32[]{:S(2)}, u32[]{:S(2)}) collective-permute-start(bf16[128,1024]{1,0:T(8,128)(2,1)S(1)} %collective-permute-done.6), channel_id=1, source_target_pairs={{0,1},{1,2},{2,3},{3,4},{4,5},{5,6},{6,7},{7,8},{8,9},{9,10},{10,1... | collective-permute-start | bytes 786440 | tf_op jit(solution)/shard_map/ppermute | solution.py:19
  88.8 13.8 %copy-start = (bf16[1,128,1024]{2,1,0:T(8,128)(2,1)S(1)}, bf16[1,128,1024]{2,1,0:T(8,128)(2,1)}, u32[]{:S(2)}) copy-start(bf16[1,128,1024]{2,1,0:T(8,128)(2,1)} %param.10) | copy-start | bytes 786436
  102.6 1.2 copy-start.5
  132.5 2.5 %copy-start.6 = (f32[1024]{0:T(1024)S(1)}, f32[1024]{0:T(1024)}, u32[]{:S(2)}) copy-start(f32[1024]{0:T(1024)} %param.15) | copy-start | bytes 12292
  134.8 3.3 %copy-start.1 = (bf16[128,1024]{1,0:T(8,128)(2,1)}, bf16[128,1024]{1,0:T(8,128)(2,1)S(1)}, u32[]{:S(2)}) copy-start(bf16[128,1024]{1,0:T(8,128)(2,1)S(1)} %get-tuple-element.27) | copy-start | bytes 786436
  135.0 11.0 %copy-start.2 = (f32[9,1024]{1,0:T(8,128)S(1)}, f32[9,1024]{1,0:T(8,128)}, u32[]{:S(2)}) copy-start(f32[9,1024]{1,0:T(8,128)} %param.17) | copy-start | bytes 110596
  135.0 11.0 %copy-start.7 = (s32[8]{0:T(128)S(1)}, s32[8]{0:T(128)}, u32[]{:S(2)}) copy-start(s32[8]{0:T(128)} %param.11) | copy-start | bytes 100
  138.1 58.4 %copy-start.3 = (f32[1024]{0:T(1024)S(1)}, f32[1024]{0:T(1024)}, u32[]{:S(2)}) copy-start(f32[1024]{0:T(1024)} %param.19) | copy-start | bytes 12292
  138.1 58.4 %copy-start.4 = (f32[1024]{0:T(1024)S(1)}, f32[1024]{0:T(1024)}, u32[]{:S(2)}) copy-start(f32[1024]{0:T(1024)} %param.18) | copy-start | bytes 12292
  138.3 9.0 %collective-permute-start.8 = (bf16[4,1024]{1,0:T(4,128)(2,1)S(1)}, bf16[4,1024]{1,0:T(4,128)(2,1)S(1)}, u32[]{:S(2)}, u32[]{:S(2)}) collective-permute-start(bf16[4,1024]{1,0:T(4,128)(2,1)S(1)} %get-tuple-element.13), channel_id=1, source_target_pairs={{0,1},{1,2},{2,3},{3,4},{4,5},{5,6},{6,7},{7,8},{8,9},{9,10},{10,1... | collective-permute-start | bytes 24584 | tf_op jit(solution)/shard_map/ppermute | solution.py:29
  140.5 6.9 %collective-permute-start.9 = (bf16[4,1024]{1,0:T(4,128)(2,1)S(1)}, bf16[4,1024]{1,0:T(4,128)(2,1)S(1)}, u32[]{:S(2)}, u32[]{:S(2)}) collective-permute-start(bf16[4,1024]{1,0:T(4,128)(2,1)S(1)} %get-tuple-element.14), channel_id=1, source_target_pairs={{1,0},{2,1},{3,2},{4,3},{5,4},{6,5},{7,6},{8,7},{9,8},{10,9},{11,1... | collective-permute-start | bytes 24584 | tf_op jit(solution)/shard_map/ppermute | solution.py:31
Sparse Core Ops, SparseCore 0:
  11.9 99.2 all-gather.1

commit v15 on v13

--- a/solution.py
+++ b/solution.py
@@ -69,7 +69,7 @@
 def attend(normed, weights, key_value, allowed):
     rows, width = normed.shape
     keys = key_value.shape[0]
-    tile = 128
+    tile = 4 * HEAD_DIM
     steps = width // tile
     return pl.pallas_call(
         attend_kernel,

time: 205 us -> 205 us (level)
  no operation moved by 1% of the time
where the time goes in v15:
time: 205 us; the launch traced here: 203 us
  waiting for transfers between devices  80.3 us (39%)
  blocking collectives  48.5 us (24%)
  starting transfers between devices  23 us (11%)
  between operations  15.1 us (7%)
  matrix products  14.1 us (7%)
  Pallas kernels  11.7 us (6%)
  other arithmetic  8.61 us (4%)
  local copies, waits for them, and re-layouts  2.22 us (1%)
    ppermute x8, waiting for transfers between devices, passed_along(): lax.ppermute(value, axis, [(source, source + steps) for source in range(f...  74.4 us
    psum x4, blocking collectives, on_device(): moments = lax.psum(moments, axis)  48.5 us
    ppermute x8, starting transfers between devices, passed_along(): lax.ppermute(value, axis, [(source, source + steps) for source in range(f...  15.3 us
    dot_general x3, matrix products, contract_with(): return jnp.dot(left, rows_piece, preferred_element_type=jnp.float32)  14.1 us
    pallas_call x1, Pallas kernels, attend(): pl.pallas_call(attend_kernel, out_shape=jax.ShapeDtypeStruct((rows, width...  11.7 us
    all_gather x1, waiting for transfers between devices, on_device(): lax.all_gather(jnp.concatenate([w_qkv, w_out, w_pw1], axis=1), TM, axis=0...  5.85 us
    ppermute x1, starting transfers between devices, with_halo(): lax.ppermute(head, axis, [((i + 1) % count, i) for i in range(ends)])  5.51 us
  transfers between devices with their start and end apart: 11, of which 9 were waited for; matrix products, arithmetic and copies ran while one was open for 4% of the time, Pallas kernels for 0%

profile of v15, /device:TPU:6, one launch (start us, length us, event | category | flops | bytes accessed | tf_op | source)
XLA Modules:
  0.0 203.5 jit_solution(17197768076992037592)
XLA Ops:
  8.9 1.9 collective-permute-start
  10.8 8.1 %collective-permute-done = bf16[128,1024]{1,0:T(8,128)(2,1)S(1)} collective-permute-done((bf16[128,1024]{1,0:T(8,128)(2,1)}, bf16[128,1024]{1,0:T(8,128)(2,1)S(1)}, u32[]{:S(2)}, u32[]{:S(2)}) %collective-permute-start) | collective-permute-done | bytes 262176 | tf_op jit(solution)/shard_map/ppermute | solution.py:19
  18.9 1.9 collective-permute-start.1
  20.8 7.9 %collective-permute-done.1 = bf16[128,1024]{1,0:T(8,128)(2,1)S(1)} collective-permute-done((bf16[128,1024]{1,0:T(8,128)(2,1)S(1)}, bf16[128,1024]{1,0:T(8,128)(2,1)S(1)}, u32[]{:S(2)}, u32[]{:S(2)}) %collective-permute-start.1) | collective-permute-done | bytes 262176 | tf_op jit(solution)/shard_map/ppermute | solution.py:19
  28.7 1.9 collective-permute-start.2
  30.6 9.5 %collective-permute-done.2 = bf16[128,1024]{1,0:T(8,128)(2,1)S(1)} collective-permute-done((bf16[128,1024]{1,0:T(8,128)(2,1)S(1)}, bf16[128,1024]{1,0:T(8,128)(2,1)S(1)}, u32[]{:S(2)}, u32[]{:S(2)}) %collective-permute-start.2) | collective-permute-done | bytes 262176 | tf_op jit(solution)/shard_map/ppermute | solution.py:19
  40.1 1.9 collective-permute-start.3
  42.0 9.7 %collective-permute-done.3 = bf16[128,1024]{1,0:T(8,128)(2,1)S(1)} collective-permute-done((bf16[128,1024]{1,0:T(8,128)(2,1)S(1)}, bf16[128,1024]{1,0:T(8,128)(2,1)S(1)}, u32[]{:S(2)}, u32[]{:S(2)}) %collective-permute-start.3) | collective-permute-done | bytes 262176 | tf_op jit(solution)/shard_map/ppermute | solution.py:19
  53.6 7.9 %collective-permute-done.4 = bf16[128,1024]{1,0:T(8,128)(2,1)S(1)} collective-permute-done((bf16[128,1024]{1,0:T(8,128)(2,1)S(1)}, bf16[128,1024]{1,0:T(8,128)(2,1)S(1)}, u32[]{:S(2)}, u32[]{:S(2)}) %collective-permute-start.4) | collective-permute-done | bytes 262176 | tf_op jit(solution)/shard_map/ppermute | solution.py:19
  61.5 1.9 collective-permute-start.5
  63.5 7.8 %collective-permute-done.5 = bf16[128,1024]{1,0:T(8,128)(2,1)S(1)} collective-permute-done((bf16[128,1024]{1,0:T(8,128)(2,1)S(1)}, bf16[128,1024]{1,0:T(8,128)(2,1)S(1)}, u32[]{:S(2)}, u32[]{:S(2)}) %collective-permute-start.5) | collective-permute-done | bytes 262176 | tf_op jit(solution)/shard_map/ppermute | solution.py:19
  75.2 11.7 %collective-permute-done.6 = bf16[128,1024]{1,0:T(8,128)(2,1)S(1)} collective-permute-done((bf16[128,1024]{1,0:T(8,128)(2,1)S(1)}, bf16[128,1024]{1,0:T(8,128)(2,1)S(1)}, u32[]{:S(2)}, u32[]{:S(2)}) %collective-permute-start.6) | collective-permute-done | bytes 262176 | tf_op jit(solution)/shard_map/ppermute | solution.py:19
  90.5 11.9 %collective-permute-done.7 = bf16[128,1024]{1,0:T(8,128)(2,1)S(1)} collective-permute-done((bf16[128,1024]{1,0:T(8,128)(2,1)S(1)}, bf16[128,1024]{1,0:T(8,128)(2,1)S(1)}, u32[]{:S(2)}, u32[]{:S(2)}) %collective-permute-start.7) | collective-permute-done | bytes 262176 | tf_op jit(solution)/shard_map/ppermute | solution.py:19
  105.3 5.8 %all-gather.2.cloned.1.call-done.wq_ref = bf16[1024,6144]{1,0:T(8,128)(2,1)} async-done(((bf16[16,6144]{1,0:T(8,128)(2,1)}), bf16[1024,6144]{1,0:T(8,128)(2,1)}) %all-gather.2.cloned.1.call-update) | async-done | bytes 12582928 | tf_op jit(solution)/shard_map/all_gather | solution.py:107
  111.2 8.8 %convolution_convert_fusion.k_ref.v_ref = bf16[1152,2048]{1,0:T(8,128)(2,1)} fusion(bf16[1152,1024]{1,0:T(8,128)(2,1)S(1)} %fusion.4, bf16[1024,6144]{1,0:T(8,128)(2,1)} %all-gather.2.cloned.1.call-done.wq_ref), kind=kOutput, calls=%fused_computation | convolution fusion | flops 4834197504 | bytes 11272192 | tf_op jit(solution)/shard_map/dot_general | solution.py:45
  120.0 11.7 %shard_map.113 = bf16[128,1024]{1,0:T(8,128)(2,1)} custom-call(bf16[128,1024]{1,0:T(8,128)(2,1)} %slice.108.x_ref, bf16[1024,6144]{1,0:T(8,128)(2,1)} %all-gather.2.cloned.1.call-done.wq_ref, bf16[1152,2048]{1,0:T(8,128)(2,1)} %convolution_convert_fusion.k_ref.v_ref, bf16[1152,2048]{1,0:T(8,128)(2,1)} %convolution_convert_fusion.k_ref.v_ref, ...), custom_call_target="tpu_custom_call" | custom-call | flops 2684354560 | bytes 7929856 | tf_op jit(solution)/shard_map/pallas_call | solution.py:74
  131.7 2.2 %convert_reduce_fusion.1 = (f32[128]{0:T(128)S(1)}, bf16[128,1024]{1,0:T(8,128)(2,1)S(1)}) fusion(bf16[128,1024]{1,0:T(8,128)(2,1)} %shard_map.113, bf16[1024,6144]{1,0:T(8,128)(2,1)} %all-gather.2.cloned.1.call-done.wq_ref, bf16[1,128,1024]{2,1,0:T(8,128)(2,1)S(1)} %copy-done, pred[128]{0:T(512)(128)(4,1)S(1)} %broadcast_compare_fusion), kind=kOutput, calls=%fused_computation.19 | convolution fusion | flops 269221760 | bytes 2884224 | tf_op jit(solution)/shard_map/dot_general | solution.py:45
  134.2 3.0 %fusion.5 = f32[128,2048]{1,0:T(8,128)S(1)} fusion(bf16[1024,6144]{1,0:T(8,128)(2,1)} %all-gather.2.cloned.1.call-done.wq_ref, bf16[128,1024]{1,0:T(8,128)(2,1)S(1)} %get-tuple-element.27, f32[1024]{0:T(1024)S(1)} %copy-done.6, f32[128]{0:T(128)S(1)} %add_rsqrt_fusion.2, f32[128]{0:T(128)S(1)} %broadcast_multiply_fusion.1), kind=kOutput, calls=%fused_computation.8 | convolution fusion | flops 537526272 | bytes 5510144 | tf_op jit(solution)/shard_map/dot_general | solution.py:45
  137.4 2.2 %collective-permute-start.8 = (bf16[4,1024]{1,0:T(4,128)(2,1)S(1)}, bf16[4,1024]{1,0:T(4,128)(2,1)S(1)}, u32[]{:S(2)}, u32[]{:S(2)}) collective-permute-start(bf16[4,1024]{1,0:T(4,128)(2,1)S(1)} %get-tuple-element.13), channel_id=1, source_target_pairs={{0,1},{1,2},{2,3},{3,4},{4,5},{5,6},{6,7},{7,8},{8,9},{9,10},{10,1... | collective-permute-start | bytes 24584 | tf_op jit(solution)/shard_map/ppermute | solution.py:29
  139.6 5.5 %collective-permute-start.9 = (bf16[4,1024]{1,0:T(4,128)(2,1)S(1)}, bf16[4,1024]{1,0:T(4,128)(2,1)S(1)}, u32[]{:S(2)}, u32[]{:S(2)}) collective-permute-start(bf16[4,1024]{1,0:T(4,128)(2,1)S(1)} %get-tuple-element.14), channel_id=1, source_target_pairs={{1,0},{2,1},{3,2},{4,3},{5,4},{6,5},{7,6},{8,7},{9,8},{10,9},{11,1... | collective-permute-start | bytes 24584 | tf_op jit(solution)/shard_map/ppermute | solution.py:31
  147.2 2.5 %all-reduce.3 = (f32[1024]{0:T(1024)S(1)}, f32[1024]{0:T(1024)S(1)}) all-reduce(f32[1024]{0:T(1024)S(1)} %get-tuple-element.3, f32[1024]{0:T(1024)S(1)} %get-tuple-element.2), channel_id=1, replica_groups=mesh['call'=8,'x'=4,'y'=8,'core'=2] {'core'}, use_global_device_ids=true, to_apply=%region_11.12 | all-reduce | flops 2048 | bytes 16384 | tf_op jit(solution)/shard_map/psum | solution.py:145
  149.7 15.7 %all-reduce = (f32[1024]{0:T(1024)S(1)}, f32[1024]{0:T(1024)S(1)}) all-reduce(f32[1024]{0:T(1024)S(1)} %get-tuple-element.10, f32[1024]{0:T(1024)S(1)} %get-tuple-element.11), channel_id=1, replica_groups=mesh['call'=8,'x'=4,'y'=8,'core'=2] {'y'}, use_global_device_ids=true, to_apply=%region_12.13 | all-reduce | flops 2048 | bytes 16384 | tf_op jit(solution)/shard_map/psum | solution.py:145
  165.3 11.1 %all-reduce.2 = (f32[1024]{0:T(1024)S(1)}, f32[1024]{0:T(1024)S(1)}) all-reduce(f32[1024]{0:T(1024)S(1)} %get-tuple-element.4, f32[1024]{0:T(1024)S(1)} %get-tuple-element.5), channel_id=1, replica_groups=mesh['call'=8,'x'=4,'y'=8,'core'=2] {'x'}, use_global_device_ids=true, to_apply=%region_13.14 | all-reduce | flops 2048 | bytes 16384 | tf_op jit(solution)/shard_map/psum | solution.py:145
  176.5 19.2 %all-reduce.1 = (f32[1024]{0:T(1024)S(1)}, f32[1024]{0:T(1024)S(1)}) all-reduce(f32[1024]{0:T(1024)S(1)} %get-tuple-element.8, f32[1024]{0:T(1024)S(1)} %get-tuple-element.9), channel_id=1, replica_groups=mesh['call'=8,'x'=4,'y'=8,'core'=2] {'call'}, use_global_device_ids=true, to_apply=%region_14.15 | all-reduce | flops 2048 | bytes 16384 | tf_op jit(solution)/shard_map/psum | solution.py:145
  (56 shorter events, 16.6 us)
Async XLA Ops:
  7.2 104.0 %all-gather.2.cloned.1.call-start = ((), (), s32[]{:S(2)}) async-start(), calls=%async_computation | async-start | bytes 12779520 | tf_op jit(solution)/shard_map/all_gather | solution.py:107
  8.9 10.0 %collective-permute-start = (bf16[128,1024]{1,0:T(8,128)(2,1)}, bf16[128,1024]{1,0:T(8,128)(2,1)S(1)}, u32[]{:S(2)}, u32[]{:S(2)}) collective-permute-start(bf16[128,1024]{1,0:T(8,128)(2,1)} %bitcast.18), channel_id=1, source_target_pairs={{0,1},{1,2},{2,3},{3,4},{4,5},{5,6},{6,7},{7,8},{8,9},{9,10},{10,1... | collective-permute-start | bytes 786440 | tf_op jit(solution)/shard_map/ppermute | solution.py:19
  18.9 9.8 %collective-permute-start.1 = (bf16[128,1024]{1,0:T(8,128)(2,1)S(1)}, bf16[128,1024]{1,0:T(8,128)(2,1)S(1)}, u32[]{:S(2)}, u32[]{:S(2)}) collective-permute-start(bf16[128,1024]{1,0:T(8,128)(2,1)S(1)} %collective-permute-done), channel_id=1, source_target_pairs={{0,1},{1,2},{2,3},{3,4},{4,5},{5,6},{6,7},{7,8},{8,9},{9,10},{10,1... | collective-permute-start | bytes 786440 | tf_op jit(solution)/shard_map/ppermute | solution.py:19
  28.7 11.4 %collective-permute-start.2 = (bf16[128,1024]{1,0:T(8,128)(2,1)S(1)}, bf16[128,1024]{1,0:T(8,128)(2,1)S(1)}, u32[]{:S(2)}, u32[]{:S(2)}) collective-permute-start(bf16[128,1024]{1,0:T(8,128)(2,1)S(1)} %collective-permute-done.1), channel_id=1, source_target_pairs={{0,1},{1,2},{2,3},{3,4},{4,5},{5,6},{6,7},{7,8},{8,9},{9,10},{10,1... | collective-permute-start | bytes 786440 | tf_op jit(solution)/shard_map/ppermute | solution.py:19
  40.1 11.6 %collective-permute-start.3 = (bf16[128,1024]{1,0:T(8,128)(2,1)S(1)}, bf16[128,1024]{1,0:T(8,128)(2,1)S(1)}, u32[]{:S(2)}, u32[]{:S(2)}) collective-permute-start(bf16[128,1024]{1,0:T(8,128)(2,1)S(1)} %collective-permute-done.2), channel_id=1, source_target_pairs={{0,1},{1,2},{2,3},{3,4},{4,5},{5,6},{6,7},{7,8},{8,9},{9,10},{10,1... | collective-permute-start | bytes 786440 | tf_op jit(solution)/shard_map/ppermute | solution.py:19
  51.7 9.8 %collective-permute-start.4 = (bf16[128,1024]{1,0:T(8,128)(2,1)S(1)}, bf16[128,1024]{1,0:T(8,128)(2,1)S(1)}, u32[]{:S(2)}, u32[]{:S(2)}) collective-permute-start(bf16[128,1024]{1,0:T(8,128)(2,1)S(1)} %collective-permute-done.3), channel_id=1, source_target_pairs={{0,1},{1,2},{2,3},{3,4},{4,5},{5,6},{6,7},{7,8},{8,9},{9,10},{10,1... | collective-permute-start | bytes 786440 | tf_op jit(solution)/shard_map/ppermute | solution.py:19
  61.5 9.8 %collective-permute-start.5 = (bf16[128,1024]{1,0:T(8,128)(2,1)S(1)}, bf16[128,1024]{1,0:T(8,128)(2,1)S(1)}, u32[]{:S(2)}, u32[]{:S(2)}) collective-permute-start(bf16[128,1024]{1,0:T(8,128)(2,1)S(1)} %collective-permute-done.4), channel_id=1, source_target_pairs={{0,1},{1,2},{2,3},{3,4},{4,5},{5,6},{6,7},{7,8},{8,9},{9,10},{10,1... | collective-permute-start | bytes 786440 | tf_op jit(solution)/shard_map/ppermute | solution.py:19
  71.3 15.5 %collective-permute-start.6 = (bf16[128,1024]{1,0:T(8,128)(2,1)S(1)}, bf16[128,1024]{1,0:T(8,128)(2,1)S(1)}, u32[]{:S(2)}, u32[]{:S(2)}) collective-permute-start(bf16[128,1024]{1,0:T(8,128)(2,1)S(1)} %collective-permute-done.5), channel_id=1, source_target_pairs={{0,1},{1,2},{2,3},{3,4},{4,5},{5,6},{6,7},{7,8},{8,9},{9,10},{10,1... | collective-permute-start | bytes 786440 | tf_op jit(solution)/shard_map/ppermute | solution.py:19
  86.9 15.5 %collective-permute-start.7 = (bf16[128,1024]{1,0:T(8,128)(2,1)S(1)}, bf16[128,1024]{1,0:T(8,128)(2,1)S(1)}, u32[]{:S(2)}, u32[]{:S(2)}) collective-permute-start(bf16[128,1024]{1,0:T(8,128)(2,1)S(1)} %collective-permute-done.6), channel_id=1, source_target_pairs={{0,1},{1,2},{2,3},{3,4},{4,5},{5,6},{6,7},{7,8},{8,9},{9,10},{10,1... | collective-permute-start | bytes 786440 | tf_op jit(solution)/shard_map/ppermute | solution.py:19
  88.8 13.8 %copy-start = (bf16[1,128,1024]{2,1,0:T(8,128)(2,1)S(1)}, bf16[1,128,1024]{2,1,0:T(8,128)(2,1)}, u32[]{:S(2)}) copy-start(bf16[1,128,1024]{2,1,0:T(8,128)(2,1)} %param.10) | copy-start | bytes 786436
  102.6 1.2 copy-start.5
  131.7 2.5 %copy-start.6 = (f32[1024]{0:T(1024)S(1)}, f32[1024]{0:T(1024)}, u32[]{:S(2)}) copy-start(f32[1024]{0:T(1024)} %param.15) | copy-start | bytes 12292
  133.9 3.3 %copy-start.1 = (bf16[128,1024]{1,0:T(8,128)(2,1)}, bf16[128,1024]{1,0:T(8,128)(2,1)S(1)}, u32[]{:S(2)}) copy-start(bf16[128,1024]{1,0:T(8,128)(2,1)S(1)} %get-tuple-element.27) | copy-start | bytes 786436
  134.2 11.0 %copy-start.2 = (f32[9,1024]{1,0:T(8,128)S(1)}, f32[9,1024]{1,0:T(8,128)}, u32[]{:S(2)}) copy-start(f32[9,1024]{1,0:T(8,128)} %param.17) | copy-start | bytes 110596
  134.2 11.0 %copy-start.7 = (s32[8]{0:T(128)S(1)}, s32[8]{0:T(128)}, u32[]{:S(2)}) copy-start(s32[8]{0:T(128)} %param.11) | copy-start | bytes 100
  137.2 58.5 %copy-start.3 = (f32[1024]{0:T(1024)S(1)}, f32[1024]{0:T(1024)}, u32[]{:S(2)}) copy-start(f32[1024]{0:T(1024)} %param.19) | copy-start | bytes 12292
  137.2 58.5 %copy-start.4 = (f32[1024]{0:T(1024)S(1)}, f32[1024]{0:T(1024)}, u32[]{:S(2)}) copy-start(f32[1024]{0:T(1024)} %param.18) | copy-start | bytes 12292
  137.4 9.0 %collective-permute-start.8 = (bf16[4,1024]{1,0:T(4,128)(2,1)S(1)}, bf16[4,1024]{1,0:T(4,128)(2,1)S(1)}, u32[]{:S(2)}, u32[]{:S(2)}) collective-permute-start(bf16[4,1024]{1,0:T(4,128)(2,1)S(1)} %get-tuple-element.13), channel_id=1, source_target_pairs={{0,1},{1,2},{2,3},{3,4},{4,5},{5,6},{6,7},{7,8},{8,9},{9,10},{10,1... | collective-permute-start | bytes 24584 | tf_op jit(solution)/shard_map/ppermute | solution.py:29
  139.6 6.9 %collective-permute-start.9 = (bf16[4,1024]{1,0:T(4,128)(2,1)S(1)}, bf16[4,1024]{1,0:T(4,128)(2,1)S(1)}, u32[]{:S(2)}, u32[]{:S(2)}) collective-permute-start(bf16[4,1024]{1,0:T(4,128)(2,1)S(1)} %get-tuple-element.14), channel_id=1, source_target_pairs={{1,0},{2,1},{3,2},{4,3},{5,4},{6,5},{7,6},{8,7},{9,8},{10,9},{11,1... | collective-permute-start | bytes 24584 | tf_op jit(solution)/shard_map/ppermute | solution.py:31
Sparse Core Ops, SparseCore 0:
  11.9 99.2 all-gather.1

commit v16 on v13

--- a/solution.py
+++ b/solution.py
@@ -100,6 +100,7 @@
     head_count = model_width // HEAD_DIM
     length = lax.dynamic_index_in_dim(lengths, lax.axis_index("call"), 0, keepdims=False)
     first_row = lax.axis_index(TM) * frame_count
+    core = lax.axis_index("core")
     query_pos = first_row + jnp.arange(frame_count, dtype=jnp.int32)
     frame_valid = query_pos < length
     qkv_cols = w_qkv.shape[1]
@@ -132,7 +133,16 @@
     expanded = contract_with(conv_in, weights[:, qkv_cols + out_cols :])
     gated = expanded[:, :model_width] * jax.nn.sigmoid(expanded[:, model_width:])
     gated = jnp.where(frame_valid[:, None], gated, 0.0).astype(jnp.bfloat16)
-    padded = with_halo(gated, TM, KERNEL // 2)
+    width = KERNEL // 2
+    head, tail = gated[:width], gated[frame_count - width :]
+    count = lax.axis_size(TM)
+    from_partner = lax.ppermute(jnp.where(core == 0, tail, head), "core", [(0, 1), (1, 0)])
+    chip_pairs = [(i, i + 1) if i % 2 else (i, i - 1) for i in range(count)]
+    chip_pairs = [(a, b) for a, b in chip_pairs if 0 <= b < count]
+    from_chip = lax.ppermute(jnp.where(core == 1, tail, head), TM, chip_pairs)
+    before = jnp.where(core == 1, from_partner, from_chip)
+    after = jnp.where(core == 0, from_partner, from_chip)
+    padded = jnp.concatenate([before, gated, after], axis=0)
     depthwise = jnp.zeros((frame_count, model_width), jnp.float32)
     for tap_index in range(KERNEL):
         depthwise = (

time: 205 us -> 205 us (level)
  transfers between devices with their start and end apart: 11 -> 11, of which waited for: 9 -> 10; matrix products, arithmetic and copies ran while one was open for 4% -> 4% of each run, Pallas kernels for 0% -> 0%
where the time goes in v16:
time: 205 us; the launch traced here: 203 us
  waiting for transfers between devices  80.6 us (39%)
  blocking collectives  48.5 us (24%)
  starting transfers between devices  22.9 us (11%)
  between operations  15.1 us (7%)
  matrix products  14.1 us (7%)
  Pallas kernels  11.4 us (6%)
  other arithmetic  8.65 us (4%)
  local copies, waits for them, and re-layouts  2.21 us (1%)
    ppermute x8, waiting for transfers between devices, passed_along(): lax.ppermute(value, axis, [(source, source + steps) for source in range(f...  74.4 us
    psum x4, blocking collectives, on_device(): moments = lax.psum(moments, axis)  48.5 us
    ppermute x8, starting transfers between devices, passed_along(): lax.ppermute(value, axis, [(source, source + steps) for source in range(f...  15.3 us
    dot_general x3, matrix products, contract_with(): return jnp.dot(left, rows_piece, preferred_element_type=jnp.float32)  14.1 us
    pallas_call x1, Pallas kernels, attend(): pl.pallas_call(attend_kernel, out_shape=jax.ShapeDtypeStruct((rows, width...  11.4 us
    all_gather x1, waiting for transfers between devices, on_device(): lax.all_gather(jnp.concatenate([w_qkv, w_out, w_pw1], axis=1), TM, axis=0...  5.85 us
    ppermute x1, starting transfers between devices, on_device(): from_chip = lax.ppermute(jnp.where(core == 1, tail, head), TM, chip_pairs)  5.41 us
  transfers between devices with their start and end apart: 11, of which 10 were waited for; matrix products, arithmetic and copies ran while one was open for 4% of the time, Pallas kernels for 0%

profile of v16, /device:TPU:6, one launch (start us, length us, event | category | flops | bytes accessed | tf_op | source)
XLA Modules:
  0.0 203.5 jit_solution(9209875101381876855)
XLA Ops:
  8.9 1.9 collective-permute-start
  10.8 8.1 %collective-permute-done = bf16[128,1024]{1,0:T(8,128)(2,1)S(1)} collective-permute-done((bf16[128,1024]{1,0:T(8,128)(2,1)}, bf16[128,1024]{1,0:T(8,128)(2,1)S(1)}, u32[]{:S(2)}, u32[]{:S(2)}) %collective-permute-start) | collective-permute-done | bytes 262176 | tf_op jit(solution)/shard_map/ppermute | solution.py:19
  18.9 1.9 collective-permute-start.1
  20.8 7.9 %collective-permute-done.1 = bf16[128,1024]{1,0:T(8,128)(2,1)S(1)} collective-permute-done((bf16[128,1024]{1,0:T(8,128)(2,1)S(1)}, bf16[128,1024]{1,0:T(8,128)(2,1)S(1)}, u32[]{:S(2)}, u32[]{:S(2)}) %collective-permute-start.1) | collective-permute-done | bytes 262176 | tf_op jit(solution)/shard_map/ppermute | solution.py:19
  28.7 1.9 collective-permute-start.2
  30.6 9.5 %collective-permute-done.2 = bf16[128,1024]{1,0:T(8,128)(2,1)S(1)} collective-permute-done((bf16[128,1024]{1,0:T(8,128)(2,1)S(1)}, bf16[128,1024]{1,0:T(8,128)(2,1)S(1)}, u32[]{:S(2)}, u32[]{:S(2)}) %collective-permute-start.2) | collective-permute-done | bytes 262176 | tf_op jit(solution)/shard_map/ppermute | solution.py:19
  42.0 9.7 %collective-permute-done.3 = bf16[128,1024]{1,0:T(8,128)(2,1)S(1)} collective-permute-done((bf16[128,1024]{1,0:T(8,128)(2,1)S(1)}, bf16[128,1024]{1,0:T(8,128)(2,1)S(1)}, u32[]{:S(2)}, u32[]{:S(2)}) %collective-permute-start.3) | collective-permute-done | bytes 262176 | tf_op jit(solution)/shard_map/ppermute | solution.py:19
  51.7 1.9 collective-permute-start.4
  53.6 8.0 %collective-permute-done.4 = bf16[128,1024]{1,0:T(8,128)(2,1)S(1)} collective-permute-done((bf16[128,1024]{1,0:T(8,128)(2,1)S(1)}, bf16[128,1024]{1,0:T(8,128)(2,1)S(1)}, u32[]{:S(2)}, u32[]{:S(2)}) %collective-permute-start.4) | collective-permute-done | bytes 262176 | tf_op jit(solution)/shard_map/ppermute | solution.py:19
  61.6 1.9 collective-permute-start.5
  63.5 7.8 %collective-permute-done.5 = bf16[128,1024]{1,0:T(8,128)(2,1)S(1)} collective-permute-done((bf16[128,1024]{1,0:T(8,128)(2,1)S(1)}, bf16[128,1024]{1,0:T(8,128)(2,1)S(1)}, u32[]{:S(2)}, u32[]{:S(2)}) %collective-permute-start.5) | collective-permute-done | bytes 262176 | tf_op jit(solution)/shard_map/ppermute | solution.py:19
  75.2 11.7 %collective-permute-done.6 = bf16[128,1024]{1,0:T(8,128)(2,1)S(1)} collective-permute-done((bf16[128,1024]{1,0:T(8,128)(2,1)S(1)}, bf16[128,1024]{1,0:T(8,128)(2,1)S(1)}, u32[]{:S(2)}, u32[]{:S(2)}) %collective-permute-start.6) | collective-permute-done | bytes 262176 | tf_op jit(solution)/shard_map/ppermute | solution.py:19
  90.6 11.8 %collective-permute-done.7 = bf16[128,1024]{1,0:T(8,128)(2,1)S(1)} collective-permute-done((bf16[128,1024]{1,0:T(8,128)(2,1)S(1)}, bf16[128,1024]{1,0:T(8,128)(2,1)S(1)}, u32[]{:S(2)}, u32[]{:S(2)}) %collective-permute-start.7) | collective-permute-done | bytes 262176 | tf_op jit(solution)/shard_map/ppermute | solution.py:19
  105.3 5.9 %all-gather.2.cloned.1.call-done.wq_ref = bf16[1024,6144]{1,0:T(8,128)(2,1)} async-done(((bf16[16,6144]{1,0:T(8,128)(2,1)}), bf16[1024,6144]{1,0:T(8,128)(2,1)}) %all-gather.2.cloned.1.call-update) | async-done | bytes 12582928 | tf_op jit(solution)/shard_map/all_gather | solution.py:108
  111.2 8.8 %convolution_convert_fusion.k_ref.v_ref = bf16[1152,2048]{1,0:T(8,128)(2,1)} fusion(bf16[1152,1024]{1,0:T(8,128)(2,1)S(1)} %fusion.4, bf16[1024,6144]{1,0:T(8,128)(2,1)} %all-gather.2.cloned.1.call-done.wq_ref), kind=kOutput, calls=%fused_computation | convolution fusion | flops 4834197504 | bytes 11272192 | tf_op jit(solution)/shard_map/dot_general | solution.py:45
  120.0 11.4 %shard_map.113 = bf16[128,1024]{1,0:T(8,128)(2,1)} custom-call(bf16[128,1024]{1,0:T(8,128)(2,1)} %slice.108.x_ref, bf16[1024,6144]{1,0:T(8,128)(2,1)} %all-gather.2.cloned.1.call-done.wq_ref, bf16[1152,2048]{1,0:T(8,128)(2,1)} %convolution_convert_fusion.k_ref.v_ref, bf16[1152,2048]{1,0:T(8,128)(2,1)} %convolution_convert_fusion.k_ref.v_ref, ...), custom_call_target="tpu_custom_call" | custom-call | flops 1476395008 | bytes 7929856 | tf_op jit(solution)/shard_map/pallas_call | solution.py:74
  131.4 2.2 %convert_reduce_fusion.1 = (f32[128]{0:T(128)S(1)}, bf16[128,1024]{1,0:T(8,128)(2,1)S(1)}) fusion(bf16[128,1024]{1,0:T(8,128)(2,1)} %shard_map.113, bf16[1024,6144]{1,0:T(8,128)(2,1)} %all-gather.2.cloned.1.call-done.wq_ref, bf16[1,128,1024]{2,1,0:T(8,128)(2,1)S(1)} %copy-done, pred[128]{0:T(512)(128)(4,1)S(1)} %broadcast_compare_fusion), kind=kOutput, calls=%fused_computation.19 | convolution fusion | flops 269221760 | bytes 2884224 | tf_op jit(solution)/shard_map/dot_general | solution.py:45
  133.9 3.0 %fusion.5 = f32[128,2048]{1,0:T(8,128)S(1)} fusion(bf16[1024,6144]{1,0:T(8,128)(2,1)} %all-gather.2.cloned.1.call-done.wq_ref, bf16[128,1024]{1,0:T(8,128)(2,1)S(1)} %get-tuple-element.29, f32[1024]{0:T(1024)S(1)} %copy-done.6, f32[128]{0:T(128)S(1)} %add_rsqrt_fusion.2, f32[128]{0:T(128)S(1)} %broadcast_multiply_fusion.1), kind=kOutput, calls=%fused_computation.8 | convolution fusion | flops 537526272 | bytes 5510144 | tf_op jit(solution)/shard_map/dot_general | solution.py:45
  137.2 2.2 %collective-permute-start.8 = (bf16[4,1024]{1,0:T(4,128)(2,1)S(1)}, bf16[4,1024]{1,0:T(4,128)(2,1)S(1)}, u32[]{:S(2)}, u32[]{:S(2)}) collective-permute-start(bf16[4,1024]{1,0:T(4,128)(2,1)S(1)} %get-tuple-element.14), channel_id=1, source_target_pairs={{0,1},{1,0},{2,3},{3,2},{4,5},{5,4},{6,7},{7,6},{8,9},{9,8},{10,11... | collective-permute-start | bytes 24584 | tf_op jit(solution)/shard_map/ppermute | solution.py:139
  139.3 5.4 %collective-permute-start.9 = (bf16[4,1024]{1,0:T(4,128)(2,1)S(1)}, bf16[4,1024]{1,0:T(4,128)(2,1)S(1)}, u32[]{:S(2)}, u32[]{:S(2)}) collective-permute-start(bf16[4,1024]{1,0:T(4,128)(2,1)S(1)} %get-tuple-element.13), channel_id=1, source_target_pairs={{1,2},{2,1},{3,4},{4,3},{5,6},{6,5},{7,8},{8,7},{9,10},{10,9},{11,... | collective-permute-start | bytes 24584 | tf_op jit(solution)/shard_map/ppermute | solution.py:142
  147.1 2.5 %all-reduce.3 = (f32[1024]{0:T(1024)S(1)}, f32[1024]{0:T(1024)S(1)}) all-reduce(f32[1024]{0:T(1024)S(1)} %get-tuple-element.3, f32[1024]{0:T(1024)S(1)} %get-tuple-element.2), channel_id=1, replica_groups=mesh['call'=8,'x'=4,'y'=8,'core'=2] {'core'}, use_global_device_ids=true, to_apply=%region_11.12 | all-reduce | flops 2048 | bytes 16384 | tf_op jit(solution)/shard_map/psum | solution.py:155
  149.6 15.7 %all-reduce = (f32[1024]{0:T(1024)S(1)}, f32[1024]{0:T(1024)S(1)}) all-reduce(f32[1024]{0:T(1024)S(1)} %get-tuple-element.10, f32[1024]{0:T(1024)S(1)} %get-tuple-element.11), channel_id=1, replica_groups=mesh['call'=8,'x'=4,'y'=8,'core'=2] {'y'}, use_global_device_ids=true, to_apply=%region_12.13 | all-reduce | flops 2048 | bytes 16384 | tf_op jit(solution)/shard_map/psum | solution.py:155
  165.3 10.4 %all-reduce.2 = (f32[1024]{0:T(1024)S(1)}, f32[1024]{0:T(1024)S(1)}) all-reduce(f32[1024]{0:T(1024)S(1)} %get-tuple-element.4, f32[1024]{0:T(1024)S(1)} %get-tuple-element.5), channel_id=1, replica_groups=mesh['call'=8,'x'=4,'y'=8,'core'=2] {'x'}, use_global_device_ids=true, to_apply=%region_13.14 | all-reduce | flops 2048 | bytes 16384 | tf_op jit(solution)/shard_map/psum | solution.py:155
  175.7 20.0 %all-reduce.1 = (f32[1024]{0:T(1024)S(1)}, f32[1024]{0:T(1024)S(1)}) all-reduce(f32[1024]{0:T(1024)S(1)} %get-tuple-element.8, f32[1024]{0:T(1024)S(1)} %get-tuple-element.9), channel_id=1, replica_groups=mesh['call'=8,'x'=4,'y'=8,'core'=2] {'call'}, use_global_device_ids=true, to_apply=%region_14.15 | all-reduce | flops 2048 | bytes 16384 | tf_op jit(solution)/shard_map/psum | solution.py:155
  (57 shorter events, 17.0 us)
Async XLA Ops:
  7.2 104.0 %all-gather.2.cloned.1.call-start = ((), (), s32[]{:S(2)}) async-start(), calls=%async_computation | async-start | bytes 12779520 | tf_op jit(solution)/shard_map/all_gather | solution.py:108
  8.9 10.0 %collective-permute-start = (bf16[128,1024]{1,0:T(8,128)(2,1)}, bf16[128,1024]{1,0:T(8,128)(2,1)S(1)}, u32[]{:S(2)}, u32[]{:S(2)}) collective-permute-start(bf16[128,1024]{1,0:T(8,128)(2,1)} %bitcast.18), channel_id=1, source_target_pairs={{0,1},{1,2},{2,3},{3,4},{4,5},{5,6},{6,7},{7,8},{8,9},{9,10},{10,1... | collective-permute-start | bytes 786440 | tf_op jit(solution)/shard_map/ppermute | solution.py:19
  18.9 9.8 %collective-permute-start.1 = (bf16[128,1024]{1,0:T(8,128)(2,1)S(1)}, bf16[128,1024]{1,0:T(8,128)(2,1)S(1)}, u32[]{:S(2)}, u32[]{:S(2)}) collective-permute-start(bf16[128,1024]{1,0:T(8,128)(2,1)S(1)} %collective-permute-done), channel_id=1, source_target_pairs={{0,1},{1,2},{2,3},{3,4},{4,5},{5,6},{6,7},{7,8},{8,9},{9,10},{10,1... | collective-permute-start | bytes 786440 | tf_op jit(solution)/shard_map/ppermute | solution.py:19
  28.7 11.4 %collective-permute-start.2 = (bf16[128,1024]{1,0:T(8,128)(2,1)S(1)}, bf16[128,1024]{1,0:T(8,128)(2,1)S(1)}, u32[]{:S(2)}, u32[]{:S(2)}) collective-permute-start(bf16[128,1024]{1,0:T(8,128)(2,1)S(1)} %collective-permute-done.1), channel_id=1, source_target_pairs={{0,1},{1,2},{2,3},{3,4},{4,5},{5,6},{6,7},{7,8},{8,9},{9,10},{10,1... | collective-permute-start | bytes 786440 | tf_op jit(solution)/shard_map/ppermute | solution.py:19
  40.1 11.6 %collective-permute-start.3 = (bf16[128,1024]{1,0:T(8,128)(2,1)S(1)}, bf16[128,1024]{1,0:T(8,128)(2,1)S(1)}, u32[]{:S(2)}, u32[]{:S(2)}) collective-permute-start(bf16[128,1024]{1,0:T(8,128)(2,1)S(1)} %collective-permute-done.2), channel_id=1, source_target_pairs={{0,1},{1,2},{2,3},{3,4},{4,5},{5,6},{6,7},{7,8},{8,9},{9,10},{10,1... | collective-permute-start | bytes 786440 | tf_op jit(solution)/shard_map/ppermute | solution.py:19
  51.7 9.9 %collective-permute-start.4 = (bf16[128,1024]{1,0:T(8,128)(2,1)S(1)}, bf16[128,1024]{1,0:T(8,128)(2,1)S(1)}, u32[]{:S(2)}, u32[]{:S(2)}) collective-permute-start(bf16[128,1024]{1,0:T(8,128)(2,1)S(1)} %collective-permute-done.3), channel_id=1, source_target_pairs={{0,1},{1,2},{2,3},{3,4},{4,5},{5,6},{6,7},{7,8},{8,9},{9,10},{10,1... | collective-permute-start | bytes 786440 | tf_op jit(solution)/shard_map/ppermute | solution.py:19
  61.6 9.8 %collective-permute-start.5 = (bf16[128,1024]{1,0:T(8,128)(2,1)S(1)}, bf16[128,1024]{1,0:T(8,128)(2,1)S(1)}, u32[]{:S(2)}, u32[]{:S(2)}) collective-permute-start(bf16[128,1024]{1,0:T(8,128)(2,1)S(1)} %collective-permute-done.4), channel_id=1, source_target_pairs={{0,1},{1,2},{2,3},{3,4},{4,5},{5,6},{6,7},{7,8},{8,9},{9,10},{10,1... | collective-permute-start | bytes 786440 | tf_op jit(solution)/shard_map/ppermute | solution.py:19
  71.3 15.5 %collective-permute-start.6 = (bf16[128,1024]{1,0:T(8,128)(2,1)S(1)}, bf16[128,1024]{1,0:T(8,128)(2,1)S(1)}, u32[]{:S(2)}, u32[]{:S(2)}) collective-permute-start(bf16[128,1024]{1,0:T(8,128)(2,1)S(1)} %collective-permute-done.5), channel_id=1, source_target_pairs={{0,1},{1,2},{2,3},{3,4},{4,5},{5,6},{6,7},{7,8},{8,9},{9,10},{10,1... | collective-permute-start | bytes 786440 | tf_op jit(solution)/shard_map/ppermute | solution.py:19
  86.9 15.5 %collective-permute-start.7 = (bf16[128,1024]{1,0:T(8,128)(2,1)S(1)}, bf16[128,1024]{1,0:T(8,128)(2,1)S(1)}, u32[]{:S(2)}, u32[]{:S(2)}) collective-permute-start(bf16[128,1024]{1,0:T(8,128)(2,1)S(1)} %collective-permute-done.6), channel_id=1, source_target_pairs={{0,1},{1,2},{2,3},{3,4},{4,5},{5,6},{6,7},{7,8},{8,9},{9,10},{10,1... | collective-permute-start | bytes 786440 | tf_op jit(solution)/shard_map/ppermute | solution.py:19
  88.8 13.8 %copy-start = (bf16[1,128,1024]{2,1,0:T(8,128)(2,1)S(1)}, bf16[1,128,1024]{2,1,0:T(8,128)(2,1)}, u32[]{:S(2)}) copy-start(bf16[1,128,1024]{2,1,0:T(8,128)(2,1)} %param.10) | copy-start | bytes 786436
  102.7 1.2 copy-start.5
  131.4 2.5 %copy-start.6 = (f32[1024]{0:T(1024)S(1)}, f32[1024]{0:T(1024)}, u32[]{:S(2)}) copy-start(f32[1024]{0:T(1024)} %param.15) | copy-start | bytes 12292
  133.6 3.3 %copy-start.1 = (bf16[128,1024]{1,0:T(8,128)(2,1)}, bf16[128,1024]{1,0:T(8,128)(2,1)S(1)}, u32[]{:S(2)}) copy-start(bf16[128,1024]{1,0:T(8,128)(2,1)S(1)} %get-tuple-element.29) | copy-start | bytes 786436
  133.9 10.9 %copy-start.2 = (f32[9,1024]{1,0:T(8,128)S(1)}, f32[9,1024]{1,0:T(8,128)}, u32[]{:S(2)}) copy-start(f32[9,1024]{1,0:T(8,128)} %param.17) | copy-start | bytes 110596
  133.9 10.9 %copy-start.7 = (s32[8]{0:T(128)S(1)}, s32[8]{0:T(128)}, u32[]{:S(2)}) copy-start(s32[8]{0:T(128)} %param.11) | copy-start | bytes 100
  137.0 58.7 %copy-start.3 = (f32[1024]{0:T(1024)S(1)}, f32[1024]{0:T(1024)}, u32[]{:S(2)}) copy-start(f32[1024]{0:T(1024)} %param.19) | copy-start | bytes 12292
  137.0 58.7 %copy-start.4 = (f32[1024]{0:T(1024)S(1)}, f32[1024]{0:T(1024)}, u32[]{:S(2)}) copy-start(f32[1024]{0:T(1024)} %param.18) | copy-start | bytes 12292
  137.2 8.9 %collective-permute-start.8 = (bf16[4,1024]{1,0:T(4,128)(2,1)S(1)}, bf16[4,1024]{1,0:T(4,128)(2,1)S(1)}, u32[]{:S(2)}, u32[]{:S(2)}) collective-permute-start(bf16[4,1024]{1,0:T(4,128)(2,1)S(1)} %get-tuple-element.14), channel_id=1, source_target_pairs={{0,1},{1,0},{2,3},{3,2},{4,5},{5,4},{6,7},{7,6},{8,9},{9,8},{10,11... | collective-permute-start | bytes 24584 | tf_op jit(solution)/shard_map/ppermute | solution.py:139
  139.3 7.1 %collective-permute-start.9 = (bf16[4,1024]{1,0:T(4,128)(2,1)S(1)}, bf16[4,1024]{1,0:T(4,128)(2,1)S(1)}, u32[]{:S(2)}, u32[]{:S(2)}) collective-permute-start(bf16[4,1024]{1,0:T(4,128)(2,1)S(1)} %get-tuple-element.13), channel_id=1, source_target_pairs={{1,2},{2,1},{3,4},{4,3},{5,6},{6,5},{7,8},{8,7},{9,10},{10,9},{11,... | collective-permute-start | bytes 24584 | tf_op jit(solution)/shard_map/ppermute | solution.py:142
Sparse Core Ops, SparseCore 0:
  11.9 99.2 all-gather.1

commit v17 on v13

--- a/solution.py
+++ b/solution.py
@@ -10,7 +10,8 @@
 SPAN = 128
 LEFT = 1024
 KERNEL = 9
-TM = ("x", "y", "core")
+TM = ("x", "ya", "yb", "core")
+CALL = ("za", "zb")
 
 
 def passed_along(value, axis, steps):
@@ -98,7 +99,7 @@
     stream = frames[0]
     frame_count, model_width = stream.shape
     head_count = model_width // HEAD_DIM
-    length = lax.dynamic_index_in_dim(lengths, lax.axis_index("call"), 0, keepdims=False)
+    length = lax.dynamic_index_in_dim(lengths, lax.axis_index(CALL), 0, keepdims=False)
     first_row = lax.axis_index(TM) * frame_count
     query_pos = first_row + jnp.arange(frame_count, dtype=jnp.int32)
     frame_valid = query_pos < length
@@ -141,7 +142,7 @@
         )
     masked = jnp.where(frame_valid[:, None], depthwise, 0.0)
     moments = (jnp.sum(masked, axis=0), jnp.sum(masked * depthwise, axis=0))
-    for axis in ("core", "y", "x", "call"):
+    for axis in ("core", "yb", "ya", "x", "zb", "za"):
         moments = lax.psum(moments, axis)
     first_moment, second_moment = moments
     count_all = jnp.sum(lengths).astype(jnp.float32)
@@ -170,13 +171,13 @@
     ).reshape(-1, 3)
     grid = grid - grid[:, :1]
     assert (grid == expect[None]).all()
-    return Mesh(devices.reshape(calls, xs, ys, cores), ("call",) + TM)
+    return Mesh(devices.reshape(calls // 2, 2, xs, ys // 2, 2, cores), CALL + TM)
 
 
 def solution(mesh):
     mesh4 = physical_mesh(mesh)
     rows = P(TM, None)
-    stream = P("call", TM, None)
+    stream = P(CALL, TM, None)
     return jax.shard_map(
         on_device,
         mesh=mesh4,

time: 205 us -> 206 us (level)
  the two profiles are of different devices: /device:TPU:6 before, /device:TPU:16 now
where the time goes in v17:
time: 206 us
  waiting for transfers between devices  83.2 us (40%)
  blocking collectives  50.9 us (25%)
  starting transfers between devices  20.2 us (10%)
  between operations  15.1 us (7%)
  matrix products  14.1 us (7%)
  Pallas kernels  11.4 us (6%)
  other arithmetic  8.6 us (4%)
  local copies, waits for them, and re-layouts  2.22 us (1%)
    psum x6, blocking collectives, on_device(): moments = lax.psum(moments, axis)  50.9 us
    ppermute x8, waiting for transfers between devices, passed_along(): lax.ppermute(value, axis, [(source, source + steps) for source in range(f...  47.2 us
    all_gather x1, waiting for transfers between devices, on_device(): lax.all_gather(jnp.concatenate([w_qkv, w_out, w_pw1], axis=1), TM, axis=0...  34.3 us
    ppermute x8, starting transfers between devices, passed_along(): lax.ppermute(value, axis, [(source, source + steps) for source in range(f...  15.5 us
    dot_general x3, matrix products, contract_with(): return jnp.dot(left, rows_piece, preferred_element_type=jnp.float32)  14.1 us
    pallas_call x1, Pallas kernels, attend(): pl.pallas_call(attend_kernel, out_shape=jax.ShapeDtypeStruct((rows, width...  11.4 us
  transfers between devices with their start and end apart: 11, of which 10 were waited for; matrix products, arithmetic and copies ran while one was open for 3% of the time, Pallas kernels for 0%

profile of v17, /device:TPU:16, one launch (start us, length us, event | category | flops | bytes accessed | tf_op | source)
XLA Modules:
  0.0 205.7 jit_solution(3984788819548223086)
XLA Ops:
  8.9 1.9 collective-permute-start
  10.8 6.0 %collective-permute-done = bf16[128,1024]{1,0:T(8,128)(2,1)S(1)} collective-permute-done((bf16[128,1024]{1,0:T(8,128)(2,1)}, bf16[128,1024]{1,0:T(8,128)(2,1)S(1)}, u32[]{:S(2)}, u32[]{:S(2)}) %collective-permute-start) | collective-permute-done | bytes 262176 | tf_op jit(solution)/shard_map/ppermute | solution.py:20
  16.8 1.9 collective-permute-start.1
  18.7 5.8 %collective-permute-done.1 = bf16[128,1024]{1,0:T(8,128)(2,1)S(1)} collective-permute-done((bf16[128,1024]{1,0:T(8,128)(2,1)S(1)}, bf16[128,1024]{1,0:T(8,128)(2,1)S(1)}, u32[]{:S(2)}, u32[]{:S(2)}) %collective-permute-start.1) | collective-permute-done | bytes 262176 | tf_op jit(solution)/shard_map/ppermute | solution.py:20
  26.4 5.8 %collective-permute-done.2 = bf16[128,1024]{1,0:T(8,128)(2,1)S(1)} collective-permute-done((bf16[128,1024]{1,0:T(8,128)(2,1)S(1)}, bf16[128,1024]{1,0:T(8,128)(2,1)S(1)}, u32[]{:S(2)}, u32[]{:S(2)}) %collective-permute-start.2) | collective-permute-done | bytes 262176 | tf_op jit(solution)/shard_map/ppermute | solution.py:20
  34.1 7.4 %collective-permute-done.3 = bf16[128,1024]{1,0:T(8,128)(2,1)S(1)} collective-permute-done((bf16[128,1024]{1,0:T(8,128)(2,1)S(1)}, bf16[128,1024]{1,0:T(8,128)(2,1)S(1)}, u32[]{:S(2)}, u32[]{:S(2)}) %collective-permute-start.3) | collective-permute-done | bytes 262176 | tf_op jit(solution)/shard_map/ppermute | solution.py:20
  43.4 6.8 %collective-permute-done.4 = bf16[128,1024]{1,0:T(8,128)(2,1)S(1)} collective-permute-done((bf16[128,1024]{1,0:T(8,128)(2,1)S(1)}, bf16[128,1024]{1,0:T(8,128)(2,1)S(1)}, u32[]{:S(2)}, u32[]{:S(2)}) %collective-permute-start.4) | collective-permute-done | bytes 262176 | tf_op jit(solution)/shard_map/ppermute | solution.py:20
  52.1 6.3 %collective-permute-done.5 = bf16[128,1024]{1,0:T(8,128)(2,1)S(1)} collective-permute-done((bf16[128,1024]{1,0:T(8,128)(2,1)S(1)}, bf16[128,1024]{1,0:T(8,128)(2,1)S(1)}, u32[]{:S(2)}, u32[]{:S(2)}) %collective-permute-start.5) | collective-permute-done | bytes 262176 | tf_op jit(solution)/shard_map/ppermute | solution.py:20
  62.2 3.8 %collective-permute-done.6 = bf16[128,1024]{1,0:T(8,128)(2,1)S(1)} collective-permute-done((bf16[128,1024]{1,0:T(8,128)(2,1)S(1)}, bf16[128,1024]{1,0:T(8,128)(2,1)S(1)}, u32[]{:S(2)}, u32[]{:S(2)}) %collective-permute-start.6) | collective-permute-done | bytes 262176 | tf_op jit(solution)/shard_map/ppermute | solution.py:20
  66.1 2.1 %collective-permute-start.7 = (bf16[128,1024]{1,0:T(8,128)(2,1)S(1)}, bf16[128,1024]{1,0:T(8,128)(2,1)S(1)}, u32[]{:S(2)}, u32[]{:S(2)}) collective-permute-start(bf16[128,1024]{1,0:T(8,128)(2,1)S(1)} %collective-permute-done.6), channel_id=1, source_target_pairs={{0,1},{1,2},{2,3},{3,4},{4,5},{5,6},{6,7},{7,8},{8,9},{9,10},{10,1... | collective-permute-start | bytes 786440 | tf_op jit(solution)/shard_map/ppermute | solution.py:20
  69.9 5.4 %collective-permute-done.7 = bf16[128,1024]{1,0:T(8,128)(2,1)S(1)} collective-permute-done((bf16[128,1024]{1,0:T(8,128)(2,1)S(1)}, bf16[128,1024]{1,0:T(8,128)(2,1)S(1)}, u32[]{:S(2)}, u32[]{:S(2)}) %collective-permute-start.7) | collective-permute-done | bytes 262176 | tf_op jit(solution)/shard_map/ppermute | solution.py:20
  78.2 34.3 %all-gather.2.cloned.1.call-done.wq_ref = bf16[1024,6144]{1,0:T(8,128)(2,1)} async-done(((bf16[16,6144]{1,0:T(8,128)(2,1)}), bf16[1024,6144]{1,0:T(8,128)(2,1)}) %all-gather.2.cloned.1.call-update) | async-done | bytes 12582928 | tf_op jit(solution)/shard_map/all_gather | solution.py:108
  112.5 8.8 %convolution_convert_fusion.k_ref.v_ref = bf16[1152,2048]{1,0:T(8,128)(2,1)} fusion(bf16[1152,1024]{1,0:T(8,128)(2,1)S(1)} %fusion.4, bf16[1024,6144]{1,0:T(8,128)(2,1)} %all-gather.2.cloned.1.call-done.wq_ref), kind=kOutput, calls=%fused_computation | convolution fusion | flops 4834197504 | bytes 11272192 | tf_op jit(solution)/shard_map/dot_general | solution.py:46
  121.3 11.4 %shard_map.113 = bf16[128,1024]{1,0:T(8,128)(2,1)} custom-call(bf16[128,1024]{1,0:T(8,128)(2,1)} %slice.108.x_ref, bf16[1024,6144]{1,0:T(8,128)(2,1)} %all-gather.2.cloned.1.call-done.wq_ref, bf16[1152,2048]{1,0:T(8,128)(2,1)} %convolution_convert_fusion.k_ref.v_ref, bf16[1152,2048]{1,0:T(8,128)(2,1)} %convolution_convert_fusion.k_ref.v_ref, ...), custom_call_target="tpu_custom_call" | custom-call | flops 1476395008 | bytes 7929856 | tf_op jit(solution)/shard_map/pallas_call | solution.py:75
  132.7 2.2 %convert_reduce_fusion.1 = (f32[128]{0:T(128)S(1)}, bf16[128,1024]{1,0:T(8,128)(2,1)S(1)}) fusion(bf16[128,1024]{1,0:T(8,128)(2,1)} %shard_map.113, bf16[1024,6144]{1,0:T(8,128)(2,1)} %all-gather.2.cloned.1.call-done.wq_ref, bf16[1,128,1024]{2,1,0:T(8,128)(2,1)S(1)} %copy-done, pred[128]{0:T(512)(128)(4,1)S(1)} %broadcast_compare_fusion), kind=kOutput, calls=%fused_computation.19 | convolution fusion | flops 269221760 | bytes 2884224 | tf_op jit(solution)/shard_map/dot_general | solution.py:46
  135.3 3.0 %fusion.5 = f32[128,2048]{1,0:T(8,128)S(1)} fusion(bf16[1024,6144]{1,0:T(8,128)(2,1)} %all-gather.2.cloned.1.call-done.wq_ref, bf16[128,1024]{1,0:T(8,128)(2,1)S(1)} %get-tuple-element.31, f32[1024]{0:T(1024)S(1)} %copy-done.6, f32[128]{0:T(128)S(1)} %add_rsqrt_fusion.2, f32[128]{0:T(128)S(1)} %broadcast_multiply_fusion.1), kind=kOutput, calls=%fused_computation.8 | convolution fusion | flops 537526272 | bytes 5510144 | tf_op jit(solution)/shard_map/dot_general | solution.py:46
  138.5 2.7 %collective-permute-start.9 = (bf16[4,1024]{1,0:T(4,128)(2,1)S(1)}, bf16[4,1024]{1,0:T(4,128)(2,1)S(1)}, u32[]{:S(2)}, u32[]{:S(2)}) collective-permute-start(bf16[4,1024]{1,0:T(4,128)(2,1)S(1)} %get-tuple-element.18), channel_id=1, source_target_pairs={{1,0},{2,1},{3,2},{4,3},{5,4},{6,5},{7,6},{8,7},{9,8},{10,9},{11,1... | collective-permute-start | bytes 24584 | tf_op jit(solution)/shard_map/ppermute | solution.py:32
  141.2 1.9 collective-permute-start.8
  146.9 2.5 %all-reduce.3 = (f32[1024]{0:T(1024)S(1)}, f32[1024]{0:T(1024)S(1)}) all-reduce(f32[1024]{0:T(1024)S(1)} %get-tuple-element.3, f32[1024]{0:T(1024)S(1)} %get-tuple-element.2), channel_id=1, replica_groups=mesh['za'=4,'zb'=2,'x'=4,'ya'=4,'yb'=2,'core'=2] {'core'}, use_global_device_ids=true, to_apply=%region_13.14 | all-reduce | flops 2048 | bytes 16384 | tf_op jit(solution)/shard_map/psum | solution.py:146
  149.4 5.0 %all-reduce.4 = (f32[1024]{0:T(1024)S(1)}, f32[1024]{0:T(1024)S(1)}) all-reduce(f32[1024]{0:T(1024)S(1)} %get-tuple-element.10, f32[1024]{0:T(1024)S(1)} %get-tuple-element.11), channel_id=1, replica_groups=mesh['za'=4,'zb'=2,'x'=4,'ya'=4,'yb'=2,'core'=2] {'yb'}, use_global_device_ids=true, to_apply=%region_14.15 | all-reduce | flops 2048 | bytes 16384 | tf_op jit(solution)/shard_map/psum | solution.py:146
  154.4 11.8 %all-reduce = (f32[1024]{0:T(1024)S(1)}, f32[1024]{0:T(1024)S(1)}) all-reduce(f32[1024]{0:T(1024)S(1)} %get-tuple-element.12, f32[1024]{0:T(1024)S(1)} %get-tuple-element.13), channel_id=1, replica_groups=mesh['za'=4,'zb'=2,'x'=4,'ya'=4,'yb'=2,'core'=2] {'ya'}, use_global_device_ids=true, to_apply=%region_15.16 | all-reduce | flops 2048 | bytes 16384 | tf_op jit(solution)/shard_map/psum | solution.py:146
  166.2 11.3 %all-reduce.1 = (f32[1024]{0:T(1024)S(1)}, f32[1024]{0:T(1024)S(1)}) all-reduce(f32[1024]{0:T(1024)S(1)} %get-tuple-element.4, f32[1024]{0:T(1024)S(1)} %get-tuple-element.5), channel_id=1, replica_groups=mesh['za'=4,'zb'=2,'x'=4,'ya'=4,'yb'=2,'core'=2] {'x'}, use_global_device_ids=true, to_apply=%region_16.17 | all-reduce | flops 2048 | bytes 16384 | tf_op jit(solution)/shard_map/psum | solution.py:146
  177.5 5.0 %all-reduce.5 = (f32[1024]{0:T(1024)S(1)}, f32[1024]{0:T(1024)S(1)}) all-reduce(f32[1024]{0:T(1024)S(1)} %get-tuple-element.6, f32[1024]{0:T(1024)S(1)} %get-tuple-element.7), channel_id=1, replica_groups=mesh['za'=4,'zb'=2,'x'=4,'ya'=4,'yb'=2,'core'=2] {'zb'}, use_global_device_ids=true, to_apply=%region_17.18 | all-reduce | flops 2048 | bytes 16384 | tf_op jit(solution)/shard_map/psum | solution.py:146
  182.5 15.3 %all-reduce.2 = (f32[1024]{0:T(1024)S(1)}, f32[1024]{0:T(1024)S(1)}) all-reduce(f32[1024]{0:T(1024)S(1)} %get-tuple-element.14, f32[1024]{0:T(1024)S(1)} %get-tuple-element.15), channel_id=1, replica_groups=mesh['za'=4,'zb'=2,'x'=4,'ya'=4,'yb'=2,'core'=2] {'za'}, use_global_device_ids=true, to_apply=%region_18.19 | all-reduce | flops 2048 | bytes 16384 | tf_op jit(solution)/shard_map/psum | solution.py:146
  (58 shorter events, 22.1 us)
Async XLA Ops:
  7.2 105.4 %all-gather.2.cloned.1.call-start = ((), (), s32[]{:S(2)}) async-start(), calls=%async_computation | async-start | bytes 12779520 | tf_op jit(solution)/shard_map/all_gather | solution.py:108
  8.9 7.9 %collective-permute-start = (bf16[128,1024]{1,0:T(8,128)(2,1)}, bf16[128,1024]{1,0:T(8,128)(2,1)S(1)}, u32[]{:S(2)}, u32[]{:S(2)}) collective-permute-start(bf16[128,1024]{1,0:T(8,128)(2,1)} %bitcast.18), channel_id=1, source_target_pairs={{0,1},{1,2},{2,3},{3,4},{4,5},{5,6},{6,7},{7,8},{8,9},{9,10},{10,1... | collective-permute-start | bytes 786440 | tf_op jit(solution)/shard_map/ppermute | solution.py:20
  16.8 7.7 %collective-permute-start.1 = (bf16[128,1024]{1,0:T(8,128)(2,1)S(1)}, bf16[128,1024]{1,0:T(8,128)(2,1)S(1)}, u32[]{:S(2)}, u32[]{:S(2)}) collective-permute-start(bf16[128,1024]{1,0:T(8,128)(2,1)S(1)} %collective-permute-done), channel_id=1, source_target_pairs={{0,1},{1,2},{2,3},{3,4},{4,5},{5,6},{6,7},{7,8},{8,9},{9,10},{10,1... | collective-permute-start | bytes 786440 | tf_op jit(solution)/shard_map/ppermute | solution.py:20
  24.5 7.7 %collective-permute-start.2 = (bf16[128,1024]{1,0:T(8,128)(2,1)S(1)}, bf16[128,1024]{1,0:T(8,128)(2,1)S(1)}, u32[]{:S(2)}, u32[]{:S(2)}) collective-permute-start(bf16[128,1024]{1,0:T(8,128)(2,1)S(1)} %collective-permute-done.1), channel_id=1, source_target_pairs={{0,1},{1,2},{2,3},{3,4},{4,5},{5,6},{6,7},{7,8},{8,9},{9,10},{10,1... | collective-permute-start | bytes 786440 | tf_op jit(solution)/shard_map/ppermute | solution.py:20
  32.1 9.3 %collective-permute-start.3 = (bf16[128,1024]{1,0:T(8,128)(2,1)S(1)}, bf16[128,1024]{1,0:T(8,128)(2,1)S(1)}, u32[]{:S(2)}, u32[]{:S(2)}) collective-permute-start(bf16[128,1024]{1,0:T(8,128)(2,1)S(1)} %collective-permute-done.2), channel_id=1, source_target_pairs={{0,1},{1,2},{2,3},{3,4},{4,5},{5,6},{6,7},{7,8},{8,9},{9,10},{10,1... | collective-permute-start | bytes 786440 | tf_op jit(solution)/shard_map/ppermute | solution.py:20
  41.5 8.7 %collective-permute-start.4 = (bf16[128,1024]{1,0:T(8,128)(2,1)S(1)}, bf16[128,1024]{1,0:T(8,128)(2,1)S(1)}, u32[]{:S(2)}, u32[]{:S(2)}) collective-permute-start(bf16[128,1024]{1,0:T(8,128)(2,1)S(1)} %collective-permute-done.3), channel_id=1, source_target_pairs={{0,1},{1,2},{2,3},{3,4},{4,5},{5,6},{6,7},{7,8},{8,9},{9,10},{10,1... | collective-permute-start | bytes 786440 | tf_op jit(solution)/shard_map/ppermute | solution.py:20
  50.2 8.2 %collective-permute-start.5 = (bf16[128,1024]{1,0:T(8,128)(2,1)S(1)}, bf16[128,1024]{1,0:T(8,128)(2,1)S(1)}, u32[]{:S(2)}, u32[]{:S(2)}) collective-permute-start(bf16[128,1024]{1,0:T(8,128)(2,1)S(1)} %collective-permute-done.4), channel_id=1, source_target_pairs={{0,1},{1,2},{2,3},{3,4},{4,5},{5,6},{6,7},{7,8},{8,9},{9,10},{10,1... | collective-permute-start | bytes 786440 | tf_op jit(solution)/shard_map/ppermute | solution.py:20
  58.4 7.7 %collective-permute-start.6 = (bf16[128,1024]{1,0:T(8,128)(2,1)S(1)}, bf16[128,1024]{1,0:T(8,128)(2,1)S(1)}, u32[]{:S(2)}, u32[]{:S(2)}) collective-permute-start(bf16[128,1024]{1,0:T(8,128)(2,1)S(1)} %collective-permute-done.5), channel_id=1, source_target_pairs={{0,1},{1,2},{2,3},{3,4},{4,5},{5,6},{6,7},{7,8},{8,9},{9,10},{10,1... | collective-permute-start | bytes 786440 | tf_op jit(solution)/shard_map/ppermute | solution.py:20
  66.1 9.3 %collective-permute-start.7 = (bf16[128,1024]{1,0:T(8,128)(2,1)S(1)}, bf16[128,1024]{1,0:T(8,128)(2,1)S(1)}, u32[]{:S(2)}, u32[]{:S(2)}) collective-permute-start(bf16[128,1024]{1,0:T(8,128)(2,1)S(1)} %collective-permute-done.6), channel_id=1, source_target_pairs={{0,1},{1,2},{2,3},{3,4},{4,5},{5,6},{6,7},{7,8},{8,9},{9,10},{10,1... | collective-permute-start | bytes 786440 | tf_op jit(solution)/shard_map/ppermute | solution.py:20
  68.2 7.4 %copy-start = (bf16[1,128,1024]{2,1,0:T(8,128)(2,1)S(1)}, bf16[1,128,1024]{2,1,0:T(8,128)(2,1)}, u32[]{:S(2)}) copy-start(bf16[1,128,1024]{2,1,0:T(8,128)(2,1)} %param.10) | copy-start | bytes 786436
  75.6 1.2 copy-start.5
  132.7 2.5 %copy-start.6 = (f32[1024]{0:T(1024)S(1)}, f32[1024]{0:T(1024)}, u32[]{:S(2)}) copy-start(f32[1024]{0:T(1024)} %param.15) | copy-start | bytes 12292
  135.0 3.3 %copy-start.1 = (bf16[128,1024]{1,0:T(8,128)(2,1)}, bf16[128,1024]{1,0:T(8,128)(2,1)S(1)}, u32[]{:S(2)}) copy-start(bf16[128,1024]{1,0:T(8,128)(2,1)S(1)} %get-tuple-element.31) | copy-start | bytes 786436
  135.2 7.9 %copy-start.2 = (f32[9,1024]{1,0:T(8,128)S(1)}, f32[9,1024]{1,0:T(8,128)}, u32[]{:S(2)}) copy-start(f32[9,1024]{1,0:T(8,128)} %param.17) | copy-start | bytes 110596
  135.2 8.0 %copy-start.7 = (s32[8]{0:T(128)S(1)}, s32[8]{0:T(128)}, u32[]{:S(2)}) copy-start(s32[8]{0:T(128)} %param.11) | copy-start | bytes 100
  138.3 59.6 %copy-start.3 = (f32[1024]{0:T(1024)S(1)}, f32[1024]{0:T(1024)}, u32[]{:S(2)}) copy-start(f32[1024]{0:T(1024)} %param.19) | copy-start | bytes 12292
  138.3 59.6 %copy-start.4 = (f32[1024]{0:T(1024)S(1)}, f32[1024]{0:T(1024)}, u32[]{:S(2)}) copy-start(f32[1024]{0:T(1024)} %param.18) | copy-start | bytes 12292
  138.5 6.0 %collective-permute-start.9 = (bf16[4,1024]{1,0:T(4,128)(2,1)S(1)}, bf16[4,1024]{1,0:T(4,128)(2,1)S(1)}, u32[]{:S(2)}, u32[]{:S(2)}) collective-permute-start(bf16[4,1024]{1,0:T(4,128)(2,1)S(1)} %get-tuple-element.18), channel_id=1, source_target_pairs={{1,0},{2,1},{3,2},{4,3},{5,4},{6,5},{7,6},{8,7},{9,8},{10,9},{11,1... | collective-permute-start | bytes 24584 | tf_op jit(solution)/shard_map/ppermute | solution.py:32
  141.2 5.0 %collective-permute-start.8 = (bf16[4,1024]{1,0:T(4,128)(2,1)S(1)}, bf16[4,1024]{1,0:T(4,128)(2,1)S(1)}, u32[]{:S(2)}, u32[]{:S(2)}) collective-permute-start(bf16[4,1024]{1,0:T(4,128)(2,1)S(1)} %get-tuple-element.17), channel_id=1, source_target_pairs={{0,1},{1,2},{2,3},{3,4},{4,5},{5,6},{6,7},{7,8},{8,9},{9,10},{10,1... | collective-permute-start | bytes 24584 | tf_op jit(solution)/shard_map/ppermute | solution.py:30
Sparse Core Ops, SparseCore 0:
  11.9 100.6 all-gather.1
